TPU v7x, 32 devices: a whole 2x2x4 slice. The times are simulated.
32 devices in a mesh: sub: 2 (over x), section: 4 (over y, core), iface: 4 (over z).
Axes of the slice: x: 2, y: 2, z: 4, core: 2. Of those that a mesh axis runs over, the one named last changes fastest.
Arguments:
- previous: float32 [4, 512, 128], P('section', ('sub', 'iface')), may hold values from -6 to 6
- right_side: float32 [4, 512, 128], P('section', ('sub', 'iface')), may hold values from -96 to 96
- precond: bfloat16 [4, 8, 64, 64], P('section', ('sub', 'iface')), may hold values from -1 to 1
- couple: bfloat16 [4, 8, 64, 64], P('section', ('sub', 'iface')), may hold values from -1.5 to 1.5
- block_ids: int32 [4, 8, 8], P('section', ('sub', 'iface')), may hold values from 0 to 7, as said below
- iface_matrix: bfloat16 [4, 8, 512, 512], P('section', ('sub', 'iface')), may hold values from -1 to 2.5
- interior_coupling: bfloat16 [4, 8, 2560, 512], P('section', ('sub', 'iface')), may hold values from -0.08300781 to 0.08300781
- inv_interior: bfloat16 [4, 8, 2560, 2560], P('section', ('sub', 'iface')), may hold values from -1 to 2
Outputs:
- temperatures: float32 [4, 512, 128], P('section', ('sub', 'iface'))
Inputs may be any that keep to these rules, and one draw needn't show every extreme that they name: `block_ids`: each subdomain lists 8 different blocks, and each block of a section is listed by exactly 8 subdomains.
All inputs are finite; a program needn't handle non-finite values.
Results may differ from a plain program's by a relative error of at most 0.0018.
Values may be sent and summed in bfloat16 or wider, within the bound.
No kernel may reach another device: no remote copies, remote signals or barrier semaphores. Data moves between devices by JAX's collectives and lax.ppermute only.
A program may use at most 128 MiB of HBM per device.

v0:
```python
import jax
import jax.numpy as jnp
from jax import lax
from jax.sharding import PartitionSpec as P

SWEEPS = 4


def from_behind(block, axis, distance):
    devices = range(lax.axis_size(axis))
    route = [(i - distance, i) for i in devices if i - distance in devices]
    return lax.ppermute(block, axis, route)


def body(
    previous, right_side, precond, couple, block_ids, iface_matrix, interior_coupling, inv_interior
):
    highest = lax.Precision.HIGHEST
    section_pos = lax.axis_index("section")
    section_count = lax.axis_size("section")
    owners = lax.axis_size(("sub", "iface"))
    block_list = block_ids[0, 0]
    boundary = iface_matrix[0, 0]
    coupled = interior_coupling[0, 0]
    inverse = inv_interior[0, 0]
    bnd_width = boundary.shape[0]
    block_nodes = previous.shape[1]
    load_count = previous.shape[2]
    pick_count = block_list.shape[0]
    spread = (block_list[:, None] == jnp.arange(owners, dtype=jnp.int32)[None, :]).astype(
        jnp.float32
    )
    precond_f = precond[0].astype(jnp.float32)
    couple_f = couple[0].astype(jnp.float32)
    temps_now = previous
    for sweep_index in range(SWEEPS):
        gathered = lax.all_gather(
            temps_now.astype(jnp.bfloat16), ("sub", "iface"), axis=0, tiled=True
        )
        sub_rows = jnp.take(gathered, block_list, axis=0).reshape(bnd_width, load_count)
        interior_in = jnp.dot(coupled, sub_rows, preferred_element_type=jnp.float32).astype(
            jnp.bfloat16
        )
        interior_out = jnp.dot(inverse, interior_in, preferred_element_type=jnp.float32).astype(
            jnp.bfloat16
        )
        pulled_back = lax.dot_general(
            coupled, interior_out, (((0,), (0,)), ((), ())), preferred_element_type=jnp.float32
        )
        sub_term = jnp.dot(boundary, sub_rows, preferred_element_type=jnp.float32) - pulled_back
        terms = jnp.einsum(
            "kn,kil->nil",
            spread,
            sub_term.reshape(pick_count, block_nodes, load_count),
            precision=highest,
        )
        assembled = lax.psum_scatter(terms, ("sub", "iface"), scatter_dimension=0, tiled=True)
        upper_term = jnp.einsum("bij,bil->bjl", couple_f, temps_now, precision=highest)
        from_above = from_behind(upper_term.astype(jnp.bfloat16), "section", -1).astype(
            upper_term.dtype
        )
        base_resid = right_side - assembled - from_above
        current = temps_now
        for turn_index in range(section_count):
            residual_now = base_resid
            if turn_index > 0:
                below_value = from_behind(current.astype(jnp.bfloat16), "section", 1).astype(
                    current.dtype
                )
                residual_now = base_resid - jnp.einsum(
                    "bij,bjl->bil", couple_f, below_value, precision=highest
                )
            updated = current + jnp.einsum(
                "bij,bjl->bil", precond_f, residual_now, precision=highest
            )
            current = jnp.where(section_pos == turn_index, updated, current)
        temps_now = current
    return temps_now


def solution(mesh):
    in_specs = (
        P("section", ("sub", "iface"), None),
        P("section", ("sub", "iface"), None),
        P("section", ("sub", "iface"), None, None),
        P("section", ("sub", "iface"), None, None),
        P("section", ("sub", "iface"), None),
        P("section", ("sub", "iface"), None, None),
        P("section", ("sub", "iface"), None, None),
        P("section", ("sub", "iface"), None, None),
    )
    out_specs = P("section", ("sub", "iface"), None)
    return jax.shard_map(body, mesh=mesh, in_specs=in_specs, out_specs=out_specs, check_vma=False)
```

profile of v0, /device:TPU:1, one launch (start us, length us, event | category | flops | bytes accessed | tf_op | source)
XLA Modules:
  0.0 516.7 jit_solution(11397847396877441020)
XLA Ops:
  8.8 25.8 %all_gather.12 = bf16[8,64,128]{2,1,0:T(8,128)(2,1)S(1)} all-gather(bf16[1,64,128]{2,1,0:T(8,128)(2,1)S(1)} %convert_element_type.140), channel_id=1, replica_groups=mesh['sub'=2,'section'=4,'iface'=4] {'sub','iface'}, dimensions={0}, use_global_device_ids=true | all-gather | bytes 147456 | tf_op jit(solution)/shard_map/all_gather | solution.py:37
  35.3 10.8 %fusion.8 = bf16[128,2560]{1,0:T(8,128)(2,1)} fusion(bf16[1,1,2560,2560]{3,2,1,0:T(8,128)(2,1)} %param.17, bf16[512,128]{1,0:T(8,128)(2,1)S(1)} %bitcast.529, bf16[1,1,2560,512]{3,2,1,0:T(8,128)(2,1)S(1)} %copy-done), kind=kOutput, calls=%fused_computation.12 | convolution fusion | flops 2013921280 | bytes 16515072 | tf_op jit(solution)/shard_map/dot_general | solution.py:44
  51.3 8.6 %collective-permute-start = (bf16[1,64,128]{2,1,0:T(8,128)(2,1)S(1)}, bf16[1,64,128]{2,1,0:T(8,128)(2,1)S(1)}, u32[]{:S(2)}, u32[]{:S(2)}) collective-permute-start(bf16[1,64,128]{2,1,0:T(8,128)(2,1)S(1)} %fusion.92), channel_id=1, source_target_pairs={{4,0},{8,4},{12,8},{5,1},{9,5},{13,9},{6,2},{10,6},{14,10},{7,3},{... | collective-permute-start | bytes 49160 | tf_op jit(solution)/shard_map/ppermute | solution.py:12
  59.9 2.5 collective-permute-done
  62.5 55.1 %reduce-scatter.5.cloned.1.call-done = f32[1,64,128]{2,1,0:T(8,128)} async-done(((f32[8,64,128]{2,1,0:T(8,128)}), f32[1,64,128]{2,1,0:T(8,128)}) %reduce-scatter.5.cloned.1.call-update) | async-done | bytes 32784 | tf_op jit(solution)/shard_map/reduce_scatter | solution.py:57
  118.5 5.6 %collective-permute-start.1 = (bf16[1,64,128]{2,1,0:T(8,128)(2,1)S(1)}, bf16[1,64,128]{2,1,0:T(8,128)(2,1)S(1)}, u32[]{:S(2)}, u32[]{:S(2)}) collective-permute-start(bf16[1,64,128]{2,1,0:T(8,128)(2,1)S(1)} %get-tuple-element.6), channel_id=1, source_target_pairs={{0,4},{4,8},{8,12},{1,5},{5,9},{9,13},{2,6},{6,10},{10,14},{3,7},{... | collective-permute-start | bytes 49160 | tf_op jit(solution)/shard_map/ppermute | solution.py:12
  125.2 4.2 collective-permute-start.2
  130.6 4.2 collective-permute-start.3
  135.9 24.6 %all_gather.13 = bf16[8,64,128]{2,1,0:T(8,128)(2,1)S(1)} all-gather(bf16[1,64,128]{2,1,0:T(8,128)(2,1)S(1)} %get-tuple-element.12), channel_id=1, replica_groups=mesh['sub'=2,'section'=4,'iface'=4] {'sub','iface'}, dimensions={0}, use_global_device_ids=true | all-gather | bytes 147456 | tf_op jit(solution)/shard_map/all_gather | solution.py:37
  161.2 10.8 %fusion.11 = bf16[128,2560]{1,0:T(8,128)(2,1)} fusion(bf16[1,1,2560,2560]{3,2,1,0:T(8,128)(2,1)} %param.17, bf16[512,128]{1,0:T(8,128)(2,1)S(1)} %bitcast.531, bf16[1,1,2560,512]{3,2,1,0:T(8,128)(2,1)S(1)} %copy-done), kind=kOutput, calls=%fused_computation.13 | convolution fusion | flops 2013921280 | bytes 16515072 | tf_op jit(solution)/shard_map/dot_general | solution.py:44
  177.1 6.3 %collective-permute-start.4 = (bf16[1,64,128]{2,1,0:T(8,128)(2,1)S(1)}, bf16[1,64,128]{2,1,0:T(8,128)(2,1)S(1)}, u32[]{:S(2)}, u32[]{:S(2)}) collective-permute-start(bf16[1,64,128]{2,1,0:T(8,128)(2,1)S(1)} %fusion.93), channel_id=1, source_target_pairs={{4,0},{8,4},{12,8},{5,1},{9,5},{13,9},{6,2},{10,6},{14,10},{7,3},{... | collective-permute-start | bytes 49160 | tf_op jit(solution)/shard_map/ppermute | solution.py:12
  183.3 5.5 %collective-permute-done.4 = bf16[1,64,128]{2,1,0:T(8,128)(2,1)S(1)} collective-permute-done((bf16[1,64,128]{2,1,0:T(8,128)(2,1)S(1)}, bf16[1,64,128]{2,1,0:T(8,128)(2,1)S(1)}, u32[]{:S(2)}, u32[]{:S(2)}) %collective-permute-start.4) | collective-permute-done | bytes 16416 | tf_op jit(solution)/shard_map/ppermute | solution.py:12
  188.9 53.2 %reduce-scatter.7.cloned.1.call-done = f32[1,64,128]{2,1,0:T(8,128)} async-done(((f32[8,64,128]{2,1,0:T(8,128)}), f32[1,64,128]{2,1,0:T(8,128)}) %reduce-scatter.7.cloned.1.call-update) | async-done | bytes 32784 | tf_op jit(solution)/shard_map/reduce_scatter | solution.py:57
  243.0 5.6 %collective-permute-start.5 = (bf16[1,64,128]{2,1,0:T(8,128)(2,1)S(1)}, bf16[1,64,128]{2,1,0:T(8,128)(2,1)S(1)}, u32[]{:S(2)}, u32[]{:S(2)}) collective-permute-start(bf16[1,64,128]{2,1,0:T(8,128)(2,1)S(1)} %get-tuple-element.14), channel_id=1, source_target_pairs={{0,4},{4,8},{8,12},{1,5},{5,9},{9,13},{2,6},{6,10},{10,14},{3,7},{... | collective-permute-start | bytes 49160 | tf_op jit(solution)/shard_map/ppermute | solution.py:12
  249.7 4.2 collective-permute-start.6
  255.1 4.2 collective-permute-start.7
  260.4 24.9 %all_gather.14 = bf16[8,64,128]{2,1,0:T(8,128)(2,1)S(1)} all-gather(bf16[1,64,128]{2,1,0:T(8,128)(2,1)S(1)} %get-tuple-element.20), channel_id=1, replica_groups=mesh['sub'=2,'section'=4,'iface'=4] {'sub','iface'}, dimensions={0}, use_global_device_ids=true | all-gather | bytes 147456 | tf_op jit(solution)/shard_map/all_gather | solution.py:37
  285.9 10.8 %fusion.14 = bf16[128,2560]{1,0:T(8,128)(2,1)} fusion(bf16[1,1,2560,2560]{3,2,1,0:T(8,128)(2,1)} %param.17, bf16[512,128]{1,0:T(8,128)(2,1)S(1)} %bitcast.533, bf16[1,1,2560,512]{3,2,1,0:T(8,128)(2,1)S(1)} %copy-done), kind=kOutput, calls=%fused_computation.14 | convolution fusion | flops 2013921280 | bytes 16515072 | tf_op jit(solution)/shard_map/dot_general | solution.py:44
  301.8 6.2 %collective-permute-start.8 = (bf16[1,64,128]{2,1,0:T(8,128)(2,1)S(1)}, bf16[1,64,128]{2,1,0:T(8,128)(2,1)S(1)}, u32[]{:S(2)}, u32[]{:S(2)}) collective-permute-start(bf16[1,64,128]{2,1,0:T(8,128)(2,1)S(1)} %fusion.94), channel_id=1, source_target_pairs={{4,0},{8,4},{12,8},{5,1},{9,5},{13,9},{6,2},{10,6},{14,10},{7,3},{... | collective-permute-start | bytes 49160 | tf_op jit(solution)/shard_map/ppermute | solution.py:12
  308.0 5.6 %collective-permute-done.8 = bf16[1,64,128]{2,1,0:T(8,128)(2,1)S(1)} collective-permute-done((bf16[1,64,128]{2,1,0:T(8,128)(2,1)S(1)}, bf16[1,64,128]{2,1,0:T(8,128)(2,1)S(1)}, u32[]{:S(2)}, u32[]{:S(2)}) %collective-permute-start.8) | collective-permute-done | bytes 16416 | tf_op jit(solution)/shard_map/ppermute | solution.py:12
  313.6 53.2 %reduce-scatter.9.cloned.1.call-done = f32[1,64,128]{2,1,0:T(8,128)} async-done(((f32[8,64,128]{2,1,0:T(8,128)}), f32[1,64,128]{2,1,0:T(8,128)}) %reduce-scatter.9.cloned.1.call-update) | async-done | bytes 32784 | tf_op jit(solution)/shard_map/reduce_scatter | solution.py:57
  367.7 5.6 %collective-permute-start.9 = (bf16[1,64,128]{2,1,0:T(8,128)(2,1)S(1)}, bf16[1,64,128]{2,1,0:T(8,128)(2,1)S(1)}, u32[]{:S(2)}, u32[]{:S(2)}) collective-permute-start(bf16[1,64,128]{2,1,0:T(8,128)(2,1)S(1)} %get-tuple-element.22), channel_id=1, source_target_pairs={{0,4},{4,8},{8,12},{1,5},{5,9},{9,13},{2,6},{6,10},{10,14},{3,7},{... | collective-permute-start | bytes 49160 | tf_op jit(solution)/shard_map/ppermute | solution.py:12
  374.4 4.2 collective-permute-start.10
  379.7 4.2 collective-permute-start.11
  385.1 24.7 %all_gather.15 = bf16[8,64,128]{2,1,0:T(8,128)(2,1)S(1)} all-gather(bf16[1,64,128]{2,1,0:T(8,128)(2,1)S(1)} %get-tuple-element.28), channel_id=1, replica_groups=mesh['sub'=2,'section'=4,'iface'=4] {'sub','iface'}, dimensions={0}, use_global_device_ids=true | all-gather | bytes 147456 | tf_op jit(solution)/shard_map/all_gather | solution.py:37
  410.4 10.8 %fusion.17 = bf16[128,2560]{1,0:T(8,128)(2,1)} fusion(bf16[1,1,2560,2560]{3,2,1,0:T(8,128)(2,1)} %param.17, bf16[512,128]{1,0:T(8,128)(2,1)S(1)} %bitcast.527, bf16[1,1,2560,512]{3,2,1,0:T(8,128)(2,1)S(1)} %copy-done), kind=kOutput, calls=%fused_computation.15 | convolution fusion | flops 2013921280 | bytes 16515072 | tf_op jit(solution)/shard_map/dot_general | solution.py:44
  426.3 6.2 %collective-permute-start.12 = (bf16[1,64,128]{2,1,0:T(8,128)(2,1)S(1)}, bf16[1,64,128]{2,1,0:T(8,128)(2,1)S(1)}, u32[]{:S(2)}, u32[]{:S(2)}) collective-permute-start(bf16[1,64,128]{2,1,0:T(8,128)(2,1)S(1)} %fusion.95), channel_id=1, source_target_pairs={{4,0},{8,4},{12,8},{5,1},{9,5},{13,9},{6,2},{10,6},{14,10},{7,3},{... | collective-permute-start | bytes 49160 | tf_op jit(solution)/shard_map/ppermute | solution.py:12
  432.4 5.6 %collective-permute-done.12 = bf16[1,64,128]{2,1,0:T(8,128)(2,1)S(1)} collective-permute-done((bf16[1,64,128]{2,1,0:T(8,128)(2,1)S(1)}, bf16[1,64,128]{2,1,0:T(8,128)(2,1)S(1)}, u32[]{:S(2)}, u32[]{:S(2)}) %collective-permute-start.12) | collective-permute-done | bytes 16416 | tf_op jit(solution)/shard_map/ppermute | solution.py:12
  438.0 53.3 %reduce-scatter.11.cloned.1.call-done = f32[1,64,128]{2,1,0:T(8,128)} async-done(((f32[8,64,128]{2,1,0:T(8,128)}), f32[1,64,128]{2,1,0:T(8,128)}) %reduce-scatter.11.cloned.1.call-update) | async-done | bytes 32784 | tf_op jit(solution)/shard_map/reduce_scatter | solution.py:57
  492.2 5.5 %collective-permute-start.13 = (bf16[1,64,128]{2,1,0:T(8,128)(2,1)S(1)}, bf16[1,64,128]{2,1,0:T(8,128)(2,1)S(1)}, u32[]{:S(2)}, u32[]{:S(2)}) collective-permute-start(bf16[1,64,128]{2,1,0:T(8,128)(2,1)S(1)} %get-tuple-element.30), channel_id=1, source_target_pairs={{0,4},{4,8},{8,12},{1,5},{5,9},{9,13},{2,6},{6,10},{10,14},{3,7},{... | collective-permute-start | bytes 49160 | tf_op jit(solution)/shard_map/ppermute | solution.py:12
  498.9 4.2 collective-permute-start.14
  504.2 4.2 collective-permute-start.15
  (102 shorter events, 43.0 us)
Async XLA Ops:
  6.5 28.7 %copy-start = (bf16[1,1,2560,512]{3,2,1,0:T(8,128)(2,1)S(1)}, bf16[1,1,2560,512]{3,2,1,0:T(8,128)(2,1)}, u32[]{:S(2)}) copy-start(bf16[1,1,2560,512]{3,2,1,0:T(8,128)(2,1)} %param.16) | copy-start | bytes 7864324
  6.5 111.1 %reduce-scatter.5.cloned.1.call-start = ((), (), s32[]{:S(2)}) async-start(), calls=%async_computation.4 | async-start | bytes 294912 | tf_op jit(solution)/shard_map/reduce_scatter | solution.py:57
  46.1 1.7 copy-start.1
  46.1 3.8 copy-start.6
  46.1 5.0 copy-start.2
  46.1 5.0 copy-start.5
  46.1 71.5 %copy-start.4 = (f32[1,64,128]{2,1,0:T(8,128)S(1)}, f32[1,64,128]{2,1,0:T(8,128)}, u32[]{:S(2)}) copy-start(f32[1,64,128]{2,1,0:T(8,128)} %param.11) | copy-start | bytes 98308
  46.1 72.3 %copy-start.3 = (bf16[1,1,64,64]{3,2,1,0:T(8,128)(2,1)S(1)}, bf16[1,1,64,64]{3,2,1,0:T(8,128)(2,1)}, u32[]{:S(2)}) copy-start(bf16[1,1,64,64]{3,2,1,0:T(8,128)(2,1)} %param.12) | copy-start | bytes 24580
  51.0 191.1 %reduce-scatter.7.cloned.1.call-start = ((), (), s32[]{:S(2)}) async-start(), calls=%async_computation.5 | async-start | bytes 294912 | tf_op jit(solution)/shard_map/reduce_scatter | solution.py:57
  51.3 11.2 %collective-permute-start = (bf16[1,64,128]{2,1,0:T(8,128)(2,1)S(1)}, bf16[1,64,128]{2,1,0:T(8,128)(2,1)S(1)}, u32[]{:S(2)}, u32[]{:S(2)}) collective-permute-start(bf16[1,64,128]{2,1,0:T(8,128)(2,1)S(1)} %fusion.92), channel_id=1, source_target_pairs={{4,0},{8,4},{12,8},{5,1},{9,5},{13,9},{6,2},{10,6},{14,10},{7,3},{... | collective-permute-start | bytes 49160 | tf_op jit(solution)/shard_map/ppermute | solution.py:12
  118.5 6.4 %collective-permute-start.1 = (bf16[1,64,128]{2,1,0:T(8,128)(2,1)S(1)}, bf16[1,64,128]{2,1,0:T(8,128)(2,1)S(1)}, u32[]{:S(2)}, u32[]{:S(2)}) collective-permute-start(bf16[1,64,128]{2,1,0:T(8,128)(2,1)S(1)} %get-tuple-element.6), channel_id=1, source_target_pairs={{0,4},{4,8},{8,12},{1,5},{5,9},{9,13},{2,6},{6,10},{10,14},{3,7},{... | collective-permute-start | bytes 49160 | tf_op jit(solution)/shard_map/ppermute | solution.py:12
  125.2 5.1 collective-permute-start.2
  130.6 5.1 collective-permute-start.3
  176.8 190.0 %reduce-scatter.9.cloned.1.call-start = ((), (), s32[]{:S(2)}) async-start(), calls=%async_computation.6 | async-start | bytes 294912 | tf_op jit(solution)/shard_map/reduce_scatter | solution.py:57
  177.1 11.8 %collective-permute-start.4 = (bf16[1,64,128]{2,1,0:T(8,128)(2,1)S(1)}, bf16[1,64,128]{2,1,0:T(8,128)(2,1)S(1)}, u32[]{:S(2)}, u32[]{:S(2)}) collective-permute-start(bf16[1,64,128]{2,1,0:T(8,128)(2,1)S(1)} %fusion.93), channel_id=1, source_target_pairs={{4,0},{8,4},{12,8},{5,1},{9,5},{13,9},{6,2},{10,6},{14,10},{7,3},{... | collective-permute-start | bytes 49160 | tf_op jit(solution)/shard_map/ppermute | solution.py:12
  243.0 6.4 %collective-permute-start.5 = (bf16[1,64,128]{2,1,0:T(8,128)(2,1)S(1)}, bf16[1,64,128]{2,1,0:T(8,128)(2,1)S(1)}, u32[]{:S(2)}, u32[]{:S(2)}) collective-permute-start(bf16[1,64,128]{2,1,0:T(8,128)(2,1)S(1)} %get-tuple-element.14), channel_id=1, source_target_pairs={{0,4},{4,8},{8,12},{1,5},{5,9},{9,13},{2,6},{6,10},{10,14},{3,7},{... | collective-permute-start | bytes 49160 | tf_op jit(solution)/shard_map/ppermute | solution.py:12
  249.7 5.1 collective-permute-start.6
  255.1 5.1 collective-permute-start.7
  301.6 189.7 %reduce-scatter.11.cloned.1.call-start = ((), (), s32[]{:S(2)}) async-start(), calls=%async_computation.7 | async-start | bytes 294912 | tf_op jit(solution)/shard_map/reduce_scatter | solution.py:57
  301.8 11.8 %collective-permute-start.8 = (bf16[1,64,128]{2,1,0:T(8,128)(2,1)S(1)}, bf16[1,64,128]{2,1,0:T(8,128)(2,1)S(1)}, u32[]{:S(2)}, u32[]{:S(2)}) collective-permute-start(bf16[1,64,128]{2,1,0:T(8,128)(2,1)S(1)} %fusion.94), channel_id=1, source_target_pairs={{4,0},{8,4},{12,8},{5,1},{9,5},{13,9},{6,2},{10,6},{14,10},{7,3},{... | collective-permute-start | bytes 49160 | tf_op jit(solution)/shard_map/ppermute | solution.py:12
  367.7 6.4 %collective-permute-start.9 = (bf16[1,64,128]{2,1,0:T(8,128)(2,1)S(1)}, bf16[1,64,128]{2,1,0:T(8,128)(2,1)S(1)}, u32[]{:S(2)}, u32[]{:S(2)}) collective-permute-start(bf16[1,64,128]{2,1,0:T(8,128)(2,1)S(1)} %get-tuple-element.22), channel_id=1, source_target_pairs={{0,4},{4,8},{8,12},{1,5},{5,9},{9,13},{2,6},{6,10},{10,14},{3,7},{... | collective-permute-start | bytes 49160 | tf_op jit(solution)/shard_map/ppermute | solution.py:12
  374.4 5.1 collective-permute-start.10
  379.7 5.1 collective-permute-start.11
  426.3 11.7 %collective-permute-start.12 = (bf16[1,64,128]{2,1,0:T(8,128)(2,1)S(1)}, bf16[1,64,128]{2,1,0:T(8,128)(2,1)S(1)}, u32[]{:S(2)}, u32[]{:S(2)}) collective-permute-start(bf16[1,64,128]{2,1,0:T(8,128)(2,1)S(1)} %fusion.95), channel_id=1, source_target_pairs={{4,0},{8,4},{12,8},{5,1},{9,5},{13,9},{6,2},{10,6},{14,10},{7,3},{... | collective-permute-start | bytes 49160 | tf_op jit(solution)/shard_map/ppermute | solution.py:12
  492.2 6.4 %collective-permute-start.13 = (bf16[1,64,128]{2,1,0:T(8,128)(2,1)S(1)}, bf16[1,64,128]{2,1,0:T(8,128)(2,1)S(1)}, u32[]{:S(2)}, u32[]{:S(2)}) collective-permute-start(bf16[1,64,128]{2,1,0:T(8,128)(2,1)S(1)} %get-tuple-element.30), channel_id=1, source_target_pairs={{0,4},{4,8},{8,12},{1,5},{5,9},{9,13},{2,6},{6,10},{10,14},{3,7},{... | collective-permute-start | bytes 49160 | tf_op jit(solution)/shard_map/ppermute | solution.py:12
  498.9 5.1 collective-permute-start.14
  504.2 5.1 collective-permute-start.15
Sparse Core Ops, SparseCore 0:
  51.2 66.3 reduce-scatter.4
  176.9 65.1 reduce-scatter.6
  301.7 65.0 reduce-scatter.8
  426.2 65.0 reduce-scatter.10
where the time goes:
time: 518 us; the launch traced here: 517 us
  waiting for transfers between devices  244 us (47%)
  blocking collectives  99.9 us (19%)
  starting transfers between devices  83.2 us (16%)
  matrix products  60.5 us (12%)
  between operations  13.6 us (3%)
  local copies, waits for them, and re-layouts  9.61 us (2%)
  other arithmetic  5.62 us (1%)
    reduce_scatter x4, waiting for transfers between devices, body(): lax.psum_scatter(terms, ('sub', 'iface'), scatter_dimension=0, tiled=True)  215 us
    all_gather x4, blocking collectives, body(): lax.all_gather(temps_now.astype(jnp.bfloat16), ('sub', 'iface'), axis=0,...  99.9 us
    ppermute x16, starting transfers between devices, from_behind(): return lax.ppermute(block, axis, route)  83.1 us
    dot_general x4, matrix products, body(): jnp.dot(inverse, interior_in, preferred_element_type=jnp.float32)  43.1 us
    ppermute x16, waiting for transfers between devices, from_behind(): return lax.ppermute(block, axis, route)  29.3 us
  transfers between devices with their start and end apart: 20, of which 20 were waited for; matrix products, arithmetic and copies ran while one was open for 0% of the time, Pallas kernels for 0%

commit v1 on v0

v1 whole, which is shorter than its diff:
```python
import jax
import jax.numpy as jnp
from jax import lax
from jax.sharding import PartitionSpec as P

SWEEPS = 4
OWNERS = ("sub", "iface")


def split_bf16(value):
    high = value.astype(jnp.bfloat16)
    low = (value - high.astype(jnp.float32)).astype(jnp.bfloat16)
    return high, low


def gather_along(block, axis):
    count = lax.axis_size(axis)
    copies = jnp.broadcast_to(block[None], (count,) + block.shape)
    return lax.all_to_all(copies, axis, 0, 0, tiled=True)


def schur_rows(block_list, boundary, coupled, inverse, owners):
    picks = block_list.shape[0]
    block_nodes = boundary.shape[0] // picks
    solved = jnp.dot(inverse, coupled, preferred_element_type=jnp.float32)
    solved_hi, solved_lo = split_bf16(solved)
    contract = (((0,), (0,)), ((), ()))
    pulled = lax.dot_general(coupled, solved_hi, contract, preferred_element_type=jnp.float32)
    pulled = pulled + lax.dot_general(coupled, solved_lo, contract, preferred_element_type=jnp.float32)
    schur = boundary.astype(jnp.float32) - pulled
    listed = block_list[None, :] == jnp.arange(owners, dtype=jnp.int32)[:, None]
    slot = jnp.where(jnp.any(listed, axis=1), jnp.argmax(listed, axis=1), picks)
    padded = jnp.pad(
        schur.reshape(picks, block_nodes, picks, block_nodes), ((0, 1), (0, 0), (0, 1), (0, 0))
    )
    spread = jnp.take(jnp.take(padded, slot, axis=0), slot, axis=2)
    spread = spread.reshape(owners, block_nodes, owners * block_nodes)
    received = lax.all_to_all(spread, OWNERS, 0, 0, tiled=True)
    return jnp.sum(received, axis=0)


def chain_weights(precond_f, couple_f):
    highest = lax.Precision.HIGHEST
    sections, block_nodes = precond_f.shape[0], precond_f.shape[1]
    step = jnp.einsum("gij,gjk->gik", precond_f, couple_f, precision=highest)
    eye = jnp.eye(block_nodes, dtype=jnp.float32)
    zero = jnp.zeros_like(eye)
    rows = []
    for h in range(sections):
        if h == 0:
            row = [eye] + [zero] * (sections - 1)
        else:
            row = [-jnp.dot(step[h], rows[h - 1][k], precision=highest) for k in range(h)]
            row = row + [eye] + [zero] * (sections - 1 - h)
        rows.append(row)
    return jnp.stack([jnp.stack(row) for row in rows])


def body(
    previous, right_side, precond, couple, block_ids, iface_matrix, interior_coupling, inv_interior
):
    highest = lax.Precision.HIGHEST
    section_pos = lax.axis_index("section")
    sections = lax.axis_size("section")
    owners = lax.axis_size(OWNERS)
    block_nodes = previous.shape[1]
    load_count = previous.shape[2]
    nodes = owners * block_nodes

    tables = jnp.concatenate(
        [previous[0], precond[0, 0].astype(jnp.float32), couple[0, 0].astype(jnp.float32)],
        axis=1,
    )
    tables = gather_along(tables, "section")
    start_all = tables[:, :, :load_count]
    precond_all = tables[:, :, load_count : load_count + block_nodes]
    couple_all = tables[:, :, load_count + block_nodes :]
    weights = chain_weights(precond_all, couple_all)
    above_pos = jnp.minimum(section_pos + 1, sections - 1)
    has_above = section_pos + 1 < sections
    weights_mine = weights[section_pos]
    weights_above = weights[above_pos]
    precond_mine = precond[0, 0].astype(jnp.float32)
    couple_above = couple_all[above_pos]

    rows = schur_rows(
        block_ids[0, 0], iface_matrix[0, 0], interior_coupling[0, 0], inv_interior[0, 0], owners
    )
    rows_hi, rows_lo = split_bf16(rows)

    temps_mine = previous[0]
    temps_above = start_all[above_pos]
    rhs = right_side[0]
    for sweep_index in range(SWEEPS):
        rounded = gather_along(temps_mine.astype(jnp.bfloat16), OWNERS).reshape(nodes, load_count)
        assembled = jnp.dot(rows_hi, rounded, preferred_element_type=jnp.float32) + jnp.dot(
            rows_lo, rounded, preferred_element_type=jnp.float32
        )
        from_above = jnp.einsum("ij,il->jl", couple_above, temps_above, precision=highest)
        from_above = jnp.where(has_above, from_above, 0.0)
        residual = rhs - assembled - from_above
        update = temps_mine + jnp.dot(precond_mine, residual, precision=highest)
        updates = gather_along(update, "section")
        temps_mine = jnp.einsum("kij,kjl->il", weights_mine, updates, precision=highest)
        temps_above = jnp.einsum("kij,kjl->il", weights_above, updates, precision=highest)
    return temps_mine[None]


def solution(mesh):
    in_specs = (
        P("section", OWNERS, None),
        P("section", OWNERS, None),
        P("section", OWNERS, None, None),
        P("section", OWNERS, None, None),
        P("section", OWNERS, None),
        P("section", OWNERS, None, None),
        P("section", OWNERS, None, None),
        P("section", OWNERS, None, None),
    )
    out_specs = P("section", OWNERS, None)
    return jax.shard_map(body, mesh=mesh, in_specs=in_specs, out_specs=out_specs, check_vma=False)
```

time: 518 us -> 185 us (0.36)
  waiting for transfers between devices: 244 us -> 46.2 us
  blocking collectives: 99.9 us -> 24.4 us
  starting transfers between devices: 83.2 us -> 29.4 us
  matrix products: 60.5 us -> 34.8 us
  local copies, waits for them, and re-layouts: 9.61 us -> 32.7 us
  between operations: 13.6 us -> 0.31 us
  other arithmetic: 5.62 us -> 14.1 us
    reduce_scatter x4 -> x0, waiting for transfers between devices: 215 us -> none  [body(): lax.psum_scatter(terms, ('sub', 'iface'), scatter_dimension=0, tiled=True)]
    all_gather x4 -> x0, blocking collectives: 99.9 us -> none  [body(): lax.all_gather(temps_now.astype(jnp.bfloat16), ('sub', 'iface'), axis=0,...]
    ppermute x16 -> x0, starting transfers between devices: 83.1 us -> none  [from_behind(): return lax.ppermute(block, axis, route)]
    all_to_all x0 -> x7, waiting for transfers between devices: none -> 46.2 us  [the longest x6 23.8 us: gather_along(): return lax.all_to_all(copies, axis, 0, 0, tiled=True)]
    all_to_all x0 -> x7, starting transfers between devices: none -> 29.4 us  [the longest x6 23.3 us: gather_along(): return lax.all_to_all(copies, axis, 0, 0, tiled=True)]
    ppermute x16 -> x0, waiting for transfers between devices: 29.3 us -> none  [from_behind(): return lax.ppermute(block, axis, route)]
    dot_general x48 -> x33, matrix products: 60.5 us -> 34.8 us  [the longest x1 9.56 us: schur_rows(): solved = jnp.dot(inverse, coupled, preferred_element_type=jnp.float32)]
    all_to_all x0 -> x3, blocking collectives: none -> 24.4 us  [gather_along(): return lax.all_to_all(copies, axis, 0, 0, tiled=True)]
  transfers between devices with their start and end apart: 20 -> 7, of which waited for: 20 -> 6; matrix products, arithmetic and copies ran while one was open for 0% -> 33% of each run, Pallas kernels for 0% -> 0%
where the time goes in v1:
time: 185 us; the launch traced here: 182 us
  waiting for transfers between devices  46.2 us (25%)
  matrix products  34.8 us (19%)
  local copies, waits for them, and re-layouts  32.7 us (18%)
  starting transfers between devices  29.4 us (16%)
  blocking collectives  24.4 us (13%)
  other arithmetic  14.1 us (8%)
    all_to_all x3, blocking collectives, gather_along(): return lax.all_to_all(copies, axis, 0, 0, tiled=True)  24.4 us
    all_to_all x6, waiting for transfers between devices, gather_along(): return lax.all_to_all(copies, axis, 0, 0, tiled=True)  23.8 us
    all_to_all x6, starting transfers between devices, gather_along(): return lax.all_to_all(copies, axis, 0, 0, tiled=True)  23.3 us
    all_to_all x1, waiting for transfers between devices, schur_rows(): received = lax.all_to_all(spread, OWNERS, 0, 0, tiled=True)  22.4 us
    gather x4, local copies, waits for them, and re-layouts, schur_rows(): spread = jnp.take(jnp.take(padded, slot, axis=0), slot, axis=2)  14.4 us
    dot_general x1, matrix products, schur_rows(): solved = jnp.dot(inverse, coupled, preferred_element_type=jnp.float32)  9.56 us
    all_to_all x1, starting transfers between devices, schur_rows(): received = lax.all_to_all(spread, OWNERS, 0, 0, tiled=True)  6.11 us
    select_n x2, other arithmetic, schur_rows(): spread = jnp.take(jnp.take(padded, slot, axis=0), slot, axis=2)  5.92 us
  transfers between devices with their start and end apart: 7, of which 6 were waited for; matrix products, arithmetic and copies ran while one was open for 33% of the time, Pallas kernels for 0%

profile of v1, /device:TPU:1, one launch (start us, length us, event | category | flops | bytes accessed | tf_op | source)
XLA Modules:
  0.0 182.0 jit_solution(2213237922667810406)
XLA Ops:
  2.5 4.3 %all-to-all-start = ((f32[4,64,256]{2,1,0:T(8,128)}), f32[4,64,256]{2,1,0:T(8,128)S(1)}, u32[]{:S(2)}, u32[]{:S(2)}) async-start(f32[4,64,256]{2,1,0:T(8,128)} %broadcast_in_dim.97), calls=%async_computation | async-start | bytes 524288 | tf_op jit(solution)/shard_map/all_to_all | solution.py:19
  8.8 9.6 %fusion = f32[2560,512]{1,0:T(8,128)S(1)} fusion(bf16[1,1,2560,2560]{3,2,1,0:T(8,128)(2,1)} %param.15, bf16[1,1,2560,512]{3,2,1,0:T(8,128)(2,1)S(1)} %copy-done), kind=kOutput, calls=%fused_computation.2 | convolution fusion | flops 6710886400 | bytes 20971520 | tf_op jit(solution)/shard_map/dot_general | solution.py:25
  18.4 2.3 %copy-done.1 = f32[2560,512]{1,0:T(8,128)} copy-done((f32[2560,512]{1,0:T(8,128)}, f32[2560,512]{1,0:T(8,128)S(1)}, u32[]{:S(2)}) %copy-start.1) | copy-done | bytes 5242904
  20.7 2.6 %fusion.2 = f32[512,512]{1,0:T(8,128)} fusion(f32[2560,512]{1,0:T(8,128)S(1)} %fusion, bf16[1,1,2560,512]{3,2,1,0:T(8,128)(2,1)S(1)} %copy-done), kind=kOutput, calls=%fused_computation.5 | convolution fusion | flops 1347420160 | bytes 8912896 | tf_op jit(solution)/shard_map/dot_general | solution.py:29
  24.5 5.3 %fusion.19 = f32[512,512]{0,1:T(8,128)} fusion(f32[512,512]{1,0:T(8,128)} %fusion.2, bf16[1,1,2560,512]{3,2,1,0:T(8,128)(2,1)S(1)} %copy-done, f32[2560,512]{1,0:T(8,128)} %copy-done.1, bf16[1,1,512,512]{2,3,1,0:T(8,128)(2,1)S(1)} %copy.15), kind=kOutput, calls=%fused_computation.14 | convolution fusion | flops 1344274432 | bytes 10485760 | tf_op jit(solution)/shard_map/dot_general | solution.py:28
  29.8 2.7 %reshape.50 = f32[8,64,8,64]{1,0,3,2:T(8,128)} reshape(f32[512,512]{0,1:T(8,128)} %fusion.19) | data formatting | bytes 2097152 | tf_op jit(solution)/shard_map/reshape | solution.py:34
  32.6 2.9 %copy.16 = f32[8,64,8,64]{3,1,2,0:T(8,128)} copy(f32[8,64,8,64]{1,0,3,2:T(8,128)} %reshape.50) | data formatting | bytes 2097152 | tf_op jit(solution)/shard_map/reshape | solution.py:34
  35.5 3.5 %pad.4 = f32[9,64,9,64]{3,1,2,0:T(8,128)} pad(f32[8,64,8,64]{3,1,2,0:T(8,128)} %copy.16, f32[]{:T(128)} %constant.19.clone.1), padding=0_1x0_0x0_1x0_0 | pad | bytes 2375684 | tf_op jit(solution)/shard_map/jit(_pad)/pad | solution.py:33
  39.0 3.9 %gather_fusion = f32[8,64,9,64]{3,1,2,0:T(8,128)} fusion(f32[9,64,9,64]{3,1,2,0:T(8,128)} %pad.4, s32[1024]{0:T(1024)S(1)} %pad_clamp_fusion), kind=kCustom, calls=%fused_computation | custom fusion | bytes 2359328 | tf_op jit(solution)/shard_map/jit(_take)/gather | solution.py:36
  42.9 3.6 %broadcast_select_fusion = f32[8,64,9,64]{3,1,2,0:T(8,128)} fusion(f32[8,64,9,64]{3,1,2,0:T(8,128)} %gather_fusion, pred[8]{0:T(512)(128)(4,1)S(1)} %get-tuple-element.9), kind=kLoop, calls=%fused_computation.15 | loop fusion | flops 294912 | bytes 2359304 | tf_op jit(solution)/shard_map/jit(_take)/select_n | solution.py:36
  46.4 3.7 %gather_fusion.1 = f32[8,8,64,64]{3,2,1,0:T(8,128)} fusion(f32[8,64,9,64]{3,1,2,0:T(8,128)} %broadcast_select_fusion, s32[1024]{0:T(1024)S(1)} %pad_clamp_fusion), kind=kCustom, calls=%fused_computation.1 | custom fusion | bytes 2097184 | tf_op jit(solution)/shard_map/jit(_take)/gather | solution.py:36
  50.1 4.1 %copy.17 = f32[8,64,8,64]{3,2,1,0:T(8,128)} copy(f32[8,64,8,64]{3,1,0,2:T(8,128)} %bitcast.182) | data formatting | bytes 2097152 | tf_op jit(solution)/shard_map/jit(_take)/gather | solution.py:36
  54.2 2.7 %gather.12 = f32[8,64,512]{2,1,0:T(8,128)} reshape(f32[8,64,8,64]{3,2,1,0:T(8,128)} %copy.17) | data formatting | bytes 2097152 | tf_op jit(solution)/shard_map/jit(_take)/gather | solution.py:36
  57.1 2.4 %broadcast_select_fusion.1 = f32[8,64,512]{2,1,0:T(8,128)} fusion(f32[8,64,512]{2,1,0:T(8,128)} %gather.12, pred[512]{0:T(512)(128)(4,1)S(1)} %broadcast_in_dim.100), kind=kLoop, calls=%fused_computation.57 | loop fusion | flops 262144 | bytes 2097664 | tf_op jit(solution)/shard_map/jit(_take)/select_n | solution.py:36
  59.5 6.1 %all-to-all-start.1 = ((f32[8,64,512]{2,1,0:T(8,128)}), f32[8,64,512]{2,1,0:T(8,128)}, u32[]{:S(2)}, u32[]{:S(2)}) async-start(f32[8,64,512]{2,1,0:T(8,128)} %broadcast_select_fusion.1), calls=%async_computation.1 | async-start | bytes 2097152 | tf_op jit(solution)/shard_map/all_to_all | solution.py:38
  68.3 1.4 maximum_bitcast_fusion
  69.7 22.4 %all-to-all-done.1 = f32[8,64,512]{2,1,0:T(8,128)} async-done(((f32[8,64,512]{2,1,0:T(8,128)}), f32[8,64,512]{2,1,0:T(8,128)}, u32[]{:S(2)}, u32[]{:S(2)}) %all-to-all-start.1) | async-done | bytes 1048608 | tf_op jit(solution)/shard_map/all_to_all | solution.py:38
  92.1 1.4 broadcast_in_dim.107
  93.5 3.4 %all-to-all-start.2 = ((bf16[8,64,128]{2,1,0:T(8,128)(2,1)}), bf16[8,64,128]{2,1,0:T(8,128)(2,1)S(1)}, u32[]{:S(2)}, u32[]{:S(2)}) async-start(bf16[8,64,128]{2,1,0:T(8,128)(2,1)} %broadcast_in_dim.107), calls=%async_computation.2 | async-start | bytes 262144 | tf_op jit(solution)/shard_map/all_to_all | solution.py:19
  96.9 1.3 reduce_sum.9
  98.2 5.0 %all-to-all-done.2 = bf16[8,64,128]{2,1,0:T(8,128)(2,1)S(1)} async-done(((bf16[8,64,128]{2,1,0:T(8,128)(2,1)}), bf16[8,64,128]{2,1,0:T(8,128)(2,1)S(1)}, u32[]{:S(2)}, u32[]{:S(2)}) %all-to-all-start.2) | async-done | bytes 131104 | tf_op jit(solution)/shard_map/all_to_all | solution.py:19
  104.6 5.6 %all-to-all-start.3 = ((f32[4,64,128]{2,1,0:T(8,128)}), f32[4,64,128]{2,1,0:T(8,128)S(1)}, u32[]{:S(2)}, u32[]{:S(2)}) async-start(f32[4,64,128]{2,1,0:T(8,128)} %broadcast_in_dim.109), calls=%async_computation.3 | async-start | bytes 262144 | tf_op jit(solution)/shard_map/all_to_all | solution.py:19
  111.2 2.5 %all-to-all-done.3 = f32[4,64,128]{2,1,0:T(8,128)S(1)} async-done(((f32[4,64,128]{2,1,0:T(8,128)}), f32[4,64,128]{2,1,0:T(8,128)S(1)}, u32[]{:S(2)}, u32[]{:S(2)}) %all-to-all-start.3) | async-done | bytes 131104 | tf_op jit(solution)/shard_map/all_to_all | solution.py:19
  115.3 3.4 %all-to-all-start.4 = ((bf16[8,64,128]{2,1,0:T(8,128)(2,1)}), bf16[8,64,128]{2,1,0:T(8,128)(2,1)S(1)}, u32[]{:S(2)}, u32[]{:S(2)}) async-start(bf16[8,64,128]{2,1,0:T(8,128)(2,1)} %broadcast_in_dim.110), calls=%async_computation.4 | async-start | bytes 262144 | tf_op jit(solution)/shard_map/all_to_all | solution.py:19
  119.6 5.4 %all-to-all-done.4 = bf16[8,64,128]{2,1,0:T(8,128)(2,1)S(1)} async-done(((bf16[8,64,128]{2,1,0:T(8,128)(2,1)}), bf16[8,64,128]{2,1,0:T(8,128)(2,1)S(1)}, u32[]{:S(2)}, u32[]{:S(2)}) %all-to-all-start.4) | async-done | bytes 131104 | tf_op jit(solution)/shard_map/all_to_all | solution.py:19
  128.1 8.1 %all_to_all.50 = f32[4,64,128]{2,1,0:T(8,128)S(1)} all-to-all(f32[4,64,128]{2,1,0:T(8,128)S(1)} %broadcast_in_dim.111), channel_id=1, replica_groups=mesh['sub'=2,'section'=4,'iface'=4] {'section'}, dimensions={0} | all-to-all | bytes 262144 | tf_op jit(solution)/shard_map/all_to_all | solution.py:19
  137.8 3.4 %all-to-all-start.6 = ((bf16[8,64,128]{2,1,0:T(8,128)(2,1)}), bf16[8,64,128]{2,1,0:T(8,128)(2,1)S(1)}, u32[]{:S(2)}, u32[]{:S(2)}) async-start(bf16[8,64,128]{2,1,0:T(8,128)(2,1)} %broadcast_in_dim.112), calls=%async_computation.6 | async-start | bytes 262144 | tf_op jit(solution)/shard_map/all_to_all | solution.py:19
  142.1 5.4 %all-to-all-done.6 = bf16[8,64,128]{2,1,0:T(8,128)(2,1)S(1)} async-done(((bf16[8,64,128]{2,1,0:T(8,128)(2,1)}), bf16[8,64,128]{2,1,0:T(8,128)(2,1)S(1)}, u32[]{:S(2)}, u32[]{:S(2)}) %all-to-all-start.6) | async-done | bytes 131104 | tf_op jit(solution)/shard_map/all_to_all | solution.py:19
  150.5 8.1 %all_to_all.51 = f32[4,64,128]{2,1,0:T(8,128)S(1)} all-to-all(f32[4,64,128]{2,1,0:T(8,128)S(1)} %broadcast_in_dim.113), channel_id=1, replica_groups=mesh['sub'=2,'section'=4,'iface'=4] {'section'}, dimensions={0} | all-to-all | bytes 262144 | tf_op jit(solution)/shard_map/all_to_all | solution.py:19
  160.2 3.4 %all-to-all-start.8 = ((bf16[8,64,128]{2,1,0:T(8,128)(2,1)}), bf16[8,64,128]{2,1,0:T(8,128)(2,1)S(1)}, u32[]{:S(2)}, u32[]{:S(2)}) async-start(bf16[8,64,128]{2,1,0:T(8,128)(2,1)} %broadcast_in_dim.114), calls=%async_computation.8 | async-start | bytes 262144 | tf_op jit(solution)/shard_map/all_to_all | solution.py:19
  164.5 5.4 %all-to-all-done.8 = bf16[8,64,128]{2,1,0:T(8,128)(2,1)S(1)} async-done(((bf16[8,64,128]{2,1,0:T(8,128)(2,1)}), bf16[8,64,128]{2,1,0:T(8,128)(2,1)S(1)}, u32[]{:S(2)}, u32[]{:S(2)}) %all-to-all-start.8) | async-done | bytes 131104 | tf_op jit(solution)/shard_map/all_to_all | solution.py:19
  173.0 8.1 %all_to_all.52 = f32[4,64,128]{2,1,0:T(8,128)S(1)} all-to-all(f32[4,64,128]{2,1,0:T(8,128)S(1)} %broadcast_in_dim.115), channel_id=1, replica_groups=mesh['sub'=2,'section'=4,'iface'=4] {'section'}, dimensions={0} | all-to-all | bytes 262144 | tf_op jit(solution)/shard_map/all_to_all | solution.py:19
  (68 shorter events, 28.4 us)
Async XLA Ops:
  0.0 8.8 %copy-start = (bf16[1,1,2560,512]{3,2,1,0:T(8,128)(2,1)S(1)}, bf16[1,1,2560,512]{3,2,1,0:T(8,128)(2,1)}, u32[]{:S(2)}) copy-start(bf16[1,1,2560,512]{3,2,1,0:T(8,128)(2,1)} %param.14) | copy-start | bytes 7864324
  2.5 57.0 %all-to-all-start = ((f32[4,64,256]{2,1,0:T(8,128)}), f32[4,64,256]{2,1,0:T(8,128)S(1)}, u32[]{:S(2)}, u32[]{:S(2)}) async-start(f32[4,64,256]{2,1,0:T(8,128)} %broadcast_in_dim.97), calls=%async_computation | async-start | bytes 524288 | tf_op jit(solution)/shard_map/all_to_all | solution.py:19
  18.4 2.3 %copy-start.1 = (f32[2560,512]{1,0:T(8,128)}, f32[2560,512]{1,0:T(8,128)S(1)}, u32[]{:S(2)}) copy-start(f32[2560,512]{1,0:T(8,128)S(1)} %fusion) | copy-start | bytes 15728644
  56.9 9.3 %copy-start.5 = (f32[1,64,128]{2,1,0:T(8,128)S(1)}, f32[1,64,128]{2,1,0:T(8,128)}, u32[]{:S(2)}) copy-start(f32[1,64,128]{2,1,0:T(8,128)} %param.8) | copy-start | bytes 98308
  59.5 32.6 %all-to-all-start.1 = ((f32[8,64,512]{2,1,0:T(8,128)}), f32[8,64,512]{2,1,0:T(8,128)}, u32[]{:S(2)}, u32[]{:S(2)}) async-start(f32[8,64,512]{2,1,0:T(8,128)} %broadcast_select_fusion.1), calls=%async_computation.1 | async-start | bytes 2097152 | tf_op jit(solution)/shard_map/all_to_all | solution.py:38
  65.6 37.8 %copy-start.2 = (f32[1,64,128]{2,1,0:T(8,128)S(1)}, f32[1,64,128]{2,1,0:T(8,128)}, u32[]{:S(2)}) copy-start(f32[1,64,128]{2,1,0:T(8,128)} %param.9) | copy-start | bytes 98308
  65.6 38.2 %copy-start.4 = (bf16[1,1,64,64]{3,2,1,0:T(8,128)(2,1)S(1)}, bf16[1,1,64,64]{3,2,1,0:T(8,128)(2,1)}, u32[]{:S(2)}) copy-start(bf16[1,1,64,64]{3,2,1,0:T(8,128)(2,1)} %param.10) | copy-start | bytes 24580
  66.9 43.2 %copy-start.3 = (f32[4,64,64]{2,1,0:T(8,128)}, f32[4,64,64]{2,1,0:T(8,128)S(1)}, u32[]{:S(2)}) copy-start(f32[4,64,64]{2,1,0:T(8,128)S(1)} %slice.32) | copy-start | bytes 196612
  93.5 9.7 %all-to-all-start.2 = ((bf16[8,64,128]{2,1,0:T(8,128)(2,1)}), bf16[8,64,128]{2,1,0:T(8,128)(2,1)S(1)}, u32[]{:S(2)}, u32[]{:S(2)}) async-start(bf16[8,64,128]{2,1,0:T(8,128)(2,1)} %broadcast_in_dim.107), calls=%async_computation.2 | async-start | bytes 262144 | tf_op jit(solution)/shard_map/all_to_all | solution.py:19
  104.6 9.2 %all-to-all-start.3 = ((f32[4,64,128]{2,1,0:T(8,128)}), f32[4,64,128]{2,1,0:T(8,128)S(1)}, u32[]{:S(2)}, u32[]{:S(2)}) async-start(f32[4,64,128]{2,1,0:T(8,128)} %broadcast_in_dim.109), calls=%async_computation.3 | async-start | bytes 262144 | tf_op jit(solution)/shard_map/all_to_all | solution.py:19
  115.3 9.7 %all-to-all-start.4 = ((bf16[8,64,128]{2,1,0:T(8,128)(2,1)}), bf16[8,64,128]{2,1,0:T(8,128)(2,1)S(1)}, u32[]{:S(2)}, u32[]{:S(2)}) async-start(bf16[8,64,128]{2,1,0:T(8,128)(2,1)} %broadcast_in_dim.110), calls=%async_computation.4 | async-start | bytes 262144 | tf_op jit(solution)/shard_map/all_to_all | solution.py:19
  137.8 9.7 %all-to-all-start.6 = ((bf16[8,64,128]{2,1,0:T(8,128)(2,1)}), bf16[8,64,128]{2,1,0:T(8,128)(2,1)S(1)}, u32[]{:S(2)}, u32[]{:S(2)}) async-start(bf16[8,64,128]{2,1,0:T(8,128)(2,1)} %broadcast_in_dim.112), calls=%async_computation.6 | async-start | bytes 262144 | tf_op jit(solution)/shard_map/all_to_all | solution.py:19
  160.2 9.7 %all-to-all-start.8 = ((bf16[8,64,128]{2,1,0:T(8,128)(2,1)}), bf16[8,64,128]{2,1,0:T(8,128)(2,1)S(1)}, u32[]{:S(2)}, u32[]{:S(2)}) async-start(bf16[8,64,128]{2,1,0:T(8,128)(2,1)} %broadcast_in_dim.114), calls=%async_computation.8 | async-start | bytes 262144 | tf_op jit(solution)/shard_map/all_to_all | solution.py:19

commit v2 on v1

--- a/solution.py
+++ b/solution.py
@@ -8,9 +8,8 @@
 
 
 def split_bf16(value):
-    high = value.astype(jnp.bfloat16)
-    low = (value - high.astype(jnp.float32)).astype(jnp.bfloat16)
-    return high, low
+    high = lax.reduce_precision(value, exponent_bits=8, mantissa_bits=7)
+    return high.astype(jnp.bfloat16), (value - high).astype(jnp.bfloat16)
 
 
 def gather_along(block, axis):
@@ -28,12 +27,18 @@
     pulled = lax.dot_general(coupled, solved_hi, contract, preferred_element_type=jnp.float32)
     pulled = pulled + lax.dot_general(coupled, solved_lo, contract, preferred_element_type=jnp.float32)
     schur = boundary.astype(jnp.float32) - pulled
-    listed = block_list[None, :] == jnp.arange(owners, dtype=jnp.int32)[:, None]
-    slot = jnp.where(jnp.any(listed, axis=1), jnp.argmax(listed, axis=1), picks)
-    padded = jnp.pad(
-        schur.reshape(picks, block_nodes, picks, block_nodes), ((0, 1), (0, 0), (0, 1), (0, 0))
-    )
-    spread = jnp.take(jnp.take(padded, slot, axis=0), slot, axis=2)
+    node = jnp.arange(owners * block_nodes, dtype=jnp.int32)
+    sub = jnp.arange(picks * block_nodes, dtype=jnp.int32)
+    target = jnp.repeat(block_list, block_nodes) * block_nodes + sub % block_nodes
+    place = (target[:, None] == node[None, :]).astype(jnp.bfloat16)
+    schur_hi, schur_lo = split_bf16(schur)
+    contract_rows = (((0,), (0,)), ((), ()))
+    spread = jnp.zeros((owners * block_nodes, owners * block_nodes), jnp.float32)
+    for part in (schur_hi, schur_lo):
+        moved = lax.dot_general(place, part, contract_rows, preferred_element_type=jnp.float32)
+        spread = spread + jnp.dot(
+            moved.astype(jnp.bfloat16), place, preferred_element_type=jnp.float32
+        )
     spread = spread.reshape(owners, block_nodes, owners * block_nodes)
     received = lax.all_to_all(spread, OWNERS, 0, 0, tiled=True)
     return jnp.sum(received, axis=0)

time: 185 us -> 160 us (0.86)
  local copies, waits for them, and re-layouts: 32.7 us -> 9.26 us
  other arithmetic: 14.1 us -> 6.15 us
  matrix products: 34.8 us -> 41.6 us
    gather x4 -> x0, local copies, waits for them, and re-layouts: 14.4 us -> none  [schur_rows(): spread = jnp.take(jnp.take(padded, slot, axis=0), slot, axis=2)]
    dot_general x0 -> x2, matrix products: none -> 6.83 us  [schur_rows(): jnp.dot(moved.astype(jnp.bfloat16), place, preferred_element_type=jnp.flo...]
    select_n x2 -> x0, other arithmetic: 5.92 us -> none  [schur_rows(): spread = jnp.take(jnp.take(padded, slot, axis=0), slot, axis=2)]
    reshape x2 -> x0, local copies, waits for them, and re-layouts: 5.64 us -> none  [schur_rows(): schur.reshape(picks, block_nodes, picks, block_nodes)]
    pad x1 -> x0, local copies, waits for them, and re-layouts: 3.48 us -> none  [schur_rows(): jnp.pad(schur.reshape(picks, block_nodes, picks, block_nodes), ((0, 1), (...]
  transfers between devices with their start and end apart: 7 -> 7, of which waited for: 6 -> 6; matrix products, arithmetic and copies ran while one was open for 33% -> 22% of each run, Pallas kernels for 0% -> 0%
where the time goes in v2:
time: 160 us; the launch traced here: 157 us
  waiting for transfers between devices  46.2 us (29%)
  matrix products  41.6 us (26%)
  starting transfers between devices  29.5 us (18%)
  blocking collectives  24.4 us (15%)
  local copies, waits for them, and re-layouts  9.26 us (6%)
  other arithmetic  6.15 us (4%)
    all_to_all x3, blocking collectives, gather_along(): return lax.all_to_all(copies, axis, 0, 0, tiled=True)  24.4 us
    all_to_all x6, waiting for transfers between devices, gather_along(): return lax.all_to_all(copies, axis, 0, 0, tiled=True)  23.8 us
    all_to_all x6, starting transfers between devices, gather_along(): return lax.all_to_all(copies, axis, 0, 0, tiled=True)  23.3 us
    all_to_all x1, waiting for transfers between devices, schur_rows(): received = lax.all_to_all(spread, OWNERS, 0, 0, tiled=True)  22.4 us
    dot_general x1, matrix products, schur_rows(): solved = jnp.dot(inverse, coupled, preferred_element_type=jnp.float32)  9.56 us
    dot_general x2, matrix products, schur_rows(): jnp.dot(moved.astype(jnp.bfloat16), place, preferred_element_type=jnp.flo...  6.83 us
    all_to_all x1, starting transfers between devices, schur_rows(): received = lax.all_to_all(spread, OWNERS, 0, 0, tiled=True)  6.1 us
    dot_general x1, matrix products, schur_rows(): lax.dot_general(coupled, solved_hi, contract, preferred_element_type=jnp....  5.32 us
  transfers between devices with their start and end apart: 7, of which 6 were waited for; matrix products, arithmetic and copies ran while one was open for 22% of the time, Pallas kernels for 0%

profile of v2, /device:TPU:1, one launch (start us, length us, event | category | flops | bytes accessed | tf_op | source)
XLA Modules:
  0.0 157.4 jit_solution(11380307952325765899)
XLA Ops:
  2.5 4.3 %all-to-all-start = ((f32[4,64,256]{2,1,0:T(8,128)}), f32[4,64,256]{2,1,0:T(8,128)S(1)}, u32[]{:S(2)}, u32[]{:S(2)}) async-start(f32[4,64,256]{2,1,0:T(8,128)} %broadcast_in_dim.31), calls=%async_computation | async-start | bytes 524288 | tf_op jit(solution)/shard_map/all_to_all | solution.py:18
  6.7 9.6 %fusion = f32[2560,512]{1,0:T(8,128)S(1)} fusion(bf16[1,1,2560,2560]{3,2,1,0:T(8,128)(2,1)} %param.15, bf16[1,1,2560,512]{3,2,1,0:T(8,128)(2,1)S(1)} %copy-done), kind=kOutput, calls=%fused_computation | convolution fusion | flops 6710886400 | bytes 20971520 | tf_op jit(solution)/shard_map/dot_general | solution.py:24
  16.3 2.3 %copy-done.1 = f32[2560,512]{1,0:T(8,128)} copy-done((f32[2560,512]{1,0:T(8,128)}, f32[2560,512]{1,0:T(8,128)S(1)}, u32[]{:S(2)}) %copy-start.1) | copy-done | bytes 5242904
  18.7 2.5 %fusion.3 = f32[512,512]{1,0:T(8,128)} fusion(f32[2560,512]{1,0:T(8,128)S(1)} %fusion, bf16[1,1,2560,512]{3,2,1,0:T(8,128)(2,1)S(1)} %copy-done), kind=kOutput, calls=%fused_computation.5 | convolution fusion | flops 1346109440 | bytes 8912896 | tf_op jit(solution)/shard_map/dot_general | solution.py:28
  21.2 1.3 copy.9
  22.6 5.3 %fusion.15 = f32[512,512]{0,1:T(8,128)} fusion(f32[512,512]{1,0:T(8,128)} %fusion.3, bf16[1,1,2560,512]{3,2,1,0:T(8,128)(2,1)S(1)} %copy-done, f32[2560,512]{1,0:T(8,128)} %copy-done.1, bf16[1,1,512,512]{2,3,1,0:T(8,128)(2,1)S(1)} %copy.9), kind=kOutput, calls=%fused_computation.15 | convolution fusion | flops 1345585152 | bytes 10485760 | tf_op jit(solution)/shard_map/dot_general | solution.py:27
  28.0 3.3 %fusion.18 = f32[512,512]{1,0:T(8,128)} fusion(f32[512,512]{0,1:T(8,128)} %fusion.15, s32[512]{0:T(512)S(1)} %fusion.78), kind=kOutput, calls=%fused_computation.18 | convolution fusion | flops 538443776 | bytes 2099200 | tf_op jit(solution)/shard_map/dot_general | solution.py:39
  31.2 3.6 %convolution_add_fusion = f32[512,512]{1,0:T(8,128)} fusion(f32[512,512]{1,0:T(8,128)} %fusion.18, f32[512,512]{0,1:T(8,128)} %fusion.15, s32[512]{0:T(512)S(1)} %fusion.78), kind=kOutput, calls=%fused_computation.12 | convolution fusion | flops 538968064 | bytes 3147776 | tf_op jit(solution)/shard_map/dot_general | solution.py:39
  34.8 6.1 %all-to-all-start.1 = ((f32[8,64,512]{2,1,0:T(8,128)}), f32[8,64,512]{2,1,0:T(8,128)}, u32[]{:S(2)}, u32[]{:S(2)}) async-start(f32[8,64,512]{2,1,0:T(8,128)} %bitcast.187), calls=%async_computation.1 | async-start | bytes 2097152 | tf_op jit(solution)/shard_map/all_to_all | solution.py:43
  43.6 1.4 maximum_bitcast_fusion
  45.0 22.4 %all-to-all-done.1 = f32[8,64,512]{2,1,0:T(8,128)} async-done(((f32[8,64,512]{2,1,0:T(8,128)}), f32[8,64,512]{2,1,0:T(8,128)}, u32[]{:S(2)}, u32[]{:S(2)}) %all-to-all-start.1) | async-done | bytes 1048608 | tf_op jit(solution)/shard_map/all_to_all | solution.py:43
  67.4 1.4 broadcast_in_dim.34
  68.8 3.4 %all-to-all-start.2 = ((bf16[8,64,128]{2,1,0:T(8,128)(2,1)}), bf16[8,64,128]{2,1,0:T(8,128)(2,1)S(1)}, u32[]{:S(2)}, u32[]{:S(2)}) async-start(bf16[8,64,128]{2,1,0:T(8,128)(2,1)} %broadcast_in_dim.34), calls=%async_computation.2 | async-start | bytes 262144 | tf_op jit(solution)/shard_map/all_to_all | solution.py:18
  72.2 1.3 reduce_sum.9
  73.5 5.0 %all-to-all-done.2 = bf16[8,64,128]{2,1,0:T(8,128)(2,1)S(1)} async-done(((bf16[8,64,128]{2,1,0:T(8,128)(2,1)}), bf16[8,64,128]{2,1,0:T(8,128)(2,1)S(1)}, u32[]{:S(2)}, u32[]{:S(2)}) %all-to-all-start.2) | async-done | bytes 131104 | tf_op jit(solution)/shard_map/all_to_all | solution.py:18
  79.9 5.6 %all-to-all-start.3 = ((f32[4,64,128]{2,1,0:T(8,128)}), f32[4,64,128]{2,1,0:T(8,128)S(1)}, u32[]{:S(2)}, u32[]{:S(2)}) async-start(f32[4,64,128]{2,1,0:T(8,128)} %broadcast_in_dim.36), calls=%async_computation.3 | async-start | bytes 262144 | tf_op jit(solution)/shard_map/all_to_all | solution.py:18
  85.5 1.1 pad_maximum_fusion
  86.6 2.5 %all-to-all-done.3 = f32[4,64,128]{2,1,0:T(8,128)S(1)} async-done(((f32[4,64,128]{2,1,0:T(8,128)}), f32[4,64,128]{2,1,0:T(8,128)S(1)}, u32[]{:S(2)}, u32[]{:S(2)}) %all-to-all-start.3) | async-done | bytes 131104 | tf_op jit(solution)/shard_map/all_to_all | solution.py:18
  90.7 3.4 %all-to-all-start.4 = ((bf16[8,64,128]{2,1,0:T(8,128)(2,1)}), bf16[8,64,128]{2,1,0:T(8,128)(2,1)S(1)}, u32[]{:S(2)}, u32[]{:S(2)}) async-start(bf16[8,64,128]{2,1,0:T(8,128)(2,1)} %broadcast_in_dim.37), calls=%async_computation.4 | async-start | bytes 262144 | tf_op jit(solution)/shard_map/all_to_all | solution.py:18
  95.0 5.4 %all-to-all-done.4 = bf16[8,64,128]{2,1,0:T(8,128)(2,1)S(1)} async-done(((bf16[8,64,128]{2,1,0:T(8,128)(2,1)}), bf16[8,64,128]{2,1,0:T(8,128)(2,1)S(1)}, u32[]{:S(2)}, u32[]{:S(2)}) %all-to-all-start.4) | async-done | bytes 131104 | tf_op jit(solution)/shard_map/all_to_all | solution.py:18
  100.5 0.9 fusion.27
  101.5 1.0 fusion.26
  103.4 8.1 %all_to_all.50 = f32[4,64,128]{2,1,0:T(8,128)S(1)} all-to-all(f32[4,64,128]{2,1,0:T(8,128)S(1)} %broadcast_in_dim.38), channel_id=1, replica_groups=mesh['sub'=2,'section'=4,'iface'=4] {'section'}, dimensions={0} | all-to-all | bytes 262144 | tf_op jit(solution)/shard_map/all_to_all | solution.py:18
  113.1 3.4 %all-to-all-start.6 = ((bf16[8,64,128]{2,1,0:T(8,128)(2,1)}), bf16[8,64,128]{2,1,0:T(8,128)(2,1)S(1)}, u32[]{:S(2)}, u32[]{:S(2)}) async-start(bf16[8,64,128]{2,1,0:T(8,128)(2,1)} %broadcast_in_dim.39), calls=%async_computation.6 | async-start | bytes 262144 | tf_op jit(solution)/shard_map/all_to_all | solution.py:18
  117.4 5.4 %all-to-all-done.6 = bf16[8,64,128]{2,1,0:T(8,128)(2,1)S(1)} async-done(((bf16[8,64,128]{2,1,0:T(8,128)(2,1)}), bf16[8,64,128]{2,1,0:T(8,128)(2,1)S(1)}, u32[]{:S(2)}, u32[]{:S(2)}) %all-to-all-start.6) | async-done | bytes 131104 | tf_op jit(solution)/shard_map/all_to_all | solution.py:18
  123.0 0.9 fusion.24
  123.9 1.0 fusion.23
  125.9 8.1 %all_to_all.51 = f32[4,64,128]{2,1,0:T(8,128)S(1)} all-to-all(f32[4,64,128]{2,1,0:T(8,128)S(1)} %broadcast_in_dim.40), channel_id=1, replica_groups=mesh['sub'=2,'section'=4,'iface'=4] {'section'}, dimensions={0} | all-to-all | bytes 262144 | tf_op jit(solution)/shard_map/all_to_all | solution.py:18
  135.6 3.4 %all-to-all-start.8 = ((bf16[8,64,128]{2,1,0:T(8,128)(2,1)}), bf16[8,64,128]{2,1,0:T(8,128)(2,1)S(1)}, u32[]{:S(2)}, u32[]{:S(2)}) async-start(bf16[8,64,128]{2,1,0:T(8,128)(2,1)} %broadcast_in_dim.41), calls=%async_computation.8 | async-start | bytes 262144 | tf_op jit(solution)/shard_map/all_to_all | solution.py:18
  139.9 5.4 %all-to-all-done.8 = bf16[8,64,128]{2,1,0:T(8,128)(2,1)S(1)} async-done(((bf16[8,64,128]{2,1,0:T(8,128)(2,1)}), bf16[8,64,128]{2,1,0:T(8,128)(2,1)S(1)}, u32[]{:S(2)}, u32[]{:S(2)}) %all-to-all-start.8) | async-done | bytes 131104 | tf_op jit(solution)/shard_map/all_to_all | solution.py:18
  146.4 1.0 fusion.20
  148.3 8.1 %all_to_all.52 = f32[4,64,128]{2,1,0:T(8,128)S(1)} all-to-all(f32[4,64,128]{2,1,0:T(8,128)S(1)} %broadcast_in_dim.82), channel_id=1, replica_groups=mesh['sub'=2,'section'=4,'iface'=4] {'section'}, dimensions={0} | all-to-all | bytes 262144 | tf_op jit(solution)/shard_map/all_to_all | solution.py:18
  (61 shorter events, 19.1 us)
Async XLA Ops:
  0.0 6.7 %copy-start = (bf16[1,1,2560,512]{3,2,1,0:T(8,128)(2,1)S(1)}, bf16[1,1,2560,512]{3,2,1,0:T(8,128)(2,1)}, u32[]{:S(2)}) copy-start(bf16[1,1,2560,512]{3,2,1,0:T(8,128)(2,1)} %param.14) | copy-start | bytes 7864324
  2.5 32.3 %all-to-all-start = ((f32[4,64,256]{2,1,0:T(8,128)}), f32[4,64,256]{2,1,0:T(8,128)S(1)}, u32[]{:S(2)}, u32[]{:S(2)}) async-start(f32[4,64,256]{2,1,0:T(8,128)} %broadcast_in_dim.31), calls=%async_computation | async-start | bytes 524288 | tf_op jit(solution)/shard_map/all_to_all | solution.py:18
  16.3 2.4 %copy-start.1 = (f32[2560,512]{1,0:T(8,128)}, f32[2560,512]{1,0:T(8,128)S(1)}, u32[]{:S(2)}) copy-start(f32[2560,512]{1,0:T(8,128)S(1)} %fusion) | copy-start | bytes 15728644
  18.7 3.8 %copy-start.6 = (s32[1,1,8]{2,1,0:T(1,128)S(1)}, s32[1,1,8]{2,1,0:T(1,128)}, u32[]{:S(2)}) copy-start(s32[1,1,8]{2,1,0:T(1,128)} %param.12) | copy-start | bytes 100
  31.2 10.3 %copy-start.5 = (f32[1,64,128]{2,1,0:T(8,128)S(1)}, f32[1,64,128]{2,1,0:T(8,128)}, u32[]{:S(2)}) copy-start(f32[1,64,128]{2,1,0:T(8,128)} %param.8) | copy-start | bytes 98308
  34.8 32.6 %all-to-all-start.1 = ((f32[8,64,512]{2,1,0:T(8,128)}), f32[8,64,512]{2,1,0:T(8,128)}, u32[]{:S(2)}, u32[]{:S(2)}) async-start(f32[8,64,512]{2,1,0:T(8,128)} %bitcast.187), calls=%async_computation.1 | async-start | bytes 2097152 | tf_op jit(solution)/shard_map/all_to_all | solution.py:43
  40.9 37.8 %copy-start.2 = (f32[1,64,128]{2,1,0:T(8,128)S(1)}, f32[1,64,128]{2,1,0:T(8,128)}, u32[]{:S(2)}) copy-start(f32[1,64,128]{2,1,0:T(8,128)} %param.9) | copy-start | bytes 98308
  40.9 38.2 %copy-start.4 = (bf16[1,1,64,64]{3,2,1,0:T(8,128)(2,1)S(1)}, bf16[1,1,64,64]{3,2,1,0:T(8,128)(2,1)}, u32[]{:S(2)}) copy-start(bf16[1,1,64,64]{3,2,1,0:T(8,128)(2,1)} %param.10) | copy-start | bytes 24580
  42.3 43.2 %copy-start.3 = (f32[4,64,64]{2,1,0:T(8,128)}, f32[4,64,64]{2,1,0:T(8,128)S(1)}, u32[]{:S(2)}) copy-start(f32[4,64,64]{2,1,0:T(8,128)S(1)} %slice.28) | copy-start | bytes 196612
  68.8 9.7 %all-to-all-start.2 = ((bf16[8,64,128]{2,1,0:T(8,128)(2,1)}), bf16[8,64,128]{2,1,0:T(8,128)(2,1)S(1)}, u32[]{:S(2)}, u32[]{:S(2)}) async-start(bf16[8,64,128]{2,1,0:T(8,128)(2,1)} %broadcast_in_dim.34), calls=%async_computation.2 | async-start | bytes 262144 | tf_op jit(solution)/shard_map/all_to_all | solution.py:18
  79.9 9.2 %all-to-all-start.3 = ((f32[4,64,128]{2,1,0:T(8,128)}), f32[4,64,128]{2,1,0:T(8,128)S(1)}, u32[]{:S(2)}, u32[]{:S(2)}) async-start(f32[4,64,128]{2,1,0:T(8,128)} %broadcast_in_dim.36), calls=%async_computation.3 | async-start | bytes 262144 | tf_op jit(solution)/shard_map/all_to_all | solution.py:18
  90.7 9.7 %all-to-all-start.4 = ((bf16[8,64,128]{2,1,0:T(8,128)(2,1)}), bf16[8,64,128]{2,1,0:T(8,128)(2,1)S(1)}, u32[]{:S(2)}, u32[]{:S(2)}) async-start(bf16[8,64,128]{2,1,0:T(8,128)(2,1)} %broadcast_in_dim.37), calls=%async_computation.4 | async-start | bytes 262144 | tf_op jit(solution)/shard_map/all_to_all | solution.py:18
  113.1 9.7 %all-to-all-start.6 = ((bf16[8,64,128]{2,1,0:T(8,128)(2,1)}), bf16[8,64,128]{2,1,0:T(8,128)(2,1)S(1)}, u32[]{:S(2)}, u32[]{:S(2)}) async-start(bf16[8,64,128]{2,1,0:T(8,128)(2,1)} %broadcast_in_dim.39), calls=%async_computation.6 | async-start | bytes 262144 | tf_op jit(solution)/shard_map/all_to_all | solution.py:18
  135.6 9.7 %all-to-all-start.8 = ((bf16[8,64,128]{2,1,0:T(8,128)(2,1)}), bf16[8,64,128]{2,1,0:T(8,128)(2,1)S(1)}, u32[]{:S(2)}, u32[]{:S(2)}) async-start(bf16[8,64,128]{2,1,0:T(8,128)(2,1)} %broadcast_in_dim.41), calls=%async_computation.8 | async-start | bytes 262144 | tf_op jit(solution)/shard_map/all_to_all | solution.py:18

commit v3 on v2

--- a/solution.py
+++ b/solution.py
@@ -39,9 +39,7 @@
         spread = spread + jnp.dot(
             moved.astype(jnp.bfloat16), place, preferred_element_type=jnp.float32
         )
-    spread = spread.reshape(owners, block_nodes, owners * block_nodes)
-    received = lax.all_to_all(spread, OWNERS, 0, 0, tiled=True)
-    return jnp.sum(received, axis=0)
+    return spread.reshape(owners, block_nodes, owners * block_nodes)
 
 
 def chain_weights(precond_f, couple_f):
@@ -64,7 +62,7 @@
 def body(
     previous, right_side, precond, couple, block_ids, iface_matrix, interior_coupling, inv_interior
 ):
-    highest = lax.Precision.HIGHEST
+    high = lax.Precision.HIGH
     section_pos = lax.axis_index("section")
     sections = lax.axis_size("section")
     owners = lax.axis_size(OWNERS)
@@ -88,26 +86,33 @@
     precond_mine = precond[0, 0].astype(jnp.float32)
     couple_above = couple_all[above_pos]
 
-    rows = schur_rows(
+    first_rounded = gather_along(previous[0].astype(jnp.bfloat16), OWNERS)
+    spread = schur_rows(
         block_ids[0, 0], iface_matrix[0, 0], interior_coupling[0, 0], inv_interior[0, 0], owners
     )
+    first_rounded, tables, spread = lax.optimization_barrier((first_rounded, tables, spread))
+    rows = jnp.sum(lax.all_to_all(spread, OWNERS, 0, 0, tiled=True), axis=0)
     rows_hi, rows_lo = split_bf16(rows)
 
     temps_mine = previous[0]
     temps_above = start_all[above_pos]
     rhs = right_side[0]
     for sweep_index in range(SWEEPS):
-        rounded = gather_along(temps_mine.astype(jnp.bfloat16), OWNERS).reshape(nodes, load_count)
+        if sweep_index == 0:
+            rounded = first_rounded
+        else:
+            rounded = gather_along(temps_mine.astype(jnp.bfloat16), OWNERS)
+        rounded = rounded.reshape(nodes, load_count)
         assembled = jnp.dot(rows_hi, rounded, preferred_element_type=jnp.float32) + jnp.dot(
             rows_lo, rounded, preferred_element_type=jnp.float32
         )
-        from_above = jnp.einsum("ij,il->jl", couple_above, temps_above, precision=highest)
+        from_above = jnp.einsum("ij,il->jl", couple_above, temps_above, precision=high)
         from_above = jnp.where(has_above, from_above, 0.0)
         residual = rhs - assembled - from_above
-        update = temps_mine + jnp.dot(precond_mine, residual, precision=highest)
+        update = temps_mine + jnp.dot(precond_mine, residual, precision=high)
         updates = gather_along(update, "section")
-        temps_mine = jnp.einsum("kij,kjl->il", weights_mine, updates, precision=highest)
-        temps_above = jnp.einsum("kij,kjl->il", weights_above, updates, precision=highest)
+        temps_mine = jnp.einsum("kij,kjl->il", weights_mine, updates, precision=high)
+        temps_above = jnp.einsum("kij,kjl->il", weights_above, updates, precision=high)
     return temps_mine[None]
 
 

time: 160 us -> 157 us (0.981)
    all_to_all x6, starting transfers between devices: 23.3 us -> 26.5 us  [gather_along(): return lax.all_to_all(copies, axis, 0, 0, tiled=True)]
    all_to_all x1, starting transfers between devices: 6.1 us -> 4.37 us  [body(): rows = jnp.sum(lax.all_to_all(spread, OWNERS, 0, 0, tiled=True), axis=0)]
    all_to_all x6, waiting for transfers between devices: 23.8 us -> 22.2 us  [gather_along(): return lax.all_to_all(copies, axis, 0, 0, tiled=True)]
    unnamed x15 -> x17, local copies, waits for them, and re-layouts: 3.62 us -> 3.62 us
  transfers between devices with their start and end apart: 7 -> 7, of which waited for: 6 -> 6; matrix products, arithmetic and copies ran while one was open for 22% -> 20% of each run, Pallas kernels for 0% -> 0%
where the time goes in v3:
time: 157 us; the launch traced here: 154 us
  waiting for transfers between devices  44.7 us (28%)
  matrix products  41 us (26%)
  starting transfers between devices  30.8 us (20%)
  blocking collectives  24.4 us (16%)
  local copies, waits for them, and re-layouts  8.06 us (5%)
  other arithmetic  4.95 us (3%)
    all_to_all x6, starting transfers between devices, gather_along(): return lax.all_to_all(copies, axis, 0, 0, tiled=True)  26.5 us
    all_to_all x3, blocking collectives, gather_along(): return lax.all_to_all(copies, axis, 0, 0, tiled=True)  24.4 us
    all_to_all x1, waiting for transfers between devices, body(): rows = jnp.sum(lax.all_to_all(spread, OWNERS, 0, 0, tiled=True), axis=0)  22.5 us
    all_to_all x6, waiting for transfers between devices, gather_along(): return lax.all_to_all(copies, axis, 0, 0, tiled=True)  22.2 us
    dot_general x1, matrix products, schur_rows(): solved = jnp.dot(inverse, coupled, preferred_element_type=jnp.float32)  9.56 us
    dot_general x2, matrix products, schur_rows(): jnp.dot(moved.astype(jnp.bfloat16), place, preferred_element_type=jnp.flo...  6.77 us
    dot_general x1, matrix products, schur_rows(): lax.dot_general(coupled, solved_hi, contract, preferred_element_type=jnp....  5.31 us
    all_to_all x1, starting transfers between devices, body(): rows = jnp.sum(lax.all_to_all(spread, OWNERS, 0, 0, tiled=True), axis=0)  4.37 us
  transfers between devices with their start and end apart: 7, of which 6 were waited for; matrix products, arithmetic and copies ran while one was open for 20% of the time, Pallas kernels for 0%

profile of v3, /device:TPU:1, one launch (start us, length us, event | category | flops | bytes accessed | tf_op | source)
XLA Modules:
  0.0 154.2 jit_solution(2306995800305554455)
XLA Ops:
  2.5 4.3 %all-to-all-start = ((f32[4,64,256]{2,1,0:T(8,128)}), f32[4,64,256]{2,1,0:T(8,128)S(1)}, u32[]{:S(2)}, u32[]{:S(2)}) async-start(f32[4,64,256]{2,1,0:T(8,128)} %broadcast_in_dim.31), calls=%async_computation | async-start | bytes 524288 | tf_op jit(solution)/shard_map/all_to_all | solution.py:18
  6.7 9.6 %fusion = f32[2560,512]{1,0:T(8,128)S(1)} fusion(bf16[1,1,2560,2560]{3,2,1,0:T(8,128)(2,1)} %param.15, bf16[1,1,2560,512]{3,2,1,0:T(8,128)(2,1)S(1)} %copy-done), kind=kOutput, calls=%fused_computation | convolution fusion | flops 6710886400 | bytes 20971520 | tf_op jit(solution)/shard_map/dot_general | solution.py:24
  16.3 2.3 %copy-done.1 = f32[2560,512]{1,0:T(8,128)} copy-done((f32[2560,512]{1,0:T(8,128)}, f32[2560,512]{1,0:T(8,128)S(1)}, u32[]{:S(2)}) %copy-start.1) | copy-done | bytes 5242904
  18.7 2.5 %fusion.3 = f32[512,512]{1,0:T(8,128)} fusion(f32[2560,512]{1,0:T(8,128)S(1)} %fusion, bf16[1,1,2560,512]{3,2,1,0:T(8,128)(2,1)S(1)} %copy-done), kind=kOutput, calls=%fused_computation.5 | convolution fusion | flops 1346109440 | bytes 8912896 | tf_op jit(solution)/shard_map/dot_general | solution.py:28
  21.2 1.3 copy.9
  22.6 5.3 %fusion.15 = f32[512,512]{0,1:T(8,128)} fusion(f32[512,512]{1,0:T(8,128)} %fusion.3, bf16[1,1,2560,512]{3,2,1,0:T(8,128)(2,1)S(1)} %copy-done, f32[2560,512]{1,0:T(8,128)} %copy-done.1, bf16[1,1,512,512]{2,3,1,0:T(8,128)(2,1)S(1)} %copy.9), kind=kOutput, calls=%fused_computation.15 | convolution fusion | flops 1345585152 | bytes 10485760 | tf_op jit(solution)/shard_map/dot_general | solution.py:27
  27.9 3.2 %fusion.18 = f32[512,512]{1,0:T(8,128)} fusion(f32[512,512]{0,1:T(8,128)} %fusion.15, s32[512]{0:T(512)S(1)} %fusion.78), kind=kOutput, calls=%fused_computation.18 | convolution fusion | flops 538443776 | bytes 2099200 | tf_op jit(solution)/shard_map/dot_general | solution.py:39
  31.9 6.1 %all-to-all-start.1 = ((bf16[8,64,128]{2,1,0:T(8,128)(2,1)}), bf16[8,64,128]{2,1,0:T(8,128)(2,1)S(1)}, u32[]{:S(2)}, u32[]{:S(2)}) async-start(bf16[8,64,128]{2,1,0:T(8,128)(2,1)} %broadcast_in_dim.33), calls=%async_computation.1 | async-start | bytes 262144 | tf_op jit(solution)/shard_map/all_to_all | solution.py:18
  38.0 3.5 %convolution_add_fusion = f32[512,512]{1,0:T(8,128)} fusion(f32[512,512]{1,0:T(8,128)} %fusion.18, f32[512,512]{0,1:T(8,128)} %fusion.15, s32[512]{0:T(512)S(1)} %fusion.78), kind=kOutput, calls=%fused_computation.12 | convolution fusion | flops 538968064 | bytes 3147776 | tf_op jit(solution)/shard_map/dot_general | solution.py:39
  41.6 3.1 %all-to-all-done.1 = bf16[8,64,128]{2,1,0:T(8,128)(2,1)S(1)} async-done(((bf16[8,64,128]{2,1,0:T(8,128)(2,1)}), bf16[8,64,128]{2,1,0:T(8,128)(2,1)S(1)}, u32[]{:S(2)}, u32[]{:S(2)}) %all-to-all-start.1) | async-done | bytes 131104 | tf_op jit(solution)/shard_map/all_to_all | solution.py:18
  44.7 4.4 %all-to-all-start.2 = ((f32[8,64,512]{2,1,0:T(8,128)}), f32[8,64,512]{2,1,0:T(8,128)}, u32[]{:S(2)}, u32[]{:S(2)}) async-start(f32[8,64,512]{2,1,0:T(8,128)} %bitcast.187), calls=%async_computation.2 | async-start | bytes 2097152 | tf_op jit(solution)/shard_map/all_to_all | solution.py:94
  51.5 22.5 %all-to-all-done.2 = f32[8,64,512]{2,1,0:T(8,128)} async-done(((f32[8,64,512]{2,1,0:T(8,128)}), f32[8,64,512]{2,1,0:T(8,128)}, u32[]{:S(2)}, u32[]{:S(2)}) %all-to-all-start.2) | async-done | bytes 1048608 | tf_op jit(solution)/shard_map/all_to_all | solution.py:94
  74.0 1.3 reduce_sum.9
  76.7 6.0 %all-to-all-start.3 = ((f32[4,64,128]{2,1,0:T(8,128)}), f32[4,64,128]{2,1,0:T(8,128)S(1)}, u32[]{:S(2)}, u32[]{:S(2)}) async-start(f32[4,64,128]{2,1,0:T(8,128)} %broadcast_in_dim.36), calls=%async_computation.3 | async-start | bytes 262144 | tf_op jit(solution)/shard_map/all_to_all | solution.py:18
  82.6 1.1 pad_maximum_fusion
  83.7 2.5 %all-to-all-done.3 = f32[4,64,128]{2,1,0:T(8,128)S(1)} async-done(((f32[4,64,128]{2,1,0:T(8,128)}), f32[4,64,128]{2,1,0:T(8,128)S(1)}, u32[]{:S(2)}, u32[]{:S(2)}) %all-to-all-start.3) | async-done | bytes 131104 | tf_op jit(solution)/shard_map/all_to_all | solution.py:18
  87.8 3.4 %all-to-all-start.4 = ((bf16[8,64,128]{2,1,0:T(8,128)(2,1)}), bf16[8,64,128]{2,1,0:T(8,128)(2,1)S(1)}, u32[]{:S(2)}, u32[]{:S(2)}) async-start(bf16[8,64,128]{2,1,0:T(8,128)(2,1)} %broadcast_in_dim.37), calls=%async_computation.4 | async-start | bytes 262144 | tf_op jit(solution)/shard_map/all_to_all | solution.py:18
  92.0 5.5 %all-to-all-done.4 = bf16[8,64,128]{2,1,0:T(8,128)(2,1)S(1)} async-done(((bf16[8,64,128]{2,1,0:T(8,128)(2,1)}), bf16[8,64,128]{2,1,0:T(8,128)(2,1)S(1)}, u32[]{:S(2)}, u32[]{:S(2)}) %all-to-all-start.4) | async-done | bytes 131104 | tf_op jit(solution)/shard_map/all_to_all | solution.py:18
  97.6 0.9 fusion.27
  98.6 1.0 fusion.26
  100.5 8.1 %all_to_all.50 = f32[4,64,128]{2,1,0:T(8,128)S(1)} all-to-all(f32[4,64,128]{2,1,0:T(8,128)S(1)} %broadcast_in_dim.38), channel_id=1, replica_groups=mesh['sub'=2,'section'=4,'iface'=4] {'section'}, dimensions={0} | all-to-all | bytes 262144 | tf_op jit(solution)/shard_map/all_to_all | solution.py:18
  110.1 3.4 %all-to-all-start.6 = ((bf16[8,64,128]{2,1,0:T(8,128)(2,1)}), bf16[8,64,128]{2,1,0:T(8,128)(2,1)S(1)}, u32[]{:S(2)}, u32[]{:S(2)}) async-start(bf16[8,64,128]{2,1,0:T(8,128)(2,1)} %broadcast_in_dim.39), calls=%async_computation.6 | async-start | bytes 262144 | tf_op jit(solution)/shard_map/all_to_all | solution.py:18
  114.3 5.5 %all-to-all-done.6 = bf16[8,64,128]{2,1,0:T(8,128)(2,1)S(1)} async-done(((bf16[8,64,128]{2,1,0:T(8,128)(2,1)}), bf16[8,64,128]{2,1,0:T(8,128)(2,1)S(1)}, u32[]{:S(2)}, u32[]{:S(2)}) %all-to-all-start.6) | async-done | bytes 131104 | tf_op jit(solution)/shard_map/all_to_all | solution.py:18
  120.0 0.9 fusion.24
  120.9 1.0 fusion.23
  121.9 0.9 fusion.22
  122.8 8.1 %all_to_all.51 = f32[4,64,128]{2,1,0:T(8,128)S(1)} all-to-all(f32[4,64,128]{2,1,0:T(8,128)S(1)} %broadcast_in_dim.40), channel_id=1, replica_groups=mesh['sub'=2,'section'=4,'iface'=4] {'section'}, dimensions={0} | all-to-all | bytes 262144 | tf_op jit(solution)/shard_map/all_to_all | solution.py:18
  132.5 3.4 %all-to-all-start.8 = ((bf16[8,64,128]{2,1,0:T(8,128)(2,1)}), bf16[8,64,128]{2,1,0:T(8,128)(2,1)S(1)}, u32[]{:S(2)}, u32[]{:S(2)}) async-start(bf16[8,64,128]{2,1,0:T(8,128)(2,1)} %broadcast_in_dim.41), calls=%async_computation.8 | async-start | bytes 262144 | tf_op jit(solution)/shard_map/all_to_all | solution.py:18
  136.7 5.5 %all-to-all-done.8 = bf16[8,64,128]{2,1,0:T(8,128)(2,1)S(1)} async-done(((bf16[8,64,128]{2,1,0:T(8,128)(2,1)}), bf16[8,64,128]{2,1,0:T(8,128)(2,1)S(1)}, u32[]{:S(2)}, u32[]{:S(2)}) %all-to-all-start.8) | async-done | bytes 131104 | tf_op jit(solution)/shard_map/all_to_all | solution.py:18
  142.4 0.9 fusion.21
  143.3 1.0 fusion.20
  145.2 8.1 %all_to_all.52 = f32[4,64,128]{2,1,0:T(8,128)S(1)} all-to-all(f32[4,64,128]{2,1,0:T(8,128)S(1)} %broadcast_in_dim.82), channel_id=1, replica_groups=mesh['sub'=2,'section'=4,'iface'=4] {'section'}, dimensions={0} | all-to-all | bytes 262144 | tf_op jit(solution)/shard_map/all_to_all | solution.py:18
  (64 shorter events, 17.2 us)
Async XLA Ops:
  0.0 6.7 %copy-start = (bf16[1,1,2560,512]{3,2,1,0:T(8,128)(2,1)S(1)}, bf16[1,1,2560,512]{3,2,1,0:T(8,128)(2,1)}, u32[]{:S(2)}) copy-start(bf16[1,1,2560,512]{3,2,1,0:T(8,128)(2,1)} %param.14) | copy-start | bytes 7864324
  2.5 28.7 %all-to-all-start = ((f32[4,64,256]{2,1,0:T(8,128)}), f32[4,64,256]{2,1,0:T(8,128)S(1)}, u32[]{:S(2)}, u32[]{:S(2)}) async-start(f32[4,64,256]{2,1,0:T(8,128)} %broadcast_in_dim.31), calls=%async_computation | async-start | bytes 524288 | tf_op jit(solution)/shard_map/all_to_all | solution.py:18
  16.3 2.3 %copy-start.1 = (f32[2560,512]{1,0:T(8,128)}, f32[2560,512]{1,0:T(8,128)S(1)}, u32[]{:S(2)}) copy-start(f32[2560,512]{1,0:T(8,128)S(1)} %fusion) | copy-start | bytes 15728644
  18.7 3.8 %copy-start.7 = (s32[1,1,8]{2,1,0:T(1,128)S(1)}, s32[1,1,8]{2,1,0:T(1,128)}, u32[]{:S(2)}) copy-start(s32[1,1,8]{2,1,0:T(1,128)} %param.12) | copy-start | bytes 100
  27.9 3.2 %copy-start.6 = (f32[1,64,128]{2,1,0:T(8,128)S(1)}, f32[1,64,128]{2,1,0:T(8,128)}, u32[]{:S(2)}) copy-start(f32[1,64,128]{2,1,0:T(8,128)} %param.8) | copy-start | bytes 98308
  31.2 18.1 %copy-start.2 = (f32[4,64,256]{2,1,0:T(8,128)}, f32[4,64,256]{2,1,0:T(8,128)S(1)}, u32[]{:S(2)}) copy-start(f32[4,64,256]{2,1,0:T(8,128)S(1)} %all-to-all-done) | copy-start | bytes 786436
  31.9 12.8 %all-to-all-start.1 = ((bf16[8,64,128]{2,1,0:T(8,128)(2,1)}), bf16[8,64,128]{2,1,0:T(8,128)(2,1)S(1)}, u32[]{:S(2)}, u32[]{:S(2)}) async-start(bf16[8,64,128]{2,1,0:T(8,128)(2,1)} %broadcast_in_dim.33), calls=%async_computation.1 | async-start | bytes 262144 | tf_op jit(solution)/shard_map/all_to_all | solution.py:18
  44.7 30.8 %copy-start.3 = (f32[1,64,128]{2,1,0:T(8,128)S(1)}, f32[1,64,128]{2,1,0:T(8,128)}, u32[]{:S(2)}) copy-start(f32[1,64,128]{2,1,0:T(8,128)} %param.9) | copy-start | bytes 98308
  44.7 29.3 %all-to-all-start.2 = ((f32[8,64,512]{2,1,0:T(8,128)}), f32[8,64,512]{2,1,0:T(8,128)}, u32[]{:S(2)}, u32[]{:S(2)}) async-start(f32[8,64,512]{2,1,0:T(8,128)} %bitcast.187), calls=%async_computation.2 | async-start | bytes 2097152 | tf_op jit(solution)/shard_map/all_to_all | solution.py:94
  49.1 26.8 %copy-start.5 = (bf16[1,1,64,64]{3,2,1,0:T(8,128)(2,1)S(1)}, bf16[1,1,64,64]{3,2,1,0:T(8,128)(2,1)}, u32[]{:S(2)}) copy-start(bf16[1,1,64,64]{3,2,1,0:T(8,128)(2,1)} %param.10) | copy-start | bytes 24580
  49.3 27.4 %copy-start.4 = (f32[4,64,64]{2,1,0:T(8,128)}, f32[4,64,64]{2,1,0:T(8,128)S(1)}, u32[]{:S(2)}) copy-start(f32[4,64,64]{2,1,0:T(8,128)S(1)} %slice.28) | copy-start | bytes 196612
  49.6 26.0 %slice-start = ((f32[4,64,256]{2,1,0:T(8,128)}), f32[4,64,128]{2,1,0:T(8,128)S(1)}, s32[]{:S(2)}) async-start(f32[4,64,256]{2,1,0:T(8,128)} %copy-done.2), calls=%async_computation.10 | async-start | bytes 262144 | tf_op jit(solution)/shard_map/slice | solution.py:78
  76.7 9.6 %all-to-all-start.3 = ((f32[4,64,128]{2,1,0:T(8,128)}), f32[4,64,128]{2,1,0:T(8,128)S(1)}, u32[]{:S(2)}, u32[]{:S(2)}) async-start(f32[4,64,128]{2,1,0:T(8,128)} %broadcast_in_dim.36), calls=%async_computation.3 | async-start | bytes 262144 | tf_op jit(solution)/shard_map/all_to_all | solution.py:18
  87.8 9.7 %all-to-all-start.4 = ((bf16[8,64,128]{2,1,0:T(8,128)(2,1)}), bf16[8,64,128]{2,1,0:T(8,128)(2,1)S(1)}, u32[]{:S(2)}, u32[]{:S(2)}) async-start(bf16[8,64,128]{2,1,0:T(8,128)(2,1)} %broadcast_in_dim.37), calls=%async_computation.4 | async-start | bytes 262144 | tf_op jit(solution)/shard_map/all_to_all | solution.py:18
  110.1 9.7 %all-to-all-start.6 = ((bf16[8,64,128]{2,1,0:T(8,128)(2,1)}), bf16[8,64,128]{2,1,0:T(8,128)(2,1)S(1)}, u32[]{:S(2)}, u32[]{:S(2)}) async-start(bf16[8,64,128]{2,1,0:T(8,128)(2,1)} %broadcast_in_dim.39), calls=%async_computation.6 | async-start | bytes 262144 | tf_op jit(solution)/shard_map/all_to_all | solution.py:18
  132.5 9.7 %all-to-all-start.8 = ((bf16[8,64,128]{2,1,0:T(8,128)(2,1)}), bf16[8,64,128]{2,1,0:T(8,128)(2,1)S(1)}, u32[]{:S(2)}, u32[]{:S(2)}) async-start(bf16[8,64,128]{2,1,0:T(8,128)(2,1)} %broadcast_in_dim.41), calls=%async_computation.8 | async-start | bytes 262144 | tf_op jit(solution)/shard_map/all_to_all | solution.py:18

commit v4 on v3

--- a/solution.py
+++ b/solution.py
@@ -21,25 +21,29 @@
 def schur_rows(block_list, boundary, coupled, inverse, owners):
     picks = block_list.shape[0]
     block_nodes = boundary.shape[0] // picks
+    nodes = owners * block_nodes
+    contract = (((0,), (0,)), ((), ()))
+    node = jnp.arange(nodes, dtype=jnp.int32)
+    slot_node = jnp.arange(picks * block_nodes, dtype=jnp.int32)
+    target = jnp.repeat(block_list, block_nodes) * block_nodes + slot_node % block_nodes
+    place = (target[:, None] == node[None, :]).astype(jnp.bfloat16)
+
+    def moved(matrix):
+        rows = lax.dot_general(place, matrix, contract, preferred_element_type=jnp.float32)
+        return jnp.dot(rows.astype(jnp.bfloat16), place, preferred_element_type=jnp.float32)
+
+    if picks == owners:
+        coupled = jnp.dot(coupled, place, preferred_element_type=jnp.float32).astype(jnp.bfloat16)
+        boundary = moved(boundary)
     solved = jnp.dot(inverse, coupled, preferred_element_type=jnp.float32)
     solved_hi, solved_lo = split_bf16(solved)
-    contract = (((0,), (0,)), ((), ()))
     pulled = lax.dot_general(coupled, solved_hi, contract, preferred_element_type=jnp.float32)
     pulled = pulled + lax.dot_general(coupled, solved_lo, contract, preferred_element_type=jnp.float32)
     schur = boundary.astype(jnp.float32) - pulled
-    node = jnp.arange(owners * block_nodes, dtype=jnp.int32)
-    sub = jnp.arange(picks * block_nodes, dtype=jnp.int32)
-    target = jnp.repeat(block_list, block_nodes) * block_nodes + sub % block_nodes
-    place = (target[:, None] == node[None, :]).astype(jnp.bfloat16)
-    schur_hi, schur_lo = split_bf16(schur)
-    contract_rows = (((0,), (0,)), ((), ()))
-    spread = jnp.zeros((owners * block_nodes, owners * block_nodes), jnp.float32)
-    for part in (schur_hi, schur_lo):
-        moved = lax.dot_general(place, part, contract_rows, preferred_element_type=jnp.float32)
-        spread = spread + jnp.dot(
-            moved.astype(jnp.bfloat16), place, preferred_element_type=jnp.float32
-        )
-    return spread.reshape(owners, block_nodes, owners * block_nodes)
+    if picks != owners:
+        schur_hi, schur_lo = split_bf16(schur)
+        schur = moved(schur_hi) + moved(schur_lo)
+    return schur.reshape(owners, block_nodes, nodes)
 
 
 def chain_weights(precond_f, couple_f):
@@ -92,7 +96,7 @@
     )
     first_rounded, tables, spread = lax.optimization_barrier((first_rounded, tables, spread))
     rows = jnp.sum(lax.all_to_all(spread, OWNERS, 0, 0, tiled=True), axis=0)
-    rows_hi, rows_lo = split_bf16(rows)
+    rows_hi, rows_lo = split_bf16(jnp.dot(precond_mine, rows, precision=lax.Precision.HIGHEST))
 
     temps_mine = previous[0]
     temps_above = start_all[above_pos]
@@ -103,13 +107,13 @@
         else:
             rounded = gather_along(temps_mine.astype(jnp.bfloat16), OWNERS)
         rounded = rounded.reshape(nodes, load_count)
-        assembled = jnp.dot(rows_hi, rounded, preferred_element_type=jnp.float32) + jnp.dot(
-            rows_lo, rounded, preferred_element_type=jnp.float32
-        )
         from_above = jnp.einsum("ij,il->jl", couple_above, temps_above, precision=high)
         from_above = jnp.where(has_above, from_above, 0.0)
-        residual = rhs - assembled - from_above
-        update = temps_mine + jnp.dot(precond_mine, residual, precision=high)
+        known = temps_mine + jnp.dot(precond_mine, rhs - from_above, precision=high)
+        update = known - (
+            jnp.dot(rows_hi, rounded, preferred_element_type=jnp.float32)
+            + jnp.dot(rows_lo, rounded, preferred_element_type=jnp.float32)
+        )
         updates = gather_along(update, "section")
         temps_mine = jnp.einsum("kij,kjl->il", weights_mine, updates, precision=high)
         temps_above = jnp.einsum("kij,kjl->il", weights_above, updates, precision=high)

time: 157 us -> 142 us (0.904)
  matrix products: 41 us -> 32.1 us
  waiting for transfers between devices: 44.7 us -> 39.8 us
  local copies, waits for them, and re-layouts: 8.06 us -> 4.97 us
  other arithmetic: 4.95 us -> 7.09 us
    all_to_all x6, waiting for transfers between devices: 22.2 us -> 18.3 us  [gather_along(): return lax.all_to_all(copies, axis, 0, 0, tiled=True)]
    unnamed x17 -> x10, local copies, waits for them, and re-layouts: 3.62 us -> 0.02 us
    dot_general x1, matrix products: 5.31 us -> 2.52 us  [schur_rows(): lax.dot_general(coupled, solved_hi, contract, preferred_element_type=jnp....]
    dot_general x4, matrix products: 2.91 us -> 0.65 us  [body(): jnp.dot(rows_lo, rounded, preferred_element_type=jnp.float32)]
    dot_general x3, matrix products: 2.54 us -> 0.73 us  [body(): jnp.einsum('kij,kjl->il', weights_above, updates, precision=high)]
    dot_general x6 -> x7, matrix products: 9.58 us -> 8.1 us  [the longest x1 3.34 us: moved(): jnp.dot(rows.astype(jnp.bfloat16), place, preferred_element_type=jnp.floa...]
  transfers between devices with their start and end apart: 7 -> 7, of which waited for: 6 -> 6; matrix products, arithmetic and copies ran while one was open for 20% -> 23% of each run, Pallas kernels for 0% -> 0%
where the time goes in v4:
time: 142 us; the launch traced here: 139 us
  waiting for transfers between devices  39.8 us (28%)
  matrix products  32.1 us (23%)
  starting transfers between devices  30.7 us (22%)
  blocking collectives  24.4 us (17%)
  other arithmetic  7.09 us (5%)
  local copies, waits for them, and re-layouts  4.97 us (4%)
    all_to_all x6, starting transfers between devices, gather_along(): return lax.all_to_all(copies, axis, 0, 0, tiled=True)  26.5 us
    all_to_all x3, blocking collectives, gather_along(): return lax.all_to_all(copies, axis, 0, 0, tiled=True)  24.4 us
    all_to_all x1, waiting for transfers between devices, body(): rows = jnp.sum(lax.all_to_all(spread, OWNERS, 0, 0, tiled=True), axis=0)  21.5 us
    all_to_all x6, waiting for transfers between devices, gather_along(): return lax.all_to_all(copies, axis, 0, 0, tiled=True)  18.3 us
    dot_general x1, matrix products, schur_rows(): solved = jnp.dot(inverse, coupled, preferred_element_type=jnp.float32)  10 us
    all_to_all x1, starting transfers between devices, body(): rows = jnp.sum(lax.all_to_all(spread, OWNERS, 0, 0, tiled=True), axis=0)  4.24 us
    broadcast_in_dim x9, local copies, waits for them, and re-layouts, gather_along(): copies = jnp.broadcast_to(block[None], (count,) + block.shape)  4.09 us
    dot_general x4, matrix products, body(): jnp.einsum('kij,kjl->il', weights_mine, updates, precision=high)  3.42 us
  transfers between devices with their start and end apart: 7, of which 6 were waited for; matrix products, arithmetic and copies ran while one was open for 23% of the time, Pallas kernels for 0%

profile of v4, /device:TPU:1, one launch (start us, length us, event | category | flops | bytes accessed | tf_op | source)
XLA Modules:
  0.0 139.4 jit_solution(6392939302842731888)
XLA Ops:
  0.0 0.9 bitcast_convert_fusion
  2.4 4.3 %all-to-all-start = ((f32[4,64,256]{2,1,0:T(8,128)}), f32[4,64,256]{2,1,0:T(8,128)S(1)}, u32[]{:S(2)}, u32[]{:S(2)}) async-start(f32[4,64,256]{2,1,0:T(8,128)} %broadcast_in_dim.31), calls=%async_computation | async-start | bytes 524288 | tf_op jit(solution)/shard_map/all_to_all | solution.py:18
  8.2 1.7 %convolution_convert_fusion = bf16[512,2560]{1,0:T(8,128)(2,1)S(1)} fusion(bf16[1,1,2560,512]{3,2,1,0:T(8,128)(2,1)S(1)} %copy-done, s32[512]{0:T(512)S(1)} %fusion.63), kind=kOutput, calls=%fused_computation.5 | convolution fusion | flops 1344012288 | bytes 5244928 | tf_op jit(solution)/shard_map/dot_general | solution.py:36
  9.9 10.0 %fusion = f32[512,2560]{1,0:T(8,128)S(1)} fusion(bf16[512,2560]{1,0:T(8,128)(2,1)S(1)} %convolution_convert_fusion, bf16[1,1,2560,2560]{3,2,1,0:T(8,128)(2,1)} %param.15), kind=kOutput, calls=%fused_computation | convolution fusion | flops 6710886400 | bytes 20971520 | tf_op jit(solution)/shard_map/dot_general | solution.py:38
  20.0 1.6 %fusion.3 = f32[512,512]{1,0:T(8,128)S(1)} fusion(bf16[512,2560]{1,0:T(8,128)(2,1)S(1)} %convolution_convert_fusion, f32[512,2560]{1,0:T(8,128)S(1)} %fusion), kind=kOutput, calls=%fused_computation.6 | convolution fusion | flops 1346109440 | bytes 8912896 | tf_op jit(solution)/shard_map/dot_general | solution.py:41
  21.6 2.5 %fusion.7 = f32[512,512]{1,0:T(8,128)} fusion(f32[512,512]{1,0:T(8,128)S(1)} %fusion.3, bf16[512,2560]{1,0:T(8,128)(2,1)S(1)} %convolution_convert_fusion, f32[512,2560]{1,0:T(8,128)S(1)} %fusion), kind=kOutput, calls=%fused_computation.10 | convolution fusion | flops 1345060864 | bytes 9961472 | tf_op jit(solution)/shard_map/dot_general | solution.py:40
  25.4 6.1 %all-to-all-start.1 = ((bf16[8,64,128]{2,1,0:T(8,128)(2,1)}), bf16[8,64,128]{2,1,0:T(8,128)(2,1)S(1)}, u32[]{:S(2)}, u32[]{:S(2)}) async-start(bf16[8,64,128]{2,1,0:T(8,128)(2,1)} %broadcast_in_dim.34), calls=%async_computation.1 | async-start | bytes 262144 | tf_op jit(solution)/shard_map/all_to_all | solution.py:18
  31.5 3.3 %convolution_subtract_fusion = f32[512,512]{1,0:T(8,128)} fusion(f32[512,512]{1,0:T(8,128)} %fusion.7, bf16[1,1,512,512]{3,2,1,0:T(8,128)(2,1)} %param.13, s32[512]{0:T(512)S(1)} %fusion.63), kind=kOutput, calls=%fused_computation.9 | convolution fusion | flops 537919488 | bytes 2623488 | tf_op jit(solution)/shard_map/dot_general | solution.py:33
  34.9 3.2 %all-to-all-done.1 = bf16[8,64,128]{2,1,0:T(8,128)(2,1)S(1)} async-done(((bf16[8,64,128]{2,1,0:T(8,128)(2,1)}), bf16[8,64,128]{2,1,0:T(8,128)(2,1)S(1)}, u32[]{:S(2)}, u32[]{:S(2)}) %all-to-all-start.1) | async-done | bytes 131104 | tf_op jit(solution)/shard_map/all_to_all | solution.py:18
  38.1 4.2 %all-to-all-start.2 = ((f32[8,64,512]{2,1,0:T(8,128)}), f32[8,64,512]{2,1,0:T(8,128)}, u32[]{:S(2)}, u32[]{:S(2)}) async-start(f32[8,64,512]{2,1,0:T(8,128)} %bitcast.191), calls=%async_computation.2 | async-start | bytes 2097152 | tf_op jit(solution)/shard_map/all_to_all | solution.py:98
  44.1 1.7 %maximum_bitcast_fusion = (f32[1,4,64,64]{3,2,1,0:T(8,128)S(1)}, f32[1,4,64,64]{3,2,1,0:T(8,128)}, f32[1,4,64,64]{3,2,1,0:T(8,128)}, f32[1,4,64,64]{3,2,1,0:T(8,128)}) fusion(f32[1,64,64]{2,1,0:T(8,128)S(1)} %broadcast.45, f32[1,64,64]{2,1,0:T(8,128)} %fusion.53, f32[4]{0:T(128)} %pad.20.clone, f32[1,64,64]{2,1,0:T(8,128)S(1)} %bitcast.194, ...), kind=kLoop, calls=%fused_computation.64 | loop fusion | flops 163840 | bytes 393232 | tf_op jit(solution)/shard_map/stack | solution.py:63
  45.8 21.5 %all-to-all-done.2 = f32[8,64,512]{2,1,0:T(8,128)} async-done(((f32[8,64,512]{2,1,0:T(8,128)}), f32[8,64,512]{2,1,0:T(8,128)}, u32[]{:S(2)}, u32[]{:S(2)}) %all-to-all-start.2) | async-done | bytes 1048608 | tf_op jit(solution)/shard_map/all_to_all | solution.py:98
  67.3 1.3 reduce_sum.9
  69.8 6.0 %all-to-all-start.3 = ((f32[4,64,128]{2,1,0:T(8,128)}), f32[4,64,128]{2,1,0:T(8,128)S(1)}, u32[]{:S(2)}, u32[]{:S(2)}) async-start(f32[4,64,128]{2,1,0:T(8,128)} %broadcast_in_dim.36), calls=%async_computation.3 | async-start | bytes 262144 | tf_op jit(solution)/shard_map/all_to_all | solution.py:18
  75.8 1.1 pad_maximum_fusion
  76.9 2.5 %all-to-all-done.3 = f32[4,64,128]{2,1,0:T(8,128)S(1)} async-done(((f32[4,64,128]{2,1,0:T(8,128)}), f32[4,64,128]{2,1,0:T(8,128)S(1)}, u32[]{:S(2)}, u32[]{:S(2)}) %all-to-all-start.3) | async-done | bytes 131104 | tf_op jit(solution)/shard_map/all_to_all | solution.py:18
  79.4 0.9 fusion.79
  80.9 3.4 %all-to-all-start.4 = ((bf16[8,64,128]{2,1,0:T(8,128)(2,1)}), bf16[8,64,128]{2,1,0:T(8,128)(2,1)S(1)}, u32[]{:S(2)}, u32[]{:S(2)}) async-start(bf16[8,64,128]{2,1,0:T(8,128)(2,1)} %broadcast_in_dim.37), calls=%async_computation.4 | async-start | bytes 262144 | tf_op jit(solution)/shard_map/all_to_all | solution.py:18
  84.5 1.0 fusion.16
  85.5 0.9 fusion.15
  86.4 4.2 %all-to-all-done.4 = bf16[8,64,128]{2,1,0:T(8,128)(2,1)S(1)} async-done(((bf16[8,64,128]{2,1,0:T(8,128)(2,1)}), bf16[8,64,128]{2,1,0:T(8,128)(2,1)S(1)}, u32[]{:S(2)}, u32[]{:S(2)}) %all-to-all-start.4) | async-done | bytes 131104 | tf_op jit(solution)/shard_map/all_to_all | solution.py:18
  91.0 8.1 %all_to_all.50 = f32[4,64,128]{2,1,0:T(8,128)S(1)} all-to-all(f32[4,64,128]{2,1,0:T(8,128)S(1)} %broadcast_in_dim.38), channel_id=1, replica_groups=mesh['sub'=2,'section'=4,'iface'=4] {'section'}, dimensions={0} | all-to-all | bytes 262144 | tf_op jit(solution)/shard_map/all_to_all | solution.py:18
  100.6 3.4 %all-to-all-start.6 = ((bf16[8,64,128]{2,1,0:T(8,128)(2,1)}), bf16[8,64,128]{2,1,0:T(8,128)(2,1)S(1)}, u32[]{:S(2)}, u32[]{:S(2)}) async-start(bf16[8,64,128]{2,1,0:T(8,128)(2,1)} %broadcast_in_dim.39), calls=%async_computation.6 | async-start | bytes 262144 | tf_op jit(solution)/shard_map/all_to_all | solution.py:18
  104.2 1.0 fusion.13
  105.2 0.9 fusion.12
  106.1 4.2 %all-to-all-done.6 = bf16[8,64,128]{2,1,0:T(8,128)(2,1)S(1)} async-done(((bf16[8,64,128]{2,1,0:T(8,128)(2,1)}), bf16[8,64,128]{2,1,0:T(8,128)(2,1)S(1)}, u32[]{:S(2)}, u32[]{:S(2)}) %all-to-all-start.6) | async-done | bytes 131104 | tf_op jit(solution)/shard_map/all_to_all | solution.py:18
  110.7 8.1 %all_to_all.51 = f32[4,64,128]{2,1,0:T(8,128)S(1)} all-to-all(f32[4,64,128]{2,1,0:T(8,128)S(1)} %broadcast_in_dim.40), channel_id=1, replica_groups=mesh['sub'=2,'section'=4,'iface'=4] {'section'}, dimensions={0} | all-to-all | bytes 262144 | tf_op jit(solution)/shard_map/all_to_all | solution.py:18
  120.3 3.4 %all-to-all-start.8 = ((bf16[8,64,128]{2,1,0:T(8,128)(2,1)}), bf16[8,64,128]{2,1,0:T(8,128)(2,1)S(1)}, u32[]{:S(2)}, u32[]{:S(2)}) async-start(bf16[8,64,128]{2,1,0:T(8,128)(2,1)} %broadcast_in_dim.41), calls=%async_computation.8 | async-start | bytes 262144 | tf_op jit(solution)/shard_map/all_to_all | solution.py:18
  124.0 1.0 fusion.10
  125.0 0.9 fusion.9
  125.9 4.2 %all-to-all-done.8 = bf16[8,64,128]{2,1,0:T(8,128)(2,1)S(1)} async-done(((bf16[8,64,128]{2,1,0:T(8,128)(2,1)}), bf16[8,64,128]{2,1,0:T(8,128)(2,1)S(1)}, u32[]{:S(2)}, u32[]{:S(2)}) %all-to-all-start.8) | async-done | bytes 131104 | tf_op jit(solution)/shard_map/all_to_all | solution.py:18
  130.4 8.1 %all_to_all.52 = f32[4,64,128]{2,1,0:T(8,128)S(1)} all-to-all(f32[4,64,128]{2,1,0:T(8,128)S(1)} %broadcast_in_dim.82), channel_id=1, replica_groups=mesh['sub'=2,'section'=4,'iface'=4] {'section'}, dimensions={0} | all-to-all | bytes 262144 | tf_op jit(solution)/shard_map/all_to_all | solution.py:18
  (56 shorter events, 13.5 us)
Async XLA Ops:
  0.0 8.2 %copy-start = (bf16[1,1,2560,512]{3,2,1,0:T(8,128)(2,1)S(1)}, bf16[1,1,2560,512]{3,2,1,0:T(8,128)(2,1)}, u32[]{:S(2)}) copy-start(bf16[1,1,2560,512]{3,2,1,0:T(8,128)(2,1)} %param.14) | copy-start | bytes 7864324
  2.4 22.2 %all-to-all-start = ((f32[4,64,256]{2,1,0:T(8,128)}), f32[4,64,256]{2,1,0:T(8,128)S(1)}, u32[]{:S(2)}, u32[]{:S(2)}) async-start(f32[4,64,256]{2,1,0:T(8,128)} %broadcast_in_dim.31), calls=%async_computation | async-start | bytes 524288 | tf_op jit(solution)/shard_map/all_to_all | solution.py:18
  21.5 3.1 %copy-start.4 = (f32[1,64,128]{2,1,0:T(8,128)S(1)}, f32[1,64,128]{2,1,0:T(8,128)}, u32[]{:S(2)}) copy-start(f32[1,64,128]{2,1,0:T(8,128)} %param.8) | copy-start | bytes 98308
  25.4 12.8 %all-to-all-start.1 = ((bf16[8,64,128]{2,1,0:T(8,128)(2,1)}), bf16[8,64,128]{2,1,0:T(8,128)(2,1)S(1)}, u32[]{:S(2)}, u32[]{:S(2)}) async-start(bf16[8,64,128]{2,1,0:T(8,128)(2,1)} %broadcast_in_dim.34), calls=%async_computation.1 | async-start | bytes 262144 | tf_op jit(solution)/shard_map/all_to_all | solution.py:18
  34.8 8.9 %copy-start.3 = (f32[1,64,128]{2,1,0:T(8,128)S(1)}, f32[1,64,128]{2,1,0:T(8,128)}, u32[]{:S(2)}) copy-start(f32[1,64,128]{2,1,0:T(8,128)} %param.9) | copy-start | bytes 98308
  34.8 9.1 %copy-start.1 = (bf16[1,1,64,64]{3,2,1,0:T(8,128)(2,1)S(1)}, bf16[1,1,64,64]{3,2,1,0:T(8,128)(2,1)}, u32[]{:S(2)}) copy-start(bf16[1,1,64,64]{3,2,1,0:T(8,128)(2,1)} %param.10) | copy-start | bytes 24580
  34.9 33.9 %copy-start.2 = (f32[4,64,64]{2,1,0:T(8,128)}, f32[4,64,64]{2,1,0:T(8,128)S(1)}, u32[]{:S(2)}) copy-start(f32[4,64,64]{2,1,0:T(8,128)S(1)} %slice.28) | copy-start | bytes 196612
  38.1 29.2 %all-to-all-start.2 = ((f32[8,64,512]{2,1,0:T(8,128)}), f32[8,64,512]{2,1,0:T(8,128)}, u32[]{:S(2)}, u32[]{:S(2)}) async-start(f32[8,64,512]{2,1,0:T(8,128)} %bitcast.191), calls=%async_computation.2 | async-start | bytes 2097152 | tf_op jit(solution)/shard_map/all_to_all | solution.py:98
  69.8 9.6 %all-to-all-start.3 = ((f32[4,64,128]{2,1,0:T(8,128)}), f32[4,64,128]{2,1,0:T(8,128)S(1)}, u32[]{:S(2)}, u32[]{:S(2)}) async-start(f32[4,64,128]{2,1,0:T(8,128)} %broadcast_in_dim.36), calls=%async_computation.3 | async-start | bytes 262144 | tf_op jit(solution)/shard_map/all_to_all | solution.py:18
  80.9 9.7 %all-to-all-start.4 = ((bf16[8,64,128]{2,1,0:T(8,128)(2,1)}), bf16[8,64,128]{2,1,0:T(8,128)(2,1)S(1)}, u32[]{:S(2)}, u32[]{:S(2)}) async-start(bf16[8,64,128]{2,1,0:T(8,128)(2,1)} %broadcast_in_dim.37), calls=%async_computation.4 | async-start | bytes 262144 | tf_op jit(solution)/shard_map/all_to_all | solution.py:18
  100.6 9.7 %all-to-all-start.6 = ((bf16[8,64,128]{2,1,0:T(8,128)(2,1)}), bf16[8,64,128]{2,1,0:T(8,128)(2,1)S(1)}, u32[]{:S(2)}, u32[]{:S(2)}) async-start(bf16[8,64,128]{2,1,0:T(8,128)(2,1)} %broadcast_in_dim.39), calls=%async_computation.6 | async-start | bytes 262144 | tf_op jit(solution)/shard_map/all_to_all | solution.py:18
  120.3 9.7 %all-to-all-start.8 = ((bf16[8,64,128]{2,1,0:T(8,128)(2,1)}), bf16[8,64,128]{2,1,0:T(8,128)(2,1)S(1)}, u32[]{:S(2)}, u32[]{:S(2)}) async-start(bf16[8,64,128]{2,1,0:T(8,128)(2,1)} %broadcast_in_dim.41), calls=%async_computation.8 | async-start | bytes 262144 | tf_op jit(solution)/shard_map/all_to_all | solution.py:18

commit v5 on v4

--- a/solution.py
+++ b/solution.py
@@ -78,6 +78,8 @@
         [previous[0], precond[0, 0].astype(jnp.float32), couple[0, 0].astype(jnp.float32)],
         axis=1,
     )
+    first_rounded = gather_along(previous[0].astype(jnp.bfloat16), OWNERS)
+    first_rounded, tables = lax.optimization_barrier((first_rounded, tables))
     tables = gather_along(tables, "section")
     start_all = tables[:, :, :load_count]
     precond_all = tables[:, :, load_count : load_count + block_nodes]
@@ -90,11 +92,10 @@
     precond_mine = precond[0, 0].astype(jnp.float32)
     couple_above = couple_all[above_pos]
 
-    first_rounded = gather_along(previous[0].astype(jnp.bfloat16), OWNERS)
     spread = schur_rows(
         block_ids[0, 0], iface_matrix[0, 0], interior_coupling[0, 0], inv_interior[0, 0], owners
     )
-    first_rounded, tables, spread = lax.optimization_barrier((first_rounded, tables, spread))
+    tables, spread = lax.optimization_barrier((tables, spread))
     rows = jnp.sum(lax.all_to_all(spread, OWNERS, 0, 0, tiled=True), axis=0)
     rows_hi, rows_lo = split_bf16(jnp.dot(precond_mine, rows, precision=lax.Precision.HIGHEST))
 

time: 142 us -> 140 us (0.986)
  other arithmetic: 7.09 us -> 4.84 us
  starting transfers between devices: 30.7 us -> 32.2 us
    all_to_all x1, starting transfers between devices: 4.24 us -> 5.73 us  [body(): rows = jnp.sum(lax.all_to_all(spread, OWNERS, 0, 0, tiled=True), axis=0)]
    all_to_all x6, waiting for transfers between devices: 18.3 us -> 16.9 us  [gather_along(): return lax.all_to_all(copies, axis, 0, 0, tiled=True)]
  transfers between devices with their start and end apart: 7 -> 7, of which waited for: 6 -> 6; matrix products, arithmetic and copies ran while one was open for 23% -> 22% of each run, Pallas kernels for 0% -> 0%
where the time goes in v5:
time: 140 us; the launch traced here: 138 us
  waiting for transfers between devices  39.5 us (28%)
  starting transfers between devices  32.2 us (23%)
  matrix products  32.1 us (23%)
  blocking collectives  24.4 us (17%)
  other arithmetic  4.84 us (3%)
  local copies, waits for them, and re-layouts  4.47 us (3%)
    all_to_all x6, starting transfers between devices, gather_along(): return lax.all_to_all(copies, axis, 0, 0, tiled=True)  26.4 us
    all_to_all x3, blocking collectives, gather_along(): return lax.all_to_all(copies, axis, 0, 0, tiled=True)  24.4 us
    all_to_all x1, waiting for transfers between devices, body(): rows = jnp.sum(lax.all_to_all(spread, OWNERS, 0, 0, tiled=True), axis=0)  22.7 us
    all_to_all x6, waiting for transfers between devices, gather_along(): return lax.all_to_all(copies, axis, 0, 0, tiled=True)  16.9 us
    dot_general x1, matrix products, schur_rows(): solved = jnp.dot(inverse, coupled, preferred_element_type=jnp.float32)  10.1 us
    all_to_all x1, starting transfers between devices, body(): rows = jnp.sum(lax.all_to_all(spread, OWNERS, 0, 0, tiled=True), axis=0)  5.73 us
    broadcast_in_dim x9, local copies, waits for them, and re-layouts, gather_along(): copies = jnp.broadcast_to(block[None], (count,) + block.shape)  4.1 us
    dot_general x4, matrix products, body(): jnp.einsum('kij,kjl->il', weights_mine, updates, precision=high)  3.42 us
  transfers between devices with their start and end apart: 7, of which 6 were waited for; matrix products, arithmetic and copies ran while one was open for 22% of the time, Pallas kernels for 0%

profile of v5, /device:TPU:1, one launch (start us, length us, event | category | flops | bytes accessed | tf_op | source)
XLA Modules:
  0.0 137.8 jit_solution(7844895187482701667)
XLA Ops:
  0.0 0.9 convert_bitcast_fusion
  1.6 6.4 %all-to-all-start = ((bf16[8,64,128]{2,1,0:T(8,128)(2,1)}), bf16[8,64,128]{2,1,0:T(8,128)(2,1)S(1)}, u32[]{:S(2)}, u32[]{:S(2)}) async-start(bf16[8,64,128]{2,1,0:T(8,128)(2,1)} %broadcast_in_dim.32), calls=%async_computation | async-start | bytes 262144 | tf_op jit(solution)/shard_map/all_to_all | solution.py:18
  8.8 1.7 %convolution_convert_fusion = bf16[512,2560]{1,0:T(8,128)(2,1)S(1)} fusion(bf16[1,1,2560,512]{3,2,1,0:T(8,128)(2,1)S(1)} %copy-done, s32[512]{0:T(512)S(1)} %fusion.63), kind=kOutput, calls=%fused_computation.5 | convolution fusion | flops 1344012288 | bytes 5244928 | tf_op jit(solution)/shard_map/dot_general | solution.py:36
  10.5 10.1 %fusion = f32[512,2560]{1,0:T(8,128)S(1)} fusion(bf16[512,2560]{1,0:T(8,128)(2,1)S(1)} %convolution_convert_fusion, bf16[1,1,2560,2560]{3,2,1,0:T(8,128)(2,1)} %param.15), kind=kOutput, calls=%fused_computation | convolution fusion | flops 6710886400 | bytes 20971520 | tf_op jit(solution)/shard_map/dot_general | solution.py:38
  20.6 1.6 %fusion.3 = f32[512,512]{1,0:T(8,128)S(1)} fusion(bf16[512,2560]{1,0:T(8,128)(2,1)S(1)} %convolution_convert_fusion, f32[512,2560]{1,0:T(8,128)S(1)} %fusion), kind=kOutput, calls=%fused_computation.6 | convolution fusion | flops 1346109440 | bytes 8912896 | tf_op jit(solution)/shard_map/dot_general | solution.py:41
  22.2 2.5 %fusion.7 = f32[512,512]{1,0:T(8,128)} fusion(f32[512,512]{1,0:T(8,128)S(1)} %fusion.3, bf16[512,2560]{1,0:T(8,128)(2,1)S(1)} %convolution_convert_fusion, f32[512,2560]{1,0:T(8,128)S(1)} %fusion), kind=kOutput, calls=%fused_computation.10 | convolution fusion | flops 1345060864 | bytes 9961472 | tf_op jit(solution)/shard_map/dot_general | solution.py:40
  25.5 4.3 %all-to-all-start.1 = ((f32[4,64,256]{2,1,0:T(8,128)}), f32[4,64,256]{2,1,0:T(8,128)S(1)}, u32[]{:S(2)}, u32[]{:S(2)}) async-start(f32[4,64,256]{2,1,0:T(8,128)} %broadcast_in_dim.33), calls=%async_computation.1 | async-start | bytes 524288 | tf_op jit(solution)/shard_map/all_to_all | solution.py:18
  29.8 3.3 %convolution_subtract_fusion = f32[512,512]{1,0:T(8,128)} fusion(f32[512,512]{1,0:T(8,128)} %fusion.7, bf16[1,1,512,512]{3,2,1,0:T(8,128)(2,1)} %param.13, s32[512]{0:T(512)S(1)} %fusion.63), kind=kOutput, calls=%fused_computation.9 | convolution fusion | flops 537919488 | bytes 2623488 | tf_op jit(solution)/shard_map/dot_general | solution.py:33
  33.3 1.7 %all-to-all-done.1 = f32[4,64,256]{2,1,0:T(8,128)S(1)} async-done(((f32[4,64,256]{2,1,0:T(8,128)}), f32[4,64,256]{2,1,0:T(8,128)S(1)}, u32[]{:S(2)}, u32[]{:S(2)}) %all-to-all-start.1) | async-done | bytes 262176 | tf_op jit(solution)/shard_map/all_to_all | solution.py:18
  35.0 5.7 %all-to-all-start.2 = ((f32[8,64,512]{2,1,0:T(8,128)}), f32[8,64,512]{2,1,0:T(8,128)}, u32[]{:S(2)}, u32[]{:S(2)}) async-start(f32[8,64,512]{2,1,0:T(8,128)} %bitcast.191), calls=%async_computation.2 | async-start | bytes 2097152 | tf_op jit(solution)/shard_map/all_to_all | solution.py:99
  43.4 22.7 %all-to-all-done.2 = f32[8,64,512]{2,1,0:T(8,128)} async-done(((f32[8,64,512]{2,1,0:T(8,128)}), f32[8,64,512]{2,1,0:T(8,128)}, u32[]{:S(2)}, u32[]{:S(2)}) %all-to-all-start.2) | async-done | bytes 1048608 | tf_op jit(solution)/shard_map/all_to_all | solution.py:99
  66.1 1.3 reduce_sum.9
  68.6 5.7 %all-to-all-start.3 = ((f32[4,64,128]{2,1,0:T(8,128)}), f32[4,64,128]{2,1,0:T(8,128)S(1)}, u32[]{:S(2)}, u32[]{:S(2)}) async-start(f32[4,64,128]{2,1,0:T(8,128)} %broadcast_in_dim.36), calls=%async_computation.3 | async-start | bytes 262144 | tf_op jit(solution)/shard_map/all_to_all | solution.py:18
  74.2 1.1 pad_maximum_fusion
  75.3 2.5 %all-to-all-done.3 = f32[4,64,128]{2,1,0:T(8,128)S(1)} async-done(((f32[4,64,128]{2,1,0:T(8,128)}), f32[4,64,128]{2,1,0:T(8,128)S(1)}, u32[]{:S(2)}, u32[]{:S(2)}) %all-to-all-start.3) | async-done | bytes 131104 | tf_op jit(solution)/shard_map/all_to_all | solution.py:18
  77.8 0.9 fusion.79
  79.3 3.4 %all-to-all-start.4 = ((bf16[8,64,128]{2,1,0:T(8,128)(2,1)}), bf16[8,64,128]{2,1,0:T(8,128)(2,1)S(1)}, u32[]{:S(2)}, u32[]{:S(2)}) async-start(bf16[8,64,128]{2,1,0:T(8,128)(2,1)} %broadcast_in_dim.37), calls=%async_computation.4 | async-start | bytes 262144 | tf_op jit(solution)/shard_map/all_to_all | solution.py:18
  83.0 1.0 fusion.16
  84.0 0.9 fusion.15
  84.9 4.2 %all-to-all-done.4 = bf16[8,64,128]{2,1,0:T(8,128)(2,1)S(1)} async-done(((bf16[8,64,128]{2,1,0:T(8,128)(2,1)}), bf16[8,64,128]{2,1,0:T(8,128)(2,1)S(1)}, u32[]{:S(2)}, u32[]{:S(2)}) %all-to-all-start.4) | async-done | bytes 131104 | tf_op jit(solution)/shard_map/all_to_all | solution.py:18
  89.4 8.1 %all_to_all.50 = f32[4,64,128]{2,1,0:T(8,128)S(1)} all-to-all(f32[4,64,128]{2,1,0:T(8,128)S(1)} %broadcast_in_dim.38), channel_id=1, replica_groups=mesh['sub'=2,'section'=4,'iface'=4] {'section'}, dimensions={0} | all-to-all | bytes 262144 | tf_op jit(solution)/shard_map/all_to_all | solution.py:18
  97.5 0.9 fusion.80
  99.1 3.4 %all-to-all-start.6 = ((bf16[8,64,128]{2,1,0:T(8,128)(2,1)}), bf16[8,64,128]{2,1,0:T(8,128)(2,1)S(1)}, u32[]{:S(2)}, u32[]{:S(2)}) async-start(bf16[8,64,128]{2,1,0:T(8,128)(2,1)} %broadcast_in_dim.39), calls=%async_computation.6 | async-start | bytes 262144 | tf_op jit(solution)/shard_map/all_to_all | solution.py:18
  102.7 1.0 fusion.13
  103.7 0.9 fusion.12
  104.6 4.2 %all-to-all-done.6 = bf16[8,64,128]{2,1,0:T(8,128)(2,1)S(1)} async-done(((bf16[8,64,128]{2,1,0:T(8,128)(2,1)}), bf16[8,64,128]{2,1,0:T(8,128)(2,1)S(1)}, u32[]{:S(2)}, u32[]{:S(2)}) %all-to-all-start.6) | async-done | bytes 131104 | tf_op jit(solution)/shard_map/all_to_all | solution.py:18
  109.1 8.1 %all_to_all.51 = f32[4,64,128]{2,1,0:T(8,128)S(1)} all-to-all(f32[4,64,128]{2,1,0:T(8,128)S(1)} %broadcast_in_dim.40), channel_id=1, replica_groups=mesh['sub'=2,'section'=4,'iface'=4] {'section'}, dimensions={0} | all-to-all | bytes 262144 | tf_op jit(solution)/shard_map/all_to_all | solution.py:18
  118.8 3.4 %all-to-all-start.8 = ((bf16[8,64,128]{2,1,0:T(8,128)(2,1)}), bf16[8,64,128]{2,1,0:T(8,128)(2,1)S(1)}, u32[]{:S(2)}, u32[]{:S(2)}) async-start(bf16[8,64,128]{2,1,0:T(8,128)(2,1)} %broadcast_in_dim.41), calls=%async_computation.8 | async-start | bytes 262144 | tf_op jit(solution)/shard_map/all_to_all | solution.py:18
  122.4 1.0 fusion.10
  123.4 0.9 fusion.9
  124.3 4.2 %all-to-all-done.8 = bf16[8,64,128]{2,1,0:T(8,128)(2,1)S(1)} async-done(((bf16[8,64,128]{2,1,0:T(8,128)(2,1)}), bf16[8,64,128]{2,1,0:T(8,128)(2,1)S(1)}, u32[]{:S(2)}, u32[]{:S(2)}) %all-to-all-start.8) | async-done | bytes 131104 | tf_op jit(solution)/shard_map/all_to_all | solution.py:18
  128.8 8.1 %all_to_all.52 = f32[4,64,128]{2,1,0:T(8,128)S(1)} all-to-all(f32[4,64,128]{2,1,0:T(8,128)S(1)} %broadcast_in_dim.82), channel_id=1, replica_groups=mesh['sub'=2,'section'=4,'iface'=4] {'section'}, dimensions={0} | all-to-all | bytes 262144 | tf_op jit(solution)/shard_map/all_to_all | solution.py:18
  (58 shorter events, 11.6 us)
Async XLA Ops:
  0.0 8.8 %copy-start = (bf16[1,1,2560,512]{3,2,1,0:T(8,128)(2,1)S(1)}, bf16[1,1,2560,512]{3,2,1,0:T(8,128)(2,1)}, u32[]{:S(2)}) copy-start(bf16[1,1,2560,512]{3,2,1,0:T(8,128)(2,1)} %param.14) | copy-start | bytes 7864324
  1.6 23.2 %all-to-all-start = ((bf16[8,64,128]{2,1,0:T(8,128)(2,1)}), bf16[8,64,128]{2,1,0:T(8,128)(2,1)S(1)}, u32[]{:S(2)}, u32[]{:S(2)}) async-start(bf16[8,64,128]{2,1,0:T(8,128)(2,1)} %broadcast_in_dim.32), calls=%async_computation | async-start | bytes 262144 | tf_op jit(solution)/shard_map/all_to_all | solution.py:18
  22.1 2.6 %copy-start.1 = (bf16[1,1,64,64]{3,2,1,0:T(8,128)(2,1)S(1)}, bf16[1,1,64,64]{3,2,1,0:T(8,128)(2,1)}, u32[]{:S(2)}) copy-start(bf16[1,1,64,64]{3,2,1,0:T(8,128)(2,1)} %param.10) | copy-start | bytes 24580
  22.1 2.5 %copy-start.5 = (bf16[1,1,64,64]{3,2,1,0:T(8,128)(2,1)S(1)}, bf16[1,1,64,64]{3,2,1,0:T(8,128)(2,1)}, u32[]{:S(2)}) copy-start(bf16[1,1,64,64]{3,2,1,0:T(8,128)(2,1)} %param.11) | copy-start | bytes 24580
  22.2 2.5 %copy-start.4 = (f32[1,64,128]{2,1,0:T(8,128)S(1)}, f32[1,64,128]{2,1,0:T(8,128)}, u32[]{:S(2)}) copy-start(f32[1,64,128]{2,1,0:T(8,128)} %param.8) | copy-start | bytes 98308
  25.5 9.5 %all-to-all-start.1 = ((f32[4,64,256]{2,1,0:T(8,128)}), f32[4,64,256]{2,1,0:T(8,128)S(1)}, u32[]{:S(2)}, u32[]{:S(2)}) async-start(f32[4,64,256]{2,1,0:T(8,128)} %broadcast_in_dim.33), calls=%async_computation.1 | async-start | bytes 524288 | tf_op jit(solution)/shard_map/all_to_all | solution.py:18
  33.2 9.0 %copy-start.3 = (f32[1,64,128]{2,1,0:T(8,128)S(1)}, f32[1,64,128]{2,1,0:T(8,128)}, u32[]{:S(2)}) copy-start(f32[1,64,128]{2,1,0:T(8,128)} %param.9) | copy-start | bytes 98308
  35.0 31.0 %all-to-all-start.2 = ((f32[8,64,512]{2,1,0:T(8,128)}), f32[8,64,512]{2,1,0:T(8,128)}, u32[]{:S(2)}, u32[]{:S(2)}) async-start(f32[8,64,512]{2,1,0:T(8,128)} %bitcast.191), calls=%async_computation.2 | async-start | bytes 2097152 | tf_op jit(solution)/shard_map/all_to_all | solution.py:99
  40.8 1.3 copy-start.2
  68.6 9.3 %all-to-all-start.3 = ((f32[4,64,128]{2,1,0:T(8,128)}), f32[4,64,128]{2,1,0:T(8,128)S(1)}, u32[]{:S(2)}, u32[]{:S(2)}) async-start(f32[4,64,128]{2,1,0:T(8,128)} %broadcast_in_dim.36), calls=%async_computation.3 | async-start | bytes 262144 | tf_op jit(solution)/shard_map/all_to_all | solution.py:18
  79.3 9.7 %all-to-all-start.4 = ((bf16[8,64,128]{2,1,0:T(8,128)(2,1)}), bf16[8,64,128]{2,1,0:T(8,128)(2,1)S(1)}, u32[]{:S(2)}, u32[]{:S(2)}) async-start(bf16[8,64,128]{2,1,0:T(8,128)(2,1)} %broadcast_in_dim.37), calls=%async_computation.4 | async-start | bytes 262144 | tf_op jit(solution)/shard_map/all_to_all | solution.py:18
  99.1 9.7 %all-to-all-start.6 = ((bf16[8,64,128]{2,1,0:T(8,128)(2,1)}), bf16[8,64,128]{2,1,0:T(8,128)(2,1)S(1)}, u32[]{:S(2)}, u32[]{:S(2)}) async-start(bf16[8,64,128]{2,1,0:T(8,128)(2,1)} %broadcast_in_dim.39), calls=%async_computation.6 | async-start | bytes 262144 | tf_op jit(solution)/shard_map/all_to_all | solution.py:18
  118.8 9.7 %all-to-all-start.8 = ((bf16[8,64,128]{2,1,0:T(8,128)(2,1)}), bf16[8,64,128]{2,1,0:T(8,128)(2,1)S(1)}, u32[]{:S(2)}, u32[]{:S(2)}) async-start(bf16[8,64,128]{2,1,0:T(8,128)(2,1)} %broadcast_in_dim.41), calls=%async_computation.8 | async-start | bytes 262144 | tf_op jit(solution)/shard_map/all_to_all | solution.py:18

commit v6 on v5

--- a/solution.py
+++ b/solution.py
@@ -16,6 +16,15 @@
     count = lax.axis_size(axis)
     copies = jnp.broadcast_to(block[None], (count,) + block.shape)
     return lax.all_to_all(copies, axis, 0, 0, tiled=True)
+
+
+def ring_parts(block, axis):
+    count = lax.axis_size(axis)
+    parts = [block]
+    for distance in range(1, count):
+        route = [(i, (i + distance) % count) for i in range(count)]
+        parts.append(lax.ppermute(block, axis, route))
+    return jnp.stack(parts)
 
 
 def schur_rows(block_list, boundary, coupled, inverse, owners):
@@ -87,8 +96,9 @@
     weights = chain_weights(precond_all, couple_all)
     above_pos = jnp.minimum(section_pos + 1, sections - 1)
     has_above = section_pos + 1 < sections
-    weights_mine = weights[section_pos]
-    weights_above = weights[above_pos]
+    behind = (section_pos - jnp.arange(sections)) % sections
+    weights_mine = jnp.take(weights[section_pos], behind, axis=0)
+    weights_above = jnp.take(weights[above_pos], behind, axis=0)
     precond_mine = precond[0, 0].astype(jnp.float32)
     couple_above = couple_all[above_pos]
 
@@ -115,7 +125,7 @@
             jnp.dot(rows_hi, rounded, preferred_element_type=jnp.float32)
             + jnp.dot(rows_lo, rounded, preferred_element_type=jnp.float32)
         )
-        updates = gather_along(update, "section")
+        updates = ring_parts(update, "section")
         temps_mine = jnp.einsum("kij,kjl->il", weights_mine, updates, precision=high)
         temps_above = jnp.einsum("kij,kjl->il", weights_above, updates, precision=high)
     return temps_mine[None]

time: 140 us -> 139 us (level)
  blocking collectives: 24.4 us -> 0 us
  starting transfers between devices: 32.2 us -> 42.1 us
  waiting for transfers between devices: 39.5 us -> 47.7 us
  local copies, waits for them, and re-layouts: 4.47 us -> 7.64 us
  matrix products: 32.1 us -> 34 us
    all_to_all x3 -> x0, blocking collectives: 24.4 us -> none  [gather_along(): return lax.all_to_all(copies, axis, 0, 0, tiled=True)]
    ppermute x0 -> x12, starting transfers between devices: none -> 15.6 us  [ring_parts(): parts.append(lax.ppermute(block, axis, route))]
    all_to_all x6 -> x5, starting transfers between devices: 26.4 us -> 20.8 us  [gather_along(): return lax.all_to_all(copies, axis, 0, 0, tiled=True)]
    all_to_all x6 -> x5, waiting for transfers between devices: 16.9 us -> 21.7 us  [gather_along(): return lax.all_to_all(copies, axis, 0, 0, tiled=True)]
    ppermute x0 -> x12, waiting for transfers between devices: none -> 3.34 us  [ring_parts(): parts.append(lax.ppermute(block, axis, route))]
    gather x0 -> x2, local copies, waits for them, and re-layouts: none -> 3.17 us  [the longest x1 1.59 us: body(): weights_mine = jnp.take(weights[section_pos], behind, axis=0)]
    dot_general x3, matrix products: 0.73 us -> 3.05 us  [body(): jnp.einsum('kij,kjl->il', weights_above, updates, precision=high)]
    another operation x2, other arithmetic: 1.87 us -> 0.13 us  [chain_weights(): return jnp.stack([jnp.stack(row) for row in rows])]
  transfers between devices with their start and end apart: 7 -> 18, of which waited for: 6 -> 10; matrix products, arithmetic and copies ran while one was open for 22% -> 22% of each run, Pallas kernels for 0% -> 0%
where the time goes in v6:
time: 139 us; the launch traced here: 136 us
  waiting for transfers between devices  47.7 us (34%)
  starting transfers between devices  42.1 us (30%)
  matrix products  34 us (24%)
  local copies, waits for them, and re-layouts  7.64 us (5%)
  other arithmetic  4.3 us (3%)
    all_to_all x1, waiting for transfers between devices, body(): rows = jnp.sum(lax.all_to_all(spread, OWNERS, 0, 0, tiled=True), axis=0)  22.7 us
    all_to_all x5, waiting for transfers between devices, gather_along(): return lax.all_to_all(copies, axis, 0, 0, tiled=True)  21.7 us
    all_to_all x5, starting transfers between devices, gather_along(): return lax.all_to_all(copies, axis, 0, 0, tiled=True)  20.8 us
    ppermute x12, starting transfers between devices, ring_parts(): parts.append(lax.ppermute(block, axis, route))  15.6 us
    dot_general x1, matrix products, schur_rows(): solved = jnp.dot(inverse, coupled, preferred_element_type=jnp.float32)  10.1 us
    all_to_all x1, starting transfers between devices, body(): rows = jnp.sum(lax.all_to_all(spread, OWNERS, 0, 0, tiled=True), axis=0)  5.72 us
    dot_general x4, matrix products, body(): jnp.einsum('kij,kjl->il', weights_mine, updates, precision=high)  3.97 us
    broadcast_in_dim x5, local copies, waits for them, and re-layouts, gather_along(): copies = jnp.broadcast_to(block[None], (count,) + block.shape)  3.37 us
  transfers between devices with their start and end apart: 18, of which 10 were waited for; matrix products, arithmetic and copies ran while one was open for 22% of the time, Pallas kernels for 0%

profile of v6, /device:TPU:1, one launch (start us, length us, event | category | flops | bytes accessed | tf_op | source)
XLA Modules:
  0.0 136.1 jit_solution(8235826898477450872)
XLA Ops:
  1.6 6.4 %all-to-all-start = ((bf16[8,64,128]{2,1,0:T(8,128)(2,1)}), bf16[8,64,128]{2,1,0:T(8,128)(2,1)S(1)}, u32[]{:S(2)}, u32[]{:S(2)}) async-start(bf16[8,64,128]{2,1,0:T(8,128)(2,1)} %broadcast_in_dim.57), calls=%async_computation | async-start | bytes 262144 | tf_op jit(solution)/shard_map/all_to_all | solution.py:18
  8.8 1.7 %convolution_convert_fusion = bf16[512,2560]{1,0:T(8,128)(2,1)S(1)} fusion(bf16[1,1,2560,512]{3,2,1,0:T(8,128)(2,1)S(1)} %copy-done, s32[512]{0:T(512)S(1)} %fusion.77), kind=kOutput, calls=%fused_computation.7 | convolution fusion | flops 1344012288 | bytes 5244928 | tf_op jit(solution)/shard_map/dot_general | solution.py:45
  10.5 10.1 %fusion = f32[512,2560]{1,0:T(8,128)S(1)} fusion(bf16[512,2560]{1,0:T(8,128)(2,1)S(1)} %convolution_convert_fusion, bf16[1,1,2560,2560]{3,2,1,0:T(8,128)(2,1)} %param.17), kind=kOutput, calls=%fused_computation.2 | convolution fusion | flops 6710886400 | bytes 20971520 | tf_op jit(solution)/shard_map/dot_general | solution.py:47
  20.6 1.6 %fusion.3 = f32[512,512]{1,0:T(8,128)S(1)} fusion(bf16[512,2560]{1,0:T(8,128)(2,1)S(1)} %convolution_convert_fusion, f32[512,2560]{1,0:T(8,128)S(1)} %fusion), kind=kOutput, calls=%fused_computation.8 | convolution fusion | flops 1346109440 | bytes 8912896 | tf_op jit(solution)/shard_map/dot_general | solution.py:50
  22.2 2.5 %fusion.7 = f32[512,512]{1,0:T(8,128)} fusion(f32[512,512]{1,0:T(8,128)S(1)} %fusion.3, bf16[512,2560]{1,0:T(8,128)(2,1)S(1)} %convolution_convert_fusion, f32[512,2560]{1,0:T(8,128)S(1)} %fusion), kind=kOutput, calls=%fused_computation.12 | convolution fusion | flops 1345060864 | bytes 9961472 | tf_op jit(solution)/shard_map/dot_general | solution.py:49
  25.5 3.4 %convolution_subtract_fusion = f32[512,512]{1,0:T(8,128)} fusion(f32[512,512]{1,0:T(8,128)} %fusion.7, bf16[1,1,512,512]{3,2,1,0:T(8,128)(2,1)} %param.15, s32[512]{0:T(512)S(1)} %fusion.77), kind=kOutput, calls=%fused_computation.11 | convolution fusion | flops 537919488 | bytes 2623488 | tf_op jit(solution)/shard_map/dot_general | solution.py:42
  29.6 4.3 %all-to-all-start.1 = ((f32[4,64,256]{2,1,0:T(8,128)}), f32[4,64,256]{2,1,0:T(8,128)S(1)}, u32[]{:S(2)}, u32[]{:S(2)}) async-start(f32[4,64,256]{2,1,0:T(8,128)} %broadcast_in_dim.58), calls=%async_computation.1 | async-start | bytes 524288 | tf_op jit(solution)/shard_map/all_to_all | solution.py:18
  34.5 4.6 %all-to-all-done.1 = f32[4,64,256]{2,1,0:T(8,128)S(1)} async-done(((f32[4,64,256]{2,1,0:T(8,128)}), f32[4,64,256]{2,1,0:T(8,128)S(1)}, u32[]{:S(2)}, u32[]{:S(2)}) %all-to-all-start.1) | async-done | bytes 262176 | tf_op jit(solution)/shard_map/all_to_all | solution.py:18
  39.1 5.7 %all-to-all-start.2 = ((f32[8,64,512]{2,1,0:T(8,128)}), f32[8,64,512]{2,1,0:T(8,128)}, u32[]{:S(2)}, u32[]{:S(2)}) async-start(f32[8,64,512]{2,1,0:T(8,128)} %bitcast.182), calls=%async_computation.2 | async-start | bytes 2097152 | tf_op jit(solution)/shard_map/all_to_all | solution.py:109
  47.4 22.7 %all-to-all-done.2 = f32[8,64,512]{2,1,0:T(8,128)} async-done(((f32[8,64,512]{2,1,0:T(8,128)}), f32[8,64,512]{2,1,0:T(8,128)}, u32[]{:S(2)}, u32[]{:S(2)}) %all-to-all-start.2) | async-done | bytes 1048608 | tf_op jit(solution)/shard_map/all_to_all | solution.py:109
  70.1 1.3 reduce_sum.9
  71.8 1.5 %fusion.17 = f32[64,128]{1,0:T(8,128)} fusion(f32[64,128]{1,0:T(8,128)} %fusion.18, f32[64,128]{1,0:T(8,128)S(1)} %fusion.104, bf16[64,512]{1,0:T(8,128)(2,1)S(1)} %get-tuple-element.14, bf16[512,128]{1,0:T(8,128)(2,1)S(1)} %bitcast.175), kind=kOutput, calls=%fused_computation.41 | convolution fusion | flops 8404992 | bytes 294912 | tf_op jit(solution)/shard_map/dot_general | solution.py:126
  73.3 2.4 %collective-permute-start.2 = (f32[64,128]{1,0:T(8,128)}, f32[64,128]{1,0:T(8,128)}, u32[]{:S(2)}, u32[]{:S(2)}) collective-permute-start(f32[64,128]{1,0:T(8,128)} %fusion.17), channel_id=1, source_target_pairs={{0,12},{4,0},{8,4},{12,8},{1,13},{5,1},{9,5},{13,9},{2,14},{6,2},{... | collective-permute-start | bytes 98312 | tf_op jit(solution)/shard_map/ppermute | solution.py:26
  76.1 1.3 collective-permute-start
  78.1 1.6 %gather_fusion = f32[4,64,64]{2,1,0:T(8,128)S(1)} fusion(f32[4,64,64]{2,1,0:T(8,128)} %get-tuple-element.13, s32[1024]{0:T(1024)} %pad_clamp_fusion), kind=kCustom, calls=%fused_computation.clone | custom fusion | bytes 131088 | tf_op jit(solution)/shard_map/jit(_take)/gather | solution.py:100
  79.7 1.6 %gather_fusion.1 = f32[4,64,64]{2,1,0:T(8,128)S(1)} fusion(f32[4,64,64]{2,1,0:T(8,128)} %get-tuple-element.12, s32[1024]{0:T(1024)} %pad_clamp_fusion), kind=kCustom, calls=%fused_computation.1.clone | custom fusion | bytes 131088 | tf_op jit(solution)/shard_map/jit(_take)/gather | solution.py:101
  81.3 1.1 fusion.101
  82.4 1.1 convolution_bitcast_fusion.9
  84.2 3.4 %all-to-all-start.3 = ((bf16[8,64,128]{2,1,0:T(8,128)(2,1)}), bf16[8,64,128]{2,1,0:T(8,128)(2,1)S(1)}, u32[]{:S(2)}, u32[]{:S(2)}) async-start(bf16[8,64,128]{2,1,0:T(8,128)(2,1)} %broadcast_in_dim.61), calls=%async_computation.3 | async-start | bytes 262144 | tf_op jit(solution)/shard_map/all_to_all | solution.py:18
  87.6 1.0 fusion.16
  88.7 5.9 %all-to-all-done.3 = bf16[8,64,128]{2,1,0:T(8,128)(2,1)S(1)} async-done(((bf16[8,64,128]{2,1,0:T(8,128)(2,1)}), bf16[8,64,128]{2,1,0:T(8,128)(2,1)S(1)}, u32[]{:S(2)}, u32[]{:S(2)}) %all-to-all-start.3) | async-done | bytes 131104 | tf_op jit(solution)/shard_map/all_to_all | solution.py:18
  95.4 1.0 collective-permute-start.4
  97.3 1.2 collective-permute-done.5
  99.5 1.0 convolution_bitcast_fusion.6
  101.1 3.4 %all-to-all-start.4 = ((bf16[8,64,128]{2,1,0:T(8,128)(2,1)}), bf16[8,64,128]{2,1,0:T(8,128)(2,1)S(1)}, u32[]{:S(2)}, u32[]{:S(2)}) async-start(bf16[8,64,128]{2,1,0:T(8,128)(2,1)} %broadcast_in_dim.62), calls=%async_computation.4 | async-start | bytes 262144 | tf_op jit(solution)/shard_map/all_to_all | solution.py:18
  104.5 1.0 fusion.13
  105.6 5.3 %all-to-all-done.4 = bf16[8,64,128]{2,1,0:T(8,128)(2,1)S(1)} async-done(((bf16[8,64,128]{2,1,0:T(8,128)(2,1)}), bf16[8,64,128]{2,1,0:T(8,128)(2,1)S(1)}, u32[]{:S(2)}, u32[]{:S(2)}) %all-to-all-start.4) | async-done | bytes 131104 | tf_op jit(solution)/shard_map/all_to_all | solution.py:18
  111.2 3.1 %collective-permute-start.8 = (f32[64,128]{1,0:T(8,128)S(1)}, f32[64,128]{1,0:T(8,128)S(1)}, u32[]{:S(2)}, u32[]{:S(2)}) collective-permute-start(f32[64,128]{1,0:T(8,128)S(1)} %fusion.11), channel_id=1, source_target_pairs={{0,12},{4,0},{8,4},{12,8},{1,13},{5,1},{9,5},{13,9},{2,14},{6,2},{... | collective-permute-start | bytes 98312 | tf_op jit(solution)/shard_map/ppermute | solution.py:26
  114.9 1.1 collective-permute-start.6
  119.7 3.4 %all-to-all-start.5 = ((bf16[8,64,128]{2,1,0:T(8,128)(2,1)}), bf16[8,64,128]{2,1,0:T(8,128)(2,1)S(1)}, u32[]{:S(2)}, u32[]{:S(2)}) async-start(bf16[8,64,128]{2,1,0:T(8,128)(2,1)} %broadcast_in_dim.63), calls=%async_computation.5 | async-start | bytes 262144 | tf_op jit(solution)/shard_map/all_to_all | solution.py:18
  123.4 5.9 %all-to-all-done.5 = bf16[8,64,128]{2,1,0:T(8,128)(2,1)S(1)} async-done(((bf16[8,64,128]{2,1,0:T(8,128)(2,1)}), bf16[8,64,128]{2,1,0:T(8,128)(2,1)S(1)}, u32[]{:S(2)}, u32[]{:S(2)}) %all-to-all-start.5) | async-done | bytes 131104 | tf_op jit(solution)/shard_map/all_to_all | solution.py:18
  129.7 2.8 %collective-permute-start.11 = (f32[64,128]{1,0:T(8,128)S(1)}, f32[64,128]{1,0:T(8,128)S(1)}, u32[]{:S(2)}, u32[]{:S(2)}) collective-permute-start(f32[64,128]{1,0:T(8,128)S(1)} %fusion.8), channel_id=1, source_target_pairs={{0,12},{4,0},{8,4},{12,8},{1,13},{5,1},{9,5},{13,9},{2,14},{6,2},{... | collective-permute-start | bytes 98312 | tf_op jit(solution)/shard_map/ppermute | solution.py:26
  (87 shorter events, 21.7 us)
Async XLA Ops:
  0.0 8.8 %copy-start = (bf16[1,1,2560,512]{3,2,1,0:T(8,128)(2,1)S(1)}, bf16[1,1,2560,512]{3,2,1,0:T(8,128)(2,1)}, u32[]{:S(2)}) copy-start(bf16[1,1,2560,512]{3,2,1,0:T(8,128)(2,1)} %param.16) | copy-start | bytes 7864324
  1.6 27.3 %all-to-all-start = ((bf16[8,64,128]{2,1,0:T(8,128)(2,1)}), bf16[8,64,128]{2,1,0:T(8,128)(2,1)S(1)}, u32[]{:S(2)}, u32[]{:S(2)}) async-start(bf16[8,64,128]{2,1,0:T(8,128)(2,1)} %broadcast_in_dim.57), calls=%async_computation | async-start | bytes 262144 | tf_op jit(solution)/shard_map/all_to_all | solution.py:18
  22.1 3.2 %copy-start.1 = (bf16[1,1,64,64]{3,2,1,0:T(8,128)(2,1)S(1)}, bf16[1,1,64,64]{3,2,1,0:T(8,128)(2,1)}, u32[]{:S(2)}) copy-start(bf16[1,1,64,64]{3,2,1,0:T(8,128)(2,1)} %param.12) | copy-start | bytes 24580
  22.2 3.2 %copy-start.8 = (bf16[1,1,64,64]{3,2,1,0:T(8,128)(2,1)S(1)}, bf16[1,1,64,64]{3,2,1,0:T(8,128)(2,1)}, u32[]{:S(2)}) copy-start(bf16[1,1,64,64]{3,2,1,0:T(8,128)(2,1)} %param.13) | copy-start | bytes 24580
  22.2 3.2 %copy-start.6 = (f32[1,64,128]{2,1,0:T(8,128)S(1)}, f32[1,64,128]{2,1,0:T(8,128)}, u32[]{:S(2)}) copy-start(f32[1,64,128]{2,1,0:T(8,128)} %param.10) | copy-start | bytes 98308
  29.6 9.5 %all-to-all-start.1 = ((f32[4,64,256]{2,1,0:T(8,128)}), f32[4,64,256]{2,1,0:T(8,128)S(1)}, u32[]{:S(2)}, u32[]{:S(2)}) async-start(f32[4,64,256]{2,1,0:T(8,128)} %broadcast_in_dim.58), calls=%async_computation.1 | async-start | bytes 524288 | tf_op jit(solution)/shard_map/all_to_all | solution.py:18
  39.1 31.0 %all-to-all-start.2 = ((f32[8,64,512]{2,1,0:T(8,128)}), f32[8,64,512]{2,1,0:T(8,128)}, u32[]{:S(2)}, u32[]{:S(2)}) async-start(f32[8,64,512]{2,1,0:T(8,128)} %bitcast.182), calls=%async_computation.2 | async-start | bytes 2097152 | tf_op jit(solution)/shard_map/all_to_all | solution.py:109
  44.8 1.6 %copy-start.4 = (f32[1,64,128]{2,1,0:T(8,128)S(1)}, f32[1,64,128]{2,1,0:T(8,128)}, u32[]{:S(2)}) copy-start(f32[1,64,128]{2,1,0:T(8,128)} %param.11) | copy-start | bytes 98308
  44.8 1.9 %copy-start.7 = (f32[1,64,128]{2,1,0:T(8,128)S(1)}, f32[1,64,128]{2,1,0:T(8,128)}, u32[]{:S(2)}) copy-start(f32[1,64,128]{2,1,0:T(8,128)} %param.10) | copy-start | bytes 98308
  44.9 1.5 %copy-start.2 = (f32[4,64,64]{2,1,0:T(8,128)}, f32[4,64,64]{2,1,0:T(8,128)S(1)}, u32[]{:S(2)}) copy-start(f32[4,64,64]{2,1,0:T(8,128)S(1)} %slice.32) | copy-start | bytes 196612
  71.6 15.9 %copy-start.3 = (f32[4,64,64]{2,1,0:T(8,128)S(1)}, f32[4,64,64]{2,1,0:T(8,128)}, u32[]{:S(2)}) copy-start(f32[4,64,64]{2,1,0:T(8,128)} %copy-done.2) | copy-start | bytes 196612
  73.3 7.9 %collective-permute-start.2 = (f32[64,128]{1,0:T(8,128)}, f32[64,128]{1,0:T(8,128)}, u32[]{:S(2)}, u32[]{:S(2)}) collective-permute-start(f32[64,128]{1,0:T(8,128)} %fusion.17), channel_id=1, source_target_pairs={{0,12},{4,0},{8,4},{12,8},{1,13},{5,1},{9,5},{13,9},{2,14},{6,2},{... | collective-permute-start | bytes 98312 | tf_op jit(solution)/shard_map/ppermute | solution.py:26
  75.7 5.6 %collective-permute-start.1 = (f32[64,128]{1,0:T(8,128)}, f32[64,128]{1,0:T(8,128)}, u32[]{:S(2)}, u32[]{:S(2)}) collective-permute-start(f32[64,128]{1,0:T(8,128)} %fusion.17), channel_id=1, source_target_pairs={{0,8},{4,12},{8,0},{12,4},{1,9},{5,13},{9,1},{13,5},{2,10},{6,14},... | collective-permute-start | bytes 98312 | tf_op jit(solution)/shard_map/ppermute | solution.py:26
  76.1 5.2 %collective-permute-start = (f32[64,128]{1,0:T(8,128)}, f32[64,128]{1,0:T(8,128)}, u32[]{:S(2)}, u32[]{:S(2)}) collective-permute-start(f32[64,128]{1,0:T(8,128)} %fusion.17), channel_id=1, source_target_pairs={{0,4},{4,8},{8,12},{12,0},{1,5},{5,9},{9,13},{13,1},{2,6},{6,10},{... | collective-permute-start | bytes 98312 | tf_op jit(solution)/shard_map/ppermute | solution.py:26
  78.1 45.0 %copy-start.5 = (f32[1,64,128]{2,1,0:T(8,128)S(1)}, f32[1,64,128]{2,1,0:T(8,128)}, u32[]{:S(2)}) copy-start(f32[1,64,128]{2,1,0:T(8,128)} %param.11) | copy-start | bytes 98308
  82.4 52.8 %copy-start.9 = (pred[4]{0:T(512)(128)(4,1)S(1)}, pred[4]{0:T(512)(128)(4,1)}, u32[]{:S(2)}) copy-start(pred[4]{0:T(512)(128)(4,1)} %compare_and_fusion) | copy-start | bytes 16
  84.2 10.4 %all-to-all-start.3 = ((bf16[8,64,128]{2,1,0:T(8,128)(2,1)}), bf16[8,64,128]{2,1,0:T(8,128)(2,1)S(1)}, u32[]{:S(2)}, u32[]{:S(2)}) async-start(bf16[8,64,128]{2,1,0:T(8,128)(2,1)} %broadcast_in_dim.61), calls=%async_computation.3 | async-start | bytes 262144 | tf_op jit(solution)/shard_map/all_to_all | solution.py:18
  94.9 3.5 %collective-permute-start.5 = (f32[64,128]{1,0:T(8,128)S(1)}, f32[64,128]{1,0:T(8,128)S(1)}, u32[]{:S(2)}, u32[]{:S(2)}) collective-permute-start(f32[64,128]{1,0:T(8,128)S(1)} %fusion.14), channel_id=1, source_target_pairs={{0,12},{4,0},{8,4},{12,8},{1,13},{5,1},{9,5},{13,9},{2,14},{6,2},{... | collective-permute-start | bytes 98312 | tf_op jit(solution)/shard_map/ppermute | solution.py:26
  95.4 3.1 %collective-permute-start.4 = (f32[64,128]{1,0:T(8,128)S(1)}, f32[64,128]{1,0:T(8,128)S(1)}, u32[]{:S(2)}, u32[]{:S(2)}) collective-permute-start(f32[64,128]{1,0:T(8,128)S(1)} %fusion.14), channel_id=1, source_target_pairs={{0,8},{4,12},{8,0},{12,4},{1,9},{5,13},{9,1},{13,5},{2,10},{6,14},... | collective-permute-start | bytes 98312 | tf_op jit(solution)/shard_map/ppermute | solution.py:26
  96.3 2.1 %collective-permute-start.3 = (f32[64,128]{1,0:T(8,128)S(1)}, f32[64,128]{1,0:T(8,128)S(1)}, u32[]{:S(2)}, u32[]{:S(2)}) collective-permute-start(f32[64,128]{1,0:T(8,128)S(1)} %fusion.14), channel_id=1, source_target_pairs={{0,4},{4,8},{8,12},{12,0},{1,5},{5,9},{9,13},{13,1},{2,6},{6,10},{... | collective-permute-start | bytes 98312 | tf_op jit(solution)/shard_map/ppermute | solution.py:26
  101.1 9.8 %all-to-all-start.4 = ((bf16[8,64,128]{2,1,0:T(8,128)(2,1)}), bf16[8,64,128]{2,1,0:T(8,128)(2,1)S(1)}, u32[]{:S(2)}, u32[]{:S(2)}) async-start(bf16[8,64,128]{2,1,0:T(8,128)(2,1)} %broadcast_in_dim.62), calls=%async_computation.4 | async-start | bytes 262144 | tf_op jit(solution)/shard_map/all_to_all | solution.py:18
  111.2 5.2 %collective-permute-start.8 = (f32[64,128]{1,0:T(8,128)S(1)}, f32[64,128]{1,0:T(8,128)S(1)}, u32[]{:S(2)}, u32[]{:S(2)}) collective-permute-start(f32[64,128]{1,0:T(8,128)S(1)} %fusion.11), channel_id=1, source_target_pairs={{0,12},{4,0},{8,4},{12,8},{1,13},{5,1},{9,5},{13,9},{2,14},{6,2},{... | collective-permute-start | bytes 98312 | tf_op jit(solution)/shard_map/ppermute | solution.py:26
  114.3 2.8 %collective-permute-start.7 = (f32[64,128]{1,0:T(8,128)S(1)}, f32[64,128]{1,0:T(8,128)S(1)}, u32[]{:S(2)}, u32[]{:S(2)}) collective-permute-start(f32[64,128]{1,0:T(8,128)S(1)} %fusion.11), channel_id=1, source_target_pairs={{0,8},{4,12},{8,0},{12,4},{1,9},{5,13},{9,1},{13,5},{2,10},{6,14},... | collective-permute-start | bytes 98312 | tf_op jit(solution)/shard_map/ppermute | solution.py:26
  114.9 2.1 %collective-permute-start.6 = (f32[64,128]{1,0:T(8,128)S(1)}, f32[64,128]{1,0:T(8,128)S(1)}, u32[]{:S(2)}, u32[]{:S(2)}) collective-permute-start(f32[64,128]{1,0:T(8,128)S(1)} %fusion.11), channel_id=1, source_target_pairs={{0,4},{4,8},{8,12},{12,0},{1,5},{5,9},{9,13},{13,1},{2,6},{6,10},{... | collective-permute-start | bytes 98312 | tf_op jit(solution)/shard_map/ppermute | solution.py:26
  119.7 9.7 %all-to-all-start.5 = ((bf16[8,64,128]{2,1,0:T(8,128)(2,1)}), bf16[8,64,128]{2,1,0:T(8,128)(2,1)S(1)}, u32[]{:S(2)}, u32[]{:S(2)}) async-start(bf16[8,64,128]{2,1,0:T(8,128)(2,1)} %broadcast_in_dim.63), calls=%async_computation.5 | async-start | bytes 262144 | tf_op jit(solution)/shard_map/all_to_all | solution.py:18
  129.7 5.1 %collective-permute-start.11 = (f32[64,128]{1,0:T(8,128)S(1)}, f32[64,128]{1,0:T(8,128)S(1)}, u32[]{:S(2)}, u32[]{:S(2)}) collective-permute-start(f32[64,128]{1,0:T(8,128)S(1)} %fusion.8), channel_id=1, source_target_pairs={{0,12},{4,0},{8,4},{12,8},{1,13},{5,1},{9,5},{13,9},{2,14},{6,2},{... | collective-permute-start | bytes 98312 | tf_op jit(solution)/shard_map/ppermute | solution.py:26
  132.4 2.8 %collective-permute-start.10 = (f32[64,128]{1,0:T(8,128)S(1)}, f32[64,128]{1,0:T(8,128)S(1)}, u32[]{:S(2)}, u32[]{:S(2)}) collective-permute-start(f32[64,128]{1,0:T(8,128)S(1)} %fusion.8), channel_id=1, source_target_pairs={{0,8},{4,12},{8,0},{12,4},{1,9},{5,13},{9,1},{13,5},{2,10},{6,14},... | collective-permute-start | bytes 98312 | tf_op jit(solution)/shard_map/ppermute | solution.py:26
  133.3 1.9 %collective-permute-start.9 = (f32[64,128]{1,0:T(8,128)S(1)}, f32[64,128]{1,0:T(8,128)S(1)}, u32[]{:S(2)}, u32[]{:S(2)}) collective-permute-start(f32[64,128]{1,0:T(8,128)S(1)} %fusion.8), channel_id=1, source_target_pairs={{0,4},{4,8},{8,12},{12,0},{1,5},{5,9},{9,13},{13,1},{2,6},{6,10},{... | collective-permute-start | bytes 98312 | tf_op jit(solution)/shard_map/ppermute | solution.py:26

commit v7 on v6

--- a/solution.py
+++ b/solution.py
@@ -25,6 +25,19 @@
         route = [(i, (i + distance) % count) for i in range(count)]
         parts.append(lax.ppermute(block, axis, route))
     return jnp.stack(parts)
+
+
+def gather_owners(block):
+    inner = ring_parts(block, "iface")
+    outer = ring_parts(inner, "sub")
+    return outer.reshape((-1,) + block.shape)
+
+
+def ring_owner_order():
+    subs, ifaces = lax.axis_size("sub"), lax.axis_size("iface")
+    sub_back = (lax.axis_index("sub") - jnp.arange(subs)[:, None]) % subs
+    iface_back = (lax.axis_index("iface") - jnp.arange(ifaces)[None, :]) % ifaces
+    return (sub_back * ifaces + iface_back).reshape(-1)
 
 
 def schur_rows(block_list, boundary, coupled, inverse, owners):
@@ -87,7 +100,7 @@
         [previous[0], precond[0, 0].astype(jnp.float32), couple[0, 0].astype(jnp.float32)],
         axis=1,
     )
-    first_rounded = gather_along(previous[0].astype(jnp.bfloat16), OWNERS)
+    first_rounded = gather_owners(previous[0].astype(jnp.bfloat16))
     first_rounded, tables = lax.optimization_barrier((first_rounded, tables))
     tables = gather_along(tables, "section")
     start_all = tables[:, :, :load_count]
@@ -107,6 +120,8 @@
     )
     tables, spread = lax.optimization_barrier((tables, spread))
     rows = jnp.sum(lax.all_to_all(spread, OWNERS, 0, 0, tiled=True), axis=0)
+    rows = jnp.take(rows.reshape(block_nodes, owners, block_nodes), ring_owner_order(), axis=1)
+    rows = rows.reshape(block_nodes, nodes)
     rows_hi, rows_lo = split_bf16(jnp.dot(precond_mine, rows, precision=lax.Precision.HIGHEST))
 
     temps_mine = previous[0]
@@ -116,7 +131,7 @@
         if sweep_index == 0:
             rounded = first_rounded
         else:
-            rounded = gather_along(temps_mine.astype(jnp.bfloat16), OWNERS)
+            rounded = gather_owners(temps_mine.astype(jnp.bfloat16))
         rounded = rounded.reshape(nodes, load_count)
         from_above = jnp.einsum("ij,il->jl", couple_above, temps_above, precision=high)
         from_above = jnp.where(has_above, from_above, 0.0)

time: 139 us -> 143 us (1.029)
  other arithmetic: 4.3 us -> 6.94 us
  local copies, waits for them, and re-layouts: 7.64 us -> 9.47 us
  matrix products: 34 us -> 32.2 us
    ppermute x12 -> x28, waiting for transfers between devices: 3.34 us -> 21.1 us  [ring_parts(): parts.append(lax.ppermute(block, axis, route))]
    all_to_all x5 -> x1, waiting for transfers between devices: 21.7 us -> 4.69 us  [gather_along(): return lax.all_to_all(copies, axis, 0, 0, tiled=True)]
    ppermute x12 -> x28, starting transfers between devices: 15.6 us -> 31.9 us  [ring_parts(): parts.append(lax.ppermute(block, axis, route))]
    all_to_all x5 -> x1, starting transfers between devices: 20.8 us -> 6.03 us  [gather_along(): return lax.all_to_all(copies, axis, 0, 0, tiled=True)]
    broadcast_in_dim x5 -> x1, local copies, waits for them, and re-layouts: 3.37 us -> 0.72 us  [gather_along(): copies = jnp.broadcast_to(block[None], (count,) + block.shape)]
    reshape x0 -> x2, local copies, waits for them, and re-layouts: none -> 1.76 us  [body(): rows.reshape(block_nodes, owners, block_nodes)]
    gather x0 -> x1, local copies, waits for them, and re-layouts: none -> 1.63 us  [body(): jnp.take(rows.reshape(block_nodes, owners, block_nodes), ring_owner_order...]
  transfers between devices with their start and end apart: 18 -> 30, of which waited for: 10 -> 19; matrix products, arithmetic and copies ran while one was open for 22% -> 23% of each run, Pallas kernels for 0% -> 0%
where the time goes in v7:
time: 143 us; the launch traced here: 140 us
  waiting for transfers between devices  48.5 us (34%)
  starting transfers between devices  42.7 us (30%)
  matrix products  32.2 us (23%)
  local copies, waits for them, and re-layouts  9.47 us (7%)
  other arithmetic  6.94 us (5%)
    ppermute x28, starting transfers between devices, ring_parts(): parts.append(lax.ppermute(block, axis, route))  31.9 us
    all_to_all x1, waiting for transfers between devices, body(): rows = jnp.sum(lax.all_to_all(spread, OWNERS, 0, 0, tiled=True), axis=0)  22.7 us
    ppermute x28, waiting for transfers between devices, ring_parts(): parts.append(lax.ppermute(block, axis, route))  21.1 us
    dot_general x1, matrix products, schur_rows(): solved = jnp.dot(inverse, coupled, preferred_element_type=jnp.float32)  10.1 us
    all_to_all x1, starting transfers between devices, gather_along(): return lax.all_to_all(copies, axis, 0, 0, tiled=True)  6.03 us
    all_to_all x1, starting transfers between devices, body(): rows = jnp.sum(lax.all_to_all(spread, OWNERS, 0, 0, tiled=True), axis=0)  4.73 us
    all_to_all x1, waiting for transfers between devices, gather_along(): return lax.all_to_all(copies, axis, 0, 0, tiled=True)  4.69 us
    dot_general x1, matrix products, moved(): jnp.dot(rows.astype(jnp.bfloat16), place, preferred_element_type=jnp.floa...  3.36 us
  transfers between devices with their start and end apart: 30, of which 19 were waited for; matrix products, arithmetic and copies ran while one was open for 23% of the time, Pallas kernels for 0%

profile of v7, /device:TPU:1, one launch (start us, length us, event | category | flops | bytes accessed | tf_op | source)
XLA Modules:
  0.0 140.2 jit_solution(13891480069170671949)
XLA Ops:
  0.9 4.2 %collective-permute-start.2 = (bf16[64,128]{1,0:T(8,128)(2,1)S(1)}, bf16[64,128]{1,0:T(8,128)(2,1)S(1)}, u32[]{:S(2)}, u32[]{:S(2)}) collective-permute-start(bf16[64,128]{1,0:T(8,128)(2,1)S(1)} %get-tuple-element.29), channel_id=1, source_target_pairs={{0,3},{1,0},{2,1},{3,2},{4,7},{5,4},{6,5},{7,6},{8,11},{9,8},{10,9... | collective-permute-start | bytes 49160 | tf_op jit(solution)/shard_map/ppermute | solution.py:26
  6.4 1.7 %convolution_convert_fusion = bf16[512,2560]{1,0:T(8,128)(2,1)S(1)} fusion(bf16[1,1,2560,512]{3,2,1,0:T(8,128)(2,1)S(1)} %copy-done, s32[512]{0:T(512)S(1)} %fusion.77), kind=kOutput, calls=%fused_computation.8 | convolution fusion | flops 1344012288 | bytes 5244928 | tf_op jit(solution)/shard_map/dot_general | solution.py:58
  8.1 10.1 %fusion = f32[512,2560]{1,0:T(8,128)S(1)} fusion(bf16[512,2560]{1,0:T(8,128)(2,1)S(1)} %convolution_convert_fusion, bf16[1,1,2560,2560]{3,2,1,0:T(8,128)(2,1)} %param.17), kind=kOutput, calls=%fused_computation.3 | convolution fusion | flops 6710886400 | bytes 20971520 | tf_op jit(solution)/shard_map/dot_general | solution.py:60
  18.2 1.6 %fusion.3 = f32[512,512]{1,0:T(8,128)S(1)} fusion(bf16[512,2560]{1,0:T(8,128)(2,1)S(1)} %convolution_convert_fusion, f32[512,2560]{1,0:T(8,128)S(1)} %fusion), kind=kOutput, calls=%fused_computation.9 | convolution fusion | flops 1346109440 | bytes 8912896 | tf_op jit(solution)/shard_map/dot_general | solution.py:63
  19.8 2.5 %fusion.7 = f32[512,512]{1,0:T(8,128)} fusion(f32[512,512]{1,0:T(8,128)S(1)} %fusion.3, bf16[512,2560]{1,0:T(8,128)(2,1)S(1)} %convolution_convert_fusion, f32[512,2560]{1,0:T(8,128)S(1)} %fusion), kind=kOutput, calls=%fused_computation.13 | convolution fusion | flops 1345060864 | bytes 9961472 | tf_op jit(solution)/shard_map/dot_general | solution.py:62
  23.1 3.4 %convolution_subtract_fusion = f32[512,512]{1,0:T(8,128)} fusion(f32[512,512]{1,0:T(8,128)} %fusion.7, bf16[1,1,512,512]{3,2,1,0:T(8,128)(2,1)} %param.15, s32[512]{0:T(512)S(1)} %fusion.77), kind=kOutput, calls=%fused_computation.12 | convolution fusion | flops 537919488 | bytes 2623488 | tf_op jit(solution)/shard_map/dot_general | solution.py:55
  27.4 1.3 collective-permute-start.3
  29.2 1.3 collective-permute-done.3
  31.3 6.0 %all-to-all-start = ((f32[4,64,256]{2,1,0:T(8,128)}), f32[4,64,256]{2,1,0:T(8,128)S(1)}, u32[]{:S(2)}, u32[]{:S(2)}) async-start(f32[4,64,256]{2,1,0:T(8,128)} %broadcast_in_dim.42), calls=%async_computation | async-start | bytes 524288 | tf_op jit(solution)/shard_map/all_to_all | solution.py:18
  37.8 4.7 %all-to-all-done = f32[4,64,256]{2,1,0:T(8,128)S(1)} async-done(((f32[4,64,256]{2,1,0:T(8,128)}), f32[4,64,256]{2,1,0:T(8,128)S(1)}, u32[]{:S(2)}, u32[]{:S(2)}) %all-to-all-start) | async-done | bytes 262176 | tf_op jit(solution)/shard_map/all_to_all | solution.py:18
  42.5 4.7 %all-to-all-start.1 = ((f32[8,64,512]{2,1,0:T(8,128)}), f32[8,64,512]{2,1,0:T(8,128)}, u32[]{:S(2)}, u32[]{:S(2)}) async-start(f32[8,64,512]{2,1,0:T(8,128)} %bitcast.213), calls=%async_computation.1 | async-start | bytes 2097152 | tf_op jit(solution)/shard_map/all_to_all | solution.py:122
  49.9 22.7 %all-to-all-done.1 = f32[8,64,512]{2,1,0:T(8,128)} async-done(((f32[8,64,512]{2,1,0:T(8,128)}), f32[8,64,512]{2,1,0:T(8,128)}, u32[]{:S(2)}, u32[]{:S(2)}) %all-to-all-start.1) | async-done | bytes 1048608 | tf_op jit(solution)/shard_map/all_to_all | solution.py:122
  72.5 2.0 %reduce_sum.9 = f32[64,512]{1,0:T(8,128)} reduce(f32[8,64,512]{2,1,0:T(8,128)} %all-to-all-done.1, f32[]{:T(128)} %constant.84.clone.1), dimensions={0}, to_apply=%region_0.2 | reduce | flops 229376 | bytes 1179652 | tf_op jit(solution)/shard_map/reduce_sum | solution.py:122
  76.3 1.6 %gather_fusion = f32[8,64,64]{2,1,0:T(8,128)S(1)} fusion(f32[64,8,64]{2,0,1:T(8,128)} %copy.10, s32[1024]{0:T(1024)} %pad_clamp_fusion), kind=kCustom, calls=%fused_computation.2 | custom fusion | bytes 262176 | tf_op jit(solution)/shard_map/jit(_take)/gather | solution.py:123
  80.8 1.5 %fusion.17 = f32[64,128]{1,0:T(8,128)} fusion(f32[64,128]{1,0:T(8,128)} %fusion.18, f32[64,128]{1,0:T(8,128)S(1)} %fusion.113, bf16[64,512]{1,0:T(8,128)(2,1)S(1)} %get-tuple-element.14, bf16[512,128]{1,0:T(8,128)(2,1)S(1)} %bitcast.206), kind=kOutput, calls=%fused_computation.42 | convolution fusion | flops 8404992 | bytes 294912 | tf_op jit(solution)/shard_map/dot_general | solution.py:141
  82.3 2.4 %collective-permute-start.6 = (f32[64,128]{1,0:T(8,128)}, f32[64,128]{1,0:T(8,128)}, u32[]{:S(2)}, u32[]{:S(2)}) collective-permute-start(f32[64,128]{1,0:T(8,128)} %fusion.17), channel_id=1, source_target_pairs={{0,12},{4,0},{8,4},{12,8},{1,13},{5,1},{9,5},{13,9},{2,14},{6,2},{... | collective-permute-start | bytes 98312 | tf_op jit(solution)/shard_map/ppermute | solution.py:26
  85.0 1.3 collective-permute-start.4
  87.0 1.6 %gather_fusion.1 = f32[4,64,64]{2,1,0:T(8,128)S(1)} fusion(f32[4,64,64]{2,1,0:T(8,128)} %get-tuple-element.13, s32[1024]{0:T(1024)} %pad_clamp_fusion.1), kind=kCustom, calls=%fused_computation.clone | custom fusion | bytes 131088 | tf_op jit(solution)/shard_map/jit(_take)/gather | solution.py:113
  88.6 1.6 %gather_fusion.2 = f32[4,64,64]{2,1,0:T(8,128)S(1)} fusion(f32[4,64,64]{2,1,0:T(8,128)} %get-tuple-element.12, s32[1024]{0:T(1024)} %pad_clamp_fusion.1), kind=kCustom, calls=%fused_computation.1.clone | custom fusion | bytes 131088 | tf_op jit(solution)/shard_map/jit(_take)/gather | solution.py:114
  91.5 1.4 collective-permute-start.7
  95.0 1.8 %collective-permute-done.7 = bf16[64,128]{1,0:T(8,128)(2,1)S(1)} collective-permute-done((bf16[64,128]{1,0:T(8,128)(2,1)S(1)}, bf16[64,128]{1,0:T(8,128)(2,1)S(1)}, u32[]{:S(2)}, u32[]{:S(2)}) %collective-permute-start.7) | collective-permute-done | bytes 16416 | tf_op jit(solution)/shard_map/ppermute | solution.py:26
  97.1 3.0 %collective-permute-done.10 = bf16[4,64,128]{2,1,0:T(8,128)(2,1)S(1)} collective-permute-done((bf16[4,64,128]{2,1,0:T(8,128)(2,1)S(1)}, bf16[4,64,128]{2,1,0:T(8,128)(2,1)S(1)}, u32[]{:S(2)}, u32[]{:S(2)}) %collective-permute-start.10) | collective-permute-done | bytes 65568 | tf_op jit(solution)/shard_map/ppermute | solution.py:26
  100.4 1.6 %collective-permute-start.13 = (f32[64,128]{1,0:T(8,128)S(1)}, f32[64,128]{1,0:T(8,128)S(1)}, u32[]{:S(2)}, u32[]{:S(2)}) collective-permute-start(f32[64,128]{1,0:T(8,128)S(1)} %fusion.14), channel_id=1, source_target_pairs={{0,12},{4,0},{8,4},{12,8},{1,13},{5,1},{9,5},{13,9},{2,14},{6,2},{... | collective-permute-start | bytes 98312 | tf_op jit(solution)/shard_map/ppermute | solution.py:26
  106.1 1.5 %collective-permute-start.16 = (bf16[64,128]{1,0:T(8,128)(2,1)S(1)}, bf16[64,128]{1,0:T(8,128)(2,1)S(1)}, u32[]{:S(2)}, u32[]{:S(2)}) collective-permute-start(bf16[64,128]{1,0:T(8,128)(2,1)S(1)} %get-tuple-element.32), channel_id=1, source_target_pairs={{0,3},{1,0},{2,1},{3,2},{4,7},{5,4},{6,5},{7,6},{8,11},{9,8},{10,9... | collective-permute-start | bytes 49160 | tf_op jit(solution)/shard_map/ppermute | solution.py:26
  108.7 2.4 %collective-permute-done.15 = bf16[64,128]{1,0:T(8,128)(2,1)S(1)} collective-permute-done((bf16[64,128]{1,0:T(8,128)(2,1)S(1)}, bf16[64,128]{1,0:T(8,128)(2,1)S(1)}, u32[]{:S(2)}, u32[]{:S(2)}) %collective-permute-start.15) | collective-permute-done | bytes 16416 | tf_op jit(solution)/shard_map/ppermute | solution.py:26
  112.5 2.6 %collective-permute-done.17 = bf16[4,64,128]{2,1,0:T(8,128)(2,1)S(1)} collective-permute-done((bf16[4,64,128]{2,1,0:T(8,128)(2,1)S(1)}, bf16[4,64,128]{2,1,0:T(8,128)(2,1)S(1)}, u32[]{:S(2)}, u32[]{:S(2)}) %collective-permute-start.17) | collective-permute-done | bytes 65568 | tf_op jit(solution)/shard_map/ppermute | solution.py:26
  115.5 4.5 %collective-permute-start.20 = (f32[64,128]{1,0:T(8,128)S(1)}, f32[64,128]{1,0:T(8,128)S(1)}, u32[]{:S(2)}, u32[]{:S(2)}) collective-permute-start(f32[64,128]{1,0:T(8,128)S(1)} %fusion.11), channel_id=1, source_target_pairs={{0,12},{4,0},{8,4},{12,8},{1,13},{5,1},{9,5},{13,9},{2,14},{6,2},{... | collective-permute-start | bytes 98312 | tf_op jit(solution)/shard_map/ppermute | solution.py:26
  124.3 1.4 collective-permute-start.21
  126.0 1.4 collective-permute-done.22
  127.4 1.4 collective-permute-done.21
  129.3 2.7 %collective-permute-done.24 = bf16[4,64,128]{2,1,0:T(8,128)(2,1)S(1)} collective-permute-done((bf16[4,64,128]{2,1,0:T(8,128)(2,1)S(1)}, bf16[4,64,128]{2,1,0:T(8,128)(2,1)S(1)}, u32[]{:S(2)}, u32[]{:S(2)}) %collective-permute-start.24) | collective-permute-done | bytes 65568 | tf_op jit(solution)/shard_map/ppermute | solution.py:26
  132.3 4.2 %collective-permute-start.27 = (f32[64,128]{1,0:T(8,128)S(1)}, f32[64,128]{1,0:T(8,128)S(1)}, u32[]{:S(2)}, u32[]{:S(2)}) collective-permute-start(f32[64,128]{1,0:T(8,128)S(1)} %fusion.8), channel_id=1, source_target_pairs={{0,12},{4,0},{8,4},{12,8},{1,13},{5,1},{9,5},{13,9},{2,14},{6,2},{... | collective-permute-start | bytes 98312 | tf_op jit(solution)/shard_map/ppermute | solution.py:26
  (128 shorter events, 33.9 us)
Async XLA Ops:
  0.9 26.4 %collective-permute-start.2 = (bf16[64,128]{1,0:T(8,128)(2,1)S(1)}, bf16[64,128]{1,0:T(8,128)(2,1)S(1)}, u32[]{:S(2)}, u32[]{:S(2)}) collective-permute-start(bf16[64,128]{1,0:T(8,128)(2,1)S(1)} %get-tuple-element.29), channel_id=1, source_target_pairs={{0,3},{1,0},{2,1},{3,2},{4,7},{5,4},{6,5},{7,6},{8,11},{9,8},{10,9... | collective-permute-start | bytes 49160 | tf_op jit(solution)/shard_map/ppermute | solution.py:26
  5.1 22.3 %collective-permute-start.1 = (bf16[64,128]{1,0:T(8,128)(2,1)S(1)}, bf16[64,128]{1,0:T(8,128)(2,1)S(1)}, u32[]{:S(2)}, u32[]{:S(2)}) collective-permute-start(bf16[64,128]{1,0:T(8,128)(2,1)S(1)} %get-tuple-element.29), channel_id=1, source_target_pairs={{0,2},{1,3},{2,0},{3,1},{4,6},{5,7},{6,4},{7,5},{8,10},{9,11},{10,... | collective-permute-start | bytes 49160 | tf_op jit(solution)/shard_map/ppermute | solution.py:26
  5.1 22.3 %collective-permute-start = (bf16[64,128]{1,0:T(8,128)(2,1)S(1)}, bf16[64,128]{1,0:T(8,128)(2,1)S(1)}, u32[]{:S(2)}, u32[]{:S(2)}) collective-permute-start(bf16[64,128]{1,0:T(8,128)(2,1)S(1)} %get-tuple-element.29), channel_id=1, source_target_pairs={{0,1},{1,2},{2,3},{3,0},{4,5},{5,6},{6,7},{7,4},{8,9},{9,10},{10,1... | collective-permute-start | bytes 49160 | tf_op jit(solution)/shard_map/ppermute | solution.py:26
  27.4 3.2 %collective-permute-start.3 = (bf16[4,64,128]{2,1,0:T(8,128)(2,1)S(1)}, bf16[4,64,128]{2,1,0:T(8,128)(2,1)S(1)}, u32[]{:S(2)}, u32[]{:S(2)}) collective-permute-start(bf16[4,64,128]{2,1,0:T(8,128)(2,1)S(1)} %get-tuple-element.25), channel_id=1, source_target_pairs={{0,16},{16,0},{1,17},{17,1},{2,18},{18,2},{3,19},{19,3},{4,20},{20... | collective-permute-start | bytes 196616 | tf_op jit(solution)/shard_map/ppermute | solution.py:26
  31.3 11.2 %all-to-all-start = ((f32[4,64,256]{2,1,0:T(8,128)}), f32[4,64,256]{2,1,0:T(8,128)S(1)}, u32[]{:S(2)}, u32[]{:S(2)}) async-start(f32[4,64,256]{2,1,0:T(8,128)} %broadcast_in_dim.42), calls=%async_computation | async-start | bytes 524288 | tf_op jit(solution)/shard_map/all_to_all | solution.py:18
  42.5 30.0 %all-to-all-start.1 = ((f32[8,64,512]{2,1,0:T(8,128)}), f32[8,64,512]{2,1,0:T(8,128)}, u32[]{:S(2)}, u32[]{:S(2)}) async-start(f32[8,64,512]{2,1,0:T(8,128)} %bitcast.213), calls=%async_computation.1 | async-start | bytes 2097152 | tf_op jit(solution)/shard_map/all_to_all | solution.py:122
  82.3 25.8 %copy-start.3 = (f32[4,64,64]{2,1,0:T(8,128)S(1)}, f32[4,64,64]{2,1,0:T(8,128)}, u32[]{:S(2)}) copy-start(f32[4,64,64]{2,1,0:T(8,128)} %copy-done.2) | copy-start | bytes 196612
  82.3 7.9 %collective-permute-start.6 = (f32[64,128]{1,0:T(8,128)}, f32[64,128]{1,0:T(8,128)}, u32[]{:S(2)}, u32[]{:S(2)}) collective-permute-start(f32[64,128]{1,0:T(8,128)} %fusion.17), channel_id=1, source_target_pairs={{0,12},{4,0},{8,4},{12,8},{1,13},{5,1},{9,5},{13,9},{2,14},{6,2},{... | collective-permute-start | bytes 98312 | tf_op jit(solution)/shard_map/ppermute | solution.py:26
  84.7 5.6 %collective-permute-start.5 = (f32[64,128]{1,0:T(8,128)}, f32[64,128]{1,0:T(8,128)}, u32[]{:S(2)}, u32[]{:S(2)}) collective-permute-start(f32[64,128]{1,0:T(8,128)} %fusion.17), channel_id=1, source_target_pairs={{0,8},{4,12},{8,0},{12,4},{1,9},{5,13},{9,1},{13,5},{2,10},{6,14},... | collective-permute-start | bytes 98312 | tf_op jit(solution)/shard_map/ppermute | solution.py:26
  85.0 5.2 %collective-permute-start.4 = (f32[64,128]{1,0:T(8,128)}, f32[64,128]{1,0:T(8,128)}, u32[]{:S(2)}, u32[]{:S(2)}) collective-permute-start(f32[64,128]{1,0:T(8,128)} %fusion.17), channel_id=1, source_target_pairs={{0,4},{4,8},{8,12},{12,0},{1,5},{5,9},{9,13},{13,1},{2,6},{6,10},{... | collective-permute-start | bytes 98312 | tf_op jit(solution)/shard_map/ppermute | solution.py:26
  87.0 21.0 %copy-start.5 = (f32[1,64,128]{2,1,0:T(8,128)S(1)}, f32[1,64,128]{2,1,0:T(8,128)}, u32[]{:S(2)}) copy-start(f32[1,64,128]{2,1,0:T(8,128)} %param.11) | copy-start | bytes 98308
  91.4 3.6 %collective-permute-start.9 = (bf16[64,128]{1,0:T(8,128)(2,1)S(1)}, bf16[64,128]{1,0:T(8,128)(2,1)S(1)}, u32[]{:S(2)}, u32[]{:S(2)}) collective-permute-start(bf16[64,128]{1,0:T(8,128)(2,1)S(1)} %get-tuple-element.30), channel_id=1, source_target_pairs={{0,3},{1,0},{2,1},{3,2},{4,7},{5,4},{6,5},{7,6},{8,11},{9,8},{10,9... | collective-permute-start | bytes 49160 | tf_op jit(solution)/shard_map/ppermute | solution.py:26
  91.4 3.6 %collective-permute-start.8 = (bf16[64,128]{1,0:T(8,128)(2,1)S(1)}, bf16[64,128]{1,0:T(8,128)(2,1)S(1)}, u32[]{:S(2)}, u32[]{:S(2)}) collective-permute-start(bf16[64,128]{1,0:T(8,128)(2,1)S(1)} %get-tuple-element.30), channel_id=1, source_target_pairs={{0,2},{1,3},{2,0},{3,1},{4,6},{5,7},{6,4},{7,5},{8,10},{9,11},{10,... | collective-permute-start | bytes 49160 | tf_op jit(solution)/shard_map/ppermute | solution.py:26
  91.5 5.3 %collective-permute-start.7 = (bf16[64,128]{1,0:T(8,128)(2,1)S(1)}, bf16[64,128]{1,0:T(8,128)(2,1)S(1)}, u32[]{:S(2)}, u32[]{:S(2)}) collective-permute-start(bf16[64,128]{1,0:T(8,128)(2,1)S(1)} %get-tuple-element.30), channel_id=1, source_target_pairs={{0,1},{1,2},{2,3},{3,0},{4,5},{5,6},{6,7},{7,4},{8,9},{9,10},{10,1... | collective-permute-start | bytes 49160 | tf_op jit(solution)/shard_map/ppermute | solution.py:26
  96.9 3.2 %collective-permute-start.10 = (bf16[4,64,128]{2,1,0:T(8,128)(2,1)S(1)}, bf16[4,64,128]{2,1,0:T(8,128)(2,1)S(1)}, u32[]{:S(2)}, u32[]{:S(2)}) collective-permute-start(bf16[4,64,128]{2,1,0:T(8,128)(2,1)S(1)} %get-tuple-element.21), channel_id=1, source_target_pairs={{0,16},{16,0},{1,17},{17,1},{2,18},{18,2},{3,19},{19,3},{4,20},{20... | collective-permute-start | bytes 196616 | tf_op jit(solution)/shard_map/ppermute | solution.py:26
  100.4 3.9 %collective-permute-start.13 = (f32[64,128]{1,0:T(8,128)S(1)}, f32[64,128]{1,0:T(8,128)S(1)}, u32[]{:S(2)}, u32[]{:S(2)}) collective-permute-start(f32[64,128]{1,0:T(8,128)S(1)} %fusion.14), channel_id=1, source_target_pairs={{0,12},{4,0},{8,4},{12,8},{1,13},{5,1},{9,5},{13,9},{2,14},{6,2},{... | collective-permute-start | bytes 98312 | tf_op jit(solution)/shard_map/ppermute | solution.py:26
  102.0 2.8 %collective-permute-start.12 = (f32[64,128]{1,0:T(8,128)S(1)}, f32[64,128]{1,0:T(8,128)S(1)}, u32[]{:S(2)}, u32[]{:S(2)}) collective-permute-start(f32[64,128]{1,0:T(8,128)S(1)} %fusion.14), channel_id=1, source_target_pairs={{0,8},{4,12},{8,0},{12,4},{1,9},{5,13},{9,1},{13,5},{2,10},{6,14},... | collective-permute-start | bytes 98312 | tf_op jit(solution)/shard_map/ppermute | solution.py:26
  102.8 2.0 %collective-permute-start.11 = (f32[64,128]{1,0:T(8,128)S(1)}, f32[64,128]{1,0:T(8,128)S(1)}, u32[]{:S(2)}, u32[]{:S(2)}) collective-permute-start(f32[64,128]{1,0:T(8,128)S(1)} %fusion.14), channel_id=1, source_target_pairs={{0,4},{4,8},{8,12},{12,0},{1,5},{5,9},{9,13},{13,1},{2,6},{6,10},{... | collective-permute-start | bytes 98312 | tf_op jit(solution)/shard_map/ppermute | solution.py:26
  106.1 2.6 %collective-permute-start.16 = (bf16[64,128]{1,0:T(8,128)(2,1)S(1)}, bf16[64,128]{1,0:T(8,128)(2,1)S(1)}, u32[]{:S(2)}, u32[]{:S(2)}) collective-permute-start(bf16[64,128]{1,0:T(8,128)(2,1)S(1)} %get-tuple-element.32), channel_id=1, source_target_pairs={{0,3},{1,0},{2,1},{3,2},{4,7},{5,4},{6,5},{7,6},{8,11},{9,8},{10,9... | collective-permute-start | bytes 49160 | tf_op jit(solution)/shard_map/ppermute | solution.py:26
  107.5 3.5 %collective-permute-start.15 = (bf16[64,128]{1,0:T(8,128)(2,1)S(1)}, bf16[64,128]{1,0:T(8,128)(2,1)S(1)}, u32[]{:S(2)}, u32[]{:S(2)}) collective-permute-start(bf16[64,128]{1,0:T(8,128)(2,1)S(1)} %get-tuple-element.32), channel_id=1, source_target_pairs={{0,2},{1,3},{2,0},{3,1},{4,6},{5,7},{6,4},{7,5},{8,10},{9,11},{10,... | collective-permute-start | bytes 49160 | tf_op jit(solution)/shard_map/ppermute | solution.py:26
  107.5 4.4 %collective-permute-start.14 = (bf16[64,128]{1,0:T(8,128)(2,1)S(1)}, bf16[64,128]{1,0:T(8,128)(2,1)S(1)}, u32[]{:S(2)}, u32[]{:S(2)}) collective-permute-start(bf16[64,128]{1,0:T(8,128)(2,1)S(1)} %get-tuple-element.32), channel_id=1, source_target_pairs={{0,1},{1,2},{2,3},{3,0},{4,5},{5,6},{6,7},{7,4},{8,9},{9,10},{10,1... | collective-permute-start | bytes 49160 | tf_op jit(solution)/shard_map/ppermute | solution.py:26
  112.0 3.2 %collective-permute-start.17 = (bf16[4,64,128]{2,1,0:T(8,128)(2,1)S(1)}, bf16[4,64,128]{2,1,0:T(8,128)(2,1)S(1)}, u32[]{:S(2)}, u32[]{:S(2)}) collective-permute-start(bf16[4,64,128]{2,1,0:T(8,128)(2,1)S(1)} %get-tuple-element.19), channel_id=1, source_target_pairs={{0,16},{16,0},{1,17},{17,1},{2,18},{18,2},{3,19},{19,3},{4,20},{20... | collective-permute-start | bytes 196616 | tf_op jit(solution)/shard_map/ppermute | solution.py:26
  115.5 6.6 %collective-permute-start.20 = (f32[64,128]{1,0:T(8,128)S(1)}, f32[64,128]{1,0:T(8,128)S(1)}, u32[]{:S(2)}, u32[]{:S(2)}) collective-permute-start(f32[64,128]{1,0:T(8,128)S(1)} %fusion.11), channel_id=1, source_target_pairs={{0,12},{4,0},{8,4},{12,8},{1,13},{5,1},{9,5},{13,9},{2,14},{6,2},{... | collective-permute-start | bytes 98312 | tf_op jit(solution)/shard_map/ppermute | solution.py:26
  120.0 2.8 %collective-permute-start.19 = (f32[64,128]{1,0:T(8,128)S(1)}, f32[64,128]{1,0:T(8,128)S(1)}, u32[]{:S(2)}, u32[]{:S(2)}) collective-permute-start(f32[64,128]{1,0:T(8,128)S(1)} %fusion.11), channel_id=1, source_target_pairs={{0,8},{4,12},{8,0},{12,4},{1,9},{5,13},{9,1},{13,5},{2,10},{6,14},... | collective-permute-start | bytes 98312 | tf_op jit(solution)/shard_map/ppermute | solution.py:26
  120.6 2.1 %collective-permute-start.18 = (f32[64,128]{1,0:T(8,128)S(1)}, f32[64,128]{1,0:T(8,128)S(1)}, u32[]{:S(2)}, u32[]{:S(2)}) collective-permute-start(f32[64,128]{1,0:T(8,128)S(1)} %fusion.11), channel_id=1, source_target_pairs={{0,4},{4,8},{8,12},{12,0},{1,5},{5,9},{9,13},{13,1},{2,6},{6,10},{... | collective-permute-start | bytes 98312 | tf_op jit(solution)/shard_map/ppermute | solution.py:26
  123.4 2.6 %collective-permute-start.23 = (bf16[64,128]{1,0:T(8,128)(2,1)S(1)}, bf16[64,128]{1,0:T(8,128)(2,1)S(1)}, u32[]{:S(2)}, u32[]{:S(2)}) collective-permute-start(bf16[64,128]{1,0:T(8,128)(2,1)S(1)} %get-tuple-element.34), channel_id=1, source_target_pairs={{0,3},{1,0},{2,1},{3,2},{4,7},{5,4},{6,5},{7,6},{8,11},{9,8},{10,9... | collective-permute-start | bytes 49160 | tf_op jit(solution)/shard_map/ppermute | solution.py:26
  123.9 3.5 %collective-permute-start.22 = (bf16[64,128]{1,0:T(8,128)(2,1)S(1)}, bf16[64,128]{1,0:T(8,128)(2,1)S(1)}, u32[]{:S(2)}, u32[]{:S(2)}) collective-permute-start(bf16[64,128]{1,0:T(8,128)(2,1)S(1)} %get-tuple-element.34), channel_id=1, source_target_pairs={{0,2},{1,3},{2,0},{3,1},{4,6},{5,7},{6,4},{7,5},{8,10},{9,11},{10,... | collective-permute-start | bytes 49160 | tf_op jit(solution)/shard_map/ppermute | solution.py:26
  124.3 4.4 %collective-permute-start.21 = (bf16[64,128]{1,0:T(8,128)(2,1)S(1)}, bf16[64,128]{1,0:T(8,128)(2,1)S(1)}, u32[]{:S(2)}, u32[]{:S(2)}) collective-permute-start(bf16[64,128]{1,0:T(8,128)(2,1)S(1)} %get-tuple-element.34), channel_id=1, source_target_pairs={{0,1},{1,2},{2,3},{3,0},{4,5},{5,6},{6,7},{7,4},{8,9},{9,10},{10,1... | collective-permute-start | bytes 49160 | tf_op jit(solution)/shard_map/ppermute | solution.py:26
  128.8 3.2 %collective-permute-start.24 = (bf16[4,64,128]{2,1,0:T(8,128)(2,1)S(1)}, bf16[4,64,128]{2,1,0:T(8,128)(2,1)S(1)}, u32[]{:S(2)}, u32[]{:S(2)}) collective-permute-start(bf16[4,64,128]{2,1,0:T(8,128)(2,1)S(1)} %get-tuple-element.17), channel_id=1, source_target_pairs={{0,16},{16,0},{1,17},{17,1},{2,18},{18,2},{3,19},{19,3},{4,20},{20... | collective-permute-start | bytes 196616 | tf_op jit(solution)/shard_map/ppermute | solution.py:26
  132.3 6.5 %collective-permute-start.27 = (f32[64,128]{1,0:T(8,128)S(1)}, f32[64,128]{1,0:T(8,128)S(1)}, u32[]{:S(2)}, u32[]{:S(2)}) collective-permute-start(f32[64,128]{1,0:T(8,128)S(1)} %fusion.8), channel_id=1, source_target_pairs={{0,12},{4,0},{8,4},{12,8},{1,13},{5,1},{9,5},{13,9},{2,14},{6,2},{... | collective-permute-start | bytes 98312 | tf_op jit(solution)/shard_map/ppermute | solution.py:26
  136.4 2.8 %collective-permute-start.26 = (f32[64,128]{1,0:T(8,128)S(1)}, f32[64,128]{1,0:T(8,128)S(1)}, u32[]{:S(2)}, u32[]{:S(2)}) collective-permute-start(f32[64,128]{1,0:T(8,128)S(1)} %fusion.8), channel_id=1, source_target_pairs={{0,8},{4,12},{8,0},{12,4},{1,9},{5,13},{9,1},{13,5},{2,10},{6,14},... | collective-permute-start | bytes 98312 | tf_op jit(solution)/shard_map/ppermute | solution.py:26
  137.3 1.9 %collective-permute-start.25 = (f32[64,128]{1,0:T(8,128)S(1)}, f32[64,128]{1,0:T(8,128)S(1)}, u32[]{:S(2)}, u32[]{:S(2)}) collective-permute-start(f32[64,128]{1,0:T(8,128)S(1)} %fusion.8), channel_id=1, source_target_pairs={{0,4},{4,8},{8,12},{12,0},{1,5},{5,9},{9,13},{13,1},{2,6},{6,10},{... | collective-permute-start | bytes 98312 | tf_op jit(solution)/shard_map/ppermute | solution.py:26
  (8 other events, 41.0 us)

commit v8 on v7

--- a/solution.py
+++ b/solution.py
@@ -10,12 +10,6 @@
 def split_bf16(value):
     high = lax.reduce_precision(value, exponent_bits=8, mantissa_bits=7)
     return high.astype(jnp.bfloat16), (value - high).astype(jnp.bfloat16)
-
-
-def gather_along(block, axis):
-    count = lax.axis_size(axis)
-    copies = jnp.broadcast_to(block[None], (count,) + block.shape)
-    return lax.all_to_all(copies, axis, 0, 0, tiled=True)
 
 
 def ring_parts(block, axis):
@@ -101,15 +95,14 @@
         axis=1,
     )
     first_rounded = gather_owners(previous[0].astype(jnp.bfloat16))
-    first_rounded, tables = lax.optimization_barrier((first_rounded, tables))
-    tables = gather_along(tables, "section")
+    behind = (section_pos - jnp.arange(sections)) % sections
+    tables = jnp.take(ring_parts(tables, "section"), behind, axis=0)
     start_all = tables[:, :, :load_count]
     precond_all = tables[:, :, load_count : load_count + block_nodes]
     couple_all = tables[:, :, load_count + block_nodes :]
     weights = chain_weights(precond_all, couple_all)
     above_pos = jnp.minimum(section_pos + 1, sections - 1)
     has_above = section_pos + 1 < sections
-    behind = (section_pos - jnp.arange(sections)) % sections
     weights_mine = jnp.take(weights[section_pos], behind, axis=0)
     weights_above = jnp.take(weights[above_pos], behind, axis=0)
     precond_mine = precond[0, 0].astype(jnp.float32)
@@ -118,11 +111,14 @@
     spread = schur_rows(
         block_ids[0, 0], iface_matrix[0, 0], interior_coupling[0, 0], inv_interior[0, 0], owners
     )
-    tables, spread = lax.optimization_barrier((tables, spread))
+    first_rounded, tables, spread = lax.optimization_barrier((first_rounded, tables, spread))
     rows = jnp.sum(lax.all_to_all(spread, OWNERS, 0, 0, tiled=True), axis=0)
-    rows = jnp.take(rows.reshape(block_nodes, owners, block_nodes), ring_owner_order(), axis=1)
-    rows = rows.reshape(block_nodes, nodes)
     rows_hi, rows_lo = split_bf16(jnp.dot(precond_mine, rows, precision=lax.Precision.HIGHEST))
+    node = jnp.arange(nodes, dtype=jnp.int32)
+    source = jnp.repeat(ring_owner_order(), block_nodes) * block_nodes + node % block_nodes
+    order = (node[:, None] == source[None, :]).astype(jnp.bfloat16)
+    rows_hi = jnp.dot(rows_hi, order, preferred_element_type=jnp.float32).astype(jnp.bfloat16)
+    rows_lo = jnp.dot(rows_lo, order, preferred_element_type=jnp.float32).astype(jnp.bfloat16)
 
     temps_mine = previous[0]
     temps_above = start_all[above_pos]

time: 143 us -> 135 us (0.944)
  waiting for transfers between devices: 48.5 us -> 39 us
  matrix products: 32.2 us -> 37.1 us
  local copies, waits for them, and re-layouts: 9.47 us -> 5.69 us
    ppermute x28 -> x31, starting transfers between devices: 31.9 us -> 38.3 us  [ring_parts(): parts.append(lax.ppermute(block, axis, route))]
    all_to_all x1 -> x0, starting transfers between devices: 6.03 us -> none  [gather_along(): return lax.all_to_all(copies, axis, 0, 0, tiled=True)]
    all_to_all x1 -> x0, waiting for transfers between devices: 4.69 us -> none  [gather_along(): return lax.all_to_all(copies, axis, 0, 0, tiled=True)]
    ppermute x28 -> x31, waiting for transfers between devices: 21.1 us -> 16.8 us  [ring_parts(): parts.append(lax.ppermute(block, axis, route))]
    dot_general x4, matrix products: 1.65 us -> 3.92 us  [body(): jnp.einsum('ij,il->jl', couple_above, temps_above, precision=high)]
    dot_general x0 -> x2, matrix products: none -> 1.99 us  [the longest x1 1.01 us: body(): jnp.dot(rows_hi, order, preferred_element_type=jnp.float32)]
    reshape x2 -> x0, local copies, waits for them, and re-layouts: 1.76 us -> none  [body(): rows.reshape(block_nodes, owners, block_nodes)]
  transfers between devices with their start and end apart: 30 -> 32, of which waited for: 19 -> 16; matrix products, arithmetic and copies ran while one was open for 23% -> 27% of each run, Pallas kernels for 0% -> 0%
where the time goes in v8:
time: 135 us; the launch traced here: 132 us
  starting transfers between devices  43.1 us (32%)
  waiting for transfers between devices  39 us (29%)
  matrix products  37.1 us (27%)
  other arithmetic  7.05 us (5%)
  local copies, waits for them, and re-layouts  5.69 us (4%)
    ppermute x31, starting transfers between devices, ring_parts(): parts.append(lax.ppermute(block, axis, route))  38.3 us
    all_to_all x1, waiting for transfers between devices, body(): rows = jnp.sum(lax.all_to_all(spread, OWNERS, 0, 0, tiled=True), axis=0)  22.1 us
    ppermute x31, waiting for transfers between devices, ring_parts(): parts.append(lax.ppermute(block, axis, route))  16.8 us
    dot_general x1, matrix products, schur_rows(): solved = jnp.dot(inverse, coupled, preferred_element_type=jnp.float32)  10.1 us
    all_to_all x1, starting transfers between devices, body(): rows = jnp.sum(lax.all_to_all(spread, OWNERS, 0, 0, tiled=True), axis=0)  4.76 us
    dot_general x4, matrix products, body(): jnp.einsum('ij,il->jl', couple_above, temps_above, precision=high)  3.92 us
    dot_general x4, matrix products, body(): jnp.einsum('kij,kjl->il', weights_mine, updates, precision=high)  3.79 us
    dot_general x1, matrix products, moved(): jnp.dot(rows.astype(jnp.bfloat16), place, preferred_element_type=jnp.floa...  3.37 us
  transfers between devices with their start and end apart: 32, of which 16 were waited for; matrix products, arithmetic and copies ran while one was open for 27% of the time, Pallas kernels for 0%

profile of v8, /device:TPU:1, one launch (start us, length us, event | category | flops | bytes accessed | tf_op | source)
XLA Modules:
  0.0 132.4 jit_solution(14710993897243401882)
XLA Ops:
  1.8 2.7 %collective-permute-start.1 = (f32[64,256]{1,0:T(8,128)S(1)}, f32[64,256]{1,0:T(8,128)S(1)}, u32[]{:S(2)}, u32[]{:S(2)}) collective-permute-start(f32[64,256]{1,0:T(8,128)S(1)} %pad_maximum_fusion.15), channel_id=1, source_target_pairs={{0,8},{4,12},{8,0},{12,4},{1,9},{5,13},{9,1},{13,5},{2,10},{6,14},... | collective-permute-start | bytes 196616 | tf_op jit(solution)/shard_map/ppermute | solution.py:20
  5.3 3.3 %collective-permute-start.5 = (bf16[64,128]{1,0:T(8,128)(2,1)S(1)}, bf16[64,128]{1,0:T(8,128)(2,1)S(1)}, u32[]{:S(2)}, u32[]{:S(2)}) collective-permute-start(bf16[64,128]{1,0:T(8,128)(2,1)S(1)} %get-tuple-element.24), channel_id=1, source_target_pairs={{0,3},{1,0},{2,1},{3,2},{4,7},{5,4},{6,5},{7,6},{8,11},{9,8},{10,9... | collective-permute-start | bytes 49160 | tf_op jit(solution)/shard_map/ppermute | solution.py:20
  11.7 1.7 %convolution_convert_fusion = bf16[512,2560]{1,0:T(8,128)(2,1)S(1)} fusion(bf16[1,1,2560,512]{3,2,1,0:T(8,128)(2,1)S(1)} %copy-done, s32[512]{0:T(512)S(1)} %fusion.83), kind=kOutput, calls=%fused_computation.8 | convolution fusion | flops 1344012288 | bytes 5244928 | tf_op jit(solution)/shard_map/dot_general | solution.py:52
  13.5 10.1 %fusion = f32[512,2560]{1,0:T(8,128)S(1)} fusion(bf16[512,2560]{1,0:T(8,128)(2,1)S(1)} %convolution_convert_fusion, bf16[1,1,2560,2560]{3,2,1,0:T(8,128)(2,1)} %param.17), kind=kOutput, calls=%fused_computation.3 | convolution fusion | flops 6710886400 | bytes 20971520 | tf_op jit(solution)/shard_map/dot_general | solution.py:54
  23.5 1.6 %fusion.3 = f32[512,512]{1,0:T(8,128)S(1)} fusion(bf16[512,2560]{1,0:T(8,128)(2,1)S(1)} %convolution_convert_fusion, f32[512,2560]{1,0:T(8,128)S(1)} %fusion), kind=kOutput, calls=%fused_computation.9 | convolution fusion | flops 1346109440 | bytes 8912896 | tf_op jit(solution)/shard_map/dot_general | solution.py:57
  25.1 2.6 %fusion.7 = f32[512,512]{1,0:T(8,128)} fusion(f32[512,512]{1,0:T(8,128)S(1)} %fusion.3, bf16[512,2560]{1,0:T(8,128)(2,1)S(1)} %convolution_convert_fusion, f32[512,2560]{1,0:T(8,128)S(1)} %fusion), kind=kOutput, calls=%fused_computation.13 | convolution fusion | flops 1345060864 | bytes 9961472 | tf_op jit(solution)/shard_map/dot_general | solution.py:56
  28.3 3.4 %convolution_subtract_fusion = f32[512,512]{1,0:T(8,128)} fusion(f32[512,512]{1,0:T(8,128)} %fusion.7, bf16[1,1,512,512]{3,2,1,0:T(8,128)(2,1)} %param.15, s32[512]{0:T(512)S(1)} %fusion.83), kind=kOutput, calls=%fused_computation.12 | convolution fusion | flops 537919488 | bytes 2623488 | tf_op jit(solution)/shard_map/dot_general | solution.py:49
  31.8 2.2 %collective-permute-start = (f32[64,256]{1,0:T(8,128)S(1)}, f32[64,256]{1,0:T(8,128)S(1)}, u32[]{:S(2)}, u32[]{:S(2)}) collective-permute-start(f32[64,256]{1,0:T(8,128)S(1)} %pad_maximum_fusion.15), channel_id=1, source_target_pairs={{0,4},{4,8},{8,12},{12,0},{1,5},{5,9},{9,13},{13,1},{2,6},{6,10},{... | collective-permute-start | bytes 196616 | tf_op jit(solution)/shard_map/ppermute | solution.py:20
  34.0 1.3 collective-permute-start.6
  37.4 4.8 %all-to-all-start = ((f32[8,64,512]{2,1,0:T(8,128)}), f32[8,64,512]{2,1,0:T(8,128)}, u32[]{:S(2)}, u32[]{:S(2)}) async-start(f32[8,64,512]{2,1,0:T(8,128)} %bitcast.214), calls=%async_computation | async-start | bytes 2097152 | tf_op jit(solution)/shard_map/all_to_all | solution.py:115
  45.1 22.1 %all-to-all-done = f32[8,64,512]{2,1,0:T(8,128)} async-done(((f32[8,64,512]{2,1,0:T(8,128)}), f32[8,64,512]{2,1,0:T(8,128)}, u32[]{:S(2)}, u32[]{:S(2)}) %all-to-all-start) | async-done | bytes 1048608 | tf_op jit(solution)/shard_map/all_to_all | solution.py:115
  67.2 1.3 reduce_sum.9
  70.9 1.5 %fusion.17 = f32[64,128]{1,0:T(8,128)} fusion(f32[64,128]{1,0:T(8,128)} %fusion.18, f32[64,128]{1,0:T(8,128)S(1)} %fusion.118, bf16[64,512]{1,0:T(8,128)(2,1)S(1)} %convolution_convert_fusion.2, bf16[512,128]{1,0:T(8,128)(2,1)S(1)} %bitcast.207), kind=kOutput, calls=%fused_computation.44 | convolution fusion | flops 8404992 | bytes 294912 | tf_op jit(solution)/shard_map/dot_general | solution.py:137
  72.4 2.6 %collective-permute-start.9 = (f32[64,128]{1,0:T(8,128)}, f32[64,128]{1,0:T(8,128)}, u32[]{:S(2)}, u32[]{:S(2)}) collective-permute-start(f32[64,128]{1,0:T(8,128)} %fusion.17), channel_id=1, source_target_pairs={{0,12},{4,0},{8,4},{12,8},{1,13},{5,1},{9,5},{13,9},{2,14},{6,2},{... | collective-permute-start | bytes 98312 | tf_op jit(solution)/shard_map/ppermute | solution.py:20
  77.4 1.6 %gather_fusion.1 = f32[4,64,64]{2,1,0:T(8,128)S(1)} fusion(f32[4,64,64]{2,1,0:T(8,128)} %get-tuple-element.11, s32[1024]{0:T(1024)} %pad_clamp_fusion), kind=kCustom, calls=%fused_computation.clone | custom fusion | bytes 131088 | tf_op jit(solution)/shard_map/jit(_take)/gather | solution.py:106
  79.0 1.6 %gather_fusion.2 = f32[4,64,64]{2,1,0:T(8,128)S(1)} fusion(f32[4,64,64]{2,1,0:T(8,128)} %get-tuple-element.10, s32[1024]{0:T(1024)} %pad_clamp_fusion), kind=kCustom, calls=%fused_computation.1.clone | custom fusion | bytes 131088 | tf_op jit(solution)/shard_map/jit(_take)/gather | solution.py:107
  80.6 1.1 fusion.115
  81.9 1.4 %collective-permute-start.10 = (bf16[64,128]{1,0:T(8,128)(2,1)S(1)}, bf16[64,128]{1,0:T(8,128)(2,1)S(1)}, u32[]{:S(2)}, u32[]{:S(2)}) collective-permute-start(bf16[64,128]{1,0:T(8,128)(2,1)S(1)} %get-tuple-element.26), channel_id=1, source_target_pairs={{0,1},{1,2},{2,3},{3,0},{4,5},{5,6},{6,7},{7,4},{8,9},{9,10},{10,1... | collective-permute-start | bytes 49160 | tf_op jit(solution)/shard_map/ppermute | solution.py:20
  83.3 1.1 convolution_bitcast_fusion.9
  85.4 1.2 collective-permute-done.10
  86.7 1.5 %collective-permute-start.13 = (bf16[4,64,128]{2,1,0:T(8,128)(2,1)S(1)}, bf16[4,64,128]{2,1,0:T(8,128)(2,1)S(1)}, u32[]{:S(2)}, u32[]{:S(2)}) collective-permute-start(bf16[4,64,128]{2,1,0:T(8,128)(2,1)S(1)} %get-tuple-element.17), channel_id=1, source_target_pairs={{0,16},{16,0},{1,17},{17,1},{2,18},{18,2},{3,19},{19,3},{4,20},{20... | collective-permute-start | bytes 196616 | tf_op jit(solution)/shard_map/ppermute | solution.py:20
  88.3 1.6 %collective-permute-done.13 = bf16[4,64,128]{2,1,0:T(8,128)(2,1)S(1)} collective-permute-done((bf16[4,64,128]{2,1,0:T(8,128)(2,1)S(1)}, bf16[4,64,128]{2,1,0:T(8,128)(2,1)S(1)}, u32[]{:S(2)}, u32[]{:S(2)}) %collective-permute-start.13) | collective-permute-done | bytes 65568 | tf_op jit(solution)/shard_map/ppermute | solution.py:20
  90.2 2.4 %collective-permute-start.16 = (f32[64,128]{1,0:T(8,128)S(1)}, f32[64,128]{1,0:T(8,128)S(1)}, u32[]{:S(2)}, u32[]{:S(2)}) collective-permute-start(f32[64,128]{1,0:T(8,128)S(1)} %fusion.14), channel_id=1, source_target_pairs={{0,12},{4,0},{8,4},{12,8},{1,13},{5,1},{9,5},{13,9},{2,14},{6,2},{... | collective-permute-start | bytes 98312 | tf_op jit(solution)/shard_map/ppermute | solution.py:20
  97.1 1.6 %collective-permute-start.19 = (bf16[64,128]{1,0:T(8,128)(2,1)S(1)}, bf16[64,128]{1,0:T(8,128)(2,1)S(1)}, u32[]{:S(2)}, u32[]{:S(2)}) collective-permute-start(bf16[64,128]{1,0:T(8,128)(2,1)S(1)} %get-tuple-element.28), channel_id=1, source_target_pairs={{0,3},{1,0},{2,1},{3,2},{4,7},{5,4},{6,5},{7,6},{8,11},{9,8},{10,9... | collective-permute-start | bytes 49160 | tf_op jit(solution)/shard_map/ppermute | solution.py:20
  100.2 2.1 %collective-permute-done.18 = bf16[64,128]{1,0:T(8,128)(2,1)S(1)} collective-permute-done((bf16[64,128]{1,0:T(8,128)(2,1)S(1)}, bf16[64,128]{1,0:T(8,128)(2,1)S(1)}, u32[]{:S(2)}, u32[]{:S(2)}) %collective-permute-start.18) | collective-permute-done | bytes 16416 | tf_op jit(solution)/shard_map/ppermute | solution.py:20
  103.7 2.7 %collective-permute-done.20 = bf16[4,64,128]{2,1,0:T(8,128)(2,1)S(1)} collective-permute-done((bf16[4,64,128]{2,1,0:T(8,128)(2,1)S(1)}, bf16[4,64,128]{2,1,0:T(8,128)(2,1)S(1)}, u32[]{:S(2)}, u32[]{:S(2)}) %collective-permute-start.20) | collective-permute-done | bytes 65568 | tf_op jit(solution)/shard_map/ppermute | solution.py:20
  106.7 4.3 %collective-permute-start.23 = (f32[64,128]{1,0:T(8,128)S(1)}, f32[64,128]{1,0:T(8,128)S(1)}, u32[]{:S(2)}, u32[]{:S(2)}) collective-permute-start(f32[64,128]{1,0:T(8,128)S(1)} %fusion.11), channel_id=1, source_target_pairs={{0,12},{4,0},{8,4},{12,8},{1,13},{5,1},{9,5},{13,9},{2,14},{6,2},{... | collective-permute-start | bytes 98312 | tf_op jit(solution)/shard_map/ppermute | solution.py:20
  116.4 1.4 %collective-permute-start.24 = (bf16[64,128]{1,0:T(8,128)(2,1)S(1)}, bf16[64,128]{1,0:T(8,128)(2,1)S(1)}, u32[]{:S(2)}, u32[]{:S(2)}) collective-permute-start(bf16[64,128]{1,0:T(8,128)(2,1)S(1)} %get-tuple-element.30), channel_id=1, source_target_pairs={{0,1},{1,2},{2,3},{3,0},{4,5},{5,6},{6,7},{7,4},{8,9},{9,10},{10,1... | collective-permute-start | bytes 49160 | tf_op jit(solution)/shard_map/ppermute | solution.py:20
  119.6 1.4 %collective-permute-done.24 = bf16[64,128]{1,0:T(8,128)(2,1)S(1)} collective-permute-done((bf16[64,128]{1,0:T(8,128)(2,1)S(1)}, bf16[64,128]{1,0:T(8,128)(2,1)S(1)}, u32[]{:S(2)}, u32[]{:S(2)}) %collective-permute-start.24) | collective-permute-done | bytes 16416 | tf_op jit(solution)/shard_map/ppermute | solution.py:20
  121.4 2.7 %collective-permute-done.27 = bf16[4,64,128]{2,1,0:T(8,128)(2,1)S(1)} collective-permute-done((bf16[4,64,128]{2,1,0:T(8,128)(2,1)S(1)}, bf16[4,64,128]{2,1,0:T(8,128)(2,1)S(1)}, u32[]{:S(2)}, u32[]{:S(2)}) %collective-permute-start.27) | collective-permute-done | bytes 65568 | tf_op jit(solution)/shard_map/ppermute | solution.py:20
  124.5 4.2 %collective-permute-start.30 = (f32[64,128]{1,0:T(8,128)S(1)}, f32[64,128]{1,0:T(8,128)S(1)}, u32[]{:S(2)}, u32[]{:S(2)}) collective-permute-start(f32[64,128]{1,0:T(8,128)S(1)} %fusion.8), channel_id=1, source_target_pairs={{0,12},{4,0},{8,4},{12,8},{1,13},{5,1},{9,5},{13,9},{2,14},{6,2},{... | collective-permute-start | bytes 98312 | tf_op jit(solution)/shard_map/ppermute | solution.py:20
  129.4 1.1 collective-permute-start.28
  (126 shorter events, 35.9 us)
Async XLA Ops:
  1.7 33.5 %collective-permute-start.2 = (f32[64,256]{1,0:T(8,128)S(1)}, f32[64,256]{1,0:T(8,128)S(1)}, u32[]{:S(2)}, u32[]{:S(2)}) collective-permute-start(f32[64,256]{1,0:T(8,128)S(1)} %pad_maximum_fusion.15), channel_id=1, source_target_pairs={{0,12},{4,0},{8,4},{12,8},{1,13},{5,1},{9,5},{13,9},{2,14},{6,2},{... | collective-permute-start | bytes 196616 | tf_op jit(solution)/shard_map/ppermute | solution.py:20
  1.8 33.5 %collective-permute-start.1 = (f32[64,256]{1,0:T(8,128)S(1)}, f32[64,256]{1,0:T(8,128)S(1)}, u32[]{:S(2)}, u32[]{:S(2)}) collective-permute-start(f32[64,256]{1,0:T(8,128)S(1)} %pad_maximum_fusion.15), channel_id=1, source_target_pairs={{0,8},{4,12},{8,0},{12,4},{1,9},{5,13},{9,1},{13,5},{2,10},{6,14},... | collective-permute-start | bytes 196616 | tf_op jit(solution)/shard_map/ppermute | solution.py:20
  5.3 26.4 %collective-permute-start.5 = (bf16[64,128]{1,0:T(8,128)(2,1)S(1)}, bf16[64,128]{1,0:T(8,128)(2,1)S(1)}, u32[]{:S(2)}, u32[]{:S(2)}) collective-permute-start(bf16[64,128]{1,0:T(8,128)(2,1)S(1)} %get-tuple-element.24), channel_id=1, source_target_pairs={{0,3},{1,0},{2,1},{3,2},{4,7},{5,4},{6,5},{7,6},{8,11},{9,8},{10,9... | collective-permute-start | bytes 49160 | tf_op jit(solution)/shard_map/ppermute | solution.py:20
  8.6 25.3 %collective-permute-start.4 = (bf16[64,128]{1,0:T(8,128)(2,1)S(1)}, bf16[64,128]{1,0:T(8,128)(2,1)S(1)}, u32[]{:S(2)}, u32[]{:S(2)}) collective-permute-start(bf16[64,128]{1,0:T(8,128)(2,1)S(1)} %get-tuple-element.24), channel_id=1, source_target_pairs={{0,2},{1,3},{2,0},{3,1},{4,6},{5,7},{6,4},{7,5},{8,10},{9,11},{10,... | collective-permute-start | bytes 49160 | tf_op jit(solution)/shard_map/ppermute | solution.py:20
  8.6 25.3 %collective-permute-start.3 = (bf16[64,128]{1,0:T(8,128)(2,1)S(1)}, bf16[64,128]{1,0:T(8,128)(2,1)S(1)}, u32[]{:S(2)}, u32[]{:S(2)}) collective-permute-start(bf16[64,128]{1,0:T(8,128)(2,1)S(1)} %get-tuple-element.24), channel_id=1, source_target_pairs={{0,1},{1,2},{2,3},{3,0},{4,5},{5,6},{6,7},{7,4},{8,9},{9,10},{10,1... | collective-permute-start | bytes 49160 | tf_op jit(solution)/shard_map/ppermute | solution.py:20
  31.8 3.5 %collective-permute-start = (f32[64,256]{1,0:T(8,128)S(1)}, f32[64,256]{1,0:T(8,128)S(1)}, u32[]{:S(2)}, u32[]{:S(2)}) collective-permute-start(f32[64,256]{1,0:T(8,128)S(1)} %pad_maximum_fusion.15), channel_id=1, source_target_pairs={{0,4},{4,8},{8,12},{12,0},{1,5},{5,9},{9,13},{13,1},{2,6},{6,10},{... | collective-permute-start | bytes 196616 | tf_op jit(solution)/shard_map/ppermute | solution.py:20
  34.0 3.4 %collective-permute-start.6 = (bf16[4,64,128]{2,1,0:T(8,128)(2,1)S(1)}, bf16[4,64,128]{2,1,0:T(8,128)(2,1)S(1)}, u32[]{:S(2)}, u32[]{:S(2)}) collective-permute-start(bf16[4,64,128]{2,1,0:T(8,128)(2,1)S(1)} %get-tuple-element.19), channel_id=1, source_target_pairs={{0,16},{16,0},{1,17},{17,1},{2,18},{18,2},{3,19},{19,3},{4,20},{20... | collective-permute-start | bytes 196616 | tf_op jit(solution)/shard_map/ppermute | solution.py:20
  37.4 29.8 %all-to-all-start = ((f32[8,64,512]{2,1,0:T(8,128)}), f32[8,64,512]{2,1,0:T(8,128)}, u32[]{:S(2)}, u32[]{:S(2)}) async-start(f32[8,64,512]{2,1,0:T(8,128)} %bitcast.214), calls=%async_computation | async-start | bytes 2097152 | tf_op jit(solution)/shard_map/all_to_all | solution.py:115
  72.4 8.1 %collective-permute-start.9 = (f32[64,128]{1,0:T(8,128)}, f32[64,128]{1,0:T(8,128)}, u32[]{:S(2)}, u32[]{:S(2)}) collective-permute-start(f32[64,128]{1,0:T(8,128)} %fusion.17), channel_id=1, source_target_pairs={{0,12},{4,0},{8,4},{12,8},{1,13},{5,1},{9,5},{13,9},{2,14},{6,2},{... | collective-permute-start | bytes 98312 | tf_op jit(solution)/shard_map/ppermute | solution.py:20
  75.1 5.5 %collective-permute-start.8 = (f32[64,128]{1,0:T(8,128)}, f32[64,128]{1,0:T(8,128)}, u32[]{:S(2)}, u32[]{:S(2)}) collective-permute-start(f32[64,128]{1,0:T(8,128)} %fusion.17), channel_id=1, source_target_pairs={{0,8},{4,12},{8,0},{12,4},{1,9},{5,13},{9,1},{13,5},{2,10},{6,14},... | collective-permute-start | bytes 98312 | tf_op jit(solution)/shard_map/ppermute | solution.py:20
  76.0 4.6 %collective-permute-start.7 = (f32[64,128]{1,0:T(8,128)}, f32[64,128]{1,0:T(8,128)}, u32[]{:S(2)}, u32[]{:S(2)}) collective-permute-start(f32[64,128]{1,0:T(8,128)} %fusion.17), channel_id=1, source_target_pairs={{0,4},{4,8},{8,12},{12,0},{1,5},{5,9},{9,13},{13,1},{2,6},{6,10},{... | collective-permute-start | bytes 98312 | tf_op jit(solution)/shard_map/ppermute | solution.py:20
  81.7 3.6 %collective-permute-start.12 = (bf16[64,128]{1,0:T(8,128)(2,1)S(1)}, bf16[64,128]{1,0:T(8,128)(2,1)S(1)}, u32[]{:S(2)}, u32[]{:S(2)}) collective-permute-start(bf16[64,128]{1,0:T(8,128)(2,1)S(1)} %get-tuple-element.26), channel_id=1, source_target_pairs={{0,3},{1,0},{2,1},{3,2},{4,7},{5,4},{6,5},{7,6},{8,11},{9,8},{10,9... | collective-permute-start | bytes 49160 | tf_op jit(solution)/shard_map/ppermute | solution.py:20
  81.8 3.6 %collective-permute-start.11 = (bf16[64,128]{1,0:T(8,128)(2,1)S(1)}, bf16[64,128]{1,0:T(8,128)(2,1)S(1)}, u32[]{:S(2)}, u32[]{:S(2)}) collective-permute-start(bf16[64,128]{1,0:T(8,128)(2,1)S(1)} %get-tuple-element.26), channel_id=1, source_target_pairs={{0,2},{1,3},{2,0},{3,1},{4,6},{5,7},{6,4},{7,5},{8,10},{9,11},{10,... | collective-permute-start | bytes 49160 | tf_op jit(solution)/shard_map/ppermute | solution.py:20
  81.9 4.8 %collective-permute-start.10 = (bf16[64,128]{1,0:T(8,128)(2,1)S(1)}, bf16[64,128]{1,0:T(8,128)(2,1)S(1)}, u32[]{:S(2)}, u32[]{:S(2)}) collective-permute-start(bf16[64,128]{1,0:T(8,128)(2,1)S(1)} %get-tuple-element.26), channel_id=1, source_target_pairs={{0,1},{1,2},{2,3},{3,0},{4,5},{5,6},{6,7},{7,4},{8,9},{9,10},{10,1... | collective-permute-start | bytes 49160 | tf_op jit(solution)/shard_map/ppermute | solution.py:20
  86.7 3.2 %collective-permute-start.13 = (bf16[4,64,128]{2,1,0:T(8,128)(2,1)S(1)}, bf16[4,64,128]{2,1,0:T(8,128)(2,1)S(1)}, u32[]{:S(2)}, u32[]{:S(2)}) collective-permute-start(bf16[4,64,128]{2,1,0:T(8,128)(2,1)S(1)} %get-tuple-element.17), channel_id=1, source_target_pairs={{0,16},{16,0},{1,17},{17,1},{2,18},{18,2},{3,19},{19,3},{4,20},{20... | collective-permute-start | bytes 196616 | tf_op jit(solution)/shard_map/ppermute | solution.py:20
  90.2 4.6 %collective-permute-start.16 = (f32[64,128]{1,0:T(8,128)S(1)}, f32[64,128]{1,0:T(8,128)S(1)}, u32[]{:S(2)}, u32[]{:S(2)}) collective-permute-start(f32[64,128]{1,0:T(8,128)S(1)} %fusion.14), channel_id=1, source_target_pairs={{0,12},{4,0},{8,4},{12,8},{1,13},{5,1},{9,5},{13,9},{2,14},{6,2},{... | collective-permute-start | bytes 98312 | tf_op jit(solution)/shard_map/ppermute | solution.py:20
  92.6 2.8 %collective-permute-start.15 = (f32[64,128]{1,0:T(8,128)S(1)}, f32[64,128]{1,0:T(8,128)S(1)}, u32[]{:S(2)}, u32[]{:S(2)}) collective-permute-start(f32[64,128]{1,0:T(8,128)S(1)} %fusion.14), channel_id=1, source_target_pairs={{0,8},{4,12},{8,0},{12,4},{1,9},{5,13},{9,1},{13,5},{2,10},{6,14},... | collective-permute-start | bytes 98312 | tf_op jit(solution)/shard_map/ppermute | solution.py:20
  93.3 2.0 %collective-permute-start.14 = (f32[64,128]{1,0:T(8,128)S(1)}, f32[64,128]{1,0:T(8,128)S(1)}, u32[]{:S(2)}, u32[]{:S(2)}) collective-permute-start(f32[64,128]{1,0:T(8,128)S(1)} %fusion.14), channel_id=1, source_target_pairs={{0,4},{4,8},{8,12},{12,0},{1,5},{5,9},{9,13},{13,1},{2,6},{6,10},{... | collective-permute-start | bytes 98312 | tf_op jit(solution)/shard_map/ppermute | solution.py:20
  97.1 3.1 %collective-permute-start.19 = (bf16[64,128]{1,0:T(8,128)(2,1)S(1)}, bf16[64,128]{1,0:T(8,128)(2,1)S(1)}, u32[]{:S(2)}, u32[]{:S(2)}) collective-permute-start(bf16[64,128]{1,0:T(8,128)(2,1)S(1)} %get-tuple-element.28), channel_id=1, source_target_pairs={{0,3},{1,0},{2,1},{3,2},{4,7},{5,4},{6,5},{7,6},{8,11},{9,8},{10,9... | collective-permute-start | bytes 49160 | tf_op jit(solution)/shard_map/ppermute | solution.py:20
  98.8 3.5 %collective-permute-start.18 = (bf16[64,128]{1,0:T(8,128)(2,1)S(1)}, bf16[64,128]{1,0:T(8,128)(2,1)S(1)}, u32[]{:S(2)}, u32[]{:S(2)}) collective-permute-start(bf16[64,128]{1,0:T(8,128)(2,1)S(1)} %get-tuple-element.28), channel_id=1, source_target_pairs={{0,2},{1,3},{2,0},{3,1},{4,6},{5,7},{6,4},{7,5},{8,10},{9,11},{10,... | collective-permute-start | bytes 49160 | tf_op jit(solution)/shard_map/ppermute | solution.py:20
  98.8 4.4 %collective-permute-start.17 = (bf16[64,128]{1,0:T(8,128)(2,1)S(1)}, bf16[64,128]{1,0:T(8,128)(2,1)S(1)}, u32[]{:S(2)}, u32[]{:S(2)}) collective-permute-start(bf16[64,128]{1,0:T(8,128)(2,1)S(1)} %get-tuple-element.28), channel_id=1, source_target_pairs={{0,1},{1,2},{2,3},{3,0},{4,5},{5,6},{6,7},{7,4},{8,9},{9,10},{10,1... | collective-permute-start | bytes 49160 | tf_op jit(solution)/shard_map/ppermute | solution.py:20
  103.2 3.2 %collective-permute-start.20 = (bf16[4,64,128]{2,1,0:T(8,128)(2,1)S(1)}, bf16[4,64,128]{2,1,0:T(8,128)(2,1)S(1)}, u32[]{:S(2)}, u32[]{:S(2)}) collective-permute-start(bf16[4,64,128]{2,1,0:T(8,128)(2,1)S(1)} %get-tuple-element.15), channel_id=1, source_target_pairs={{0,16},{16,0},{1,17},{17,1},{2,18},{18,2},{3,19},{19,3},{4,20},{20... | collective-permute-start | bytes 196616 | tf_op jit(solution)/shard_map/ppermute | solution.py:20
  106.7 6.5 %collective-permute-start.23 = (f32[64,128]{1,0:T(8,128)S(1)}, f32[64,128]{1,0:T(8,128)S(1)}, u32[]{:S(2)}, u32[]{:S(2)}) collective-permute-start(f32[64,128]{1,0:T(8,128)S(1)} %fusion.11), channel_id=1, source_target_pairs={{0,12},{4,0},{8,4},{12,8},{1,13},{5,1},{9,5},{13,9},{2,14},{6,2},{... | collective-permute-start | bytes 98312 | tf_op jit(solution)/shard_map/ppermute | solution.py:20
  111.0 2.8 %collective-permute-start.22 = (f32[64,128]{1,0:T(8,128)S(1)}, f32[64,128]{1,0:T(8,128)S(1)}, u32[]{:S(2)}, u32[]{:S(2)}) collective-permute-start(f32[64,128]{1,0:T(8,128)S(1)} %fusion.11), channel_id=1, source_target_pairs={{0,8},{4,12},{8,0},{12,4},{1,9},{5,13},{9,1},{13,5},{2,10},{6,14},... | collective-permute-start | bytes 98312 | tf_op jit(solution)/shard_map/ppermute | solution.py:20
  111.7 2.0 %collective-permute-start.21 = (f32[64,128]{1,0:T(8,128)S(1)}, f32[64,128]{1,0:T(8,128)S(1)}, u32[]{:S(2)}, u32[]{:S(2)}) collective-permute-start(f32[64,128]{1,0:T(8,128)S(1)} %fusion.11), channel_id=1, source_target_pairs={{0,4},{4,8},{8,12},{12,0},{1,5},{5,9},{9,13},{13,1},{2,6},{6,10},{... | collective-permute-start | bytes 98312 | tf_op jit(solution)/shard_map/ppermute | solution.py:20
  115.5 3.3 %collective-permute-start.26 = (bf16[64,128]{1,0:T(8,128)(2,1)S(1)}, bf16[64,128]{1,0:T(8,128)(2,1)S(1)}, u32[]{:S(2)}, u32[]{:S(2)}) collective-permute-start(bf16[64,128]{1,0:T(8,128)(2,1)S(1)} %get-tuple-element.30), channel_id=1, source_target_pairs={{0,3},{1,0},{2,1},{3,2},{4,7},{5,4},{6,5},{7,6},{8,11},{9,8},{10,9... | collective-permute-start | bytes 49160 | tf_op jit(solution)/shard_map/ppermute | solution.py:20
  116.0 3.5 %collective-permute-start.25 = (bf16[64,128]{1,0:T(8,128)(2,1)S(1)}, bf16[64,128]{1,0:T(8,128)(2,1)S(1)}, u32[]{:S(2)}, u32[]{:S(2)}) collective-permute-start(bf16[64,128]{1,0:T(8,128)(2,1)S(1)} %get-tuple-element.30), channel_id=1, source_target_pairs={{0,2},{1,3},{2,0},{3,1},{4,6},{5,7},{6,4},{7,5},{8,10},{9,11},{10,... | collective-permute-start | bytes 49160 | tf_op jit(solution)/shard_map/ppermute | solution.py:20
  116.4 4.5 %collective-permute-start.24 = (bf16[64,128]{1,0:T(8,128)(2,1)S(1)}, bf16[64,128]{1,0:T(8,128)(2,1)S(1)}, u32[]{:S(2)}, u32[]{:S(2)}) collective-permute-start(bf16[64,128]{1,0:T(8,128)(2,1)S(1)} %get-tuple-element.30), channel_id=1, source_target_pairs={{0,1},{1,2},{2,3},{3,0},{4,5},{5,6},{6,7},{7,4},{8,9},{9,10},{10,1... | collective-permute-start | bytes 49160 | tf_op jit(solution)/shard_map/ppermute | solution.py:20
  121.0 3.2 %collective-permute-start.27 = (bf16[4,64,128]{2,1,0:T(8,128)(2,1)S(1)}, bf16[4,64,128]{2,1,0:T(8,128)(2,1)S(1)}, u32[]{:S(2)}, u32[]{:S(2)}) collective-permute-start(bf16[4,64,128]{2,1,0:T(8,128)(2,1)S(1)} %get-tuple-element.13), channel_id=1, source_target_pairs={{0,16},{16,0},{1,17},{17,1},{2,18},{18,2},{3,19},{19,3},{4,20},{20... | collective-permute-start | bytes 196616 | tf_op jit(solution)/shard_map/ppermute | solution.py:20
  124.5 6.4 %collective-permute-start.30 = (f32[64,128]{1,0:T(8,128)S(1)}, f32[64,128]{1,0:T(8,128)S(1)}, u32[]{:S(2)}, u32[]{:S(2)}) collective-permute-start(f32[64,128]{1,0:T(8,128)S(1)} %fusion.8), channel_id=1, source_target_pairs={{0,12},{4,0},{8,4},{12,8},{1,13},{5,1},{9,5},{13,9},{2,14},{6,2},{... | collective-permute-start | bytes 98312 | tf_op jit(solution)/shard_map/ppermute | solution.py:20
  128.7 2.8 %collective-permute-start.29 = (f32[64,128]{1,0:T(8,128)S(1)}, f32[64,128]{1,0:T(8,128)S(1)}, u32[]{:S(2)}, u32[]{:S(2)}) collective-permute-start(f32[64,128]{1,0:T(8,128)S(1)} %fusion.8), channel_id=1, source_target_pairs={{0,8},{4,12},{8,0},{12,4},{1,9},{5,13},{9,1},{13,5},{2,10},{6,14},... | collective-permute-start | bytes 98312 | tf_op jit(solution)/shard_map/ppermute | solution.py:20
  129.4 2.1 %collective-permute-start.28 = (f32[64,128]{1,0:T(8,128)S(1)}, f32[64,128]{1,0:T(8,128)S(1)}, u32[]{:S(2)}, u32[]{:S(2)}) collective-permute-start(f32[64,128]{1,0:T(8,128)S(1)} %fusion.8), channel_id=1, source_target_pairs={{0,4},{4,8},{8,12},{12,0},{1,5},{5,9},{9,13},{13,1},{2,6},{6,10},{... | collective-permute-start | bytes 98312 | tf_op jit(solution)/shard_map/ppermute | solution.py:20
  (7 other events, 110.7 us)

commit v9 on v8

--- a/solution.py
+++ b/solution.py
@@ -111,7 +111,19 @@
     spread = schur_rows(
         block_ids[0, 0], iface_matrix[0, 0], interior_coupling[0, 0], inv_interior[0, 0], owners
     )
-    first_rounded, tables, spread = lax.optimization_barrier((first_rounded, tables, spread))
+    temps_mine = previous[0]
+    temps_above = start_all[above_pos]
+    rhs = right_side[0]
+
+    def known_part(temps_mine, temps_above):
+        from_above = jnp.einsum("ij,il->jl", couple_above, temps_above, precision=high)
+        from_above = jnp.where(has_above, from_above, 0.0)
+        return temps_mine + jnp.dot(precond_mine, rhs - from_above, precision=high)
+
+    known = known_part(temps_mine, temps_above)
+    first_rounded, weights_mine, weights_above, known, spread = lax.optimization_barrier(
+        (first_rounded, weights_mine, weights_above, known, spread)
+    )
     rows = jnp.sum(lax.all_to_all(spread, OWNERS, 0, 0, tiled=True), axis=0)
     rows_hi, rows_lo = split_bf16(jnp.dot(precond_mine, rows, precision=lax.Precision.HIGHEST))
     node = jnp.arange(nodes, dtype=jnp.int32)
@@ -120,18 +132,13 @@
     rows_hi = jnp.dot(rows_hi, order, preferred_element_type=jnp.float32).astype(jnp.bfloat16)
     rows_lo = jnp.dot(rows_lo, order, preferred_element_type=jnp.float32).astype(jnp.bfloat16)
 
-    temps_mine = previous[0]
-    temps_above = start_all[above_pos]
-    rhs = right_side[0]
     for sweep_index in range(SWEEPS):
         if sweep_index == 0:
             rounded = first_rounded
         else:
             rounded = gather_owners(temps_mine.astype(jnp.bfloat16))
+            known = known_part(temps_mine, temps_above)
         rounded = rounded.reshape(nodes, load_count)
-        from_above = jnp.einsum("ij,il->jl", couple_above, temps_above, precision=high)
-        from_above = jnp.where(has_above, from_above, 0.0)
-        known = temps_mine + jnp.dot(precond_mine, rhs - from_above, precision=high)
         update = known - (
             jnp.dot(rows_hi, rounded, preferred_element_type=jnp.float32)
             + jnp.dot(rows_lo, rounded, preferred_element_type=jnp.float32)

time: 135 us -> 133 us (0.985); the launches traced: 132 us -> 133 us
  waiting for transfers between devices: 39 us -> 52.6 us
  matrix products: 37.1 us -> 27.1 us
  starting transfers between devices: 43.1 us -> 38.8 us
  other arithmetic: 7.05 us -> 9.89 us
  local copies, waits for them, and re-layouts: 5.69 us -> 3.79 us
    ppermute x31, waiting for transfers between devices: 16.8 us -> 26.3 us  [ring_parts(): parts.append(lax.ppermute(block, axis, route))]
    all_to_all x1, waiting for transfers between devices: 22.1 us -> 26.3 us  [body(): rows = jnp.sum(lax.all_to_all(spread, OWNERS, 0, 0, tiled=True), axis=0)]
    ppermute x31, starting transfers between devices: 38.3 us -> 34.5 us  [ring_parts(): parts.append(lax.ppermute(block, axis, route))]
    dot_general x8, matrix products: 5.07 us -> 2.18 us  [the longest x4 1.65 us: known_part(): jnp.einsum('ij,il->jl', couple_above, temps_above, precision=high)]
    dot_general x4, matrix products: 3.79 us -> 1.56 us  [body(): jnp.einsum('kij,kjl->il', weights_mine, updates, precision=high)]
    dot_general x3, matrix products: 2.87 us -> 0.7 us  [body(): jnp.einsum('kij,kjl->il', weights_above, updates, precision=high)]
    another operation x10, other arithmetic: 0.96 us -> 2.44 us  [ring_parts(): return jnp.stack(parts)]
    dot_general x4, matrix products: 2 us -> 0.62 us  [body(): jnp.dot(rows_lo, rounded, preferred_element_type=jnp.float32)]
  transfers between devices with their start and end apart: 32 -> 32, of which waited for: 16 -> 23; matrix products, arithmetic and copies ran while one was open for 27% -> 25% of each run, Pallas kernels for 0% -> 0%
where the time goes in v9:
time: 133 us
  waiting for transfers between devices  52.6 us (40%)
  starting transfers between devices  38.8 us (29%)
  matrix products  27.1 us (20%)
  other arithmetic  9.89 us (7%)
  local copies, waits for them, and re-layouts  3.79 us (3%)
    ppermute x31, starting transfers between devices, ring_parts(): parts.append(lax.ppermute(block, axis, route))  34.5 us
    ppermute x31, waiting for transfers between devices, ring_parts(): parts.append(lax.ppermute(block, axis, route))  26.3 us
    all_to_all x1, waiting for transfers between devices, body(): rows = jnp.sum(lax.all_to_all(spread, OWNERS, 0, 0, tiled=True), axis=0)  26.3 us
    dot_general x1, matrix products, schur_rows(): solved = jnp.dot(inverse, coupled, preferred_element_type=jnp.float32)  10.1 us
    all_to_all x1, starting transfers between devices, body(): rows = jnp.sum(lax.all_to_all(spread, OWNERS, 0, 0, tiled=True), axis=0)  4.25 us
    dot_general x1, matrix products, moved(): jnp.dot(rows.astype(jnp.bfloat16), place, preferred_element_type=jnp.floa...  3.37 us
  transfers between devices with their start and end apart: 32, of which 23 were waited for; matrix products, arithmetic and copies ran while one was open for 25% of the time, Pallas kernels for 0%

profile of v9, /device:TPU:1, one launch (start us, length us, event | category | flops | bytes accessed | tf_op | source)
XLA Modules:
  0.0 132.6 jit_solution(14770972726361652427)
XLA Ops:
  1.7 2.6 %collective-permute-start.4 = (f32[64,256]{1,0:T(8,128)S(1)}, f32[64,256]{1,0:T(8,128)S(1)}, u32[]{:S(2)}, u32[]{:S(2)}) collective-permute-start(f32[64,256]{1,0:T(8,128)S(1)} %pad_maximum_fusion.16), channel_id=1, source_target_pairs={{0,4},{4,8},{8,12},{12,0},{1,5},{5,9},{9,13},{13,1},{2,6},{6,10},{... | collective-permute-start | bytes 196616 | tf_op jit(solution)/shard_map/ppermute | solution.py:20
  5.2 1.5 %collective-permute-start = (bf16[64,128]{1,0:T(8,128)(2,1)S(1)}, bf16[64,128]{1,0:T(8,128)(2,1)S(1)}, u32[]{:S(2)}, u32[]{:S(2)}) collective-permute-start(bf16[64,128]{1,0:T(8,128)(2,1)S(1)} %get-tuple-element.31), channel_id=1, source_target_pairs={{0,1},{1,2},{2,3},{3,0},{4,5},{5,6},{6,7},{7,4},{8,9},{9,10},{10,1... | collective-permute-start | bytes 49160 | tf_op jit(solution)/shard_map/ppermute | solution.py:20
  6.7 2.3 %collective-permute-start.1 = (bf16[64,128]{1,0:T(8,128)(2,1)S(1)}, bf16[64,128]{1,0:T(8,128)(2,1)S(1)}, u32[]{:S(2)}, u32[]{:S(2)}) collective-permute-start(bf16[64,128]{1,0:T(8,128)(2,1)S(1)} %get-tuple-element.31), channel_id=1, source_target_pairs={{0,2},{1,3},{2,0},{3,1},{4,6},{5,7},{6,4},{7,5},{8,10},{9,11},{10,... | collective-permute-start | bytes 49160 | tf_op jit(solution)/shard_map/ppermute | solution.py:20
  9.0 1.1 collective-permute-start.2
  13.0 1.7 %convolution_convert_fusion = bf16[512,2560]{1,0:T(8,128)(2,1)S(1)} fusion(bf16[1,1,2560,512]{3,2,1,0:T(8,128)(2,1)S(1)} %copy-done, s32[512]{0:T(512)S(1)} %fusion.62), kind=kOutput, calls=%fused_computation.8 | convolution fusion | flops 1344012288 | bytes 5244928 | tf_op jit(solution)/shard_map/dot_general | solution.py:52
  14.7 10.1 %fusion = f32[512,2560]{1,0:T(8,128)S(1)} fusion(bf16[512,2560]{1,0:T(8,128)(2,1)S(1)} %convolution_convert_fusion, bf16[1,1,2560,2560]{3,2,1,0:T(8,128)(2,1)} %param.17), kind=kOutput, calls=%fused_computation.3 | convolution fusion | flops 6710886400 | bytes 20971520 | tf_op jit(solution)/shard_map/dot_general | solution.py:54
  24.8 1.6 %fusion.3 = f32[512,512]{1,0:T(8,128)S(1)} fusion(bf16[512,2560]{1,0:T(8,128)(2,1)S(1)} %convolution_convert_fusion, f32[512,2560]{1,0:T(8,128)S(1)} %fusion), kind=kOutput, calls=%fused_computation.9 | convolution fusion | flops 1346109440 | bytes 8912896 | tf_op jit(solution)/shard_map/dot_general | solution.py:57
  26.4 2.6 %fusion.7 = f32[512,512]{1,0:T(8,128)} fusion(f32[512,512]{1,0:T(8,128)S(1)} %fusion.3, bf16[512,2560]{1,0:T(8,128)(2,1)S(1)} %convolution_convert_fusion, f32[512,2560]{1,0:T(8,128)S(1)} %fusion), kind=kOutput, calls=%fused_computation.13 | convolution fusion | flops 1345060864 | bytes 9961472 | tf_op jit(solution)/shard_map/dot_general | solution.py:56
  28.9 3.4 %convolution_subtract_fusion = f32[512,512]{1,0:T(8,128)} fusion(f32[512,512]{1,0:T(8,128)} %fusion.7, bf16[1,1,512,512]{3,2,1,0:T(8,128)(2,1)} %param.15, s32[512]{0:T(512)S(1)} %fusion.62), kind=kOutput, calls=%fused_computation.12 | convolution fusion | flops 537919488 | bytes 2623488 | tf_op jit(solution)/shard_map/dot_general | solution.py:49
  33.0 1.1 collective-permute-start.6
  34.7 1.2 collective-permute-start.3
  44.5 4.3 %all-to-all-start = ((f32[8,64,512]{2,1,0:T(8,128)}), f32[8,64,512]{2,1,0:T(8,128)}, u32[]{:S(2)}, u32[]{:S(2)}) async-start(f32[8,64,512]{2,1,0:T(8,128)} %bitcast.221), calls=%async_computation | async-start | bytes 2097152 | tf_op jit(solution)/shard_map/all_to_all | solution.py:127
  49.1 26.3 %all-to-all-done = f32[8,64,512]{2,1,0:T(8,128)} async-done(((f32[8,64,512]{2,1,0:T(8,128)}), f32[8,64,512]{2,1,0:T(8,128)}, u32[]{:S(2)}, u32[]{:S(2)}) %all-to-all-start) | async-done | bytes 1048608 | tf_op jit(solution)/shard_map/all_to_all | solution.py:127
  75.4 1.3 reduce_sum.9
  77.8 1.3 collective-permute-start.7
  79.1 1.0 collective-permute-start.8
  80.2 2.1 %collective-permute-done.8 = f32[64,128]{1,0:T(8,128)S(1)} collective-permute-done((f32[64,128]{1,0:T(8,128)S(1)}, f32[64,128]{1,0:T(8,128)S(1)}, u32[]{:S(2)}, u32[]{:S(2)}) %collective-permute-start.8) | collective-permute-done | bytes 32800 | tf_op jit(solution)/shard_map/ppermute | solution.py:20
  82.3 1.2 collective-permute-done.9
  83.9 3.2 %collective-permute-start.12 = (bf16[64,128]{1,0:T(8,128)(2,1)S(1)}, bf16[64,128]{1,0:T(8,128)(2,1)S(1)}, u32[]{:S(2)}, u32[]{:S(2)}) collective-permute-start(bf16[64,128]{1,0:T(8,128)(2,1)S(1)} %get-tuple-element.34), channel_id=1, source_target_pairs={{0,3},{1,0},{2,1},{3,2},{4,7},{5,4},{6,5},{7,6},{8,11},{9,8},{10,9... | collective-permute-start | bytes 49160 | tf_op jit(solution)/shard_map/ppermute | solution.py:20
  89.3 2.7 %collective-permute-done.13 = bf16[4,64,128]{2,1,0:T(8,128)(2,1)S(1)} collective-permute-done((bf16[4,64,128]{2,1,0:T(8,128)(2,1)S(1)}, bf16[4,64,128]{2,1,0:T(8,128)(2,1)S(1)}, u32[]{:S(2)}, u32[]{:S(2)}) %collective-permute-start.13) | collective-permute-done | bytes 65568 | tf_op jit(solution)/shard_map/ppermute | solution.py:20
  92.4 2.3 %collective-permute-start.14 = (f32[64,128]{1,0:T(8,128)S(1)}, f32[64,128]{1,0:T(8,128)S(1)}, u32[]{:S(2)}, u32[]{:S(2)}) collective-permute-start(f32[64,128]{1,0:T(8,128)S(1)} %fusion.14), channel_id=1, source_target_pairs={{0,4},{4,8},{8,12},{12,0},{1,5},{5,9},{9,13},{13,1},{2,6},{6,10},{... | collective-permute-start | bytes 98312 | tf_op jit(solution)/shard_map/ppermute | solution.py:20
  95.7 2.4 %collective-permute-done.15 = f32[64,128]{1,0:T(8,128)S(1)} collective-permute-done((f32[64,128]{1,0:T(8,128)S(1)}, f32[64,128]{1,0:T(8,128)S(1)}, u32[]{:S(2)}, u32[]{:S(2)}) %collective-permute-start.15) | collective-permute-done | bytes 32800 | tf_op jit(solution)/shard_map/ppermute | solution.py:20
  99.1 1.8 %collective-permute-start.17 = (bf16[64,128]{1,0:T(8,128)(2,1)S(1)}, bf16[64,128]{1,0:T(8,128)(2,1)S(1)}, u32[]{:S(2)}, u32[]{:S(2)}) collective-permute-start(bf16[64,128]{1,0:T(8,128)(2,1)S(1)} %get-tuple-element.36), channel_id=1, source_target_pairs={{0,1},{1,2},{2,3},{3,0},{4,5},{5,6},{6,7},{7,4},{8,9},{9,10},{10,1... | collective-permute-start | bytes 49160 | tf_op jit(solution)/shard_map/ppermute | solution.py:20
  100.8 1.5 %collective-permute-start.18 = (bf16[64,128]{1,0:T(8,128)(2,1)S(1)}, bf16[64,128]{1,0:T(8,128)(2,1)S(1)}, u32[]{:S(2)}, u32[]{:S(2)}) collective-permute-start(bf16[64,128]{1,0:T(8,128)(2,1)S(1)} %get-tuple-element.36), channel_id=1, source_target_pairs={{0,2},{1,3},{2,0},{3,1},{4,6},{5,7},{6,4},{7,5},{8,10},{9,11},{10,... | collective-permute-start | bytes 49160 | tf_op jit(solution)/shard_map/ppermute | solution.py:20
  105.4 2.7 %collective-permute-done.20 = bf16[4,64,128]{2,1,0:T(8,128)(2,1)S(1)} collective-permute-done((bf16[4,64,128]{2,1,0:T(8,128)(2,1)S(1)}, bf16[4,64,128]{2,1,0:T(8,128)(2,1)S(1)}, u32[]{:S(2)}, u32[]{:S(2)}) %collective-permute-start.20) | collective-permute-done | bytes 65568 | tf_op jit(solution)/shard_map/ppermute | solution.py:20
  108.5 3.0 %collective-permute-start.21 = (f32[64,128]{1,0:T(8,128)S(1)}, f32[64,128]{1,0:T(8,128)S(1)}, u32[]{:S(2)}, u32[]{:S(2)}) collective-permute-start(f32[64,128]{1,0:T(8,128)S(1)} %fusion.11), channel_id=1, source_target_pairs={{0,4},{4,8},{8,12},{12,0},{1,5},{5,9},{9,13},{13,1},{2,6},{6,10},{... | collective-permute-start | bytes 98312 | tf_op jit(solution)/shard_map/ppermute | solution.py:20
  112.5 2.3 %collective-permute-done.22 = f32[64,128]{1,0:T(8,128)S(1)} collective-permute-done((f32[64,128]{1,0:T(8,128)S(1)}, f32[64,128]{1,0:T(8,128)S(1)}, u32[]{:S(2)}, u32[]{:S(2)}) %collective-permute-start.22) | collective-permute-done | bytes 32800 | tf_op jit(solution)/shard_map/ppermute | solution.py:20
  116.3 2.1 %collective-permute-start.25 = (bf16[64,128]{1,0:T(8,128)(2,1)S(1)}, bf16[64,128]{1,0:T(8,128)(2,1)S(1)}, u32[]{:S(2)}, u32[]{:S(2)}) collective-permute-start(bf16[64,128]{1,0:T(8,128)(2,1)S(1)} %get-tuple-element.38), channel_id=1, source_target_pairs={{0,2},{1,3},{2,0},{3,1},{4,6},{5,7},{6,4},{7,5},{8,10},{9,11},{10,... | collective-permute-start | bytes 49160 | tf_op jit(solution)/shard_map/ppermute | solution.py:20
  119.7 1.0 collective-permute-done.24
  121.5 2.7 %collective-permute-done.27 = bf16[4,64,128]{2,1,0:T(8,128)(2,1)S(1)} collective-permute-done((bf16[4,64,128]{2,1,0:T(8,128)(2,1)S(1)}, bf16[4,64,128]{2,1,0:T(8,128)(2,1)S(1)}, u32[]{:S(2)}, u32[]{:S(2)}) %collective-permute-start.27) | collective-permute-done | bytes 65568 | tf_op jit(solution)/shard_map/ppermute | solution.py:20
  124.5 2.9 %collective-permute-start.28 = (f32[64,128]{1,0:T(8,128)S(1)}, f32[64,128]{1,0:T(8,128)S(1)}, u32[]{:S(2)}, u32[]{:S(2)}) collective-permute-start(f32[64,128]{1,0:T(8,128)S(1)} %fusion.8), channel_id=1, source_target_pairs={{0,4},{4,8},{8,12},{12,0},{1,5},{5,9},{9,13},{13,1},{2,6},{6,10},{... | collective-permute-start | bytes 98312 | tf_op jit(solution)/shard_map/ppermute | solution.py:20
  128.5 2.2 %collective-permute-done.29 = f32[64,128]{1,0:T(8,128)S(1)} collective-permute-done((f32[64,128]{1,0:T(8,128)S(1)}, f32[64,128]{1,0:T(8,128)S(1)}, u32[]{:S(2)}, u32[]{:S(2)}) %collective-permute-start.29) | collective-permute-done | bytes 32800 | tf_op jit(solution)/shard_map/ppermute | solution.py:20
  (125 shorter events, 32.7 us)
Async XLA Ops:
  1.7 34.2 %collective-permute-start.4 = (f32[64,256]{1,0:T(8,128)S(1)}, f32[64,256]{1,0:T(8,128)S(1)}, u32[]{:S(2)}, u32[]{:S(2)}) collective-permute-start(f32[64,256]{1,0:T(8,128)S(1)} %pad_maximum_fusion.16), channel_id=1, source_target_pairs={{0,4},{4,8},{8,12},{12,0},{1,5},{5,9},{9,13},{13,1},{2,6},{6,10},{... | collective-permute-start | bytes 196616 | tf_op jit(solution)/shard_map/ppermute | solution.py:20
  4.4 31.6 %collective-permute-start.5 = (f32[64,256]{1,0:T(8,128)S(1)}, f32[64,256]{1,0:T(8,128)S(1)}, u32[]{:S(2)}, u32[]{:S(2)}) collective-permute-start(f32[64,256]{1,0:T(8,128)S(1)} %pad_maximum_fusion.16), channel_id=1, source_target_pairs={{0,8},{4,12},{8,0},{12,4},{1,9},{5,13},{9,1},{13,5},{2,10},{6,14},... | collective-permute-start | bytes 196616 | tf_op jit(solution)/shard_map/ppermute | solution.py:20
  5.2 27.8 %collective-permute-start = (bf16[64,128]{1,0:T(8,128)(2,1)S(1)}, bf16[64,128]{1,0:T(8,128)(2,1)S(1)}, u32[]{:S(2)}, u32[]{:S(2)}) collective-permute-start(bf16[64,128]{1,0:T(8,128)(2,1)S(1)} %get-tuple-element.31), channel_id=1, source_target_pairs={{0,1},{1,2},{2,3},{3,0},{4,5},{5,6},{6,7},{7,4},{8,9},{9,10},{10,1... | collective-permute-start | bytes 49160 | tf_op jit(solution)/shard_map/ppermute | solution.py:20
  6.7 27.3 %collective-permute-start.1 = (bf16[64,128]{1,0:T(8,128)(2,1)S(1)}, bf16[64,128]{1,0:T(8,128)(2,1)S(1)}, u32[]{:S(2)}, u32[]{:S(2)}) collective-permute-start(bf16[64,128]{1,0:T(8,128)(2,1)S(1)} %get-tuple-element.31), channel_id=1, source_target_pairs={{0,2},{1,3},{2,0},{3,1},{4,6},{5,7},{6,4},{7,5},{8,10},{9,11},{10,... | collective-permute-start | bytes 49160 | tf_op jit(solution)/shard_map/ppermute | solution.py:20
  9.0 25.0 %collective-permute-start.2 = (bf16[64,128]{1,0:T(8,128)(2,1)S(1)}, bf16[64,128]{1,0:T(8,128)(2,1)S(1)}, u32[]{:S(2)}, u32[]{:S(2)}) collective-permute-start(bf16[64,128]{1,0:T(8,128)(2,1)S(1)} %get-tuple-element.31), channel_id=1, source_target_pairs={{0,3},{1,0},{2,1},{3,2},{4,7},{5,4},{6,5},{7,6},{8,11},{9,8},{10,9... | collective-permute-start | bytes 49160 | tf_op jit(solution)/shard_map/ppermute | solution.py:20
  33.0 3.7 %collective-permute-start.6 = (f32[64,256]{1,0:T(8,128)S(1)}, f32[64,256]{1,0:T(8,128)S(1)}, u32[]{:S(2)}, u32[]{:S(2)}) collective-permute-start(f32[64,256]{1,0:T(8,128)S(1)} %pad_maximum_fusion.16), channel_id=1, source_target_pairs={{0,12},{4,0},{8,4},{12,8},{1,13},{5,1},{9,5},{13,9},{2,14},{6,2},{... | collective-permute-start | bytes 196616 | tf_op jit(solution)/shard_map/ppermute | solution.py:20
  34.7 8.9 %collective-permute-start.3 = (bf16[4,64,128]{2,1,0:T(8,128)(2,1)}, bf16[4,64,128]{2,1,0:T(8,128)(2,1)}, u32[]{:S(2)}, u32[]{:S(2)}) collective-permute-start(bf16[4,64,128]{2,1,0:T(8,128)(2,1)} %get-tuple-element.27), channel_id=1, source_target_pairs={{0,16},{16,0},{1,17},{17,1},{2,18},{18,2},{3,19},{19,3},{4,20},{20... | collective-permute-start | bytes 196616 | tf_op jit(solution)/shard_map/ppermute | solution.py:20
  44.5 30.9 %all-to-all-start = ((f32[8,64,512]{2,1,0:T(8,128)}), f32[8,64,512]{2,1,0:T(8,128)}, u32[]{:S(2)}, u32[]{:S(2)}) async-start(f32[8,64,512]{2,1,0:T(8,128)} %bitcast.221), calls=%async_computation | async-start | bytes 2097152 | tf_op jit(solution)/shard_map/all_to_all | solution.py:127
  77.8 2.4 %collective-permute-start.7 = (f32[64,128]{1,0:T(8,128)S(1)}, f32[64,128]{1,0:T(8,128)S(1)}, u32[]{:S(2)}, u32[]{:S(2)}) collective-permute-start(f32[64,128]{1,0:T(8,128)S(1)} %fusion.17), channel_id=1, source_target_pairs={{0,4},{4,8},{8,12},{12,0},{1,5},{5,9},{9,13},{13,1},{2,6},{6,10},{... | collective-permute-start | bytes 98312 | tf_op jit(solution)/shard_map/ppermute | solution.py:20
  79.1 3.2 %collective-permute-start.8 = (f32[64,128]{1,0:T(8,128)S(1)}, f32[64,128]{1,0:T(8,128)S(1)}, u32[]{:S(2)}, u32[]{:S(2)}) collective-permute-start(f32[64,128]{1,0:T(8,128)S(1)} %fusion.17), channel_id=1, source_target_pairs={{0,8},{4,12},{8,0},{12,4},{1,9},{5,13},{9,1},{13,5},{2,10},{6,14},... | collective-permute-start | bytes 98312 | tf_op jit(solution)/shard_map/ppermute | solution.py:20
  80.2 3.3 %collective-permute-start.9 = (f32[64,128]{1,0:T(8,128)S(1)}, f32[64,128]{1,0:T(8,128)S(1)}, u32[]{:S(2)}, u32[]{:S(2)}) collective-permute-start(f32[64,128]{1,0:T(8,128)S(1)} %fusion.17), channel_id=1, source_target_pairs={{0,12},{4,0},{8,4},{12,8},{1,13},{5,1},{9,5},{13,9},{2,14},{6,2},{... | collective-permute-start | bytes 98312 | tf_op jit(solution)/shard_map/ppermute | solution.py:20
  83.8 4.7 %collective-permute-start.10 = (bf16[64,128]{1,0:T(8,128)(2,1)S(1)}, bf16[64,128]{1,0:T(8,128)(2,1)S(1)}, u32[]{:S(2)}, u32[]{:S(2)}) collective-permute-start(bf16[64,128]{1,0:T(8,128)(2,1)S(1)} %get-tuple-element.34), channel_id=1, source_target_pairs={{0,1},{1,2},{2,3},{3,0},{4,5},{5,6},{6,7},{7,4},{8,9},{9,10},{10,1... | collective-permute-start | bytes 49160 | tf_op jit(solution)/shard_map/ppermute | solution.py:20
  83.8 4.6 %collective-permute-start.11 = (bf16[64,128]{1,0:T(8,128)(2,1)S(1)}, bf16[64,128]{1,0:T(8,128)(2,1)S(1)}, u32[]{:S(2)}, u32[]{:S(2)}) collective-permute-start(bf16[64,128]{1,0:T(8,128)(2,1)S(1)} %get-tuple-element.34), channel_id=1, source_target_pairs={{0,2},{1,3},{2,0},{3,1},{4,6},{5,7},{6,4},{7,5},{8,10},{9,11},{10,... | collective-permute-start | bytes 49160 | tf_op jit(solution)/shard_map/ppermute | solution.py:20
  83.9 4.9 %collective-permute-start.12 = (bf16[64,128]{1,0:T(8,128)(2,1)S(1)}, bf16[64,128]{1,0:T(8,128)(2,1)S(1)}, u32[]{:S(2)}, u32[]{:S(2)}) collective-permute-start(bf16[64,128]{1,0:T(8,128)(2,1)S(1)} %get-tuple-element.34), channel_id=1, source_target_pairs={{0,3},{1,0},{2,1},{3,2},{4,7},{5,4},{6,5},{7,6},{8,11},{9,8},{10,9... | collective-permute-start | bytes 49160 | tf_op jit(solution)/shard_map/ppermute | solution.py:20
  88.9 3.2 %collective-permute-start.13 = (bf16[4,64,128]{2,1,0:T(8,128)(2,1)S(1)}, bf16[4,64,128]{2,1,0:T(8,128)(2,1)S(1)}, u32[]{:S(2)}, u32[]{:S(2)}) collective-permute-start(bf16[4,64,128]{2,1,0:T(8,128)(2,1)S(1)} %get-tuple-element.23), channel_id=1, source_target_pairs={{0,16},{16,0},{1,17},{17,1},{2,18},{18,2},{3,19},{19,3},{4,20},{20... | collective-permute-start | bytes 196616 | tf_op jit(solution)/shard_map/ppermute | solution.py:20
  92.4 3.3 %collective-permute-start.14 = (f32[64,128]{1,0:T(8,128)S(1)}, f32[64,128]{1,0:T(8,128)S(1)}, u32[]{:S(2)}, u32[]{:S(2)}) collective-permute-start(f32[64,128]{1,0:T(8,128)S(1)} %fusion.14), channel_id=1, source_target_pairs={{0,4},{4,8},{8,12},{12,0},{1,5},{5,9},{9,13},{13,1},{2,6},{6,10},{... | collective-permute-start | bytes 98312 | tf_op jit(solution)/shard_map/ppermute | solution.py:20
  94.7 3.4 %collective-permute-start.15 = (f32[64,128]{1,0:T(8,128)S(1)}, f32[64,128]{1,0:T(8,128)S(1)}, u32[]{:S(2)}, u32[]{:S(2)}) collective-permute-start(f32[64,128]{1,0:T(8,128)S(1)} %fusion.14), channel_id=1, source_target_pairs={{0,8},{4,12},{8,0},{12,4},{1,9},{5,13},{9,1},{13,5},{2,10},{6,14},... | collective-permute-start | bytes 98312 | tf_op jit(solution)/shard_map/ppermute | solution.py:20
  95.5 3.3 %collective-permute-start.16 = (f32[64,128]{1,0:T(8,128)S(1)}, f32[64,128]{1,0:T(8,128)S(1)}, u32[]{:S(2)}, u32[]{:S(2)}) collective-permute-start(f32[64,128]{1,0:T(8,128)S(1)} %fusion.14), channel_id=1, source_target_pairs={{0,12},{4,0},{8,4},{12,8},{1,13},{5,1},{9,5},{13,9},{2,14},{6,2},{... | collective-permute-start | bytes 98312 | tf_op jit(solution)/shard_map/ppermute | solution.py:20
  99.1 4.8 %collective-permute-start.17 = (bf16[64,128]{1,0:T(8,128)(2,1)S(1)}, bf16[64,128]{1,0:T(8,128)(2,1)S(1)}, u32[]{:S(2)}, u32[]{:S(2)}) collective-permute-start(bf16[64,128]{1,0:T(8,128)(2,1)S(1)} %get-tuple-element.36), channel_id=1, source_target_pairs={{0,1},{1,2},{2,3},{3,0},{4,5},{5,6},{6,7},{7,4},{8,9},{9,10},{10,1... | collective-permute-start | bytes 49160 | tf_op jit(solution)/shard_map/ppermute | solution.py:20
  100.8 3.6 %collective-permute-start.18 = (bf16[64,128]{1,0:T(8,128)(2,1)S(1)}, bf16[64,128]{1,0:T(8,128)(2,1)S(1)}, u32[]{:S(2)}, u32[]{:S(2)}) collective-permute-start(bf16[64,128]{1,0:T(8,128)(2,1)S(1)} %get-tuple-element.36), channel_id=1, source_target_pairs={{0,2},{1,3},{2,0},{3,1},{4,6},{5,7},{6,4},{7,5},{8,10},{9,11},{10,... | collective-permute-start | bytes 49160 | tf_op jit(solution)/shard_map/ppermute | solution.py:20
  102.3 2.6 %collective-permute-start.19 = (bf16[64,128]{1,0:T(8,128)(2,1)S(1)}, bf16[64,128]{1,0:T(8,128)(2,1)S(1)}, u32[]{:S(2)}, u32[]{:S(2)}) collective-permute-start(bf16[64,128]{1,0:T(8,128)(2,1)S(1)} %get-tuple-element.36), channel_id=1, source_target_pairs={{0,3},{1,0},{2,1},{3,2},{4,7},{5,4},{6,5},{7,6},{8,11},{9,8},{10,9... | collective-permute-start | bytes 49160 | tf_op jit(solution)/shard_map/ppermute | solution.py:20
  105.0 3.2 %collective-permute-start.20 = (bf16[4,64,128]{2,1,0:T(8,128)(2,1)S(1)}, bf16[4,64,128]{2,1,0:T(8,128)(2,1)S(1)}, u32[]{:S(2)}, u32[]{:S(2)}) collective-permute-start(bf16[4,64,128]{2,1,0:T(8,128)(2,1)S(1)} %get-tuple-element.21), channel_id=1, source_target_pairs={{0,16},{16,0},{1,17},{17,1},{2,18},{18,2},{3,19},{19,3},{4,20},{20... | collective-permute-start | bytes 196616 | tf_op jit(solution)/shard_map/ppermute | solution.py:20
  108.5 4.0 %collective-permute-start.21 = (f32[64,128]{1,0:T(8,128)S(1)}, f32[64,128]{1,0:T(8,128)S(1)}, u32[]{:S(2)}, u32[]{:S(2)}) collective-permute-start(f32[64,128]{1,0:T(8,128)S(1)} %fusion.11), channel_id=1, source_target_pairs={{0,4},{4,8},{8,12},{12,0},{1,5},{5,9},{9,13},{13,1},{2,6},{6,10},{... | collective-permute-start | bytes 98312 | tf_op jit(solution)/shard_map/ppermute | solution.py:20
  111.5 3.3 %collective-permute-start.22 = (f32[64,128]{1,0:T(8,128)S(1)}, f32[64,128]{1,0:T(8,128)S(1)}, u32[]{:S(2)}, u32[]{:S(2)}) collective-permute-start(f32[64,128]{1,0:T(8,128)S(1)} %fusion.11), channel_id=1, source_target_pairs={{0,8},{4,12},{8,0},{12,4},{1,9},{5,13},{9,1},{13,5},{2,10},{6,14},... | collective-permute-start | bytes 98312 | tf_op jit(solution)/shard_map/ppermute | solution.py:20
  112.4 3.3 %collective-permute-start.23 = (f32[64,128]{1,0:T(8,128)S(1)}, f32[64,128]{1,0:T(8,128)S(1)}, u32[]{:S(2)}, u32[]{:S(2)}) collective-permute-start(f32[64,128]{1,0:T(8,128)S(1)} %fusion.11), channel_id=1, source_target_pairs={{0,12},{4,0},{8,4},{12,8},{1,13},{5,1},{9,5},{13,9},{2,14},{6,2},{... | collective-permute-start | bytes 98312 | tf_op jit(solution)/shard_map/ppermute | solution.py:20
  115.9 4.9 %collective-permute-start.24 = (bf16[64,128]{1,0:T(8,128)(2,1)S(1)}, bf16[64,128]{1,0:T(8,128)(2,1)S(1)}, u32[]{:S(2)}, u32[]{:S(2)}) collective-permute-start(bf16[64,128]{1,0:T(8,128)(2,1)S(1)} %get-tuple-element.38), channel_id=1, source_target_pairs={{0,1},{1,2},{2,3},{3,0},{4,5},{5,6},{6,7},{7,4},{8,9},{9,10},{10,1... | collective-permute-start | bytes 49160 | tf_op jit(solution)/shard_map/ppermute | solution.py:20
  116.3 4.5 %collective-permute-start.25 = (bf16[64,128]{1,0:T(8,128)(2,1)S(1)}, bf16[64,128]{1,0:T(8,128)(2,1)S(1)}, u32[]{:S(2)}, u32[]{:S(2)}) collective-permute-start(bf16[64,128]{1,0:T(8,128)(2,1)S(1)} %get-tuple-element.38), channel_id=1, source_target_pairs={{0,2},{1,3},{2,0},{3,1},{4,6},{5,7},{6,4},{7,5},{8,10},{9,11},{10,... | collective-permute-start | bytes 49160 | tf_op jit(solution)/shard_map/ppermute | solution.py:20
  118.4 2.6 %collective-permute-start.26 = (bf16[64,128]{1,0:T(8,128)(2,1)S(1)}, bf16[64,128]{1,0:T(8,128)(2,1)S(1)}, u32[]{:S(2)}, u32[]{:S(2)}) collective-permute-start(bf16[64,128]{1,0:T(8,128)(2,1)S(1)} %get-tuple-element.38), channel_id=1, source_target_pairs={{0,3},{1,0},{2,1},{3,2},{4,7},{5,4},{6,5},{7,6},{8,11},{9,8},{10,9... | collective-permute-start | bytes 49160 | tf_op jit(solution)/shard_map/ppermute | solution.py:20
  121.0 3.2 %collective-permute-start.27 = (bf16[4,64,128]{2,1,0:T(8,128)(2,1)S(1)}, bf16[4,64,128]{2,1,0:T(8,128)(2,1)S(1)}, u32[]{:S(2)}, u32[]{:S(2)}) collective-permute-start(bf16[4,64,128]{2,1,0:T(8,128)(2,1)S(1)} %get-tuple-element.19), channel_id=1, source_target_pairs={{0,16},{16,0},{1,17},{17,1},{2,18},{18,2},{3,19},{19,3},{4,20},{20... | collective-permute-start | bytes 196616 | tf_op jit(solution)/shard_map/ppermute | solution.py:20
  124.5 3.9 %collective-permute-start.28 = (f32[64,128]{1,0:T(8,128)S(1)}, f32[64,128]{1,0:T(8,128)S(1)}, u32[]{:S(2)}, u32[]{:S(2)}) collective-permute-start(f32[64,128]{1,0:T(8,128)S(1)} %fusion.8), channel_id=1, source_target_pairs={{0,4},{4,8},{8,12},{12,0},{1,5},{5,9},{9,13},{13,1},{2,6},{6,10},{... | collective-permute-start | bytes 98312 | tf_op jit(solution)/shard_map/ppermute | solution.py:20
  127.4 3.3 %collective-permute-start.29 = (f32[64,128]{1,0:T(8,128)S(1)}, f32[64,128]{1,0:T(8,128)S(1)}, u32[]{:S(2)}, u32[]{:S(2)}) collective-permute-start(f32[64,128]{1,0:T(8,128)S(1)} %fusion.8), channel_id=1, source_target_pairs={{0,8},{4,12},{8,0},{12,4},{1,9},{5,13},{9,1},{13,5},{2,10},{6,14},... | collective-permute-start | bytes 98312 | tf_op jit(solution)/shard_map/ppermute | solution.py:20
  128.4 3.3 %collective-permute-start.30 = (f32[64,128]{1,0:T(8,128)S(1)}, f32[64,128]{1,0:T(8,128)S(1)}, u32[]{:S(2)}, u32[]{:S(2)}) collective-permute-start(f32[64,128]{1,0:T(8,128)S(1)} %fusion.8), channel_id=1, source_target_pairs={{0,12},{4,0},{8,4},{12,8},{1,13},{5,1},{9,5},{13,9},{2,14},{6,2},{... | collective-permute-start | bytes 98312 | tf_op jit(solution)/shard_map/ppermute | solution.py:20
  (6 other events, 46.0 us)

commit v10 on v9

--- a/solution.py
+++ b/solution.py
@@ -32,6 +32,23 @@
     sub_back = (lax.axis_index("sub") - jnp.arange(subs)[:, None]) % subs
     iface_back = (lax.axis_index("iface") - jnp.arange(ifaces)[None, :]) % ifaces
     return (sub_back * ifaces + iface_back).reshape(-1)
+
+
+def scatter_owners(terms):
+    subs, ifaces = lax.axis_size("sub"), lax.axis_size("iface")
+    sub_pos, iface_pos = lax.axis_index("sub"), lax.axis_index("iface")
+    terms = terms.reshape((subs, ifaces) + terms.shape[1:])
+    inner = lax.dynamic_index_in_dim(terms, iface_pos, axis=1, keepdims=False)
+    for distance in range(1, ifaces):
+        route = [(i, (i + distance) % ifaces) for i in range(ifaces)]
+        chunk = lax.dynamic_index_in_dim(terms, (iface_pos + distance) % ifaces, axis=1, keepdims=False)
+        inner = inner + lax.ppermute(chunk, "iface", route)
+    total = lax.dynamic_index_in_dim(inner, sub_pos, axis=0, keepdims=False)
+    for distance in range(1, subs):
+        route = [(i, (i + distance) % subs) for i in range(subs)]
+        chunk = lax.dynamic_index_in_dim(inner, (sub_pos + distance) % subs, axis=0, keepdims=False)
+        total = total + lax.ppermute(chunk, "sub", route)
+    return total
 
 
 def schur_rows(block_list, boundary, coupled, inverse, owners):
@@ -124,25 +141,31 @@
     first_rounded, weights_mine, weights_above, known, spread = lax.optimization_barrier(
         (first_rounded, weights_mine, weights_above, known, spread)
     )
-    rows = jnp.sum(lax.all_to_all(spread, OWNERS, 0, 0, tiled=True), axis=0)
-    rows_hi, rows_lo = split_bf16(jnp.dot(precond_mine, rows, precision=lax.Precision.HIGHEST))
     node = jnp.arange(nodes, dtype=jnp.int32)
     source = jnp.repeat(ring_owner_order(), block_nodes) * block_nodes + node % block_nodes
     order = (node[:, None] == source[None, :]).astype(jnp.bfloat16)
+    first_nodes = first_rounded.reshape(nodes, load_count)
+    first_nodes = jnp.dot(order, first_nodes, preferred_element_type=jnp.float32).astype(jnp.bfloat16)
+    schur_hi, schur_lo = split_bf16(spread.reshape(nodes, nodes))
+    first_terms = jnp.dot(schur_hi, first_nodes, preferred_element_type=jnp.float32) + jnp.dot(
+        schur_lo, first_nodes, preferred_element_type=jnp.float32
+    )
+    first_assembled = scatter_owners(first_terms.reshape(owners, block_nodes, load_count))
+    rows = jnp.sum(lax.all_to_all(spread, OWNERS, 0, 0, tiled=True), axis=0)
+    rows_hi, rows_lo = split_bf16(jnp.dot(precond_mine, rows, precision=lax.Precision.HIGHEST))
     rows_hi = jnp.dot(rows_hi, order, preferred_element_type=jnp.float32).astype(jnp.bfloat16)
     rows_lo = jnp.dot(rows_lo, order, preferred_element_type=jnp.float32).astype(jnp.bfloat16)
 
     for sweep_index in range(SWEEPS):
         if sweep_index == 0:
-            rounded = first_rounded
+            update = known - jnp.dot(precond_mine, first_assembled, precision=high)
         else:
-            rounded = gather_owners(temps_mine.astype(jnp.bfloat16))
+            rounded = gather_owners(temps_mine.astype(jnp.bfloat16)).reshape(nodes, load_count)
             known = known_part(temps_mine, temps_above)
-        rounded = rounded.reshape(nodes, load_count)
-        update = known - (
-            jnp.dot(rows_hi, rounded, preferred_element_type=jnp.float32)
-            + jnp.dot(rows_lo, rounded, preferred_element_type=jnp.float32)
-        )
+            update = known - (
+                jnp.dot(rows_hi, rounded, preferred_element_type=jnp.float32)
+                + jnp.dot(rows_lo, rounded, preferred_element_type=jnp.float32)
+            )
         updates = ring_parts(update, "section")
         temps_mine = jnp.einsum("kij,kjl->il", weights_mine, updates, precision=high)
         temps_above = jnp.einsum("kij,kjl->il", weights_above, updates, precision=high)

time: 133 us -> 144 us (1.083)
  starting transfers between devices: 38.8 us -> 49.2 us
  waiting for transfers between devices: 52.6 us -> 47.3 us
  matrix products: 27.1 us -> 30.3 us
  other arithmetic: 9.89 us -> 12.4 us
    all_to_all x1, waiting for transfers between devices: 26.3 us -> 0.01 us  [body(): rows = jnp.sum(lax.all_to_all(spread, OWNERS, 0, 0, tiled=True), axis=0)]
    ppermute x0 -> x4, waiting for transfers between devices: none -> 23.5 us  [the longest x3 21.8 us: scatter_owners(): inner = inner + lax.ppermute(chunk, 'iface', route)]
    ppermute x0 -> x4, starting transfers between devices: none -> 5.8 us  [the longest x3 4.63 us: scatter_owners(): inner = inner + lax.ppermute(chunk, 'iface', route)]
    ppermute x31, starting transfers between devices: 34.5 us -> 39.1 us  [ring_parts(): parts.append(lax.ppermute(block, axis, route))]
    dot_general x0 -> x4, matrix products: none -> 3.75 us  [the longest x1 1.34 us: body(): jnp.dot(schur_lo, first_nodes, preferred_element_type=jnp.float32)]
    ppermute x31, waiting for transfers between devices: 26.3 us -> 23.8 us  [ring_parts(): parts.append(lax.ppermute(block, axis, route))]
    convert_element_type x0 -> x1, other arithmetic: none -> 2.17 us  [split_bf16(): return (high.astype(jnp.bfloat16), (value - high).astype(jnp.bfloat16))]
  transfers between devices with their start and end apart: 32 -> 36, of which waited for: 23 -> 26; matrix products, arithmetic and copies ran while one was open for 25% -> 25% of each run, Pallas kernels for 0% -> 0%
where the time goes in v10:
time: 144 us; the launch traced here: 143 us
  starting transfers between devices  49.2 us (34%)
  waiting for transfers between devices  47.3 us (33%)
  matrix products  30.3 us (21%)
  other arithmetic  12.4 us (9%)
  local copies, waits for them, and re-layouts  3.13 us (2%)
    ppermute x31, starting transfers between devices, ring_parts(): parts.append(lax.ppermute(block, axis, route))  39.1 us
    ppermute x31, waiting for transfers between devices, ring_parts(): parts.append(lax.ppermute(block, axis, route))  23.8 us
    ppermute x3, waiting for transfers between devices, scatter_owners(): inner = inner + lax.ppermute(chunk, 'iface', route)  21.8 us
    dot_general x1, matrix products, schur_rows(): solved = jnp.dot(inverse, coupled, preferred_element_type=jnp.float32)  10.1 us
    ppermute x3, starting transfers between devices, scatter_owners(): inner = inner + lax.ppermute(chunk, 'iface', route)  4.63 us
    all_to_all x1, starting transfers between devices, body(): rows = jnp.sum(lax.all_to_all(spread, OWNERS, 0, 0, tiled=True), axis=0)  4.24 us
    dot_general x1, matrix products, moved(): jnp.dot(rows.astype(jnp.bfloat16), place, preferred_element_type=jnp.floa...  3.35 us
    another operation x10, other arithmetic, ring_parts(): return jnp.stack(parts)  3.07 us
  transfers between devices with their start and end apart: 36, of which 26 were waited for; matrix products, arithmetic and copies ran while one was open for 25% of the time, Pallas kernels for 0%

profile of v10, /device:TPU:1, one launch (start us, length us, event | category | flops | bytes accessed | tf_op | source)
XLA Modules:
  0.0 142.8 jit_solution(13277566256789432438)
XLA Ops:
  1.7 2.6 %collective-permute-start.4 = (f32[64,256]{1,0:T(8,128)S(1)}, f32[64,256]{1,0:T(8,128)S(1)}, u32[]{:S(2)}, u32[]{:S(2)}) collective-permute-start(f32[64,256]{1,0:T(8,128)S(1)} %pad_maximum_fusion.16), channel_id=1, source_target_pairs={{0,4},{4,8},{8,12},{12,0},{1,5},{5,9},{9,13},{13,1},{2,6},{6,10},{... | collective-permute-start | bytes 196616 | tf_op jit(solution)/shard_map/ppermute | solution.py:20
  5.2 1.5 %collective-permute-start = (bf16[64,128]{1,0:T(8,128)(2,1)S(1)}, bf16[64,128]{1,0:T(8,128)(2,1)S(1)}, u32[]{:S(2)}, u32[]{:S(2)}) collective-permute-start(bf16[64,128]{1,0:T(8,128)(2,1)S(1)} %get-tuple-element.36), channel_id=1, source_target_pairs={{0,1},{1,2},{2,3},{3,0},{4,5},{5,6},{6,7},{7,4},{8,9},{9,10},{10,1... | collective-permute-start | bytes 49160 | tf_op jit(solution)/shard_map/ppermute | solution.py:20
  6.7 2.3 %collective-permute-start.1 = (bf16[64,128]{1,0:T(8,128)(2,1)S(1)}, bf16[64,128]{1,0:T(8,128)(2,1)S(1)}, u32[]{:S(2)}, u32[]{:S(2)}) collective-permute-start(bf16[64,128]{1,0:T(8,128)(2,1)S(1)} %get-tuple-element.36), channel_id=1, source_target_pairs={{0,2},{1,3},{2,0},{3,1},{4,6},{5,7},{6,4},{7,5},{8,10},{9,11},{10,... | collective-permute-start | bytes 49160 | tf_op jit(solution)/shard_map/ppermute | solution.py:20
  11.9 1.7 %convolution_convert_fusion = bf16[512,2560]{1,0:T(8,128)(2,1)S(1)} fusion(bf16[1,1,2560,512]{3,2,1,0:T(8,128)(2,1)S(1)} %copy-done, s32[512]{0:T(512)S(1)} %fusion.73), kind=kOutput, calls=%fused_computation.8 | convolution fusion | flops 1344012288 | bytes 5244928 | tf_op jit(solution)/shard_map/dot_general | solution.py:69
  13.6 10.1 %fusion = f32[512,2560]{1,0:T(8,128)S(1)} fusion(bf16[512,2560]{1,0:T(8,128)(2,1)S(1)} %convolution_convert_fusion, bf16[1,1,2560,2560]{3,2,1,0:T(8,128)(2,1)} %param.17), kind=kOutput, calls=%fused_computation.3 | convolution fusion | flops 6710886400 | bytes 20971520 | tf_op jit(solution)/shard_map/dot_general | solution.py:71
  23.7 1.6 %fusion.3 = f32[512,512]{1,0:T(8,128)S(1)} fusion(bf16[512,2560]{1,0:T(8,128)(2,1)S(1)} %convolution_convert_fusion, f32[512,2560]{1,0:T(8,128)S(1)} %fusion), kind=kOutput, calls=%fused_computation.9 | convolution fusion | flops 1346109440 | bytes 8912896 | tf_op jit(solution)/shard_map/dot_general | solution.py:74
  25.2 2.5 %fusion.7 = f32[512,512]{1,0:T(8,128)} fusion(f32[512,512]{1,0:T(8,128)S(1)} %fusion.3, bf16[512,2560]{1,0:T(8,128)(2,1)S(1)} %convolution_convert_fusion, f32[512,2560]{1,0:T(8,128)S(1)} %fusion), kind=kOutput, calls=%fused_computation.15 | convolution fusion | flops 1345060864 | bytes 9961472 | tf_op jit(solution)/shard_map/dot_general | solution.py:73
  28.7 3.3 %convolution_subtract_fusion = f32[512,512]{1,0:T(8,128)} fusion(f32[512,512]{1,0:T(8,128)} %fusion.7, bf16[1,1,512,512]{3,2,1,0:T(8,128)(2,1)} %param.15, s32[512]{0:T(512)S(1)} %fusion.73), kind=kOutput, calls=%fused_computation.14 | convolution fusion | flops 537919488 | bytes 2623488 | tf_op jit(solution)/shard_map/dot_general | solution.py:66
  41.3 1.5 %pad_maximum_fusion.2 = bf16[2,4,64,128]{3,2,1,0:T(8,128)(2,1)} fusion(bf16[1,4,64,128]{3,2,1,0:T(8,128)(2,1)} %bitcast.5, bf16[1,4,64,128]{3,2,1,0:T(8,128)(2,1)S(1)} %get-tuple-element.31), kind=kLoop, calls=%fused_computation.79 | loop fusion | flops 65536 | bytes 262144 | tf_op jit(solution)/shard_map/stack | solution.py:21
  42.8 2.2 %fusion.23 = (bf16[512,512]{1,0:T(8,128)(2,1)}, bf16[512,512]{1,0:T(8,128)(2,1)S(1)}) fusion(f32[8,64,512]{2,1,0:T(8,128)} %bitcast.241), kind=kLoop, calls=%fused_computation.62 | loop fusion | flops 1048576 | bytes 2097152 | tf_op jit(solution)/shard_map/convert_element_type | solution.py:12
  45.0 4.2 %all-to-all-start = ((f32[8,64,512]{2,1,0:T(8,128)}), f32[8,64,512]{2,1,0:T(8,128)}, u32[]{:S(2)}, u32[]{:S(2)}) async-start(f32[8,64,512]{2,1,0:T(8,128)} %bitcast.242), calls=%async_computation | async-start | bytes 2097152 | tf_op jit(solution)/shard_map/all_to_all | solution.py:154
  54.1 2.1 %collective-permute-start.8 = (f32[2,64,128]{2,1,0:T(8,128)}, f32[2,64,128]{2,1,0:T(8,128)S(1)}, u32[]{:S(2)}, u32[]{:S(2)}) collective-permute-start(f32[2,64,128]{2,1,0:T(8,128)} %get-tuple-element.22), channel_id=1, source_target_pairs={{0,2},{1,3},{2,0},{3,1},{4,6},{5,7},{6,4},{7,5},{8,10},{9,11},{10,... | collective-permute-start | bytes 196616 | tf_op jit(solution)/shard_map/ppermute | solution.py:45
  57.4 14.4 %collective-permute-done.7 = f32[2,64,128]{2,1,0:T(8,128)S(1)} collective-permute-done((f32[2,64,128]{2,1,0:T(8,128)}, f32[2,64,128]{2,1,0:T(8,128)S(1)}, u32[]{:S(2)}, u32[]{:S(2)}) %collective-permute-start.7) | collective-permute-done | bytes 65568 | tf_op jit(solution)/shard_map/ppermute | solution.py:45
  71.8 7.5 %collective-permute-done.8 = f32[2,64,128]{2,1,0:T(8,128)S(1)} collective-permute-done((f32[2,64,128]{2,1,0:T(8,128)}, f32[2,64,128]{2,1,0:T(8,128)S(1)}, u32[]{:S(2)}, u32[]{:S(2)}) %collective-permute-start.8) | collective-permute-done | bytes 65568 | tf_op jit(solution)/shard_map/ppermute | solution.py:45
  81.3 1.7 %collective-permute-done.10 = f32[64,128]{1,0:T(8,128)S(1)} collective-permute-done((f32[64,128]{1,0:T(8,128)S(1)}, f32[64,128]{1,0:T(8,128)S(1)}, u32[]{:S(2)}, u32[]{:S(2)}) %collective-permute-start.10) | collective-permute-done | bytes 32800 | tf_op jit(solution)/shard_map/ppermute | solution.py:50
  83.8 2.3 %collective-permute-start.11 = (f32[64,128]{1,0:T(8,128)S(1)}, f32[64,128]{1,0:T(8,128)S(1)}, u32[]{:S(2)}, u32[]{:S(2)}) collective-permute-start(f32[64,128]{1,0:T(8,128)S(1)} %fusion.17), channel_id=1, source_target_pairs={{0,4},{4,8},{8,12},{12,0},{1,5},{5,9},{9,13},{13,1},{2,6},{6,10},{... | collective-permute-start | bytes 98312 | tf_op jit(solution)/shard_map/ppermute | solution.py:20
  86.1 1.5 %collective-permute-start.12 = (f32[64,128]{1,0:T(8,128)S(1)}, f32[64,128]{1,0:T(8,128)S(1)}, u32[]{:S(2)}, u32[]{:S(2)}) collective-permute-start(f32[64,128]{1,0:T(8,128)S(1)} %fusion.17), channel_id=1, source_target_pairs={{0,8},{4,12},{8,0},{12,4},{1,9},{5,13},{9,1},{13,5},{2,10},{6,14},... | collective-permute-start | bytes 98312 | tf_op jit(solution)/shard_map/ppermute | solution.py:20
  87.6 2.0 %collective-permute-done.12 = f32[64,128]{1,0:T(8,128)S(1)} collective-permute-done((f32[64,128]{1,0:T(8,128)S(1)}, f32[64,128]{1,0:T(8,128)S(1)}, u32[]{:S(2)}, u32[]{:S(2)}) %collective-permute-start.12) | collective-permute-done | bytes 32800 | tf_op jit(solution)/shard_map/ppermute | solution.py:20
  91.2 1.4 collective-permute-start.14
  98.1 1.9 %collective-permute-done.17 = bf16[4,64,128]{2,1,0:T(8,128)(2,1)S(1)} collective-permute-done((bf16[4,64,128]{2,1,0:T(8,128)(2,1)S(1)}, bf16[4,64,128]{2,1,0:T(8,128)(2,1)S(1)}, u32[]{:S(2)}, u32[]{:S(2)}) %collective-permute-start.17) | collective-permute-done | bytes 65568 | tf_op jit(solution)/shard_map/ppermute | solution.py:20
  102.5 2.2 %collective-permute-start.18 = (f32[64,128]{1,0:T(8,128)S(1)}, f32[64,128]{1,0:T(8,128)S(1)}, u32[]{:S(2)}, u32[]{:S(2)}) collective-permute-start(f32[64,128]{1,0:T(8,128)S(1)} %fusion.14), channel_id=1, source_target_pairs={{0,4},{4,8},{8,12},{12,0},{1,5},{5,9},{9,13},{13,1},{2,6},{6,10},{... | collective-permute-start | bytes 98312 | tf_op jit(solution)/shard_map/ppermute | solution.py:20
  105.8 2.3 %collective-permute-done.19 = f32[64,128]{1,0:T(8,128)S(1)} collective-permute-done((f32[64,128]{1,0:T(8,128)S(1)}, f32[64,128]{1,0:T(8,128)S(1)}, u32[]{:S(2)}, u32[]{:S(2)}) %collective-permute-start.19) | collective-permute-done | bytes 32800 | tf_op jit(solution)/shard_map/ppermute | solution.py:20
  110.4 1.8 %collective-permute-start.22 = (bf16[64,128]{1,0:T(8,128)(2,1)S(1)}, bf16[64,128]{1,0:T(8,128)(2,1)S(1)}, u32[]{:S(2)}, u32[]{:S(2)}) collective-permute-start(bf16[64,128]{1,0:T(8,128)(2,1)S(1)} %get-tuple-element.41), channel_id=1, source_target_pairs={{0,2},{1,3},{2,0},{3,1},{4,6},{5,7},{6,4},{7,5},{8,10},{9,11},{10,... | collective-permute-start | bytes 49160 | tf_op jit(solution)/shard_map/ppermute | solution.py:20
  114.8 1.5 %collective-permute-start.24 = (bf16[4,64,128]{2,1,0:T(8,128)(2,1)S(1)}, bf16[4,64,128]{2,1,0:T(8,128)(2,1)S(1)}, u32[]{:S(2)}, u32[]{:S(2)}) collective-permute-start(bf16[4,64,128]{2,1,0:T(8,128)(2,1)S(1)} %get-tuple-element.26), channel_id=1, source_target_pairs={{0,16},{16,0},{1,17},{17,1},{2,18},{18,2},{3,19},{19,3},{4,20},{20... | collective-permute-start | bytes 196616 | tf_op jit(solution)/shard_map/ppermute | solution.py:20
  116.5 1.5 %collective-permute-done.24 = bf16[4,64,128]{2,1,0:T(8,128)(2,1)S(1)} collective-permute-done((bf16[4,64,128]{2,1,0:T(8,128)(2,1)S(1)}, bf16[4,64,128]{2,1,0:T(8,128)(2,1)S(1)}, u32[]{:S(2)}, u32[]{:S(2)}) %collective-permute-start.24) | collective-permute-done | bytes 65568 | tf_op jit(solution)/shard_map/ppermute | solution.py:20
  118.3 3.0 %collective-permute-start.25 = (f32[64,128]{1,0:T(8,128)S(1)}, f32[64,128]{1,0:T(8,128)S(1)}, u32[]{:S(2)}, u32[]{:S(2)}) collective-permute-start(f32[64,128]{1,0:T(8,128)S(1)} %fusion.11), channel_id=1, source_target_pairs={{0,4},{4,8},{8,12},{12,0},{1,5},{5,9},{9,13},{13,1},{2,6},{6,10},{... | collective-permute-start | bytes 98312 | tf_op jit(solution)/shard_map/ppermute | solution.py:20
  122.3 2.3 %collective-permute-done.26 = f32[64,128]{1,0:T(8,128)S(1)} collective-permute-done((f32[64,128]{1,0:T(8,128)S(1)}, f32[64,128]{1,0:T(8,128)S(1)}, u32[]{:S(2)}, u32[]{:S(2)}) %collective-permute-start.26) | collective-permute-done | bytes 32800 | tf_op jit(solution)/shard_map/ppermute | solution.py:20
  126.4 2.2 %collective-permute-start.29 = (bf16[64,128]{1,0:T(8,128)(2,1)S(1)}, bf16[64,128]{1,0:T(8,128)(2,1)S(1)}, u32[]{:S(2)}, u32[]{:S(2)}) collective-permute-start(bf16[64,128]{1,0:T(8,128)(2,1)S(1)} %get-tuple-element.43), channel_id=1, source_target_pairs={{0,2},{1,3},{2,0},{3,1},{4,6},{5,7},{6,4},{7,5},{8,10},{9,11},{10,... | collective-permute-start | bytes 49160 | tf_op jit(solution)/shard_map/ppermute | solution.py:20
  131.2 1.4 collective-permute-start.31
  132.8 1.6 %collective-permute-done.31 = bf16[4,64,128]{2,1,0:T(8,128)(2,1)S(1)} collective-permute-done((bf16[4,64,128]{2,1,0:T(8,128)(2,1)S(1)}, bf16[4,64,128]{2,1,0:T(8,128)(2,1)S(1)}, u32[]{:S(2)}, u32[]{:S(2)}) %collective-permute-start.31) | collective-permute-done | bytes 65568 | tf_op jit(solution)/shard_map/ppermute | solution.py:20
  134.7 2.9 %collective-permute-start.32 = (f32[64,128]{1,0:T(8,128)S(1)}, f32[64,128]{1,0:T(8,128)S(1)}, u32[]{:S(2)}, u32[]{:S(2)}) collective-permute-start(f32[64,128]{1,0:T(8,128)S(1)} %fusion.8), channel_id=1, source_target_pairs={{0,4},{4,8},{8,12},{12,0},{1,5},{5,9},{9,13},{13,1},{2,6},{6,10},{... | collective-permute-start | bytes 98312 | tf_op jit(solution)/shard_map/ppermute | solution.py:20
  138.7 2.2 %collective-permute-done.33 = f32[64,128]{1,0:T(8,128)S(1)} collective-permute-done((f32[64,128]{1,0:T(8,128)S(1)}, f32[64,128]{1,0:T(8,128)S(1)}, u32[]{:S(2)}, u32[]{:S(2)}) %collective-permute-start.33) | collective-permute-done | bytes 32800 | tf_op jit(solution)/shard_map/ppermute | solution.py:20
  (143 shorter events, 48.8 us)
Async XLA Ops:
  1.7 33.4 %collective-permute-start.4 = (f32[64,256]{1,0:T(8,128)S(1)}, f32[64,256]{1,0:T(8,128)S(1)}, u32[]{:S(2)}, u32[]{:S(2)}) collective-permute-start(f32[64,256]{1,0:T(8,128)S(1)} %pad_maximum_fusion.16), channel_id=1, source_target_pairs={{0,4},{4,8},{8,12},{12,0},{1,5},{5,9},{9,13},{13,1},{2,6},{6,10},{... | collective-permute-start | bytes 196616 | tf_op jit(solution)/shard_map/ppermute | solution.py:20
  4.4 30.8 %collective-permute-start.5 = (f32[64,256]{1,0:T(8,128)S(1)}, f32[64,256]{1,0:T(8,128)S(1)}, u32[]{:S(2)}, u32[]{:S(2)}) collective-permute-start(f32[64,256]{1,0:T(8,128)S(1)} %pad_maximum_fusion.16), channel_id=1, source_target_pairs={{0,8},{4,12},{8,0},{12,4},{1,9},{5,13},{9,1},{13,5},{2,10},{6,14},... | collective-permute-start | bytes 196616 | tf_op jit(solution)/shard_map/ppermute | solution.py:20
  5.2 27.0 %collective-permute-start = (bf16[64,128]{1,0:T(8,128)(2,1)S(1)}, bf16[64,128]{1,0:T(8,128)(2,1)S(1)}, u32[]{:S(2)}, u32[]{:S(2)}) collective-permute-start(bf16[64,128]{1,0:T(8,128)(2,1)S(1)} %get-tuple-element.36), channel_id=1, source_target_pairs={{0,1},{1,2},{2,3},{3,0},{4,5},{5,6},{6,7},{7,4},{8,9},{9,10},{10,1... | collective-permute-start | bytes 49160 | tf_op jit(solution)/shard_map/ppermute | solution.py:20
  6.7 26.6 %collective-permute-start.1 = (bf16[64,128]{1,0:T(8,128)(2,1)S(1)}, bf16[64,128]{1,0:T(8,128)(2,1)S(1)}, u32[]{:S(2)}, u32[]{:S(2)}) collective-permute-start(bf16[64,128]{1,0:T(8,128)(2,1)S(1)} %get-tuple-element.36), channel_id=1, source_target_pairs={{0,2},{1,3},{2,0},{3,1},{4,6},{5,7},{6,4},{7,5},{8,10},{9,11},{10,... | collective-permute-start | bytes 49160 | tf_op jit(solution)/shard_map/ppermute | solution.py:20
  9.0 24.3 %collective-permute-start.2 = (bf16[64,128]{1,0:T(8,128)(2,1)S(1)}, bf16[64,128]{1,0:T(8,128)(2,1)S(1)}, u32[]{:S(2)}, u32[]{:S(2)}) collective-permute-start(bf16[64,128]{1,0:T(8,128)(2,1)S(1)} %get-tuple-element.36), channel_id=1, source_target_pairs={{0,3},{1,0},{2,1},{3,2},{4,7},{5,4},{6,5},{7,6},{8,11},{9,8},{10,9... | collective-permute-start | bytes 49160 | tf_op jit(solution)/shard_map/ppermute | solution.py:20
  32.2 3.7 %collective-permute-start.6 = (f32[64,256]{1,0:T(8,128)S(1)}, f32[64,256]{1,0:T(8,128)S(1)}, u32[]{:S(2)}, u32[]{:S(2)}) collective-permute-start(f32[64,256]{1,0:T(8,128)S(1)} %pad_maximum_fusion.16), channel_id=1, source_target_pairs={{0,12},{4,0},{8,4},{12,8},{1,13},{5,1},{9,5},{13,9},{2,14},{6,2},{... | collective-permute-start | bytes 196616 | tf_op jit(solution)/shard_map/ppermute | solution.py:20
  33.9 7.4 %collective-permute-start.3 = (bf16[4,64,128]{2,1,0:T(8,128)(2,1)}, bf16[4,64,128]{2,1,0:T(8,128)(2,1)}, u32[]{:S(2)}, u32[]{:S(2)}) collective-permute-start(bf16[4,64,128]{2,1,0:T(8,128)(2,1)} %get-tuple-element.32), channel_id=1, source_target_pairs={{0,16},{16,0},{1,17},{17,1},{2,18},{18,2},{3,19},{19,3},{4,20},{20... | collective-permute-start | bytes 196616 | tf_op jit(solution)/shard_map/ppermute | solution.py:20
  45.0 55.1 %all-to-all-start = ((f32[8,64,512]{2,1,0:T(8,128)}), f32[8,64,512]{2,1,0:T(8,128)}, u32[]{:S(2)}, u32[]{:S(2)}) async-start(f32[8,64,512]{2,1,0:T(8,128)} %bitcast.242), calls=%async_computation | async-start | bytes 2097152 | tf_op jit(solution)/shard_map/all_to_all | solution.py:154
  52.8 19.0 %collective-permute-start.7 = (f32[2,64,128]{2,1,0:T(8,128)}, f32[2,64,128]{2,1,0:T(8,128)S(1)}, u32[]{:S(2)}, u32[]{:S(2)}) collective-permute-start(f32[2,64,128]{2,1,0:T(8,128)} %get-tuple-element.20), channel_id=1, source_target_pairs={{0,1},{1,2},{2,3},{3,0},{4,5},{5,6},{6,7},{7,4},{8,9},{9,10},{10,1... | collective-permute-start | bytes 196616 | tf_op jit(solution)/shard_map/ppermute | solution.py:45
  54.1 25.1 %collective-permute-start.8 = (f32[2,64,128]{2,1,0:T(8,128)}, f32[2,64,128]{2,1,0:T(8,128)S(1)}, u32[]{:S(2)}, u32[]{:S(2)}) collective-permute-start(f32[2,64,128]{2,1,0:T(8,128)} %get-tuple-element.22), channel_id=1, source_target_pairs={{0,2},{1,3},{2,0},{3,1},{4,6},{5,7},{6,4},{7,5},{8,10},{9,11},{10,... | collective-permute-start | bytes 196616 | tf_op jit(solution)/shard_map/ppermute | solution.py:45
  56.2 23.0 %collective-permute-start.9 = (f32[2,64,128]{2,1,0:T(8,128)S(1)}, f32[2,64,128]{2,1,0:T(8,128)}, u32[]{:S(2)}, u32[]{:S(2)}) collective-permute-start(f32[2,64,128]{2,1,0:T(8,128)S(1)} %get-tuple-element.21), channel_id=1, source_target_pairs={{0,3},{1,0},{2,1},{3,2},{4,7},{5,4},{6,5},{7,6},{8,11},{9,8},{10,9... | collective-permute-start | bytes 196616 | tf_op jit(solution)/shard_map/ppermute | solution.py:45
  83.8 3.8 %collective-permute-start.11 = (f32[64,128]{1,0:T(8,128)S(1)}, f32[64,128]{1,0:T(8,128)S(1)}, u32[]{:S(2)}, u32[]{:S(2)}) collective-permute-start(f32[64,128]{1,0:T(8,128)S(1)} %fusion.17), channel_id=1, source_target_pairs={{0,4},{4,8},{8,12},{12,0},{1,5},{5,9},{9,13},{13,1},{2,6},{6,10},{... | collective-permute-start | bytes 98312 | tf_op jit(solution)/shard_map/ppermute | solution.py:20
  86.1 3.6 %collective-permute-start.12 = (f32[64,128]{1,0:T(8,128)S(1)}, f32[64,128]{1,0:T(8,128)S(1)}, u32[]{:S(2)}, u32[]{:S(2)}) collective-permute-start(f32[64,128]{1,0:T(8,128)S(1)} %fusion.17), channel_id=1, source_target_pairs={{0,8},{4,12},{8,0},{12,4},{1,9},{5,13},{9,1},{13,5},{2,10},{6,14},... | collective-permute-start | bytes 98312 | tf_op jit(solution)/shard_map/ppermute | solution.py:20
  87.6 3.3 %collective-permute-start.13 = (f32[64,128]{1,0:T(8,128)S(1)}, f32[64,128]{1,0:T(8,128)S(1)}, u32[]{:S(2)}, u32[]{:S(2)}) collective-permute-start(f32[64,128]{1,0:T(8,128)S(1)} %fusion.17), channel_id=1, source_target_pairs={{0,12},{4,0},{8,4},{12,8},{1,13},{5,1},{9,5},{13,9},{2,14},{6,2},{... | collective-permute-start | bytes 98312 | tf_op jit(solution)/shard_map/ppermute | solution.py:20
  91.2 4.5 %collective-permute-start.14 = (bf16[64,128]{1,0:T(8,128)(2,1)S(1)}, bf16[64,128]{1,0:T(8,128)(2,1)S(1)}, u32[]{:S(2)}, u32[]{:S(2)}) collective-permute-start(bf16[64,128]{1,0:T(8,128)(2,1)S(1)} %get-tuple-element.39), channel_id=1, source_target_pairs={{0,1},{1,2},{2,3},{3,0},{4,5},{5,6},{6,7},{7,4},{8,9},{9,10},{10,1... | collective-permute-start | bytes 49160 | tf_op jit(solution)/shard_map/ppermute | solution.py:20
  92.6 4.0 %collective-permute-start.15 = (bf16[64,128]{1,0:T(8,128)(2,1)S(1)}, bf16[64,128]{1,0:T(8,128)(2,1)S(1)}, u32[]{:S(2)}, u32[]{:S(2)}) collective-permute-start(bf16[64,128]{1,0:T(8,128)(2,1)S(1)} %get-tuple-element.39), channel_id=1, source_target_pairs={{0,2},{1,3},{2,0},{3,1},{4,6},{5,7},{6,4},{7,5},{8,10},{9,11},{10,... | collective-permute-start | bytes 49160 | tf_op jit(solution)/shard_map/ppermute | solution.py:20
  93.5 3.3 %collective-permute-start.16 = (bf16[64,128]{1,0:T(8,128)(2,1)S(1)}, bf16[64,128]{1,0:T(8,128)(2,1)S(1)}, u32[]{:S(2)}, u32[]{:S(2)}) collective-permute-start(bf16[64,128]{1,0:T(8,128)(2,1)S(1)} %get-tuple-element.39), channel_id=1, source_target_pairs={{0,3},{1,0},{2,1},{3,2},{4,7},{5,4},{6,5},{7,6},{8,11},{9,8},{10,9... | collective-permute-start | bytes 49160 | tf_op jit(solution)/shard_map/ppermute | solution.py:20
  96.8 3.2 %collective-permute-start.17 = (bf16[4,64,128]{2,1,0:T(8,128)(2,1)S(1)}, bf16[4,64,128]{2,1,0:T(8,128)(2,1)S(1)}, u32[]{:S(2)}, u32[]{:S(2)}) collective-permute-start(bf16[4,64,128]{2,1,0:T(8,128)(2,1)S(1)} %get-tuple-element.28), channel_id=1, source_target_pairs={{0,16},{16,0},{1,17},{17,1},{2,18},{18,2},{3,19},{19,3},{4,20},{20... | collective-permute-start | bytes 196616 | tf_op jit(solution)/shard_map/ppermute | solution.py:20
  102.5 3.3 %collective-permute-start.18 = (f32[64,128]{1,0:T(8,128)S(1)}, f32[64,128]{1,0:T(8,128)S(1)}, u32[]{:S(2)}, u32[]{:S(2)}) collective-permute-start(f32[64,128]{1,0:T(8,128)S(1)} %fusion.14), channel_id=1, source_target_pairs={{0,4},{4,8},{8,12},{12,0},{1,5},{5,9},{9,13},{13,1},{2,6},{6,10},{... | collective-permute-start | bytes 98312 | tf_op jit(solution)/shard_map/ppermute | solution.py:20
  104.7 3.4 %collective-permute-start.19 = (f32[64,128]{1,0:T(8,128)S(1)}, f32[64,128]{1,0:T(8,128)S(1)}, u32[]{:S(2)}, u32[]{:S(2)}) collective-permute-start(f32[64,128]{1,0:T(8,128)S(1)} %fusion.14), channel_id=1, source_target_pairs={{0,8},{4,12},{8,0},{12,4},{1,9},{5,13},{9,1},{13,5},{2,10},{6,14},... | collective-permute-start | bytes 98312 | tf_op jit(solution)/shard_map/ppermute | solution.py:20
  105.6 3.3 %collective-permute-start.20 = (f32[64,128]{1,0:T(8,128)S(1)}, f32[64,128]{1,0:T(8,128)S(1)}, u32[]{:S(2)}, u32[]{:S(2)}) collective-permute-start(f32[64,128]{1,0:T(8,128)S(1)} %fusion.14), channel_id=1, source_target_pairs={{0,12},{4,0},{8,4},{12,8},{1,13},{5,1},{9,5},{13,9},{2,14},{6,2},{... | collective-permute-start | bytes 98312 | tf_op jit(solution)/shard_map/ppermute | solution.py:20
  109.2 4.8 %collective-permute-start.21 = (bf16[64,128]{1,0:T(8,128)(2,1)S(1)}, bf16[64,128]{1,0:T(8,128)(2,1)S(1)}, u32[]{:S(2)}, u32[]{:S(2)}) collective-permute-start(bf16[64,128]{1,0:T(8,128)(2,1)S(1)} %get-tuple-element.41), channel_id=1, source_target_pairs={{0,1},{1,2},{2,3},{3,0},{4,5},{5,6},{6,7},{7,4},{8,9},{9,10},{10,1... | collective-permute-start | bytes 49160 | tf_op jit(solution)/shard_map/ppermute | solution.py:20
  110.4 4.4 %collective-permute-start.22 = (bf16[64,128]{1,0:T(8,128)(2,1)S(1)}, bf16[64,128]{1,0:T(8,128)(2,1)S(1)}, u32[]{:S(2)}, u32[]{:S(2)}) collective-permute-start(bf16[64,128]{1,0:T(8,128)(2,1)S(1)} %get-tuple-element.41), channel_id=1, source_target_pairs={{0,2},{1,3},{2,0},{3,1},{4,6},{5,7},{6,4},{7,5},{8,10},{9,11},{10,... | collective-permute-start | bytes 49160 | tf_op jit(solution)/shard_map/ppermute | solution.py:20
  114.8 3.2 %collective-permute-start.24 = (bf16[4,64,128]{2,1,0:T(8,128)(2,1)S(1)}, bf16[4,64,128]{2,1,0:T(8,128)(2,1)S(1)}, u32[]{:S(2)}, u32[]{:S(2)}) collective-permute-start(bf16[4,64,128]{2,1,0:T(8,128)(2,1)S(1)} %get-tuple-element.26), channel_id=1, source_target_pairs={{0,16},{16,0},{1,17},{17,1},{2,18},{18,2},{3,19},{19,3},{4,20},{20... | collective-permute-start | bytes 196616 | tf_op jit(solution)/shard_map/ppermute | solution.py:20
  118.3 4.0 %collective-permute-start.25 = (f32[64,128]{1,0:T(8,128)S(1)}, f32[64,128]{1,0:T(8,128)S(1)}, u32[]{:S(2)}, u32[]{:S(2)}) collective-permute-start(f32[64,128]{1,0:T(8,128)S(1)} %fusion.11), channel_id=1, source_target_pairs={{0,4},{4,8},{8,12},{12,0},{1,5},{5,9},{9,13},{13,1},{2,6},{6,10},{... | collective-permute-start | bytes 98312 | tf_op jit(solution)/shard_map/ppermute | solution.py:20
  121.3 3.3 %collective-permute-start.26 = (f32[64,128]{1,0:T(8,128)S(1)}, f32[64,128]{1,0:T(8,128)S(1)}, u32[]{:S(2)}, u32[]{:S(2)}) collective-permute-start(f32[64,128]{1,0:T(8,128)S(1)} %fusion.11), channel_id=1, source_target_pairs={{0,8},{4,12},{8,0},{12,4},{1,9},{5,13},{9,1},{13,5},{2,10},{6,14},... | collective-permute-start | bytes 98312 | tf_op jit(solution)/shard_map/ppermute | solution.py:20
  122.2 3.3 %collective-permute-start.27 = (f32[64,128]{1,0:T(8,128)S(1)}, f32[64,128]{1,0:T(8,128)S(1)}, u32[]{:S(2)}, u32[]{:S(2)}) collective-permute-start(f32[64,128]{1,0:T(8,128)S(1)} %fusion.11), channel_id=1, source_target_pairs={{0,12},{4,0},{8,4},{12,8},{1,13},{5,1},{9,5},{13,9},{2,14},{6,2},{... | collective-permute-start | bytes 98312 | tf_op jit(solution)/shard_map/ppermute | solution.py:20
  125.8 4.9 %collective-permute-start.28 = (bf16[64,128]{1,0:T(8,128)(2,1)S(1)}, bf16[64,128]{1,0:T(8,128)(2,1)S(1)}, u32[]{:S(2)}, u32[]{:S(2)}) collective-permute-start(bf16[64,128]{1,0:T(8,128)(2,1)S(1)} %get-tuple-element.43), channel_id=1, source_target_pairs={{0,1},{1,2},{2,3},{3,0},{4,5},{5,6},{6,7},{7,4},{8,9},{9,10},{10,1... | collective-permute-start | bytes 49160 | tf_op jit(solution)/shard_map/ppermute | solution.py:20
  126.4 4.2 %collective-permute-start.29 = (bf16[64,128]{1,0:T(8,128)(2,1)S(1)}, bf16[64,128]{1,0:T(8,128)(2,1)S(1)}, u32[]{:S(2)}, u32[]{:S(2)}) collective-permute-start(bf16[64,128]{1,0:T(8,128)(2,1)S(1)} %get-tuple-element.43), channel_id=1, source_target_pairs={{0,2},{1,3},{2,0},{3,1},{4,6},{5,7},{6,4},{7,5},{8,10},{9,11},{10,... | collective-permute-start | bytes 49160 | tf_op jit(solution)/shard_map/ppermute | solution.py:20
  134.7 4.0 %collective-permute-start.32 = (f32[64,128]{1,0:T(8,128)S(1)}, f32[64,128]{1,0:T(8,128)S(1)}, u32[]{:S(2)}, u32[]{:S(2)}) collective-permute-start(f32[64,128]{1,0:T(8,128)S(1)} %fusion.8), channel_id=1, source_target_pairs={{0,4},{4,8},{8,12},{12,0},{1,5},{5,9},{9,13},{13,1},{2,6},{6,10},{... | collective-permute-start | bytes 98312 | tf_op jit(solution)/shard_map/ppermute | solution.py:20
  137.7 3.3 %collective-permute-start.33 = (f32[64,128]{1,0:T(8,128)S(1)}, f32[64,128]{1,0:T(8,128)S(1)}, u32[]{:S(2)}, u32[]{:S(2)}) collective-permute-start(f32[64,128]{1,0:T(8,128)S(1)} %fusion.8), channel_id=1, source_target_pairs={{0,8},{4,12},{8,0},{12,4},{1,9},{5,13},{9,1},{13,5},{2,10},{6,14},... | collective-permute-start | bytes 98312 | tf_op jit(solution)/shard_map/ppermute | solution.py:20
  138.6 3.3 %collective-permute-start.34 = (f32[64,128]{1,0:T(8,128)S(1)}, f32[64,128]{1,0:T(8,128)S(1)}, u32[]{:S(2)}, u32[]{:S(2)}) collective-permute-start(f32[64,128]{1,0:T(8,128)S(1)} %fusion.8), channel_id=1, source_target_pairs={{0,12},{4,0},{8,4},{12,8},{1,13},{5,1},{9,5},{13,9},{2,14},{6,2},{... | collective-permute-start | bytes 98312 | tf_op jit(solution)/shard_map/ppermute | solution.py:20
  (12 other events, 163.3 us)

commit v11 on v9

--- a/solution.py
+++ b/solution.py
@@ -12,26 +12,23 @@
     return high.astype(jnp.bfloat16), (value - high).astype(jnp.bfloat16)
 
 
-def ring_parts(block, axis):
+def swap_parts(block, axis):
     count = lax.axis_size(axis)
-    parts = [block]
-    for distance in range(1, count):
-        route = [(i, (i + distance) % count) for i in range(count)]
-        parts.append(lax.ppermute(block, axis, route))
-    return jnp.stack(parts)
+    parts = block[None]
+    bit = 1
+    while bit < count:
+        route = [(i, i ^ bit) for i in range(count)]
+        parts = jnp.concatenate([parts, lax.ppermute(parts, axis, route)], axis=0)
+        bit *= 2
+    return parts
 
 
 def gather_owners(block):
-    inner = ring_parts(block, "iface")
-    outer = ring_parts(inner, "sub")
-    return outer.reshape((-1,) + block.shape)
+    return swap_parts(block, OWNERS)
 
 
-def ring_owner_order():
-    subs, ifaces = lax.axis_size("sub"), lax.axis_size("iface")
-    sub_back = (lax.axis_index("sub") - jnp.arange(subs)[:, None]) % subs
-    iface_back = (lax.axis_index("iface") - jnp.arange(ifaces)[None, :]) % ifaces
-    return (sub_back * ifaces + iface_back).reshape(-1)
+def partner_order(axis):
+    return lax.axis_index(axis) ^ jnp.arange(lax.axis_size(axis))
 
 
 def schur_rows(block_list, boundary, coupled, inverse, owners):
@@ -95,8 +92,8 @@
         axis=1,
     )
     first_rounded = gather_owners(previous[0].astype(jnp.bfloat16))
-    behind = (section_pos - jnp.arange(sections)) % sections
-    tables = jnp.take(ring_parts(tables, "section"), behind, axis=0)
+    behind = partner_order("section")
+    tables = jnp.take(swap_parts(tables, "section"), behind, axis=0)
     start_all = tables[:, :, :load_count]
     precond_all = tables[:, :, load_count : load_count + block_nodes]
     couple_all = tables[:, :, load_count + block_nodes :]
@@ -127,7 +124,7 @@
     rows = jnp.sum(lax.all_to_all(spread, OWNERS, 0, 0, tiled=True), axis=0)
     rows_hi, rows_lo = split_bf16(jnp.dot(precond_mine, rows, precision=lax.Precision.HIGHEST))
     node = jnp.arange(nodes, dtype=jnp.int32)
-    source = jnp.repeat(ring_owner_order(), block_nodes) * block_nodes + node % block_nodes
+    source = jnp.repeat(partner_order(OWNERS), block_nodes) * block_nodes + node % block_nodes
     order = (node[:, None] == source[None, :]).astype(jnp.bfloat16)
     rows_hi = jnp.dot(rows_hi, order, preferred_element_type=jnp.float32).astype(jnp.bfloat16)
     rows_lo = jnp.dot(rows_lo, order, preferred_element_type=jnp.float32).astype(jnp.bfloat16)
@@ -143,7 +140,7 @@
             jnp.dot(rows_hi, rounded, preferred_element_type=jnp.float32)
             + jnp.dot(rows_lo, rounded, preferred_element_type=jnp.float32)
         )
-        updates = ring_parts(update, "section")
+        updates = swap_parts(update, "section")
         temps_mine = jnp.einsum("kij,kjl->il", weights_mine, updates, precision=high)
         temps_above = jnp.einsum("kij,kjl->il", weights_above, updates, precision=high)
     return temps_mine[None]

time: 133 us -> 138 us (1.038)
  waiting for transfers between devices: 52.6 us -> 64.7 us
  other arithmetic: 9.89 us -> 5.02 us
  starting transfers between devices: 38.8 us -> 36.5 us
    ppermute x31 -> x22, waiting for transfers between devices: 26.3 us -> 41.5 us  [swap_parts(): parts = jnp.concatenate([parts, lax.ppermute(parts, axis, route)], axis=0)]
    all_to_all x1, waiting for transfers between devices: 26.3 us -> 23.2 us  [body(): rows = jnp.sum(lax.all_to_all(spread, OWNERS, 0, 0, tiled=True), axis=0)]
    ppermute x31 -> x22, starting transfers between devices: 34.5 us -> 32.1 us  [swap_parts(): parts = jnp.concatenate([parts, lax.ppermute(parts, axis, route)], axis=0)]
    another operation x10 -> x0, other arithmetic: 2.44 us -> none  [ring_parts(): return jnp.stack(parts)]
  transfers between devices with their start and end apart: 32 -> 23, of which waited for: 23 -> 21; matrix products, arithmetic and copies ran while one was open for 25% -> 17% of each run, Pallas kernels for 0% -> 0%
where the time goes in v11:
time: 138 us; the launch traced here: 137 us
  waiting for transfers between devices  64.7 us (47%)
  starting transfers between devices  36.5 us (26%)
  matrix products  27 us (20%)
  other arithmetic  5.02 us (4%)
  local copies, waits for them, and re-layouts  2.87 us (2%)
    ppermute x22, waiting for transfers between devices, swap_parts(): parts = jnp.concatenate([parts, lax.ppermute(parts, axis, route)], axis=0)  41.5 us
    ppermute x22, starting transfers between devices, swap_parts(): parts = jnp.concatenate([parts, lax.ppermute(parts, axis, route)], axis=0)  32.1 us
    all_to_all x1, waiting for transfers between devices, body(): rows = jnp.sum(lax.all_to_all(spread, OWNERS, 0, 0, tiled=True), axis=0)  23.2 us
    dot_general x1, matrix products, schur_rows(): solved = jnp.dot(inverse, coupled, preferred_element_type=jnp.float32)  10.1 us
    all_to_all x1, starting transfers between devices, body(): rows = jnp.sum(lax.all_to_all(spread, OWNERS, 0, 0, tiled=True), axis=0)  4.43 us
    dot_general x1, matrix products, moved(): jnp.dot(rows.astype(jnp.bfloat16), place, preferred_element_type=jnp.floa...  3.33 us
  transfers between devices with their start and end apart: 23, of which 21 were waited for; matrix products, arithmetic and copies ran while one was open for 17% of the time, Pallas kernels for 0%

profile of v11, /device:TPU:1, one launch (start us, length us, event | category | flops | bytes accessed | tf_op | source)
XLA Modules:
  0.0 136.5 jit_solution(4037524209895732921)
XLA Ops:
  2.6 2.7 %collective-permute-start = (bf16[1,64,128]{2,1,0:T(8,128)(2,1)S(1)}, bf16[1,64,128]{2,1,0:T(8,128)(2,1)S(1)}, u32[]{:S(2)}, u32[]{:S(2)}) collective-permute-start(bf16[1,64,128]{2,1,0:T(8,128)(2,1)S(1)} %convert_element_type.66), channel_id=1, source_target_pairs={{0,1},{1,0},{2,3},{3,2},{16,17},{17,16},{18,19},{19,18},{4,5},{5,4... | collective-permute-start | bytes 49160 | tf_op jit(solution)/shard_map/ppermute | solution.py:21
  6.1 1.7 %convolution_convert_fusion = bf16[512,2560]{1,0:T(8,128)(2,1)S(1)} fusion(bf16[1,1,2560,512]{3,2,1,0:T(8,128)(2,1)S(1)} %copy-done, s32[512]{0:T(512)S(1)} %fusion.56), kind=kOutput, calls=%fused_computation.8 | convolution fusion | flops 1344012288 | bytes 5244928 | tf_op jit(solution)/shard_map/dot_general | solution.py:49
  7.9 10.1 %fusion = f32[512,2560]{1,0:T(8,128)S(1)} fusion(bf16[512,2560]{1,0:T(8,128)(2,1)S(1)} %convolution_convert_fusion, bf16[1,1,2560,2560]{3,2,1,0:T(8,128)(2,1)} %param.17), kind=kOutput, calls=%fused_computation.3 | convolution fusion | flops 6710886400 | bytes 20971520 | tf_op jit(solution)/shard_map/dot_general | solution.py:51
  18.0 1.6 %fusion.3 = f32[512,512]{1,0:T(8,128)S(1)} fusion(bf16[512,2560]{1,0:T(8,128)(2,1)S(1)} %convolution_convert_fusion, f32[512,2560]{1,0:T(8,128)S(1)} %fusion), kind=kOutput, calls=%fused_computation.9 | convolution fusion | flops 1346109440 | bytes 8912896 | tf_op jit(solution)/shard_map/dot_general | solution.py:54
  19.5 2.5 %fusion.7 = f32[512,512]{1,0:T(8,128)} fusion(f32[512,512]{1,0:T(8,128)S(1)} %fusion.3, bf16[512,2560]{1,0:T(8,128)(2,1)S(1)} %convolution_convert_fusion, f32[512,2560]{1,0:T(8,128)S(1)} %fusion), kind=kOutput, calls=%fused_computation.13 | convolution fusion | flops 1345060864 | bytes 9961472 | tf_op jit(solution)/shard_map/dot_general | solution.py:53
  22.0 3.3 %convolution_subtract_fusion = f32[512,512]{1,0:T(8,128)} fusion(f32[512,512]{1,0:T(8,128)} %fusion.7, bf16[1,1,512,512]{3,2,1,0:T(8,128)(2,1)} %param.15, s32[512]{0:T(512)S(1)} %fusion.56), kind=kOutput, calls=%fused_computation.12 | convolution fusion | flops 537919488 | bytes 2623488 | tf_op jit(solution)/shard_map/dot_general | solution.py:46
  25.4 2.4 %collective-permute-start.1 = (bf16[2,64,128]{2,1,0:T(8,128)(2,1)S(1)}, bf16[2,64,128]{2,1,0:T(8,128)(2,1)S(1)}, u32[]{:S(2)}, u32[]{:S(2)}) collective-permute-start(bf16[2,64,128]{2,1,0:T(8,128)(2,1)S(1)} %pad_maximum_fusion.24), channel_id=1, source_target_pairs={{0,2},{1,3},{2,0},{3,1},{16,18},{17,19},{18,16},{19,17},{4,6},{5,7... | collective-permute-start | bytes 98312 | tf_op jit(solution)/shard_map/ppermute | solution.py:21
  27.8 2.3 %collective-permute-done.1 = bf16[2,64,128]{2,1,0:T(8,128)(2,1)S(1)} collective-permute-done((bf16[2,64,128]{2,1,0:T(8,128)(2,1)S(1)}, bf16[2,64,128]{2,1,0:T(8,128)(2,1)S(1)}, u32[]{:S(2)}, u32[]{:S(2)}) %collective-permute-start.1) | collective-permute-done | bytes 32800 | tf_op jit(solution)/shard_map/ppermute | solution.py:21
  33.3 1.3 collective-permute-done.4
  40.0 4.4 %all-to-all-start = ((f32[8,64,512]{2,1,0:T(8,128)}), f32[8,64,512]{2,1,0:T(8,128)}, u32[]{:S(2)}, u32[]{:S(2)}) async-start(f32[8,64,512]{2,1,0:T(8,128)} %bitcast.187), calls=%async_computation | async-start | bytes 2097152 | tf_op jit(solution)/shard_map/all_to_all | solution.py:124
  44.6 23.2 %all-to-all-done = f32[8,64,512]{2,1,0:T(8,128)} async-done(((f32[8,64,512]{2,1,0:T(8,128)}), f32[8,64,512]{2,1,0:T(8,128)}, u32[]{:S(2)}, u32[]{:S(2)}) %all-to-all-start) | async-done | bytes 1048608 | tf_op jit(solution)/shard_map/all_to_all | solution.py:124
  70.3 4.1 %collective-permute-start.5 = (f32[1,64,128]{2,1,0:T(8,128)S(1)}, f32[1,64,128]{2,1,0:T(8,128)S(1)}, u32[]{:S(2)}, u32[]{:S(2)}) collective-permute-start(f32[1,64,128]{2,1,0:T(8,128)S(1)} %subtract_bitcast_fusion.3), channel_id=1, source_target_pairs={{0,4},{4,0},{8,12},{12,8},{1,5},{5,1},{9,13},{13,9},{2,6},{6,2},{1... | collective-permute-start | bytes 98312 | tf_op jit(solution)/shard_map/ppermute | solution.py:21
  75.3 1.3 collective-permute-start.6
  76.6 1.8 %collective-permute-done.6 = f32[2,64,128]{2,1,0:T(8,128)S(1)} collective-permute-done((f32[2,64,128]{2,1,0:T(8,128)S(1)}, f32[2,64,128]{2,1,0:T(8,128)S(1)}, u32[]{:S(2)}, u32[]{:S(2)}) %collective-permute-start.6) | collective-permute-done | bytes 65568 | tf_op jit(solution)/shard_map/ppermute | solution.py:21
  79.0 2.3 %collective-permute-done.7 = bf16[1,64,128]{2,1,0:T(8,128)(2,1)S(1)} collective-permute-done((bf16[1,64,128]{2,1,0:T(8,128)(2,1)S(1)}, bf16[1,64,128]{2,1,0:T(8,128)(2,1)S(1)}, u32[]{:S(2)}, u32[]{:S(2)}) %collective-permute-start.7) | collective-permute-done | bytes 16416 | tf_op jit(solution)/shard_map/ppermute | solution.py:21
  81.5 3.5 %collective-permute-done.8 = bf16[2,64,128]{2,1,0:T(8,128)(2,1)S(1)} collective-permute-done((bf16[2,64,128]{2,1,0:T(8,128)(2,1)S(1)}, bf16[2,64,128]{2,1,0:T(8,128)(2,1)S(1)}, u32[]{:S(2)}, u32[]{:S(2)}) %collective-permute-start.8) | collective-permute-done | bytes 32800 | tf_op jit(solution)/shard_map/ppermute | solution.py:21
  85.5 2.9 %collective-permute-done.9 = bf16[4,64,128]{2,1,0:T(8,128)(2,1)S(1)} collective-permute-done((bf16[4,64,128]{2,1,0:T(8,128)(2,1)S(1)}, bf16[4,64,128]{2,1,0:T(8,128)(2,1)S(1)}, u32[]{:S(2)}, u32[]{:S(2)}) %collective-permute-start.9) | collective-permute-done | bytes 65568 | tf_op jit(solution)/shard_map/ppermute | solution.py:21
  88.7 4.8 %collective-permute-start.10 = (f32[1,64,128]{2,1,0:T(8,128)S(1)}, f32[1,64,128]{2,1,0:T(8,128)S(1)}, u32[]{:S(2)}, u32[]{:S(2)}) collective-permute-start(f32[1,64,128]{2,1,0:T(8,128)S(1)} %subtract_bitcast_fusion.2), channel_id=1, source_target_pairs={{0,4},{4,0},{8,12},{12,8},{1,5},{5,1},{9,13},{13,9},{2,6},{6,2},{1... | collective-permute-start | bytes 98312 | tf_op jit(solution)/shard_map/ppermute | solution.py:21
  94.4 1.3 collective-permute-start.11
  95.7 1.8 %collective-permute-done.11 = f32[2,64,128]{2,1,0:T(8,128)S(1)} collective-permute-done((f32[2,64,128]{2,1,0:T(8,128)S(1)}, f32[2,64,128]{2,1,0:T(8,128)S(1)}, u32[]{:S(2)}, u32[]{:S(2)}) %collective-permute-start.11) | collective-permute-done | bytes 65568 | tf_op jit(solution)/shard_map/ppermute | solution.py:21
  98.1 2.3 %collective-permute-done.12 = bf16[1,64,128]{2,1,0:T(8,128)(2,1)S(1)} collective-permute-done((bf16[1,64,128]{2,1,0:T(8,128)(2,1)S(1)}, bf16[1,64,128]{2,1,0:T(8,128)(2,1)S(1)}, u32[]{:S(2)}, u32[]{:S(2)}) %collective-permute-start.12) | collective-permute-done | bytes 16416 | tf_op jit(solution)/shard_map/ppermute | solution.py:21
  100.6 3.5 %collective-permute-done.13 = bf16[2,64,128]{2,1,0:T(8,128)(2,1)S(1)} collective-permute-done((bf16[2,64,128]{2,1,0:T(8,128)(2,1)S(1)}, bf16[2,64,128]{2,1,0:T(8,128)(2,1)S(1)}, u32[]{:S(2)}, u32[]{:S(2)}) %collective-permute-start.13) | collective-permute-done | bytes 32800 | tf_op jit(solution)/shard_map/ppermute | solution.py:21
  104.6 2.9 %collective-permute-done.14 = bf16[4,64,128]{2,1,0:T(8,128)(2,1)S(1)} collective-permute-done((bf16[4,64,128]{2,1,0:T(8,128)(2,1)S(1)}, bf16[4,64,128]{2,1,0:T(8,128)(2,1)S(1)}, u32[]{:S(2)}, u32[]{:S(2)}) %collective-permute-start.14) | collective-permute-done | bytes 65568 | tf_op jit(solution)/shard_map/ppermute | solution.py:21
  107.8 4.8 %collective-permute-start.15 = (f32[1,64,128]{2,1,0:T(8,128)S(1)}, f32[1,64,128]{2,1,0:T(8,128)S(1)}, u32[]{:S(2)}, u32[]{:S(2)}) collective-permute-start(f32[1,64,128]{2,1,0:T(8,128)S(1)} %subtract_bitcast_fusion.1), channel_id=1, source_target_pairs={{0,4},{4,0},{8,12},{12,8},{1,5},{5,1},{9,13},{13,9},{2,6},{6,2},{1... | collective-permute-start | bytes 98312 | tf_op jit(solution)/shard_map/ppermute | solution.py:21
  113.5 1.3 collective-permute-start.16
  114.8 1.8 %collective-permute-done.16 = f32[2,64,128]{2,1,0:T(8,128)S(1)} collective-permute-done((f32[2,64,128]{2,1,0:T(8,128)S(1)}, f32[2,64,128]{2,1,0:T(8,128)S(1)}, u32[]{:S(2)}, u32[]{:S(2)}) %collective-permute-start.16) | collective-permute-done | bytes 65568 | tf_op jit(solution)/shard_map/ppermute | solution.py:21
  117.2 2.3 %collective-permute-done.17 = bf16[1,64,128]{2,1,0:T(8,128)(2,1)S(1)} collective-permute-done((bf16[1,64,128]{2,1,0:T(8,128)(2,1)S(1)}, bf16[1,64,128]{2,1,0:T(8,128)(2,1)S(1)}, u32[]{:S(2)}, u32[]{:S(2)}) %collective-permute-start.17) | collective-permute-done | bytes 16416 | tf_op jit(solution)/shard_map/ppermute | solution.py:21
  119.7 3.5 %collective-permute-done.18 = bf16[2,64,128]{2,1,0:T(8,128)(2,1)S(1)} collective-permute-done((bf16[2,64,128]{2,1,0:T(8,128)(2,1)S(1)}, bf16[2,64,128]{2,1,0:T(8,128)(2,1)S(1)}, u32[]{:S(2)}, u32[]{:S(2)}) %collective-permute-start.18) | collective-permute-done | bytes 32800 | tf_op jit(solution)/shard_map/ppermute | solution.py:21
  123.7 2.9 %collective-permute-done.19 = bf16[4,64,128]{2,1,0:T(8,128)(2,1)S(1)} collective-permute-done((bf16[4,64,128]{2,1,0:T(8,128)(2,1)S(1)}, bf16[4,64,128]{2,1,0:T(8,128)(2,1)S(1)}, u32[]{:S(2)}, u32[]{:S(2)}) %collective-permute-start.19) | collective-permute-done | bytes 65568 | tf_op jit(solution)/shard_map/ppermute | solution.py:21
  126.9 4.8 %collective-permute-start.20 = (f32[1,64,128]{2,1,0:T(8,128)S(1)}, f32[1,64,128]{2,1,0:T(8,128)S(1)}, u32[]{:S(2)}, u32[]{:S(2)}) collective-permute-start(f32[1,64,128]{2,1,0:T(8,128)S(1)} %subtract_bitcast_fusion), channel_id=1, source_target_pairs={{0,4},{4,0},{8,12},{12,8},{1,5},{5,1},{9,13},{13,9},{2,6},{6,2},{1... | collective-permute-start | bytes 98312 | tf_op jit(solution)/shard_map/ppermute | solution.py:21
  132.6 1.3 collective-permute-start.21
  133.9 1.8 %collective-permute-done.21 = f32[2,64,128]{2,1,0:T(8,128)S(1)} collective-permute-done((f32[2,64,128]{2,1,0:T(8,128)S(1)}, f32[2,64,128]{2,1,0:T(8,128)S(1)}, u32[]{:S(2)}, u32[]{:S(2)}) %collective-permute-start.21) | collective-permute-done | bytes 65568 | tf_op jit(solution)/shard_map/ppermute | solution.py:21
  (113 shorter events, 23.4 us)
Async XLA Ops:
  0.0 6.1 %copy-start = (bf16[1,1,2560,512]{3,2,1,0:T(8,128)(2,1)S(1)}, bf16[1,1,2560,512]{3,2,1,0:T(8,128)(2,1)}, u32[]{:S(2)}) copy-start(bf16[1,1,2560,512]{3,2,1,0:T(8,128)(2,1)} %param.16) | copy-start | bytes 7864324
  1.7 28.9 %collective-permute-start.3 = (f32[1,64,256]{2,1,0:T(8,128)S(1)}, f32[1,64,256]{2,1,0:T(8,128)S(1)}, u32[]{:S(2)}, u32[]{:S(2)}) collective-permute-start(f32[1,64,256]{2,1,0:T(8,128)S(1)} %maximum_bitcast_fusion.4), channel_id=1, source_target_pairs={{0,4},{4,0},{8,12},{12,8},{1,5},{5,1},{9,13},{13,9},{2,6},{6,2},{1... | collective-permute-start | bytes 196616 | tf_op jit(solution)/shard_map/ppermute | solution.py:21
  2.6 22.8 %collective-permute-start = (bf16[1,64,128]{2,1,0:T(8,128)(2,1)S(1)}, bf16[1,64,128]{2,1,0:T(8,128)(2,1)S(1)}, u32[]{:S(2)}, u32[]{:S(2)}) collective-permute-start(bf16[1,64,128]{2,1,0:T(8,128)(2,1)S(1)} %convert_element_type.66), channel_id=1, source_target_pairs={{0,1},{1,0},{2,3},{3,2},{16,17},{17,16},{18,19},{19,18},{4,5},{5,4... | collective-permute-start | bytes 49160 | tf_op jit(solution)/shard_map/ppermute | solution.py:21
  25.4 4.7 %collective-permute-start.1 = (bf16[2,64,128]{2,1,0:T(8,128)(2,1)S(1)}, bf16[2,64,128]{2,1,0:T(8,128)(2,1)S(1)}, u32[]{:S(2)}, u32[]{:S(2)}) collective-permute-start(bf16[2,64,128]{2,1,0:T(8,128)(2,1)S(1)} %pad_maximum_fusion.24), channel_id=1, source_target_pairs={{0,2},{1,3},{2,0},{3,1},{16,18},{17,19},{18,16},{19,17},{4,6},{5,7... | collective-permute-start | bytes 98312 | tf_op jit(solution)/shard_map/ppermute | solution.py:21
  30.1 3.2 %collective-permute-start.2 = (bf16[4,64,128]{2,1,0:T(8,128)(2,1)S(1)}, bf16[4,64,128]{2,1,0:T(8,128)(2,1)S(1)}, u32[]{:S(2)}, u32[]{:S(2)}) collective-permute-start(bf16[4,64,128]{2,1,0:T(8,128)(2,1)S(1)} %pad_maximum_fusion.16), channel_id=1, source_target_pairs={{0,16},{1,17},{2,18},{3,19},{16,0},{17,1},{18,2},{19,3},{4,20},{5,... | collective-permute-start | bytes 196616 | tf_op jit(solution)/shard_map/ppermute | solution.py:21
  30.7 4.0 %collective-permute-start.4 = (f32[2,64,256]{2,1,0:T(8,128)S(1)}, f32[2,64,256]{2,1,0:T(8,128)S(1)}, u32[]{:S(2)}, u32[]{:S(2)}) collective-permute-start(f32[2,64,256]{2,1,0:T(8,128)S(1)} %pad_maximum_fusion.3), channel_id=1, source_target_pairs={{0,8},{4,12},{8,0},{12,4},{1,9},{5,13},{9,1},{13,5},{2,10},{6,14},... | collective-permute-start | bytes 393224 | tf_op jit(solution)/shard_map/ppermute | solution.py:21
  34.7 4.1 %copy-start.2 = (f32[1,64,128]{2,1,0:T(8,128)S(1)}, f32[1,64,128]{2,1,0:T(8,128)}, u32[]{:S(2)}) copy-start(f32[1,64,128]{2,1,0:T(8,128)} %param.11) | copy-start | bytes 98308
  35.2 4.5 %copy-start.1 = (bf16[1,1,64,64]{3,2,1,0:T(8,128)(2,1)S(1)}, bf16[1,1,64,64]{3,2,1,0:T(8,128)(2,1)}, u32[]{:S(2)}) copy-start(bf16[1,1,64,64]{3,2,1,0:T(8,128)(2,1)} %param.12) | copy-start | bytes 24580
  35.3 4.5 %copy-start.3 = (f32[1,64,128]{2,1,0:T(8,128)S(1)}, f32[1,64,128]{2,1,0:T(8,128)}, u32[]{:S(2)}) copy-start(f32[1,64,128]{2,1,0:T(8,128)} %param.10) | copy-start | bytes 98308
  40.0 27.8 %all-to-all-start = ((f32[8,64,512]{2,1,0:T(8,128)}), f32[8,64,512]{2,1,0:T(8,128)}, u32[]{:S(2)}, u32[]{:S(2)}) async-start(f32[8,64,512]{2,1,0:T(8,128)} %bitcast.187), calls=%async_computation | async-start | bytes 2097152 | tf_op jit(solution)/shard_map/all_to_all | solution.py:124
  70.3 4.9 %collective-permute-start.5 = (f32[1,64,128]{2,1,0:T(8,128)S(1)}, f32[1,64,128]{2,1,0:T(8,128)S(1)}, u32[]{:S(2)}, u32[]{:S(2)}) collective-permute-start(f32[1,64,128]{2,1,0:T(8,128)S(1)} %subtract_bitcast_fusion.3), channel_id=1, source_target_pairs={{0,4},{4,0},{8,12},{12,8},{1,5},{5,1},{9,13},{13,9},{2,6},{6,2},{1... | collective-permute-start | bytes 98312 | tf_op jit(solution)/shard_map/ppermute | solution.py:21
  75.3 3.1 %collective-permute-start.6 = (f32[2,64,128]{2,1,0:T(8,128)S(1)}, f32[2,64,128]{2,1,0:T(8,128)S(1)}, u32[]{:S(2)}, u32[]{:S(2)}) collective-permute-start(f32[2,64,128]{2,1,0:T(8,128)S(1)} %pad_maximum_fusion.17), channel_id=1, source_target_pairs={{0,8},{4,12},{8,0},{12,4},{1,9},{5,13},{9,1},{13,5},{2,10},{6,14},... | collective-permute-start | bytes 196616 | tf_op jit(solution)/shard_map/ppermute | solution.py:21
  78.6 2.7 %collective-permute-start.7 = (bf16[1,64,128]{2,1,0:T(8,128)(2,1)S(1)}, bf16[1,64,128]{2,1,0:T(8,128)(2,1)S(1)}, u32[]{:S(2)}, u32[]{:S(2)}) collective-permute-start(bf16[1,64,128]{2,1,0:T(8,128)(2,1)S(1)} %convert_bitcast_fusion.2), channel_id=1, source_target_pairs={{0,1},{1,0},{2,3},{3,2},{16,17},{17,16},{18,19},{19,18},{4,5},{5,4... | collective-permute-start | bytes 49160 | tf_op jit(solution)/shard_map/ppermute | solution.py:21
  81.3 3.7 %collective-permute-start.8 = (bf16[2,64,128]{2,1,0:T(8,128)(2,1)S(1)}, bf16[2,64,128]{2,1,0:T(8,128)(2,1)S(1)}, u32[]{:S(2)}, u32[]{:S(2)}) collective-permute-start(bf16[2,64,128]{2,1,0:T(8,128)(2,1)S(1)} %pad_maximum_fusion.25), channel_id=1, source_target_pairs={{0,2},{1,3},{2,0},{3,1},{16,18},{17,19},{18,16},{19,17},{4,6},{5,7... | collective-permute-start | bytes 98312 | tf_op jit(solution)/shard_map/ppermute | solution.py:21
  85.1 3.3 %collective-permute-start.9 = (bf16[4,64,128]{2,1,0:T(8,128)(2,1)S(1)}, bf16[4,64,128]{2,1,0:T(8,128)(2,1)S(1)}, u32[]{:S(2)}, u32[]{:S(2)}) collective-permute-start(bf16[4,64,128]{2,1,0:T(8,128)(2,1)S(1)} %pad_maximum_fusion.18), channel_id=1, source_target_pairs={{0,16},{1,17},{2,18},{3,19},{16,0},{17,1},{18,2},{19,3},{4,20},{5,... | collective-permute-start | bytes 196616 | tf_op jit(solution)/shard_map/ppermute | solution.py:21
  88.7 5.7 %collective-permute-start.10 = (f32[1,64,128]{2,1,0:T(8,128)S(1)}, f32[1,64,128]{2,1,0:T(8,128)S(1)}, u32[]{:S(2)}, u32[]{:S(2)}) collective-permute-start(f32[1,64,128]{2,1,0:T(8,128)S(1)} %subtract_bitcast_fusion.2), channel_id=1, source_target_pairs={{0,4},{4,0},{8,12},{12,8},{1,5},{5,1},{9,13},{13,9},{2,6},{6,2},{1... | collective-permute-start | bytes 98312 | tf_op jit(solution)/shard_map/ppermute | solution.py:21
  94.4 3.1 %collective-permute-start.11 = (f32[2,64,128]{2,1,0:T(8,128)S(1)}, f32[2,64,128]{2,1,0:T(8,128)S(1)}, u32[]{:S(2)}, u32[]{:S(2)}) collective-permute-start(f32[2,64,128]{2,1,0:T(8,128)S(1)} %pad_maximum_fusion.19), channel_id=1, source_target_pairs={{0,8},{4,12},{8,0},{12,4},{1,9},{5,13},{9,1},{13,5},{2,10},{6,14},... | collective-permute-start | bytes 196616 | tf_op jit(solution)/shard_map/ppermute | solution.py:21
  97.7 2.7 %collective-permute-start.12 = (bf16[1,64,128]{2,1,0:T(8,128)(2,1)S(1)}, bf16[1,64,128]{2,1,0:T(8,128)(2,1)S(1)}, u32[]{:S(2)}, u32[]{:S(2)}) collective-permute-start(bf16[1,64,128]{2,1,0:T(8,128)(2,1)S(1)} %convert_bitcast_fusion.1), channel_id=1, source_target_pairs={{0,1},{1,0},{2,3},{3,2},{16,17},{17,16},{18,19},{19,18},{4,5},{5,4... | collective-permute-start | bytes 49160 | tf_op jit(solution)/shard_map/ppermute | solution.py:21
  100.4 3.7 %collective-permute-start.13 = (bf16[2,64,128]{2,1,0:T(8,128)(2,1)S(1)}, bf16[2,64,128]{2,1,0:T(8,128)(2,1)S(1)}, u32[]{:S(2)}, u32[]{:S(2)}) collective-permute-start(bf16[2,64,128]{2,1,0:T(8,128)(2,1)S(1)} %pad_maximum_fusion.26), channel_id=1, source_target_pairs={{0,2},{1,3},{2,0},{3,1},{16,18},{17,19},{18,16},{19,17},{4,6},{5,7... | collective-permute-start | bytes 98312 | tf_op jit(solution)/shard_map/ppermute | solution.py:21
  104.2 3.3 %collective-permute-start.14 = (bf16[4,64,128]{2,1,0:T(8,128)(2,1)S(1)}, bf16[4,64,128]{2,1,0:T(8,128)(2,1)S(1)}, u32[]{:S(2)}, u32[]{:S(2)}) collective-permute-start(bf16[4,64,128]{2,1,0:T(8,128)(2,1)S(1)} %pad_maximum_fusion.20), channel_id=1, source_target_pairs={{0,16},{1,17},{2,18},{3,19},{16,0},{17,1},{18,2},{19,3},{4,20},{5,... | collective-permute-start | bytes 196616 | tf_op jit(solution)/shard_map/ppermute | solution.py:21
  107.8 5.7 %collective-permute-start.15 = (f32[1,64,128]{2,1,0:T(8,128)S(1)}, f32[1,64,128]{2,1,0:T(8,128)S(1)}, u32[]{:S(2)}, u32[]{:S(2)}) collective-permute-start(f32[1,64,128]{2,1,0:T(8,128)S(1)} %subtract_bitcast_fusion.1), channel_id=1, source_target_pairs={{0,4},{4,0},{8,12},{12,8},{1,5},{5,1},{9,13},{13,9},{2,6},{6,2},{1... | collective-permute-start | bytes 98312 | tf_op jit(solution)/shard_map/ppermute | solution.py:21
  113.5 3.1 %collective-permute-start.16 = (f32[2,64,128]{2,1,0:T(8,128)S(1)}, f32[2,64,128]{2,1,0:T(8,128)S(1)}, u32[]{:S(2)}, u32[]{:S(2)}) collective-permute-start(f32[2,64,128]{2,1,0:T(8,128)S(1)} %pad_maximum_fusion.21), channel_id=1, source_target_pairs={{0,8},{4,12},{8,0},{12,4},{1,9},{5,13},{9,1},{13,5},{2,10},{6,14},... | collective-permute-start | bytes 196616 | tf_op jit(solution)/shard_map/ppermute | solution.py:21
  116.8 2.7 %collective-permute-start.17 = (bf16[1,64,128]{2,1,0:T(8,128)(2,1)S(1)}, bf16[1,64,128]{2,1,0:T(8,128)(2,1)S(1)}, u32[]{:S(2)}, u32[]{:S(2)}) collective-permute-start(bf16[1,64,128]{2,1,0:T(8,128)(2,1)S(1)} %convert_bitcast_fusion), channel_id=1, source_target_pairs={{0,1},{1,0},{2,3},{3,2},{16,17},{17,16},{18,19},{19,18},{4,5},{5,4... | collective-permute-start | bytes 49160 | tf_op jit(solution)/shard_map/ppermute | solution.py:21
  119.5 3.7 %collective-permute-start.18 = (bf16[2,64,128]{2,1,0:T(8,128)(2,1)S(1)}, bf16[2,64,128]{2,1,0:T(8,128)(2,1)S(1)}, u32[]{:S(2)}, u32[]{:S(2)}) collective-permute-start(bf16[2,64,128]{2,1,0:T(8,128)(2,1)S(1)} %pad_maximum_fusion.27), channel_id=1, source_target_pairs={{0,2},{1,3},{2,0},{3,1},{16,18},{17,19},{18,16},{19,17},{4,6},{5,7... | collective-permute-start | bytes 98312 | tf_op jit(solution)/shard_map/ppermute | solution.py:21
  123.3 3.3 %collective-permute-start.19 = (bf16[4,64,128]{2,1,0:T(8,128)(2,1)S(1)}, bf16[4,64,128]{2,1,0:T(8,128)(2,1)S(1)}, u32[]{:S(2)}, u32[]{:S(2)}) collective-permute-start(bf16[4,64,128]{2,1,0:T(8,128)(2,1)S(1)} %pad_maximum_fusion.22), channel_id=1, source_target_pairs={{0,16},{1,17},{2,18},{3,19},{16,0},{17,1},{18,2},{19,3},{4,20},{5,... | collective-permute-start | bytes 196616 | tf_op jit(solution)/shard_map/ppermute | solution.py:21
  126.9 5.7 %collective-permute-start.20 = (f32[1,64,128]{2,1,0:T(8,128)S(1)}, f32[1,64,128]{2,1,0:T(8,128)S(1)}, u32[]{:S(2)}, u32[]{:S(2)}) collective-permute-start(f32[1,64,128]{2,1,0:T(8,128)S(1)} %subtract_bitcast_fusion), channel_id=1, source_target_pairs={{0,4},{4,0},{8,12},{12,8},{1,5},{5,1},{9,13},{13,9},{2,6},{6,2},{1... | collective-permute-start | bytes 98312 | tf_op jit(solution)/shard_map/ppermute | solution.py:21
  132.6 3.1 %collective-permute-start.21 = (f32[2,64,128]{2,1,0:T(8,128)S(1)}, f32[2,64,128]{2,1,0:T(8,128)S(1)}, u32[]{:S(2)}, u32[]{:S(2)}) collective-permute-start(f32[2,64,128]{2,1,0:T(8,128)S(1)} %pad_maximum_fusion.23), channel_id=1, source_target_pairs={{0,8},{4,12},{8,0},{12,4},{1,9},{5,13},{9,1},{13,5},{2,10},{6,14},... | collective-permute-start | bytes 196616 | tf_op jit(solution)/shard_map/ppermute | solution.py:21

commit v12 on v9

--- a/solution.py
+++ b/solution.py
@@ -22,9 +22,20 @@
 
 
 def gather_owners(block):
-    inner = ring_parts(block, "iface")
-    outer = ring_parts(inner, "sub")
-    return outer.reshape((-1,) + block.shape)
+    subs, ifaces = lax.axis_size("sub"), lax.axis_size("iface")
+    parts = []
+    for sub_step in range(subs):
+        for iface_step in range(ifaces):
+            if sub_step == 0 and iface_step == 0:
+                parts.append(block)
+                continue
+            route = [
+                (s * ifaces + i, ((s + sub_step) % subs) * ifaces + (i + iface_step) % ifaces)
+                for s in range(subs)
+                for i in range(ifaces)
+            ]
+            parts.append(lax.ppermute(block, OWNERS, route))
+    return jnp.stack(parts)
 
 
 def ring_owner_order():

time: 133 us -> 147 us (1.11)
  starting transfers between devices: 38.8 us -> 66.1 us
  waiting for transfers between devices: 52.6 us -> 43.5 us
  other arithmetic: 9.89 us -> 6.56 us
    ppermute x0 -> x28, starting transfers between devices: none -> 41.2 us  [gather_owners(): parts.append(lax.ppermute(block, OWNERS, route))]
    ppermute x31 -> x15, starting transfers between devices: 34.5 us -> 20.3 us  [ring_parts(): parts.append(lax.ppermute(block, axis, route))]
    ppermute x31 -> x15, waiting for transfers between devices: 26.3 us -> 13.1 us  [ring_parts(): parts.append(lax.ppermute(block, axis, route))]
    ppermute x0 -> x28, waiting for transfers between devices: none -> 7.59 us  [gather_owners(): parts.append(lax.ppermute(block, OWNERS, route))]
    all_to_all x1, waiting for transfers between devices: 26.3 us -> 22.9 us  [body(): rows = jnp.sum(lax.all_to_all(spread, OWNERS, 0, 0, tiled=True), axis=0)]
    another operation x10 -> x2, other arithmetic: 2.44 us -> 0.85 us  [ring_parts(): return jnp.stack(parts)]
  transfers between devices with their start and end apart: 32 -> 44, of which waited for: 23 -> 21; matrix products, arithmetic and copies ran while one was open for 25% -> 17% of each run, Pallas kernels for 0% -> 0%
where the time goes in v12:
time: 147 us
  starting transfers between devices  66.1 us (45%)
  waiting for transfers between devices  43.5 us (30%)
  matrix products  27 us (18%)
  other arithmetic  6.56 us (4%)
  local copies, waits for them, and re-layouts  3.19 us (2%)
    ppermute x28, starting transfers between devices, gather_owners(): parts.append(lax.ppermute(block, OWNERS, route))  41.2 us
    all_to_all x1, waiting for transfers between devices, body(): rows = jnp.sum(lax.all_to_all(spread, OWNERS, 0, 0, tiled=True), axis=0)  22.9 us
    ppermute x15, starting transfers between devices, ring_parts(): parts.append(lax.ppermute(block, axis, route))  20.3 us
    ppermute x15, waiting for transfers between devices, ring_parts(): parts.append(lax.ppermute(block, axis, route))  13.1 us
    dot_general x1, matrix products, schur_rows(): solved = jnp.dot(inverse, coupled, preferred_element_type=jnp.float32)  10.1 us
    ppermute x28, waiting for transfers between devices, gather_owners(): parts.append(lax.ppermute(block, OWNERS, route))  7.59 us
    all_to_all x1, starting transfers between devices, body(): rows = jnp.sum(lax.all_to_all(spread, OWNERS, 0, 0, tiled=True), axis=0)  4.62 us
    dot_general x1, matrix products, moved(): jnp.dot(rows.astype(jnp.bfloat16), place, preferred_element_type=jnp.floa...  3.35 us
  transfers between devices with their start and end apart: 44, of which 21 were waited for; matrix products, arithmetic and copies ran while one was open for 17% of the time, Pallas kernels for 0%

profile of v12, /device:TPU:1, one launch (start us, length us, event | category | flops | bytes accessed | tf_op | source)
XLA Modules:
  0.0 146.9 jit_solution(5411049938015458521)
XLA Ops:
  1.7 2.6 %collective-permute-start.7 = (f32[64,256]{1,0:T(8,128)S(1)}, f32[64,256]{1,0:T(8,128)S(1)}, u32[]{:S(2)}, u32[]{:S(2)}) collective-permute-start(f32[64,256]{1,0:T(8,128)S(1)} %pad_maximum_fusion.11), channel_id=1, source_target_pairs={{0,4},{4,8},{8,12},{12,0},{1,5},{5,9},{9,13},{13,1},{2,6},{6,10},{... | collective-permute-start | bytes 196616 | tf_op jit(solution)/shard_map/ppermute | solution.py:20
  6.9 2.3 %collective-permute-start.1 = (bf16[64,128]{1,0:T(8,128)(2,1)S(1)}, bf16[64,128]{1,0:T(8,128)(2,1)S(1)}, u32[]{:S(2)}, u32[]{:S(2)}) collective-permute-start(bf16[64,128]{1,0:T(8,128)(2,1)S(1)} %bitcast_convert_fusion.2), channel_id=1, source_target_pairs={{0,2},{1,3},{2,0},{3,1},{16,18},{17,19},{18,16},{19,17},{4,6},{5,7... | collective-permute-start | bytes 49160 | tf_op jit(solution)/shard_map/ppermute | solution.py:37
  11.7 1.7 %convolution_convert_fusion = bf16[512,2560]{1,0:T(8,128)(2,1)S(1)} fusion(bf16[1,1,2560,512]{3,2,1,0:T(8,128)(2,1)S(1)} %copy-done, s32[512]{0:T(512)S(1)} %fusion.61), kind=kOutput, calls=%fused_computation.8 | convolution fusion | flops 1344012288 | bytes 5244928 | tf_op jit(solution)/shard_map/dot_general | solution.py:63
  13.4 10.1 %fusion = f32[512,2560]{1,0:T(8,128)S(1)} fusion(bf16[512,2560]{1,0:T(8,128)(2,1)S(1)} %convolution_convert_fusion, bf16[1,1,2560,2560]{3,2,1,0:T(8,128)(2,1)} %param.17), kind=kOutput, calls=%fused_computation.3 | convolution fusion | flops 6710886400 | bytes 20971520 | tf_op jit(solution)/shard_map/dot_general | solution.py:65
  23.5 1.6 %fusion.3 = f32[512,512]{1,0:T(8,128)S(1)} fusion(bf16[512,2560]{1,0:T(8,128)(2,1)S(1)} %convolution_convert_fusion, f32[512,2560]{1,0:T(8,128)S(1)} %fusion), kind=kOutput, calls=%fused_computation.9 | convolution fusion | flops 1346109440 | bytes 8912896 | tf_op jit(solution)/shard_map/dot_general | solution.py:68
  25.1 2.5 %fusion.7 = f32[512,512]{1,0:T(8,128)} fusion(f32[512,512]{1,0:T(8,128)S(1)} %fusion.3, bf16[512,2560]{1,0:T(8,128)(2,1)S(1)} %convolution_convert_fusion, f32[512,2560]{1,0:T(8,128)S(1)} %fusion), kind=kOutput, calls=%fused_computation.13 | convolution fusion | flops 1345060864 | bytes 9961472 | tf_op jit(solution)/shard_map/dot_general | solution.py:67
  27.6 3.3 %convolution_subtract_fusion = f32[512,512]{1,0:T(8,128)} fusion(f32[512,512]{1,0:T(8,128)} %fusion.7, bf16[1,1,512,512]{3,2,1,0:T(8,128)(2,1)} %param.15, s32[512]{0:T(512)S(1)} %fusion.61), kind=kOutput, calls=%fused_computation.12 | convolution fusion | flops 537919488 | bytes 2623488 | tf_op jit(solution)/shard_map/dot_general | solution.py:60
  34.7 3.0 %collective-permute-start.5 = (bf16[64,128]{1,0:T(8,128)(2,1)S(1)}, bf16[64,128]{1,0:T(8,128)(2,1)S(1)}, u32[]{:S(2)}, u32[]{:S(2)}) collective-permute-start(bf16[64,128]{1,0:T(8,128)(2,1)S(1)} %bitcast_convert_fusion.2), channel_id=1, source_target_pairs={{0,18},{1,19},{2,16},{3,17},{16,2},{17,3},{18,0},{19,1},{4,22},{5,... | collective-permute-start | bytes 49160 | tf_op jit(solution)/shard_map/ppermute | solution.py:37
  38.9 2.0 %collective-permute-start.6 = (bf16[64,128]{1,0:T(8,128)(2,1)S(1)}, bf16[64,128]{1,0:T(8,128)(2,1)S(1)}, u32[]{:S(2)}, u32[]{:S(2)}) collective-permute-start(bf16[64,128]{1,0:T(8,128)(2,1)S(1)} %bitcast_convert_fusion.2), channel_id=1, source_target_pairs={{0,19},{1,16},{2,17},{3,18},{16,3},{17,0},{18,1},{19,2},{4,23},{5,... | collective-permute-start | bytes 49160 | tf_op jit(solution)/shard_map/ppermute | solution.py:37
  40.9 1.9 %collective-permute-done.6 = bf16[64,128]{1,0:T(8,128)(2,1)S(1)} collective-permute-done((bf16[64,128]{1,0:T(8,128)(2,1)S(1)}, bf16[64,128]{1,0:T(8,128)(2,1)S(1)}, u32[]{:S(2)}, u32[]{:S(2)}) %collective-permute-start.6) | collective-permute-done | bytes 16416 | tf_op jit(solution)/shard_map/ppermute | solution.py:37
  48.3 4.6 %all-to-all-start = ((f32[8,64,512]{2,1,0:T(8,128)}), f32[8,64,512]{2,1,0:T(8,128)}, u32[]{:S(2)}, u32[]{:S(2)}) async-start(f32[8,64,512]{2,1,0:T(8,128)} %bitcast.247), calls=%async_computation | async-start | bytes 2097152 | tf_op jit(solution)/shard_map/all_to_all | solution.py:138
  53.3 22.9 %all-to-all-done = f32[8,64,512]{2,1,0:T(8,128)} async-done(((f32[8,64,512]{2,1,0:T(8,128)}), f32[8,64,512]{2,1,0:T(8,128)}, u32[]{:S(2)}, u32[]{:S(2)}) %all-to-all-start) | async-done | bytes 1048608 | tf_op jit(solution)/shard_map/all_to_all | solution.py:138
  76.1 1.3 reduce_sum.9
  78.6 5.8 %collective-permute-start.10 = (f32[64,128]{1,0:T(8,128)S(1)}, f32[64,128]{1,0:T(8,128)S(1)}, u32[]{:S(2)}, u32[]{:S(2)}) collective-permute-start(f32[64,128]{1,0:T(8,128)S(1)} %sub.86), channel_id=1, source_target_pairs={{0,4},{4,8},{8,12},{12,0},{1,5},{5,9},{9,13},{13,1},{2,6},{6,10},{... | collective-permute-start | bytes 98312 | tf_op jit(solution)/shard_map/ppermute | solution.py:20
  85.4 1.7 %collective-permute-done.11 = f32[64,128]{1,0:T(8,128)S(1)} collective-permute-done((f32[64,128]{1,0:T(8,128)S(1)}, f32[64,128]{1,0:T(8,128)S(1)}, u32[]{:S(2)}, u32[]{:S(2)}) %collective-permute-start.11) | collective-permute-done | bytes 32800 | tf_op jit(solution)/shard_map/ppermute | solution.py:20
  88.3 3.2 %collective-permute-start.15 = (bf16[64,128]{1,0:T(8,128)(2,1)S(1)}, bf16[64,128]{1,0:T(8,128)(2,1)S(1)}, u32[]{:S(2)}, u32[]{:S(2)}) collective-permute-start(bf16[64,128]{1,0:T(8,128)(2,1)S(1)} %get-tuple-element.21), channel_id=1, source_target_pairs={{0,3},{1,0},{2,1},{3,2},{16,19},{17,16},{18,17},{19,18},{4,7},{5,4... | collective-permute-start | bytes 49160 | tf_op jit(solution)/shard_map/ppermute | solution.py:37
  94.8 3.3 %collective-permute-start.19 = (bf16[64,128]{1,0:T(8,128)(2,1)S(1)}, bf16[64,128]{1,0:T(8,128)(2,1)S(1)}, u32[]{:S(2)}, u32[]{:S(2)}) collective-permute-start(bf16[64,128]{1,0:T(8,128)(2,1)S(1)} %get-tuple-element.21), channel_id=1, source_target_pairs={{0,19},{1,16},{2,17},{3,18},{16,3},{17,0},{18,1},{19,2},{4,23},{5,... | collective-permute-start | bytes 49160 | tf_op jit(solution)/shard_map/ppermute | solution.py:37
  99.3 3.1 %collective-permute-start.20 = (f32[64,128]{1,0:T(8,128)S(1)}, f32[64,128]{1,0:T(8,128)S(1)}, u32[]{:S(2)}, u32[]{:S(2)}) collective-permute-start(f32[64,128]{1,0:T(8,128)S(1)} %fusion.14), channel_id=1, source_target_pairs={{0,4},{4,8},{8,12},{12,0},{1,5},{5,9},{9,13},{13,1},{2,6},{6,10},{... | collective-permute-start | bytes 98312 | tf_op jit(solution)/shard_map/ppermute | solution.py:20
  103.4 2.3 %collective-permute-done.21 = f32[64,128]{1,0:T(8,128)S(1)} collective-permute-done((f32[64,128]{1,0:T(8,128)S(1)}, f32[64,128]{1,0:T(8,128)S(1)}, u32[]{:S(2)}, u32[]{:S(2)}) %collective-permute-start.21) | collective-permute-done | bytes 32800 | tf_op jit(solution)/shard_map/ppermute | solution.py:20
  106.7 1.7 %collective-permute-start.23 = (bf16[64,128]{1,0:T(8,128)(2,1)S(1)}, bf16[64,128]{1,0:T(8,128)(2,1)S(1)}, u32[]{:S(2)}, u32[]{:S(2)}) collective-permute-start(bf16[64,128]{1,0:T(8,128)(2,1)S(1)} %get-tuple-element.19), channel_id=1, source_target_pairs={{0,1},{1,2},{2,3},{3,0},{16,17},{17,18},{18,19},{19,16},{4,5},{5,6... | collective-permute-start | bytes 49160 | tf_op jit(solution)/shard_map/ppermute | solution.py:37
  108.4 2.6 %collective-permute-start.24 = (bf16[64,128]{1,0:T(8,128)(2,1)S(1)}, bf16[64,128]{1,0:T(8,128)(2,1)S(1)}, u32[]{:S(2)}, u32[]{:S(2)}) collective-permute-start(bf16[64,128]{1,0:T(8,128)(2,1)S(1)} %get-tuple-element.19), channel_id=1, source_target_pairs={{0,2},{1,3},{2,0},{3,1},{16,18},{17,19},{18,16},{19,17},{4,6},{5,7... | collective-permute-start | bytes 49160 | tf_op jit(solution)/shard_map/ppermute | solution.py:37
  112.2 1.5 %collective-permute-start.27 = (bf16[64,128]{1,0:T(8,128)(2,1)S(1)}, bf16[64,128]{1,0:T(8,128)(2,1)S(1)}, u32[]{:S(2)}, u32[]{:S(2)}) collective-permute-start(bf16[64,128]{1,0:T(8,128)(2,1)S(1)} %get-tuple-element.19), channel_id=1, source_target_pairs={{0,17},{1,18},{2,19},{3,16},{16,1},{17,2},{18,3},{19,0},{4,21},{5,... | collective-permute-start | bytes 49160 | tf_op jit(solution)/shard_map/ppermute | solution.py:37
  115.3 2.2 %collective-permute-start.29 = (bf16[64,128]{1,0:T(8,128)(2,1)S(1)}, bf16[64,128]{1,0:T(8,128)(2,1)S(1)}, u32[]{:S(2)}, u32[]{:S(2)}) collective-permute-start(bf16[64,128]{1,0:T(8,128)(2,1)S(1)} %get-tuple-element.19), channel_id=1, source_target_pairs={{0,19},{1,16},{2,17},{3,18},{16,3},{17,0},{18,1},{19,2},{4,23},{5,... | collective-permute-start | bytes 49160 | tf_op jit(solution)/shard_map/ppermute | solution.py:37
  117.6 1.4 collective-permute-done.28
  119.3 2.7 %collective-permute-start.30 = (f32[64,128]{1,0:T(8,128)S(1)}, f32[64,128]{1,0:T(8,128)S(1)}, u32[]{:S(2)}, u32[]{:S(2)}) collective-permute-start(f32[64,128]{1,0:T(8,128)S(1)} %fusion.11), channel_id=1, source_target_pairs={{0,4},{4,8},{8,12},{12,0},{1,5},{5,9},{9,13},{13,1},{2,6},{6,10},{... | collective-permute-start | bytes 98312 | tf_op jit(solution)/shard_map/ppermute | solution.py:20
  123.1 2.2 %collective-permute-done.31 = f32[64,128]{1,0:T(8,128)S(1)} collective-permute-done((f32[64,128]{1,0:T(8,128)S(1)}, f32[64,128]{1,0:T(8,128)S(1)}, u32[]{:S(2)}, u32[]{:S(2)}) %collective-permute-start.31) | collective-permute-done | bytes 32800 | tf_op jit(solution)/shard_map/ppermute | solution.py:20
  126.4 2.0 %collective-permute-start.33 = (bf16[64,128]{1,0:T(8,128)(2,1)S(1)}, bf16[64,128]{1,0:T(8,128)(2,1)S(1)}, u32[]{:S(2)}, u32[]{:S(2)}) collective-permute-start(bf16[64,128]{1,0:T(8,128)(2,1)S(1)} %get-tuple-element.17), channel_id=1, source_target_pairs={{0,1},{1,2},{2,3},{3,0},{16,17},{17,18},{18,19},{19,16},{4,5},{5,6... | collective-permute-start | bytes 49160 | tf_op jit(solution)/shard_map/ppermute | solution.py:37
  128.4 2.2 %collective-permute-start.34 = (bf16[64,128]{1,0:T(8,128)(2,1)S(1)}, bf16[64,128]{1,0:T(8,128)(2,1)S(1)}, u32[]{:S(2)}, u32[]{:S(2)}) collective-permute-start(bf16[64,128]{1,0:T(8,128)(2,1)S(1)} %get-tuple-element.17), channel_id=1, source_target_pairs={{0,2},{1,3},{2,0},{3,1},{16,18},{17,19},{18,16},{19,17},{4,6},{5,7... | collective-permute-start | bytes 49160 | tf_op jit(solution)/shard_map/ppermute | solution.py:37
  131.6 1.6 %collective-permute-start.37 = (bf16[64,128]{1,0:T(8,128)(2,1)S(1)}, bf16[64,128]{1,0:T(8,128)(2,1)S(1)}, u32[]{:S(2)}, u32[]{:S(2)}) collective-permute-start(bf16[64,128]{1,0:T(8,128)(2,1)S(1)} %get-tuple-element.17), channel_id=1, source_target_pairs={{0,17},{1,18},{2,19},{3,16},{16,1},{17,2},{18,3},{19,0},{4,21},{5,... | collective-permute-start | bytes 49160 | tf_op jit(solution)/shard_map/ppermute | solution.py:37
  134.1 2.9 %collective-permute-start.39 = (bf16[64,128]{1,0:T(8,128)(2,1)S(1)}, bf16[64,128]{1,0:T(8,128)(2,1)S(1)}, u32[]{:S(2)}, u32[]{:S(2)}) collective-permute-start(bf16[64,128]{1,0:T(8,128)(2,1)S(1)} %get-tuple-element.17), channel_id=1, source_target_pairs={{0,19},{1,16},{2,17},{3,18},{16,3},{17,0},{18,1},{19,2},{4,23},{5,... | collective-permute-start | bytes 49160 | tf_op jit(solution)/shard_map/ppermute | solution.py:37
  139.1 2.6 %collective-permute-start.40 = (f32[64,128]{1,0:T(8,128)S(1)}, f32[64,128]{1,0:T(8,128)S(1)}, u32[]{:S(2)}, u32[]{:S(2)}) collective-permute-start(f32[64,128]{1,0:T(8,128)S(1)} %fusion.8), channel_id=1, source_target_pairs={{0,4},{4,8},{8,12},{12,0},{1,5},{5,9},{9,13},{13,1},{2,6},{6,10},{... | collective-permute-start | bytes 98312 | tf_op jit(solution)/shard_map/ppermute | solution.py:20
  142.7 2.2 %collective-permute-done.41 = f32[64,128]{1,0:T(8,128)S(1)} collective-permute-done((f32[64,128]{1,0:T(8,128)S(1)}, f32[64,128]{1,0:T(8,128)S(1)}, u32[]{:S(2)}, u32[]{:S(2)}) %collective-permute-start.41) | collective-permute-done | bytes 32800 | tf_op jit(solution)/shard_map/ppermute | solution.py:20
  (167 shorter events, 39.2 us)
Async XLA Ops:
  1.7 41.2 %collective-permute-start.7 = (f32[64,256]{1,0:T(8,128)S(1)}, f32[64,256]{1,0:T(8,128)S(1)}, u32[]{:S(2)}, u32[]{:S(2)}) collective-permute-start(f32[64,256]{1,0:T(8,128)S(1)} %pad_maximum_fusion.11), channel_id=1, source_target_pairs={{0,4},{4,8},{8,12},{12,0},{1,5},{5,9},{9,13},{13,1},{2,6},{6,10},{... | collective-permute-start | bytes 196616 | tf_op jit(solution)/shard_map/ppermute | solution.py:20
  4.4 38.5 %collective-permute-start.8 = (f32[64,256]{1,0:T(8,128)S(1)}, f32[64,256]{1,0:T(8,128)S(1)}, u32[]{:S(2)}, u32[]{:S(2)}) collective-permute-start(f32[64,256]{1,0:T(8,128)S(1)} %pad_maximum_fusion.11), channel_id=1, source_target_pairs={{0,8},{4,12},{8,0},{12,4},{1,9},{5,13},{9,1},{13,5},{2,10},{6,14},... | collective-permute-start | bytes 196616 | tf_op jit(solution)/shard_map/ppermute | solution.py:20
  4.4 38.5 %collective-permute-start.9 = (f32[64,256]{1,0:T(8,128)S(1)}, f32[64,256]{1,0:T(8,128)S(1)}, u32[]{:S(2)}, u32[]{:S(2)}) collective-permute-start(f32[64,256]{1,0:T(8,128)S(1)} %pad_maximum_fusion.11), channel_id=1, source_target_pairs={{0,12},{4,0},{8,4},{12,8},{1,13},{5,1},{9,5},{13,9},{2,14},{6,2},{... | collective-permute-start | bytes 196616 | tf_op jit(solution)/shard_map/ppermute | solution.py:20
  5.6 25.5 %collective-permute-start = (bf16[64,128]{1,0:T(8,128)(2,1)S(1)}, bf16[64,128]{1,0:T(8,128)(2,1)S(1)}, u32[]{:S(2)}, u32[]{:S(2)}) collective-permute-start(bf16[64,128]{1,0:T(8,128)(2,1)S(1)} %bitcast_convert_fusion.2), channel_id=1, source_target_pairs={{0,1},{1,2},{2,3},{3,0},{16,17},{17,18},{18,19},{19,16},{4,5},{5,6... | collective-permute-start | bytes 49160 | tf_op jit(solution)/shard_map/ppermute | solution.py:37
  6.9 25.2 %collective-permute-start.1 = (bf16[64,128]{1,0:T(8,128)(2,1)S(1)}, bf16[64,128]{1,0:T(8,128)(2,1)S(1)}, u32[]{:S(2)}, u32[]{:S(2)}) collective-permute-start(bf16[64,128]{1,0:T(8,128)(2,1)S(1)} %bitcast_convert_fusion.2), channel_id=1, source_target_pairs={{0,2},{1,3},{2,0},{3,1},{16,18},{17,19},{18,16},{19,17},{4,6},{5,7... | collective-permute-start | bytes 49160 | tf_op jit(solution)/shard_map/ppermute | solution.py:37
  33.6 5.3 %collective-permute-start.4 = (bf16[64,128]{1,0:T(8,128)(2,1)S(1)}, bf16[64,128]{1,0:T(8,128)(2,1)S(1)}, u32[]{:S(2)}, u32[]{:S(2)}) collective-permute-start(bf16[64,128]{1,0:T(8,128)(2,1)S(1)} %bitcast_convert_fusion.2), channel_id=1, source_target_pairs={{0,17},{1,18},{2,19},{3,16},{16,1},{17,2},{18,3},{19,0},{4,21},{5,... | collective-permute-start | bytes 49160 | tf_op jit(solution)/shard_map/ppermute | solution.py:37
  34.7 6.2 %collective-permute-start.5 = (bf16[64,128]{1,0:T(8,128)(2,1)S(1)}, bf16[64,128]{1,0:T(8,128)(2,1)S(1)}, u32[]{:S(2)}, u32[]{:S(2)}) collective-permute-start(bf16[64,128]{1,0:T(8,128)(2,1)S(1)} %bitcast_convert_fusion.2), channel_id=1, source_target_pairs={{0,18},{1,19},{2,16},{3,17},{16,2},{17,3},{18,0},{19,1},{4,22},{5,... | collective-permute-start | bytes 49160 | tf_op jit(solution)/shard_map/ppermute | solution.py:37
  38.9 4.0 %collective-permute-start.6 = (bf16[64,128]{1,0:T(8,128)(2,1)S(1)}, bf16[64,128]{1,0:T(8,128)(2,1)S(1)}, u32[]{:S(2)}, u32[]{:S(2)}) collective-permute-start(bf16[64,128]{1,0:T(8,128)(2,1)S(1)} %bitcast_convert_fusion.2), channel_id=1, source_target_pairs={{0,19},{1,16},{2,17},{3,18},{16,3},{17,0},{18,1},{19,2},{4,23},{5,... | collective-permute-start | bytes 49160 | tf_op jit(solution)/shard_map/ppermute | solution.py:37
  48.3 27.8 %all-to-all-start = ((f32[8,64,512]{2,1,0:T(8,128)}), f32[8,64,512]{2,1,0:T(8,128)}, u32[]{:S(2)}, u32[]{:S(2)}) async-start(f32[8,64,512]{2,1,0:T(8,128)} %bitcast.247), calls=%async_computation | async-start | bytes 2097152 | tf_op jit(solution)/shard_map/all_to_all | solution.py:138
  78.6 6.8 %collective-permute-start.10 = (f32[64,128]{1,0:T(8,128)S(1)}, f32[64,128]{1,0:T(8,128)S(1)}, u32[]{:S(2)}, u32[]{:S(2)}) collective-permute-start(f32[64,128]{1,0:T(8,128)S(1)} %sub.86), channel_id=1, source_target_pairs={{0,4},{4,8},{8,12},{12,0},{1,5},{5,9},{9,13},{13,1},{2,6},{6,10},{... | collective-permute-start | bytes 98312 | tf_op jit(solution)/shard_map/ppermute | solution.py:20
  88.1 5.4 %collective-permute-start.13 = (bf16[64,128]{1,0:T(8,128)(2,1)S(1)}, bf16[64,128]{1,0:T(8,128)(2,1)S(1)}, u32[]{:S(2)}, u32[]{:S(2)}) collective-permute-start(bf16[64,128]{1,0:T(8,128)(2,1)S(1)} %get-tuple-element.21), channel_id=1, source_target_pairs={{0,1},{1,2},{2,3},{3,0},{16,17},{17,18},{18,19},{19,16},{4,5},{5,6... | collective-permute-start | bytes 49160 | tf_op jit(solution)/shard_map/ppermute | solution.py:37
  88.2 6.6 %collective-permute-start.14 = (bf16[64,128]{1,0:T(8,128)(2,1)S(1)}, bf16[64,128]{1,0:T(8,128)(2,1)S(1)}, u32[]{:S(2)}, u32[]{:S(2)}) collective-permute-start(bf16[64,128]{1,0:T(8,128)(2,1)S(1)} %get-tuple-element.21), channel_id=1, source_target_pairs={{0,2},{1,3},{2,0},{3,1},{16,18},{17,19},{18,16},{19,17},{4,6},{5,7... | collective-permute-start | bytes 49160 | tf_op jit(solution)/shard_map/ppermute | solution.py:37
  88.3 9.8 %collective-permute-start.15 = (bf16[64,128]{1,0:T(8,128)(2,1)S(1)}, bf16[64,128]{1,0:T(8,128)(2,1)S(1)}, u32[]{:S(2)}, u32[]{:S(2)}) collective-permute-start(bf16[64,128]{1,0:T(8,128)(2,1)S(1)} %get-tuple-element.21), channel_id=1, source_target_pairs={{0,3},{1,0},{2,1},{3,2},{16,19},{17,16},{18,17},{19,18},{4,7},{5,4... | collective-permute-start | bytes 49160 | tf_op jit(solution)/shard_map/ppermute | solution.py:37
  91.5 6.6 %collective-permute-start.16 = (bf16[64,128]{1,0:T(8,128)(2,1)S(1)}, bf16[64,128]{1,0:T(8,128)(2,1)S(1)}, u32[]{:S(2)}, u32[]{:S(2)}) collective-permute-start(bf16[64,128]{1,0:T(8,128)(2,1)S(1)} %get-tuple-element.21), channel_id=1, source_target_pairs={{0,16},{1,17},{2,18},{3,19},{16,0},{17,1},{18,2},{19,3},{4,20},{5,... | collective-permute-start | bytes 49160 | tf_op jit(solution)/shard_map/ppermute | solution.py:37
  92.0 6.1 %collective-permute-start.17 = (bf16[64,128]{1,0:T(8,128)(2,1)S(1)}, bf16[64,128]{1,0:T(8,128)(2,1)S(1)}, u32[]{:S(2)}, u32[]{:S(2)}) collective-permute-start(bf16[64,128]{1,0:T(8,128)(2,1)S(1)} %get-tuple-element.21), channel_id=1, source_target_pairs={{0,17},{1,18},{2,19},{3,16},{16,1},{17,2},{18,3},{19,0},{4,21},{5,... | collective-permute-start | bytes 49160 | tf_op jit(solution)/shard_map/ppermute | solution.py:37
  93.6 4.7 %collective-permute-start.18 = (bf16[64,128]{1,0:T(8,128)(2,1)S(1)}, bf16[64,128]{1,0:T(8,128)(2,1)S(1)}, u32[]{:S(2)}, u32[]{:S(2)}) collective-permute-start(bf16[64,128]{1,0:T(8,128)(2,1)S(1)} %get-tuple-element.21), channel_id=1, source_target_pairs={{0,18},{1,19},{2,16},{3,17},{16,2},{17,3},{18,0},{19,1},{4,22},{5,... | collective-permute-start | bytes 49160 | tf_op jit(solution)/shard_map/ppermute | solution.py:37
  94.8 4.1 %collective-permute-start.19 = (bf16[64,128]{1,0:T(8,128)(2,1)S(1)}, bf16[64,128]{1,0:T(8,128)(2,1)S(1)}, u32[]{:S(2)}, u32[]{:S(2)}) collective-permute-start(bf16[64,128]{1,0:T(8,128)(2,1)S(1)} %get-tuple-element.21), channel_id=1, source_target_pairs={{0,19},{1,16},{2,17},{3,18},{16,3},{17,0},{18,1},{19,2},{4,23},{5,... | collective-permute-start | bytes 49160 | tf_op jit(solution)/shard_map/ppermute | solution.py:37
  99.3 4.1 %collective-permute-start.20 = (f32[64,128]{1,0:T(8,128)S(1)}, f32[64,128]{1,0:T(8,128)S(1)}, u32[]{:S(2)}, u32[]{:S(2)}) collective-permute-start(f32[64,128]{1,0:T(8,128)S(1)} %fusion.14), channel_id=1, source_target_pairs={{0,4},{4,8},{8,12},{12,0},{1,5},{5,9},{9,13},{13,1},{2,6},{6,10},{... | collective-permute-start | bytes 98312 | tf_op jit(solution)/shard_map/ppermute | solution.py:20
  106.7 7.6 %collective-permute-start.23 = (bf16[64,128]{1,0:T(8,128)(2,1)S(1)}, bf16[64,128]{1,0:T(8,128)(2,1)S(1)}, u32[]{:S(2)}, u32[]{:S(2)}) collective-permute-start(bf16[64,128]{1,0:T(8,128)(2,1)S(1)} %get-tuple-element.19), channel_id=1, source_target_pairs={{0,1},{1,2},{2,3},{3,0},{16,17},{17,18},{18,19},{19,16},{4,5},{5,6... | collective-permute-start | bytes 49160 | tf_op jit(solution)/shard_map/ppermute | solution.py:37
  108.4 6.9 %collective-permute-start.24 = (bf16[64,128]{1,0:T(8,128)(2,1)S(1)}, bf16[64,128]{1,0:T(8,128)(2,1)S(1)}, u32[]{:S(2)}, u32[]{:S(2)}) collective-permute-start(bf16[64,128]{1,0:T(8,128)(2,1)S(1)} %get-tuple-element.19), channel_id=1, source_target_pairs={{0,2},{1,3},{2,0},{3,1},{16,18},{17,19},{18,16},{19,17},{4,6},{5,7... | collective-permute-start | bytes 49160 | tf_op jit(solution)/shard_map/ppermute | solution.py:37
  111.1 6.4 %collective-permute-start.25 = (bf16[64,128]{1,0:T(8,128)(2,1)S(1)}, bf16[64,128]{1,0:T(8,128)(2,1)S(1)}, u32[]{:S(2)}, u32[]{:S(2)}) collective-permute-start(bf16[64,128]{1,0:T(8,128)(2,1)S(1)} %get-tuple-element.19), channel_id=1, source_target_pairs={{0,3},{1,0},{2,1},{3,2},{16,19},{17,16},{18,17},{19,18},{4,7},{5,4... | collective-permute-start | bytes 49160 | tf_op jit(solution)/shard_map/ppermute | solution.py:37
  111.1 6.4 %collective-permute-start.26 = (bf16[64,128]{1,0:T(8,128)(2,1)S(1)}, bf16[64,128]{1,0:T(8,128)(2,1)S(1)}, u32[]{:S(2)}, u32[]{:S(2)}) collective-permute-start(bf16[64,128]{1,0:T(8,128)(2,1)S(1)} %get-tuple-element.19), channel_id=1, source_target_pairs={{0,16},{1,17},{2,18},{3,19},{16,0},{17,1},{18,2},{19,3},{4,20},{5,... | collective-permute-start | bytes 49160 | tf_op jit(solution)/shard_map/ppermute | solution.py:37
  112.2 5.3 %collective-permute-start.27 = (bf16[64,128]{1,0:T(8,128)(2,1)S(1)}, bf16[64,128]{1,0:T(8,128)(2,1)S(1)}, u32[]{:S(2)}, u32[]{:S(2)}) collective-permute-start(bf16[64,128]{1,0:T(8,128)(2,1)S(1)} %get-tuple-element.19), channel_id=1, source_target_pairs={{0,17},{1,18},{2,19},{3,16},{16,1},{17,2},{18,3},{19,0},{4,21},{5,... | collective-permute-start | bytes 49160 | tf_op jit(solution)/shard_map/ppermute | solution.py:37
  114.4 4.6 %collective-permute-start.28 = (bf16[64,128]{1,0:T(8,128)(2,1)S(1)}, bf16[64,128]{1,0:T(8,128)(2,1)S(1)}, u32[]{:S(2)}, u32[]{:S(2)}) collective-permute-start(bf16[64,128]{1,0:T(8,128)(2,1)S(1)} %get-tuple-element.19), channel_id=1, source_target_pairs={{0,18},{1,19},{2,16},{3,17},{16,2},{17,3},{18,0},{19,1},{4,22},{5,... | collective-permute-start | bytes 49160 | tf_op jit(solution)/shard_map/ppermute | solution.py:37
  119.3 3.8 %collective-permute-start.30 = (f32[64,128]{1,0:T(8,128)S(1)}, f32[64,128]{1,0:T(8,128)S(1)}, u32[]{:S(2)}, u32[]{:S(2)}) collective-permute-start(f32[64,128]{1,0:T(8,128)S(1)} %fusion.11), channel_id=1, source_target_pairs={{0,4},{4,8},{8,12},{12,0},{1,5},{5,9},{9,13},{13,1},{2,6},{6,10},{... | collective-permute-start | bytes 98312 | tf_op jit(solution)/shard_map/ppermute | solution.py:20
  126.4 7.4 %collective-permute-start.33 = (bf16[64,128]{1,0:T(8,128)(2,1)S(1)}, bf16[64,128]{1,0:T(8,128)(2,1)S(1)}, u32[]{:S(2)}, u32[]{:S(2)}) collective-permute-start(bf16[64,128]{1,0:T(8,128)(2,1)S(1)} %get-tuple-element.17), channel_id=1, source_target_pairs={{0,1},{1,2},{2,3},{3,0},{16,17},{17,18},{18,19},{19,16},{4,5},{5,6... | collective-permute-start | bytes 49160 | tf_op jit(solution)/shard_map/ppermute | solution.py:37
  128.4 5.7 %collective-permute-start.34 = (bf16[64,128]{1,0:T(8,128)(2,1)S(1)}, bf16[64,128]{1,0:T(8,128)(2,1)S(1)}, u32[]{:S(2)}, u32[]{:S(2)}) collective-permute-start(bf16[64,128]{1,0:T(8,128)(2,1)S(1)} %get-tuple-element.17), channel_id=1, source_target_pairs={{0,2},{1,3},{2,0},{3,1},{16,18},{17,19},{18,16},{19,17},{4,6},{5,7... | collective-permute-start | bytes 49160 | tf_op jit(solution)/shard_map/ppermute | solution.py:37
  130.5 6.4 %collective-permute-start.35 = (bf16[64,128]{1,0:T(8,128)(2,1)S(1)}, bf16[64,128]{1,0:T(8,128)(2,1)S(1)}, u32[]{:S(2)}, u32[]{:S(2)}) collective-permute-start(bf16[64,128]{1,0:T(8,128)(2,1)S(1)} %get-tuple-element.17), channel_id=1, source_target_pairs={{0,3},{1,0},{2,1},{3,2},{16,19},{17,16},{18,17},{19,18},{4,7},{5,4... | collective-permute-start | bytes 49160 | tf_op jit(solution)/shard_map/ppermute | solution.py:37
  131.3 5.7 %collective-permute-start.36 = (bf16[64,128]{1,0:T(8,128)(2,1)S(1)}, bf16[64,128]{1,0:T(8,128)(2,1)S(1)}, u32[]{:S(2)}, u32[]{:S(2)}) collective-permute-start(bf16[64,128]{1,0:T(8,128)(2,1)S(1)} %get-tuple-element.17), channel_id=1, source_target_pairs={{0,16},{1,17},{2,18},{3,19},{16,0},{17,1},{18,2},{19,3},{4,20},{5,... | collective-permute-start | bytes 49160 | tf_op jit(solution)/shard_map/ppermute | solution.py:37
  131.6 5.4 %collective-permute-start.37 = (bf16[64,128]{1,0:T(8,128)(2,1)S(1)}, bf16[64,128]{1,0:T(8,128)(2,1)S(1)}, u32[]{:S(2)}, u32[]{:S(2)}) collective-permute-start(bf16[64,128]{1,0:T(8,128)(2,1)S(1)} %get-tuple-element.17), channel_id=1, source_target_pairs={{0,17},{1,18},{2,19},{3,16},{16,1},{17,2},{18,3},{19,0},{4,21},{5,... | collective-permute-start | bytes 49160 | tf_op jit(solution)/shard_map/ppermute | solution.py:37
  133.8 4.5 %collective-permute-start.38 = (bf16[64,128]{1,0:T(8,128)(2,1)S(1)}, bf16[64,128]{1,0:T(8,128)(2,1)S(1)}, u32[]{:S(2)}, u32[]{:S(2)}) collective-permute-start(bf16[64,128]{1,0:T(8,128)(2,1)S(1)} %get-tuple-element.17), channel_id=1, source_target_pairs={{0,18},{1,19},{2,16},{3,17},{16,2},{17,3},{18,0},{19,1},{4,22},{5,... | collective-permute-start | bytes 49160 | tf_op jit(solution)/shard_map/ppermute | solution.py:37
  134.1 4.7 %collective-permute-start.39 = (bf16[64,128]{1,0:T(8,128)(2,1)S(1)}, bf16[64,128]{1,0:T(8,128)(2,1)S(1)}, u32[]{:S(2)}, u32[]{:S(2)}) collective-permute-start(bf16[64,128]{1,0:T(8,128)(2,1)S(1)} %get-tuple-element.17), channel_id=1, source_target_pairs={{0,19},{1,16},{2,17},{3,18},{16,3},{17,0},{18,1},{19,2},{4,23},{5,... | collective-permute-start | bytes 49160 | tf_op jit(solution)/shard_map/ppermute | solution.py:37
  (16 other events, 62.8 us)

commit v13 on v9

--- a/solution.py
+++ b/solution.py
@@ -32,6 +32,23 @@
     sub_back = (lax.axis_index("sub") - jnp.arange(subs)[:, None]) % subs
     iface_back = (lax.axis_index("iface") - jnp.arange(ifaces)[None, :]) % ifaces
     return (sub_back * ifaces + iface_back).reshape(-1)
+
+
+def scatter_owners(terms):
+    subs, ifaces = lax.axis_size("sub"), lax.axis_size("iface")
+    sub_pos, iface_pos = lax.axis_index("sub"), lax.axis_index("iface")
+    terms = terms.reshape((subs, ifaces) + terms.shape[1:])
+    inner = lax.dynamic_index_in_dim(terms, iface_pos, axis=1, keepdims=False)
+    for distance in range(1, ifaces):
+        route = [(i, (i + distance) % ifaces) for i in range(ifaces)]
+        chunk = lax.dynamic_index_in_dim(terms, (iface_pos + distance) % ifaces, axis=1, keepdims=False)
+        inner = inner + lax.ppermute(chunk, "iface", route)
+    total = lax.dynamic_index_in_dim(inner, sub_pos, axis=0, keepdims=False)
+    for distance in range(1, subs):
+        route = [(i, (i + distance) % subs) for i in range(subs)]
+        chunk = lax.dynamic_index_in_dim(inner, (sub_pos + distance) % subs, axis=0, keepdims=False)
+        total = total + lax.ppermute(chunk, "sub", route)
+    return total
 
 
 def schur_rows(block_list, boundary, coupled, inverse, owners):
@@ -124,7 +141,7 @@
     first_rounded, weights_mine, weights_above, known, spread = lax.optimization_barrier(
         (first_rounded, weights_mine, weights_above, known, spread)
     )
-    rows = jnp.sum(lax.all_to_all(spread, OWNERS, 0, 0, tiled=True), axis=0)
+    rows = scatter_owners(spread)
     rows_hi, rows_lo = split_bf16(jnp.dot(precond_mine, rows, precision=lax.Precision.HIGHEST))
     node = jnp.arange(nodes, dtype=jnp.int32)
     source = jnp.repeat(ring_owner_order(), block_nodes) * block_nodes + node % block_nodes

time: 133 us -> 136 us (1.023)
  starting transfers between devices: 38.8 us -> 48.3 us
  waiting for transfers between devices: 52.6 us -> 43.1 us
  local copies, waits for them, and re-layouts: 3.79 us -> 5.81 us
    all_to_all x1 -> x0, waiting for transfers between devices: 26.3 us -> none  [body(): rows = jnp.sum(lax.all_to_all(spread, OWNERS, 0, 0, tiled=True), axis=0)]
    ppermute x0 -> x4, waiting for transfers between devices: none -> 19.1 us  [the longest x3 16.4 us: scatter_owners(): inner = inner + lax.ppermute(chunk, 'iface', route)]
    ppermute x31, starting transfers between devices: 34.5 us -> 43.8 us  [ring_parts(): parts.append(lax.ppermute(block, axis, route))]
    ppermute x0 -> x4, starting transfers between devices: none -> 4.52 us  [the longest x3 3.28 us: scatter_owners(): inner = inner + lax.ppermute(chunk, 'iface', route)]
    all_to_all x1 -> x0, starting transfers between devices: 4.25 us -> none  [body(): rows = jnp.sum(lax.all_to_all(spread, OWNERS, 0, 0, tiled=True), axis=0)]
    ppermute x31, waiting for transfers between devices: 26.3 us -> 24 us  [ring_parts(): parts.append(lax.ppermute(block, axis, route))]
    squeeze x0 -> x2, local copies, waits for them, and re-layouts: none -> 2.03 us  [the longest x1 2.01 us: scatter_owners(): lax.dynamic_index_in_dim(terms, (iface_pos + distance) % ifaces, axis=1,...]
  transfers between devices with their start and end apart: 32 -> 35, of which waited for: 23 -> 24; matrix products, arithmetic and copies ran while one was open for 25% -> 25% of each run, Pallas kernels for 0% -> 0%
where the time goes in v13:
time: 136 us; the launch traced here: 135 us
  starting transfers between devices  48.3 us (36%)
  waiting for transfers between devices  43.1 us (32%)
  matrix products  27.1 us (20%)
  other arithmetic  10.5 us (8%)
  local copies, waits for them, and re-layouts  5.81 us (4%)
    ppermute x31, starting transfers between devices, ring_parts(): parts.append(lax.ppermute(block, axis, route))  43.8 us
    ppermute x31, waiting for transfers between devices, ring_parts(): parts.append(lax.ppermute(block, axis, route))  24 us
    ppermute x3, waiting for transfers between devices, scatter_owners(): inner = inner + lax.ppermute(chunk, 'iface', route)  16.4 us
    dot_general x1, matrix products, schur_rows(): solved = jnp.dot(inverse, coupled, preferred_element_type=jnp.float32)  10 us
    dot_general x1, matrix products, moved(): jnp.dot(rows.astype(jnp.bfloat16), place, preferred_element_type=jnp.floa...  3.37 us
    ppermute x3, starting transfers between devices, scatter_owners(): inner = inner + lax.ppermute(chunk, 'iface', route)  3.28 us
  transfers between devices with their start and end apart: 35, of which 24 were waited for; matrix products, arithmetic and copies ran while one was open for 25% of the time, Pallas kernels for 0%

profile of v13, /device:TPU:1, one launch (start us, length us, event | category | flops | bytes accessed | tf_op | source)
XLA Modules:
  0.0 135.3 jit_solution(206612190776953251)
XLA Ops:
  1.7 2.6 %collective-permute-start.4 = (f32[64,256]{1,0:T(8,128)S(1)}, f32[64,256]{1,0:T(8,128)S(1)}, u32[]{:S(2)}, u32[]{:S(2)}) collective-permute-start(f32[64,256]{1,0:T(8,128)S(1)} %pad_maximum_fusion.16), channel_id=1, source_target_pairs={{0,4},{4,8},{8,12},{12,0},{1,5},{5,9},{9,13},{13,1},{2,6},{6,10},{... | collective-permute-start | bytes 196616 | tf_op jit(solution)/shard_map/ppermute | solution.py:20
  5.2 1.5 %collective-permute-start = (bf16[64,128]{1,0:T(8,128)(2,1)S(1)}, bf16[64,128]{1,0:T(8,128)(2,1)S(1)}, u32[]{:S(2)}, u32[]{:S(2)}) collective-permute-start(bf16[64,128]{1,0:T(8,128)(2,1)S(1)} %get-tuple-element.34), channel_id=1, source_target_pairs={{0,1},{1,2},{2,3},{3,0},{4,5},{5,6},{6,7},{7,4},{8,9},{9,10},{10,1... | collective-permute-start | bytes 49160 | tf_op jit(solution)/shard_map/ppermute | solution.py:20
  6.7 2.3 %collective-permute-start.1 = (bf16[64,128]{1,0:T(8,128)(2,1)S(1)}, bf16[64,128]{1,0:T(8,128)(2,1)S(1)}, u32[]{:S(2)}, u32[]{:S(2)}) collective-permute-start(bf16[64,128]{1,0:T(8,128)(2,1)S(1)} %get-tuple-element.34), channel_id=1, source_target_pairs={{0,2},{1,3},{2,0},{3,1},{4,6},{5,7},{6,4},{7,5},{8,10},{9,11},{10,... | collective-permute-start | bytes 49160 | tf_op jit(solution)/shard_map/ppermute | solution.py:20
  13.0 1.7 %convolution_convert_fusion = bf16[512,2560]{1,0:T(8,128)(2,1)S(1)} fusion(bf16[1,1,2560,512]{3,2,1,0:T(8,128)(2,1)S(1)} %copy-done, s32[512]{0:T(512)S(1)} %fusion.70), kind=kOutput, calls=%fused_computation.8 | convolution fusion | flops 1344012288 | bytes 5244928 | tf_op jit(solution)/shard_map/dot_general | solution.py:69
  14.7 10.0 %fusion = f32[512,2560]{1,0:T(8,128)S(1)} fusion(bf16[512,2560]{1,0:T(8,128)(2,1)S(1)} %convolution_convert_fusion, bf16[1,1,2560,2560]{3,2,1,0:T(8,128)(2,1)} %param.17), kind=kOutput, calls=%fused_computation.3 | convolution fusion | flops 6710886400 | bytes 20971520 | tf_op jit(solution)/shard_map/dot_general | solution.py:71
  24.8 1.6 %fusion.3 = f32[512,512]{1,0:T(8,128)S(1)} fusion(bf16[512,2560]{1,0:T(8,128)(2,1)S(1)} %convolution_convert_fusion, f32[512,2560]{1,0:T(8,128)S(1)} %fusion), kind=kOutput, calls=%fused_computation.9 | convolution fusion | flops 1346109440 | bytes 8912896 | tf_op jit(solution)/shard_map/dot_general | solution.py:74
  26.4 2.6 %fusion.7 = f32[512,512]{1,0:T(8,128)} fusion(f32[512,512]{1,0:T(8,128)S(1)} %fusion.3, bf16[512,2560]{1,0:T(8,128)(2,1)S(1)} %convolution_convert_fusion, f32[512,2560]{1,0:T(8,128)S(1)} %fusion), kind=kOutput, calls=%fused_computation.13 | convolution fusion | flops 1345060864 | bytes 9961472 | tf_op jit(solution)/shard_map/dot_general | solution.py:73
  28.9 3.4 %convolution_subtract_fusion = f32[512,512]{1,0:T(8,128)} fusion(f32[512,512]{1,0:T(8,128)} %fusion.7, bf16[1,1,512,512]{3,2,1,0:T(8,128)(2,1)} %param.15, s32[512]{0:T(512)S(1)} %fusion.70), kind=kOutput, calls=%fused_computation.12 | convolution fusion | flops 537919488 | bytes 2623488 | tf_op jit(solution)/shard_map/dot_general | solution.py:66
  34.7 1.2 collective-permute-start.3
  44.5 2.0 %dynamic-slice_bitcast_fusion.2 = (f32[2,64,512]{2,1,0:T(8,128)}, f32[2,64,512]{2,1,0:T(8,128)S(1)}, f32[2,64,512]{2,1,0:T(8,128)}) fusion(f32[2,4,64,512]{3,2,1,0:T(8,128)} %bitcast.238, s32[]{:T(128)S(6)} %select_n.162, s32[]{:T(128)S(6)} %select_n.166, s32[]{:T(128)S(6)} %select_n.164), kind=kLoop, calls=%fused_computation.73 | loop fusion | bytes 1572876 | tf_op jit(solution)/shard_map/jit(dynamic_index_in_dim)/squeeze | solution.py:44
  47.0 2.8 %collective-permute-start.9 = (f32[2,64,512]{2,1,0:T(8,128)S(1)}, f32[2,64,512]{2,1,0:T(8,128)}, u32[]{:S(2)}, u32[]{:S(2)}) collective-permute-start(f32[2,64,512]{2,1,0:T(8,128)S(1)} %get-tuple-element.17), channel_id=1, source_target_pairs={{0,3},{1,0},{2,1},{3,2},{4,7},{5,4},{6,5},{7,6},{8,11},{9,8},{10,9... | collective-permute-start | bytes 786440 | tf_op jit(solution)/shard_map/ppermute | solution.py:45
  50.8 5.8 %collective-permute-done.7 = f32[2,64,512]{2,1,0:T(8,128)} collective-permute-done((f32[2,64,512]{2,1,0:T(8,128)}, f32[2,64,512]{2,1,0:T(8,128)}, u32[]{:S(2)}, u32[]{:S(2)}) %collective-permute-start.7) | collective-permute-done | bytes 262176 | tf_op jit(solution)/shard_map/ppermute | solution.py:45
  56.6 10.6 %collective-permute-done.8 = f32[2,64,512]{2,1,0:T(8,128)} collective-permute-done((f32[2,64,512]{2,1,0:T(8,128)}, f32[2,64,512]{2,1,0:T(8,128)}, u32[]{:S(2)}, u32[]{:S(2)}) %collective-permute-start.8) | collective-permute-done | bytes 262176 | tf_op jit(solution)/shard_map/ppermute | solution.py:45
  67.2 1.3 fusion.33
  68.5 1.2 collective-permute-start.10
  69.8 2.6 %collective-permute-done.10 = f32[64,512]{1,0:T(8,128)S(1)} collective-permute-done((f32[64,512]{1,0:T(8,128)S(1)}, f32[64,512]{1,0:T(8,128)S(1)}, u32[]{:S(2)}, u32[]{:S(2)}) %collective-permute-start.10) | collective-permute-done | bytes 131104 | tf_op jit(solution)/shard_map/ppermute | solution.py:50
  73.6 3.5 %collective-permute-start.11 = (f32[64,128]{1,0:T(8,128)S(1)}, f32[64,128]{1,0:T(8,128)S(1)}, u32[]{:S(2)}, u32[]{:S(2)}) collective-permute-start(f32[64,128]{1,0:T(8,128)S(1)} %fusion.17), channel_id=1, source_target_pairs={{0,4},{4,8},{8,12},{12,0},{1,5},{5,9},{9,13},{13,1},{2,6},{6,10},{... | collective-permute-start | bytes 98312 | tf_op jit(solution)/shard_map/ppermute | solution.py:20
  78.1 1.9 %collective-permute-done.12 = f32[64,128]{1,0:T(8,128)S(1)} collective-permute-done((f32[64,128]{1,0:T(8,128)S(1)}, f32[64,128]{1,0:T(8,128)S(1)}, u32[]{:S(2)}, u32[]{:S(2)}) %collective-permute-start.12) | collective-permute-done | bytes 32800 | tf_op jit(solution)/shard_map/ppermute | solution.py:20
  81.2 5.4 %collective-permute-start.14 = (bf16[64,128]{1,0:T(8,128)(2,1)S(1)}, bf16[64,128]{1,0:T(8,128)(2,1)S(1)}, u32[]{:S(2)}, u32[]{:S(2)}) collective-permute-start(bf16[64,128]{1,0:T(8,128)(2,1)S(1)} %get-tuple-element.37), channel_id=1, source_target_pairs={{0,1},{1,2},{2,3},{3,0},{4,5},{5,6},{6,7},{7,4},{8,9},{9,10},{10,1... | collective-permute-start | bytes 49160 | tf_op jit(solution)/shard_map/ppermute | solution.py:20
  86.6 2.2 %collective-permute-start.16 = (bf16[64,128]{1,0:T(8,128)(2,1)S(1)}, bf16[64,128]{1,0:T(8,128)(2,1)S(1)}, u32[]{:S(2)}, u32[]{:S(2)}) collective-permute-start(bf16[64,128]{1,0:T(8,128)(2,1)S(1)} %get-tuple-element.37), channel_id=1, source_target_pairs={{0,3},{1,0},{2,1},{3,2},{4,7},{5,4},{6,5},{7,6},{8,11},{9,8},{10,9... | collective-permute-start | bytes 49160 | tf_op jit(solution)/shard_map/ppermute | solution.py:20
  90.1 1.3 collective-permute-start.17
  91.6 1.7 %collective-permute-done.17 = bf16[4,64,128]{2,1,0:T(8,128)(2,1)S(1)} collective-permute-done((bf16[4,64,128]{2,1,0:T(8,128)(2,1)S(1)}, bf16[4,64,128]{2,1,0:T(8,128)(2,1)S(1)}, u32[]{:S(2)}, u32[]{:S(2)}) %collective-permute-start.17) | collective-permute-done | bytes 65568 | tf_op jit(solution)/shard_map/ppermute | solution.py:20
  93.7 3.4 %collective-permute-start.18 = (f32[64,128]{1,0:T(8,128)S(1)}, f32[64,128]{1,0:T(8,128)S(1)}, u32[]{:S(2)}, u32[]{:S(2)}) collective-permute-start(f32[64,128]{1,0:T(8,128)S(1)} %fusion.14), channel_id=1, source_target_pairs={{0,4},{4,8},{8,12},{12,0},{1,5},{5,9},{9,13},{13,1},{2,6},{6,10},{... | collective-permute-start | bytes 98312 | tf_op jit(solution)/shard_map/ppermute | solution.py:20
  98.1 1.9 %collective-permute-done.19 = f32[64,128]{1,0:T(8,128)S(1)} collective-permute-done((f32[64,128]{1,0:T(8,128)S(1)}, f32[64,128]{1,0:T(8,128)S(1)}, u32[]{:S(2)}, u32[]{:S(2)}) %collective-permute-start.19) | collective-permute-done | bytes 32800 | tf_op jit(solution)/shard_map/ppermute | solution.py:20
  101.7 2.9 %collective-permute-start.22 = (bf16[64,128]{1,0:T(8,128)(2,1)S(1)}, bf16[64,128]{1,0:T(8,128)(2,1)S(1)}, u32[]{:S(2)}, u32[]{:S(2)}) collective-permute-start(bf16[64,128]{1,0:T(8,128)(2,1)S(1)} %get-tuple-element.39), channel_id=1, source_target_pairs={{0,2},{1,3},{2,0},{3,1},{4,6},{5,7},{6,4},{7,5},{8,10},{9,11},{10,... | collective-permute-start | bytes 49160 | tf_op jit(solution)/shard_map/ppermute | solution.py:20
  108.3 2.1 %collective-permute-done.24 = bf16[4,64,128]{2,1,0:T(8,128)(2,1)S(1)} collective-permute-done((bf16[4,64,128]{2,1,0:T(8,128)(2,1)S(1)}, bf16[4,64,128]{2,1,0:T(8,128)(2,1)S(1)}, u32[]{:S(2)}, u32[]{:S(2)}) %collective-permute-start.24) | collective-permute-done | bytes 65568 | tf_op jit(solution)/shard_map/ppermute | solution.py:20
  110.7 3.2 %collective-permute-start.25 = (f32[64,128]{1,0:T(8,128)S(1)}, f32[64,128]{1,0:T(8,128)S(1)}, u32[]{:S(2)}, u32[]{:S(2)}) collective-permute-start(f32[64,128]{1,0:T(8,128)S(1)} %fusion.11), channel_id=1, source_target_pairs={{0,4},{4,8},{8,12},{12,0},{1,5},{5,9},{9,13},{13,1},{2,6},{6,10},{... | collective-permute-start | bytes 98312 | tf_op jit(solution)/shard_map/ppermute | solution.py:20
  114.9 1.9 %collective-permute-done.26 = f32[64,128]{1,0:T(8,128)S(1)} collective-permute-done((f32[64,128]{1,0:T(8,128)S(1)}, f32[64,128]{1,0:T(8,128)S(1)}, u32[]{:S(2)}, u32[]{:S(2)}) %collective-permute-start.26) | collective-permute-done | bytes 32800 | tf_op jit(solution)/shard_map/ppermute | solution.py:20
  118.3 2.7 %collective-permute-start.29 = (bf16[64,128]{1,0:T(8,128)(2,1)S(1)}, bf16[64,128]{1,0:T(8,128)(2,1)S(1)}, u32[]{:S(2)}, u32[]{:S(2)}) collective-permute-start(bf16[64,128]{1,0:T(8,128)(2,1)S(1)} %get-tuple-element.41), channel_id=1, source_target_pairs={{0,2},{1,3},{2,0},{3,1},{4,6},{5,7},{6,4},{7,5},{8,10},{9,11},{10,... | collective-permute-start | bytes 49160 | tf_op jit(solution)/shard_map/ppermute | solution.py:20
  124.7 2.1 %collective-permute-done.31 = bf16[4,64,128]{2,1,0:T(8,128)(2,1)S(1)} collective-permute-done((bf16[4,64,128]{2,1,0:T(8,128)(2,1)S(1)}, bf16[4,64,128]{2,1,0:T(8,128)(2,1)S(1)}, u32[]{:S(2)}, u32[]{:S(2)}) %collective-permute-start.31) | collective-permute-done | bytes 65568 | tf_op jit(solution)/shard_map/ppermute | solution.py:20
  127.2 2.9 %collective-permute-start.32 = (f32[64,128]{1,0:T(8,128)S(1)}, f32[64,128]{1,0:T(8,128)S(1)}, u32[]{:S(2)}, u32[]{:S(2)}) collective-permute-start(f32[64,128]{1,0:T(8,128)S(1)} %fusion.8), channel_id=1, source_target_pairs={{0,4},{4,8},{8,12},{12,0},{1,5},{5,9},{9,13},{13,1},{2,6},{6,10},{... | collective-permute-start | bytes 98312 | tf_op jit(solution)/shard_map/ppermute | solution.py:20
  131.1 2.2 %collective-permute-done.33 = f32[64,128]{1,0:T(8,128)S(1)} collective-permute-done((f32[64,128]{1,0:T(8,128)S(1)}, f32[64,128]{1,0:T(8,128)S(1)}, u32[]{:S(2)}, u32[]{:S(2)}) %collective-permute-start.33) | collective-permute-done | bytes 32800 | tf_op jit(solution)/shard_map/ppermute | solution.py:20
  (131 shorter events, 40.1 us)
Async XLA Ops:
  1.7 34.3 %collective-permute-start.4 = (f32[64,256]{1,0:T(8,128)S(1)}, f32[64,256]{1,0:T(8,128)S(1)}, u32[]{:S(2)}, u32[]{:S(2)}) collective-permute-start(f32[64,256]{1,0:T(8,128)S(1)} %pad_maximum_fusion.16), channel_id=1, source_target_pairs={{0,4},{4,8},{8,12},{12,0},{1,5},{5,9},{9,13},{13,1},{2,6},{6,10},{... | collective-permute-start | bytes 196616 | tf_op jit(solution)/shard_map/ppermute | solution.py:20
  4.4 31.6 %collective-permute-start.5 = (f32[64,256]{1,0:T(8,128)S(1)}, f32[64,256]{1,0:T(8,128)S(1)}, u32[]{:S(2)}, u32[]{:S(2)}) collective-permute-start(f32[64,256]{1,0:T(8,128)S(1)} %pad_maximum_fusion.16), channel_id=1, source_target_pairs={{0,8},{4,12},{8,0},{12,4},{1,9},{5,13},{9,1},{13,5},{2,10},{6,14},... | collective-permute-start | bytes 196616 | tf_op jit(solution)/shard_map/ppermute | solution.py:20
  5.2 27.8 %collective-permute-start = (bf16[64,128]{1,0:T(8,128)(2,1)S(1)}, bf16[64,128]{1,0:T(8,128)(2,1)S(1)}, u32[]{:S(2)}, u32[]{:S(2)}) collective-permute-start(bf16[64,128]{1,0:T(8,128)(2,1)S(1)} %get-tuple-element.34), channel_id=1, source_target_pairs={{0,1},{1,2},{2,3},{3,0},{4,5},{5,6},{6,7},{7,4},{8,9},{9,10},{10,1... | collective-permute-start | bytes 49160 | tf_op jit(solution)/shard_map/ppermute | solution.py:20
  6.7 27.4 %collective-permute-start.1 = (bf16[64,128]{1,0:T(8,128)(2,1)S(1)}, bf16[64,128]{1,0:T(8,128)(2,1)S(1)}, u32[]{:S(2)}, u32[]{:S(2)}) collective-permute-start(bf16[64,128]{1,0:T(8,128)(2,1)S(1)} %get-tuple-element.34), channel_id=1, source_target_pairs={{0,2},{1,3},{2,0},{3,1},{4,6},{5,7},{6,4},{7,5},{8,10},{9,11},{10,... | collective-permute-start | bytes 49160 | tf_op jit(solution)/shard_map/ppermute | solution.py:20
  9.0 25.1 %collective-permute-start.2 = (bf16[64,128]{1,0:T(8,128)(2,1)S(1)}, bf16[64,128]{1,0:T(8,128)(2,1)S(1)}, u32[]{:S(2)}, u32[]{:S(2)}) collective-permute-start(bf16[64,128]{1,0:T(8,128)(2,1)S(1)} %get-tuple-element.34), channel_id=1, source_target_pairs={{0,3},{1,0},{2,1},{3,2},{4,7},{5,4},{6,5},{7,6},{8,11},{9,8},{10,9... | collective-permute-start | bytes 49160 | tf_op jit(solution)/shard_map/ppermute | solution.py:20
  33.0 3.7 %collective-permute-start.6 = (f32[64,256]{1,0:T(8,128)S(1)}, f32[64,256]{1,0:T(8,128)S(1)}, u32[]{:S(2)}, u32[]{:S(2)}) collective-permute-start(f32[64,256]{1,0:T(8,128)S(1)} %pad_maximum_fusion.16), channel_id=1, source_target_pairs={{0,12},{4,0},{8,4},{12,8},{1,13},{5,1},{9,5},{13,9},{2,14},{6,2},{... | collective-permute-start | bytes 196616 | tf_op jit(solution)/shard_map/ppermute | solution.py:20
  34.7 8.9 %collective-permute-start.3 = (bf16[4,64,128]{2,1,0:T(8,128)(2,1)}, bf16[4,64,128]{2,1,0:T(8,128)(2,1)}, u32[]{:S(2)}, u32[]{:S(2)}) collective-permute-start(bf16[4,64,128]{2,1,0:T(8,128)(2,1)} %get-tuple-element.30), channel_id=1, source_target_pairs={{0,16},{16,0},{1,17},{17,1},{2,18},{18,2},{3,19},{19,3},{4,20},{20... | collective-permute-start | bytes 196616 | tf_op jit(solution)/shard_map/ppermute | solution.py:20
  46.5 10.1 %collective-permute-start.7 = (f32[2,64,512]{2,1,0:T(8,128)}, f32[2,64,512]{2,1,0:T(8,128)}, u32[]{:S(2)}, u32[]{:S(2)}) collective-permute-start(f32[2,64,512]{2,1,0:T(8,128)} %get-tuple-element.16), channel_id=1, source_target_pairs={{0,1},{1,2},{2,3},{3,0},{4,5},{5,6},{6,7},{7,4},{8,9},{9,10},{10,1... | collective-permute-start | bytes 786440 | tf_op jit(solution)/shard_map/ppermute | solution.py:45
  46.9 20.3 %collective-permute-start.8 = (f32[2,64,512]{2,1,0:T(8,128)}, f32[2,64,512]{2,1,0:T(8,128)}, u32[]{:S(2)}, u32[]{:S(2)}) collective-permute-start(f32[2,64,512]{2,1,0:T(8,128)} %get-tuple-element.18), channel_id=1, source_target_pairs={{0,2},{1,3},{2,0},{3,1},{4,6},{5,7},{6,4},{7,5},{8,10},{9,11},{10,... | collective-permute-start | bytes 786440 | tf_op jit(solution)/shard_map/ppermute | solution.py:45
  47.0 20.2 %collective-permute-start.9 = (f32[2,64,512]{2,1,0:T(8,128)S(1)}, f32[2,64,512]{2,1,0:T(8,128)}, u32[]{:S(2)}, u32[]{:S(2)}) collective-permute-start(f32[2,64,512]{2,1,0:T(8,128)S(1)} %get-tuple-element.17), channel_id=1, source_target_pairs={{0,3},{1,0},{2,1},{3,2},{4,7},{5,4},{6,5},{7,6},{8,11},{9,8},{10,9... | collective-permute-start | bytes 786440 | tf_op jit(solution)/shard_map/ppermute | solution.py:45
  68.5 3.9 %collective-permute-start.10 = (f32[64,512]{1,0:T(8,128)S(1)}, f32[64,512]{1,0:T(8,128)S(1)}, u32[]{:S(2)}, u32[]{:S(2)}) collective-permute-start(f32[64,512]{1,0:T(8,128)S(1)} %dynamic-slice_bitcast_fusion.3), channel_id=1, source_target_pairs={{0,16},{16,0},{1,17},{17,1},{2,18},{18,2},{3,19},{19,3},{4,20},{20... | collective-permute-start | bytes 393224 | tf_op jit(solution)/shard_map/ppermute | solution.py:50
  73.6 4.5 %collective-permute-start.11 = (f32[64,128]{1,0:T(8,128)S(1)}, f32[64,128]{1,0:T(8,128)S(1)}, u32[]{:S(2)}, u32[]{:S(2)}) collective-permute-start(f32[64,128]{1,0:T(8,128)S(1)} %fusion.17), channel_id=1, source_target_pairs={{0,4},{4,8},{8,12},{12,0},{1,5},{5,9},{9,13},{13,1},{2,6},{6,10},{... | collective-permute-start | bytes 98312 | tf_op jit(solution)/shard_map/ppermute | solution.py:20
  77.6 3.3 %collective-permute-start.13 = (f32[64,128]{1,0:T(8,128)S(1)}, f32[64,128]{1,0:T(8,128)S(1)}, u32[]{:S(2)}, u32[]{:S(2)}) collective-permute-start(f32[64,128]{1,0:T(8,128)S(1)} %fusion.17), channel_id=1, source_target_pairs={{0,12},{4,0},{8,4},{12,8},{1,13},{5,1},{9,5},{13,9},{2,14},{6,2},{... | collective-permute-start | bytes 98312 | tf_op jit(solution)/shard_map/ppermute | solution.py:20
  81.2 8.1 %collective-permute-start.14 = (bf16[64,128]{1,0:T(8,128)(2,1)S(1)}, bf16[64,128]{1,0:T(8,128)(2,1)S(1)}, u32[]{:S(2)}, u32[]{:S(2)}) collective-permute-start(bf16[64,128]{1,0:T(8,128)(2,1)S(1)} %get-tuple-element.37), channel_id=1, source_target_pairs={{0,1},{1,2},{2,3},{3,0},{4,5},{5,6},{6,7},{7,4},{8,9},{9,10},{10,1... | collective-permute-start | bytes 49160 | tf_op jit(solution)/shard_map/ppermute | solution.py:20
  86.6 3.5 %collective-permute-start.15 = (bf16[64,128]{1,0:T(8,128)(2,1)S(1)}, bf16[64,128]{1,0:T(8,128)(2,1)S(1)}, u32[]{:S(2)}, u32[]{:S(2)}) collective-permute-start(bf16[64,128]{1,0:T(8,128)(2,1)S(1)} %get-tuple-element.37), channel_id=1, source_target_pairs={{0,2},{1,3},{2,0},{3,1},{4,6},{5,7},{6,4},{7,5},{8,10},{9,11},{10,... | collective-permute-start | bytes 49160 | tf_op jit(solution)/shard_map/ppermute | solution.py:20
  86.6 3.5 %collective-permute-start.16 = (bf16[64,128]{1,0:T(8,128)(2,1)S(1)}, bf16[64,128]{1,0:T(8,128)(2,1)S(1)}, u32[]{:S(2)}, u32[]{:S(2)}) collective-permute-start(bf16[64,128]{1,0:T(8,128)(2,1)S(1)} %get-tuple-element.37), channel_id=1, source_target_pairs={{0,3},{1,0},{2,1},{3,2},{4,7},{5,4},{6,5},{7,6},{8,11},{9,8},{10,9... | collective-permute-start | bytes 49160 | tf_op jit(solution)/shard_map/ppermute | solution.py:20
  90.1 3.2 %collective-permute-start.17 = (bf16[4,64,128]{2,1,0:T(8,128)(2,1)S(1)}, bf16[4,64,128]{2,1,0:T(8,128)(2,1)S(1)}, u32[]{:S(2)}, u32[]{:S(2)}) collective-permute-start(bf16[4,64,128]{2,1,0:T(8,128)(2,1)S(1)} %get-tuple-element.26), channel_id=1, source_target_pairs={{0,16},{16,0},{1,17},{17,1},{2,18},{18,2},{3,19},{19,3},{4,20},{20... | collective-permute-start | bytes 196616 | tf_op jit(solution)/shard_map/ppermute | solution.py:20
  93.7 4.4 %collective-permute-start.18 = (f32[64,128]{1,0:T(8,128)S(1)}, f32[64,128]{1,0:T(8,128)S(1)}, u32[]{:S(2)}, u32[]{:S(2)}) collective-permute-start(f32[64,128]{1,0:T(8,128)S(1)} %fusion.14), channel_id=1, source_target_pairs={{0,4},{4,8},{8,12},{12,0},{1,5},{5,9},{9,13},{13,1},{2,6},{6,10},{... | collective-permute-start | bytes 98312 | tf_op jit(solution)/shard_map/ppermute | solution.py:20
  97.0 3.0 %collective-permute-start.19 = (f32[64,128]{1,0:T(8,128)S(1)}, f32[64,128]{1,0:T(8,128)S(1)}, u32[]{:S(2)}, u32[]{:S(2)}) collective-permute-start(f32[64,128]{1,0:T(8,128)S(1)} %fusion.14), channel_id=1, source_target_pairs={{0,8},{4,12},{8,0},{12,4},{1,9},{5,13},{9,1},{13,5},{2,10},{6,14},... | collective-permute-start | bytes 98312 | tf_op jit(solution)/shard_map/ppermute | solution.py:20
  97.6 3.3 %collective-permute-start.20 = (f32[64,128]{1,0:T(8,128)S(1)}, f32[64,128]{1,0:T(8,128)S(1)}, u32[]{:S(2)}, u32[]{:S(2)}) collective-permute-start(f32[64,128]{1,0:T(8,128)S(1)} %fusion.14), channel_id=1, source_target_pairs={{0,12},{4,0},{8,4},{12,8},{1,13},{5,1},{9,5},{13,9},{2,14},{6,2},{... | collective-permute-start | bytes 98312 | tf_op jit(solution)/shard_map/ppermute | solution.py:20
  101.2 4.9 %collective-permute-start.21 = (bf16[64,128]{1,0:T(8,128)(2,1)S(1)}, bf16[64,128]{1,0:T(8,128)(2,1)S(1)}, u32[]{:S(2)}, u32[]{:S(2)}) collective-permute-start(bf16[64,128]{1,0:T(8,128)(2,1)S(1)} %get-tuple-element.39), channel_id=1, source_target_pairs={{0,1},{1,2},{2,3},{3,0},{4,5},{5,6},{6,7},{7,4},{8,9},{9,10},{10,1... | collective-permute-start | bytes 49160 | tf_op jit(solution)/shard_map/ppermute | solution.py:20
  101.7 4.7 %collective-permute-start.22 = (bf16[64,128]{1,0:T(8,128)(2,1)S(1)}, bf16[64,128]{1,0:T(8,128)(2,1)S(1)}, u32[]{:S(2)}, u32[]{:S(2)}) collective-permute-start(bf16[64,128]{1,0:T(8,128)(2,1)S(1)} %get-tuple-element.39), channel_id=1, source_target_pairs={{0,2},{1,3},{2,0},{3,1},{4,6},{5,7},{6,4},{7,5},{8,10},{9,11},{10,... | collective-permute-start | bytes 49160 | tf_op jit(solution)/shard_map/ppermute | solution.py:20
  107.2 3.2 %collective-permute-start.24 = (bf16[4,64,128]{2,1,0:T(8,128)(2,1)S(1)}, bf16[4,64,128]{2,1,0:T(8,128)(2,1)S(1)}, u32[]{:S(2)}, u32[]{:S(2)}) collective-permute-start(bf16[4,64,128]{2,1,0:T(8,128)(2,1)S(1)} %get-tuple-element.24), channel_id=1, source_target_pairs={{0,16},{16,0},{1,17},{17,1},{2,18},{18,2},{3,19},{19,3},{4,20},{20... | collective-permute-start | bytes 196616 | tf_op jit(solution)/shard_map/ppermute | solution.py:20
  110.7 4.2 %collective-permute-start.25 = (f32[64,128]{1,0:T(8,128)S(1)}, f32[64,128]{1,0:T(8,128)S(1)}, u32[]{:S(2)}, u32[]{:S(2)}) collective-permute-start(f32[64,128]{1,0:T(8,128)S(1)} %fusion.11), channel_id=1, source_target_pairs={{0,4},{4,8},{8,12},{12,0},{1,5},{5,9},{9,13},{13,1},{2,6},{6,10},{... | collective-permute-start | bytes 98312 | tf_op jit(solution)/shard_map/ppermute | solution.py:20
  113.9 3.0 %collective-permute-start.26 = (f32[64,128]{1,0:T(8,128)S(1)}, f32[64,128]{1,0:T(8,128)S(1)}, u32[]{:S(2)}, u32[]{:S(2)}) collective-permute-start(f32[64,128]{1,0:T(8,128)S(1)} %fusion.11), channel_id=1, source_target_pairs={{0,8},{4,12},{8,0},{12,4},{1,9},{5,13},{9,1},{13,5},{2,10},{6,14},... | collective-permute-start | bytes 98312 | tf_op jit(solution)/shard_map/ppermute | solution.py:20
  114.5 3.3 %collective-permute-start.27 = (f32[64,128]{1,0:T(8,128)S(1)}, f32[64,128]{1,0:T(8,128)S(1)}, u32[]{:S(2)}, u32[]{:S(2)}) collective-permute-start(f32[64,128]{1,0:T(8,128)S(1)} %fusion.11), channel_id=1, source_target_pairs={{0,12},{4,0},{8,4},{12,8},{1,13},{5,1},{9,5},{13,9},{2,14},{6,2},{... | collective-permute-start | bytes 98312 | tf_op jit(solution)/shard_map/ppermute | solution.py:20
  118.1 4.9 %collective-permute-start.28 = (bf16[64,128]{1,0:T(8,128)(2,1)S(1)}, bf16[64,128]{1,0:T(8,128)(2,1)S(1)}, u32[]{:S(2)}, u32[]{:S(2)}) collective-permute-start(bf16[64,128]{1,0:T(8,128)(2,1)S(1)} %get-tuple-element.41), channel_id=1, source_target_pairs={{0,1},{1,2},{2,3},{3,0},{4,5},{5,6},{6,7},{7,4},{8,9},{9,10},{10,1... | collective-permute-start | bytes 49160 | tf_op jit(solution)/shard_map/ppermute | solution.py:20
  118.3 4.6 %collective-permute-start.29 = (bf16[64,128]{1,0:T(8,128)(2,1)S(1)}, bf16[64,128]{1,0:T(8,128)(2,1)S(1)}, u32[]{:S(2)}, u32[]{:S(2)}) collective-permute-start(bf16[64,128]{1,0:T(8,128)(2,1)S(1)} %get-tuple-element.41), channel_id=1, source_target_pairs={{0,2},{1,3},{2,0},{3,1},{4,6},{5,7},{6,4},{7,5},{8,10},{9,11},{10,... | collective-permute-start | bytes 49160 | tf_op jit(solution)/shard_map/ppermute | solution.py:20
  123.7 3.2 %collective-permute-start.31 = (bf16[4,64,128]{2,1,0:T(8,128)(2,1)S(1)}, bf16[4,64,128]{2,1,0:T(8,128)(2,1)S(1)}, u32[]{:S(2)}, u32[]{:S(2)}) collective-permute-start(bf16[4,64,128]{2,1,0:T(8,128)(2,1)S(1)} %get-tuple-element.22), channel_id=1, source_target_pairs={{0,16},{16,0},{1,17},{17,1},{2,18},{18,2},{3,19},{19,3},{4,20},{20... | collective-permute-start | bytes 196616 | tf_op jit(solution)/shard_map/ppermute | solution.py:20
  127.2 4.0 %collective-permute-start.32 = (f32[64,128]{1,0:T(8,128)S(1)}, f32[64,128]{1,0:T(8,128)S(1)}, u32[]{:S(2)}, u32[]{:S(2)}) collective-permute-start(f32[64,128]{1,0:T(8,128)S(1)} %fusion.8), channel_id=1, source_target_pairs={{0,4},{4,8},{8,12},{12,0},{1,5},{5,9},{9,13},{13,1},{2,6},{6,10},{... | collective-permute-start | bytes 98312 | tf_op jit(solution)/shard_map/ppermute | solution.py:20
  130.1 3.2 %collective-permute-start.33 = (f32[64,128]{1,0:T(8,128)S(1)}, f32[64,128]{1,0:T(8,128)S(1)}, u32[]{:S(2)}, u32[]{:S(2)}) collective-permute-start(f32[64,128]{1,0:T(8,128)S(1)} %fusion.8), channel_id=1, source_target_pairs={{0,8},{4,12},{8,0},{12,4},{1,9},{5,13},{9,1},{13,5},{2,10},{6,14},... | collective-permute-start | bytes 98312 | tf_op jit(solution)/shard_map/ppermute | solution.py:20
  131.1 3.3 %collective-permute-start.34 = (f32[64,128]{1,0:T(8,128)S(1)}, f32[64,128]{1,0:T(8,128)S(1)}, u32[]{:S(2)}, u32[]{:S(2)}) collective-permute-start(f32[64,128]{1,0:T(8,128)S(1)} %fusion.8), channel_id=1, source_target_pairs={{0,12},{4,0},{8,4},{12,8},{1,13},{5,1},{9,5},{13,9},{2,14},{6,2},{... | collective-permute-start | bytes 98312 | tf_op jit(solution)/shard_map/ppermute | solution.py:20
  (8 other events, 44.4 us)

commit v14 on v9

--- a/solution.py
+++ b/solution.py
@@ -62,21 +62,20 @@
     return schur.reshape(owners, block_nodes, nodes)
 
 
-def chain_weights(precond_f, couple_f):
+def chain_weights(precond_parts, couple_parts, section_pos):
     highest = lax.Precision.HIGHEST
-    sections, block_nodes = precond_f.shape[0], precond_f.shape[1]
-    step = jnp.einsum("gij,gjk->gik", precond_f, couple_f, precision=highest)
+    sections, block_nodes = precond_parts.shape[0], precond_parts.shape[1]
+    step = jnp.einsum("dij,djk->dik", precond_parts, couple_parts, precision=highest)
     eye = jnp.eye(block_nodes, dtype=jnp.float32)
-    zero = jnp.zeros_like(eye)
-    rows = []
-    for h in range(sections):
-        if h == 0:
-            row = [eye] + [zero] * (sections - 1)
-        else:
-            row = [-jnp.dot(step[h], rows[h - 1][k], precision=highest) for k in range(h)]
-            row = row + [eye] + [zero] * (sections - 1 - h)
-        rows.append(row)
-    return jnp.stack([jnp.stack(row) for row in rows])
+    mine = [eye]
+    for distance in range(1, sections):
+        mine.append(-jnp.dot(mine[-1], step[distance - 1], precision=highest))
+    mine = jnp.stack(mine)
+    reach = (jnp.arange(sections) <= section_pos)[:, None, None]
+    mine = jnp.where(reach, mine, 0.0)
+    above = -jnp.einsum("ij,djk->dik", step[sections - 1], mine, precision=highest)
+    above = above.at[sections - 1].add(eye)
+    return mine, above
 
 
 def body(
@@ -95,24 +94,19 @@
         axis=1,
     )
     first_rounded = gather_owners(previous[0].astype(jnp.bfloat16))
-    behind = (section_pos - jnp.arange(sections)) % sections
-    tables = jnp.take(ring_parts(tables, "section"), behind, axis=0)
-    start_all = tables[:, :, :load_count]
-    precond_all = tables[:, :, load_count : load_count + block_nodes]
-    couple_all = tables[:, :, load_count + block_nodes :]
-    weights = chain_weights(precond_all, couple_all)
-    above_pos = jnp.minimum(section_pos + 1, sections - 1)
+    tables = ring_parts(tables, "section")
+    precond_parts = tables[:, :, load_count : load_count + block_nodes]
+    couple_parts = tables[:, :, load_count + block_nodes :]
+    weights_mine, weights_above = chain_weights(precond_parts, couple_parts, section_pos)
     has_above = section_pos + 1 < sections
-    weights_mine = jnp.take(weights[section_pos], behind, axis=0)
-    weights_above = jnp.take(weights[above_pos], behind, axis=0)
     precond_mine = precond[0, 0].astype(jnp.float32)
-    couple_above = couple_all[above_pos]
+    couple_above = couple_parts[sections - 1]
 
     spread = schur_rows(
         block_ids[0, 0], iface_matrix[0, 0], interior_coupling[0, 0], inv_interior[0, 0], owners
     )
     temps_mine = previous[0]
-    temps_above = start_all[above_pos]
+    temps_above = tables[sections - 1, :, :load_count]
     rhs = right_side[0]
 
     def known_part(temps_mine, temps_above):

time: 133 us -> 125 us (0.940)
  other arithmetic: 9.89 us -> 5.71 us
  local copies, waits for them, and re-layouts: 3.79 us -> 0.4 us
  starting transfers between devices: 38.8 us -> 41.2 us
  waiting for transfers between devices: 52.6 us -> 50.3 us
    ppermute x31, starting transfers between devices: 34.5 us -> 36.9 us  [ring_parts(): parts.append(lax.ppermute(block, axis, route))]
    all_to_all x1, waiting for transfers between devices: 26.3 us -> 24.2 us  [body(): rows = jnp.sum(lax.all_to_all(spread, OWNERS, 0, 0, tiled=True), axis=0)]
    gather x3 -> x0, local copies, waits for them, and re-layouts: 1.93 us -> none  [the longest x1 0.68 us: body(): weights_mine = jnp.take(weights[section_pos], behind, axis=0)]
    another operation x10, other arithmetic: 2.44 us -> 0.97 us  [ring_parts(): return jnp.stack(parts)]
  transfers between devices with their start and end apart: 32 -> 32, of which waited for: 23 -> 23; matrix products, arithmetic and copies ran while one was open for 25% -> 21% of each run, Pallas kernels for 0% -> 0%
where the time goes in v14:
time: 125 us; the launch traced here: 124 us
  waiting for transfers between devices  50.3 us (40%)
  starting transfers between devices  41.2 us (33%)
  matrix products  26.3 us (21%)
  other arithmetic  5.71 us (5%)
    ppermute x31, starting transfers between devices, ring_parts(): parts.append(lax.ppermute(block, axis, route))  36.9 us
    ppermute x31, waiting for transfers between devices, ring_parts(): parts.append(lax.ppermute(block, axis, route))  26.1 us
    all_to_all x1, waiting for transfers between devices, body(): rows = jnp.sum(lax.all_to_all(spread, OWNERS, 0, 0, tiled=True), axis=0)  24.2 us
    dot_general x1, matrix products, schur_rows(): solved = jnp.dot(inverse, coupled, preferred_element_type=jnp.float32)  10.1 us
    all_to_all x1, starting transfers between devices, body(): rows = jnp.sum(lax.all_to_all(spread, OWNERS, 0, 0, tiled=True), axis=0)  4.25 us
    dot_general x1, matrix products, moved(): jnp.dot(rows.astype(jnp.bfloat16), place, preferred_element_type=jnp.floa...  3.36 us
    dot_general x1, matrix products, schur_rows(): lax.dot_general(coupled, solved_hi, contract, preferred_element_type=jnp....  2.52 us
  transfers between devices with their start and end apart: 32, of which 23 were waited for; matrix products, arithmetic and copies ran while one was open for 21% of the time, Pallas kernels for 0%

profile of v14, /device:TPU:1, one launch (start us, length us, event | category | flops | bytes accessed | tf_op | source)
XLA Modules:
  0.0 124.3 jit_solution(15338904482695176426)
XLA Ops:
  1.8 2.6 %collective-permute-start.4 = (f32[64,256]{1,0:T(8,128)S(1)}, f32[64,256]{1,0:T(8,128)S(1)}, u32[]{:S(2)}, u32[]{:S(2)}) collective-permute-start(f32[64,256]{1,0:T(8,128)S(1)} %pad_maximum_fusion.15), channel_id=1, source_target_pairs={{0,4},{4,8},{8,12},{12,0},{1,5},{5,9},{9,13},{13,1},{2,6},{6,10},{... | collective-permute-start | bytes 196616 | tf_op jit(solution)/shard_map/ppermute | solution.py:20
  5.3 1.3 %collective-permute-start = (bf16[64,128]{1,0:T(8,128)(2,1)S(1)}, bf16[64,128]{1,0:T(8,128)(2,1)S(1)}, u32[]{:S(2)}, u32[]{:S(2)}) collective-permute-start(bf16[64,128]{1,0:T(8,128)(2,1)S(1)} %get-tuple-element.36), channel_id=1, source_target_pairs={{0,1},{1,2},{2,3},{3,0},{4,5},{5,6},{6,7},{7,4},{8,9},{9,10},{10,1... | collective-permute-start | bytes 49160 | tf_op jit(solution)/shard_map/ppermute | solution.py:20
  6.6 2.3 %collective-permute-start.1 = (bf16[64,128]{1,0:T(8,128)(2,1)S(1)}, bf16[64,128]{1,0:T(8,128)(2,1)S(1)}, u32[]{:S(2)}, u32[]{:S(2)}) collective-permute-start(bf16[64,128]{1,0:T(8,128)(2,1)S(1)} %get-tuple-element.36), channel_id=1, source_target_pairs={{0,2},{1,3},{2,0},{3,1},{4,6},{5,7},{6,4},{7,5},{8,10},{9,11},{10,... | collective-permute-start | bytes 49160 | tf_op jit(solution)/shard_map/ppermute | solution.py:20
  8.9 1.1 collective-permute-start.2
  11.6 1.7 %convolution_convert_fusion = bf16[512,2560]{1,0:T(8,128)(2,1)S(1)} fusion(bf16[1,1,2560,512]{3,2,1,0:T(8,128)(2,1)S(1)} %copy-done, s32[512]{0:T(512)S(1)} %fusion.53), kind=kOutput, calls=%fused_computation.5 | convolution fusion | flops 1344012288 | bytes 5244928 | tf_op jit(solution)/shard_map/dot_general | solution.py:52
  13.3 10.1 %fusion = f32[512,2560]{1,0:T(8,128)S(1)} fusion(bf16[512,2560]{1,0:T(8,128)(2,1)S(1)} %convolution_convert_fusion, bf16[1,1,2560,2560]{3,2,1,0:T(8,128)(2,1)} %param.17), kind=kOutput, calls=%fused_computation | convolution fusion | flops 6710886400 | bytes 20971520 | tf_op jit(solution)/shard_map/dot_general | solution.py:54
  23.4 1.6 %fusion.3 = f32[512,512]{1,0:T(8,128)S(1)} fusion(bf16[512,2560]{1,0:T(8,128)(2,1)S(1)} %convolution_convert_fusion, f32[512,2560]{1,0:T(8,128)S(1)} %fusion), kind=kOutput, calls=%fused_computation.6 | convolution fusion | flops 1346109440 | bytes 8912896 | tf_op jit(solution)/shard_map/dot_general | solution.py:57
  25.0 2.5 %fusion.7 = f32[512,512]{1,0:T(8,128)} fusion(f32[512,512]{1,0:T(8,128)S(1)} %fusion.3, bf16[512,2560]{1,0:T(8,128)(2,1)S(1)} %convolution_convert_fusion, f32[512,2560]{1,0:T(8,128)S(1)} %fusion), kind=kOutput, calls=%fused_computation.10 | convolution fusion | flops 1345060864 | bytes 9961472 | tf_op jit(solution)/shard_map/dot_general | solution.py:56
  27.5 3.4 %convolution_subtract_fusion = f32[512,512]{1,0:T(8,128)} fusion(f32[512,512]{1,0:T(8,128)} %fusion.7, bf16[1,1,512,512]{3,2,1,0:T(8,128)(2,1)} %param.15, s32[512]{0:T(512)S(1)} %fusion.53), kind=kOutput, calls=%fused_computation.9 | convolution fusion | flops 537919488 | bytes 2623488 | tf_op jit(solution)/shard_map/dot_general | solution.py:49
  30.9 1.2 collective-permute-start.5
  32.1 1.3 %collective-permute-start.3 = (bf16[4,64,128]{2,1,0:T(8,128)(2,1)S(1)}, bf16[4,64,128]{2,1,0:T(8,128)(2,1)S(1)}, u32[]{:S(2)}, u32[]{:S(2)}) collective-permute-start(bf16[4,64,128]{2,1,0:T(8,128)(2,1)S(1)} %get-tuple-element.34), channel_id=1, source_target_pairs={{0,16},{16,0},{1,17},{17,1},{2,18},{18,2},{3,19},{19,3},{4,20},{20... | collective-permute-start | bytes 196616 | tf_op jit(solution)/shard_map/ppermute | solution.py:20
  35.8 4.2 %all-to-all-start = ((f32[8,64,512]{2,1,0:T(8,128)}), f32[8,64,512]{2,1,0:T(8,128)}, u32[]{:S(2)}, u32[]{:S(2)}) async-start(f32[8,64,512]{2,1,0:T(8,128)} %bitcast.202), calls=%async_computation | async-start | bytes 2097152 | tf_op jit(solution)/shard_map/all_to_all | solution.py:121
  40.4 24.2 %all-to-all-done = f32[8,64,512]{2,1,0:T(8,128)} async-done(((f32[8,64,512]{2,1,0:T(8,128)}), f32[8,64,512]{2,1,0:T(8,128)}, u32[]{:S(2)}, u32[]{:S(2)}) %all-to-all-start) | async-done | bytes 1048608 | tf_op jit(solution)/shard_map/all_to_all | solution.py:121
  64.6 1.3 %reduce_sum.9 = f32[64,512]{1,0:T(8,128)S(1)} reduce(f32[8,64,512]{2,1,0:T(8,128)} %all-to-all-done, f32[]{:T(128)} %constant.85.clone.1), dimensions={0}, to_apply=%region_0.1 | reduce | flops 229376 | bytes 1179652 | tf_op jit(solution)/shard_map/reduce_sum | solution.py:121
  67.1 4.1 %collective-permute-start.7 = (f32[64,128]{1,0:T(8,128)S(1)}, f32[64,128]{1,0:T(8,128)S(1)}, u32[]{:S(2)}, u32[]{:S(2)}) collective-permute-start(f32[64,128]{1,0:T(8,128)S(1)} %fusion.18), channel_id=1, source_target_pairs={{0,4},{4,8},{8,12},{12,0},{1,5},{5,9},{9,13},{13,1},{2,6},{6,10},{... | collective-permute-start | bytes 98312 | tf_op jit(solution)/shard_map/ppermute | solution.py:20
  72.2 1.7 %collective-permute-done.8 = f32[64,128]{1,0:T(8,128)S(1)} collective-permute-done((f32[64,128]{1,0:T(8,128)S(1)}, f32[64,128]{1,0:T(8,128)S(1)}, u32[]{:S(2)}, u32[]{:S(2)}) %collective-permute-start.8) | collective-permute-done | bytes 32800 | tf_op jit(solution)/shard_map/ppermute | solution.py:20
  75.2 3.2 %collective-permute-start.12 = (bf16[64,128]{1,0:T(8,128)(2,1)S(1)}, bf16[64,128]{1,0:T(8,128)(2,1)S(1)}, u32[]{:S(2)}, u32[]{:S(2)}) collective-permute-start(bf16[64,128]{1,0:T(8,128)(2,1)S(1)} %get-tuple-element.37), channel_id=1, source_target_pairs={{0,3},{1,0},{2,1},{3,2},{4,7},{5,4},{6,5},{7,6},{8,11},{9,8},{10,9... | collective-permute-start | bytes 49160 | tf_op jit(solution)/shard_map/ppermute | solution.py:20
  80.7 2.7 %collective-permute-done.13 = bf16[4,64,128]{2,1,0:T(8,128)(2,1)S(1)} collective-permute-done((bf16[4,64,128]{2,1,0:T(8,128)(2,1)S(1)}, bf16[4,64,128]{2,1,0:T(8,128)(2,1)S(1)}, u32[]{:S(2)}, u32[]{:S(2)}) %collective-permute-start.13) | collective-permute-done | bytes 65568 | tf_op jit(solution)/shard_map/ppermute | solution.py:20
  83.8 2.7 %collective-permute-start.14 = (f32[64,128]{1,0:T(8,128)S(1)}, f32[64,128]{1,0:T(8,128)S(1)}, u32[]{:S(2)}, u32[]{:S(2)}) collective-permute-start(f32[64,128]{1,0:T(8,128)S(1)} %fusion.15), channel_id=1, source_target_pairs={{0,4},{4,8},{8,12},{12,0},{1,5},{5,9},{9,13},{13,1},{2,6},{6,10},{... | collective-permute-start | bytes 98312 | tf_op jit(solution)/shard_map/ppermute | solution.py:20
  87.5 2.1 %collective-permute-done.15 = f32[64,128]{1,0:T(8,128)S(1)} collective-permute-done((f32[64,128]{1,0:T(8,128)S(1)}, f32[64,128]{1,0:T(8,128)S(1)}, u32[]{:S(2)}, u32[]{:S(2)}) %collective-permute-start.15) | collective-permute-done | bytes 32800 | tf_op jit(solution)/shard_map/ppermute | solution.py:20
  90.7 1.8 %collective-permute-start.17 = (bf16[64,128]{1,0:T(8,128)(2,1)S(1)}, bf16[64,128]{1,0:T(8,128)(2,1)S(1)}, u32[]{:S(2)}, u32[]{:S(2)}) collective-permute-start(bf16[64,128]{1,0:T(8,128)(2,1)S(1)} %get-tuple-element.39), channel_id=1, source_target_pairs={{0,1},{1,2},{2,3},{3,0},{4,5},{5,6},{6,7},{7,4},{8,9},{9,10},{10,1... | collective-permute-start | bytes 49160 | tf_op jit(solution)/shard_map/ppermute | solution.py:20
  92.5 1.5 %collective-permute-start.18 = (bf16[64,128]{1,0:T(8,128)(2,1)S(1)}, bf16[64,128]{1,0:T(8,128)(2,1)S(1)}, u32[]{:S(2)}, u32[]{:S(2)}) collective-permute-start(bf16[64,128]{1,0:T(8,128)(2,1)S(1)} %get-tuple-element.39), channel_id=1, source_target_pairs={{0,2},{1,3},{2,0},{3,1},{4,6},{5,7},{6,4},{7,5},{8,10},{9,11},{10,... | collective-permute-start | bytes 49160 | tf_op jit(solution)/shard_map/ppermute | solution.py:20
  97.1 2.7 %collective-permute-done.20 = bf16[4,64,128]{2,1,0:T(8,128)(2,1)S(1)} collective-permute-done((bf16[4,64,128]{2,1,0:T(8,128)(2,1)S(1)}, bf16[4,64,128]{2,1,0:T(8,128)(2,1)S(1)}, u32[]{:S(2)}, u32[]{:S(2)}) %collective-permute-start.20) | collective-permute-done | bytes 65568 | tf_op jit(solution)/shard_map/ppermute | solution.py:20
  100.1 3.2 %collective-permute-start.21 = (f32[64,128]{1,0:T(8,128)S(1)}, f32[64,128]{1,0:T(8,128)S(1)}, u32[]{:S(2)}, u32[]{:S(2)}) collective-permute-start(f32[64,128]{1,0:T(8,128)S(1)} %fusion.12), channel_id=1, source_target_pairs={{0,4},{4,8},{8,12},{12,0},{1,5},{5,9},{9,13},{13,1},{2,6},{6,10},{... | collective-permute-start | bytes 98312 | tf_op jit(solution)/shard_map/ppermute | solution.py:20
  104.3 1.9 %collective-permute-done.22 = f32[64,128]{1,0:T(8,128)S(1)} collective-permute-done((f32[64,128]{1,0:T(8,128)S(1)}, f32[64,128]{1,0:T(8,128)S(1)}, u32[]{:S(2)}, u32[]{:S(2)}) %collective-permute-start.22) | collective-permute-done | bytes 32800 | tf_op jit(solution)/shard_map/ppermute | solution.py:20
  107.8 2.3 %collective-permute-start.25 = (bf16[64,128]{1,0:T(8,128)(2,1)S(1)}, bf16[64,128]{1,0:T(8,128)(2,1)S(1)}, u32[]{:S(2)}, u32[]{:S(2)}) collective-permute-start(bf16[64,128]{1,0:T(8,128)(2,1)S(1)} %get-tuple-element.41), channel_id=1, source_target_pairs={{0,2},{1,3},{2,0},{3,1},{4,6},{5,7},{6,4},{7,5},{8,10},{9,11},{10,... | collective-permute-start | bytes 49160 | tf_op jit(solution)/shard_map/ppermute | solution.py:20
  111.4 1.0 collective-permute-done.24
  113.1 2.7 %collective-permute-done.27 = bf16[4,64,128]{2,1,0:T(8,128)(2,1)S(1)} collective-permute-done((bf16[4,64,128]{2,1,0:T(8,128)(2,1)S(1)}, bf16[4,64,128]{2,1,0:T(8,128)(2,1)S(1)}, u32[]{:S(2)}, u32[]{:S(2)}) %collective-permute-start.27) | collective-permute-done | bytes 65568 | tf_op jit(solution)/shard_map/ppermute | solution.py:20
  116.2 2.9 %collective-permute-start.28 = (f32[64,128]{1,0:T(8,128)S(1)}, f32[64,128]{1,0:T(8,128)S(1)}, u32[]{:S(2)}, u32[]{:S(2)}) collective-permute-start(f32[64,128]{1,0:T(8,128)S(1)} %fusion.9), channel_id=1, source_target_pairs={{0,4},{4,8},{8,12},{12,0},{1,5},{5,9},{9,13},{13,1},{2,6},{6,10},{... | collective-permute-start | bytes 98312 | tf_op jit(solution)/shard_map/ppermute | solution.py:20
  119.1 1.0 collective-permute-start.29
  120.1 2.2 %collective-permute-done.29 = f32[64,128]{1,0:T(8,128)S(1)} collective-permute-done((f32[64,128]{1,0:T(8,128)S(1)}, f32[64,128]{1,0:T(8,128)S(1)}, u32[]{:S(2)}, u32[]{:S(2)}) %collective-permute-start.29) | collective-permute-done | bytes 32800 | tf_op jit(solution)/shard_map/ppermute | solution.py:20
  122.3 1.1 collective-permute-done.30
  (105 shorter events, 24.3 us)
Async XLA Ops:
  1.7 31.7 %collective-permute-start.6 = (f32[64,256]{1,0:T(8,128)S(1)}, f32[64,256]{1,0:T(8,128)S(1)}, u32[]{:S(2)}, u32[]{:S(2)}) collective-permute-start(f32[64,256]{1,0:T(8,128)S(1)} %pad_maximum_fusion.15), channel_id=1, source_target_pairs={{0,12},{4,0},{8,4},{12,8},{1,13},{5,1},{9,5},{13,9},{2,14},{6,2},{... | collective-permute-start | bytes 196616 | tf_op jit(solution)/shard_map/ppermute | solution.py:20
  1.8 31.6 %collective-permute-start.4 = (f32[64,256]{1,0:T(8,128)S(1)}, f32[64,256]{1,0:T(8,128)S(1)}, u32[]{:S(2)}, u32[]{:S(2)}) collective-permute-start(f32[64,256]{1,0:T(8,128)S(1)} %pad_maximum_fusion.15), channel_id=1, source_target_pairs={{0,4},{4,8},{8,12},{12,0},{1,5},{5,9},{9,13},{13,1},{2,6},{6,10},{... | collective-permute-start | bytes 196616 | tf_op jit(solution)/shard_map/ppermute | solution.py:20
  5.3 25.6 %collective-permute-start = (bf16[64,128]{1,0:T(8,128)(2,1)S(1)}, bf16[64,128]{1,0:T(8,128)(2,1)S(1)}, u32[]{:S(2)}, u32[]{:S(2)}) collective-permute-start(bf16[64,128]{1,0:T(8,128)(2,1)S(1)} %get-tuple-element.36), channel_id=1, source_target_pairs={{0,1},{1,2},{2,3},{3,0},{4,5},{5,6},{6,7},{7,4},{8,9},{9,10},{10,1... | collective-permute-start | bytes 49160 | tf_op jit(solution)/shard_map/ppermute | solution.py:20
  6.6 25.5 %collective-permute-start.1 = (bf16[64,128]{1,0:T(8,128)(2,1)S(1)}, bf16[64,128]{1,0:T(8,128)(2,1)S(1)}, u32[]{:S(2)}, u32[]{:S(2)}) collective-permute-start(bf16[64,128]{1,0:T(8,128)(2,1)S(1)} %get-tuple-element.36), channel_id=1, source_target_pairs={{0,2},{1,3},{2,0},{3,1},{4,6},{5,7},{6,4},{7,5},{8,10},{9,11},{10,... | collective-permute-start | bytes 49160 | tf_op jit(solution)/shard_map/ppermute | solution.py:20
  8.9 23.2 %collective-permute-start.2 = (bf16[64,128]{1,0:T(8,128)(2,1)S(1)}, bf16[64,128]{1,0:T(8,128)(2,1)S(1)}, u32[]{:S(2)}, u32[]{:S(2)}) collective-permute-start(bf16[64,128]{1,0:T(8,128)(2,1)S(1)} %get-tuple-element.36), channel_id=1, source_target_pairs={{0,3},{1,0},{2,1},{3,2},{4,7},{5,4},{6,5},{7,6},{8,11},{9,8},{10,9... | collective-permute-start | bytes 49160 | tf_op jit(solution)/shard_map/ppermute | solution.py:20
  30.9 3.2 %collective-permute-start.5 = (f32[64,256]{1,0:T(8,128)S(1)}, f32[64,256]{1,0:T(8,128)S(1)}, u32[]{:S(2)}, u32[]{:S(2)}) collective-permute-start(f32[64,256]{1,0:T(8,128)S(1)} %pad_maximum_fusion.15), channel_id=1, source_target_pairs={{0,8},{4,12},{8,0},{12,4},{1,9},{5,13},{9,1},{13,5},{2,10},{6,14},... | collective-permute-start | bytes 196616 | tf_op jit(solution)/shard_map/ppermute | solution.py:20
  32.1 3.7 %collective-permute-start.3 = (bf16[4,64,128]{2,1,0:T(8,128)(2,1)S(1)}, bf16[4,64,128]{2,1,0:T(8,128)(2,1)S(1)}, u32[]{:S(2)}, u32[]{:S(2)}) collective-permute-start(bf16[4,64,128]{2,1,0:T(8,128)(2,1)S(1)} %get-tuple-element.34), channel_id=1, source_target_pairs={{0,16},{16,0},{1,17},{17,1},{2,18},{18,2},{3,19},{19,3},{4,20},{20... | collective-permute-start | bytes 196616 | tf_op jit(solution)/shard_map/ppermute | solution.py:20
  35.8 28.8 %all-to-all-start = ((f32[8,64,512]{2,1,0:T(8,128)}), f32[8,64,512]{2,1,0:T(8,128)}, u32[]{:S(2)}, u32[]{:S(2)}) async-start(f32[8,64,512]{2,1,0:T(8,128)} %bitcast.202), calls=%async_computation | async-start | bytes 2097152 | tf_op jit(solution)/shard_map/all_to_all | solution.py:121
  67.1 5.1 %collective-permute-start.7 = (f32[64,128]{1,0:T(8,128)S(1)}, f32[64,128]{1,0:T(8,128)S(1)}, u32[]{:S(2)}, u32[]{:S(2)}) collective-permute-start(f32[64,128]{1,0:T(8,128)S(1)} %fusion.18), channel_id=1, source_target_pairs={{0,4},{4,8},{8,12},{12,0},{1,5},{5,9},{9,13},{13,1},{2,6},{6,10},{... | collective-permute-start | bytes 98312 | tf_op jit(solution)/shard_map/ppermute | solution.py:20
  71.2 2.8 %collective-permute-start.8 = (f32[64,128]{1,0:T(8,128)S(1)}, f32[64,128]{1,0:T(8,128)S(1)}, u32[]{:S(2)}, u32[]{:S(2)}) collective-permute-start(f32[64,128]{1,0:T(8,128)S(1)} %fusion.18), channel_id=1, source_target_pairs={{0,8},{4,12},{8,0},{12,4},{1,9},{5,13},{9,1},{13,5},{2,10},{6,14},... | collective-permute-start | bytes 98312 | tf_op jit(solution)/shard_map/ppermute | solution.py:20
  71.5 3.3 %collective-permute-start.9 = (f32[64,128]{1,0:T(8,128)S(1)}, f32[64,128]{1,0:T(8,128)S(1)}, u32[]{:S(2)}, u32[]{:S(2)}) collective-permute-start(f32[64,128]{1,0:T(8,128)S(1)} %fusion.18), channel_id=1, source_target_pairs={{0,12},{4,0},{8,4},{12,8},{1,13},{5,1},{9,5},{13,9},{2,14},{6,2},{... | collective-permute-start | bytes 98312 | tf_op jit(solution)/shard_map/ppermute | solution.py:20
  75.1 4.4 %collective-permute-start.10 = (bf16[64,128]{1,0:T(8,128)(2,1)S(1)}, bf16[64,128]{1,0:T(8,128)(2,1)S(1)}, u32[]{:S(2)}, u32[]{:S(2)}) collective-permute-start(bf16[64,128]{1,0:T(8,128)(2,1)S(1)} %get-tuple-element.37), channel_id=1, source_target_pairs={{0,1},{1,2},{2,3},{3,0},{4,5},{5,6},{6,7},{7,4},{8,9},{9,10},{10,1... | collective-permute-start | bytes 49160 | tf_op jit(solution)/shard_map/ppermute | solution.py:20
  75.1 4.4 %collective-permute-start.11 = (bf16[64,128]{1,0:T(8,128)(2,1)S(1)}, bf16[64,128]{1,0:T(8,128)(2,1)S(1)}, u32[]{:S(2)}, u32[]{:S(2)}) collective-permute-start(bf16[64,128]{1,0:T(8,128)(2,1)S(1)} %get-tuple-element.37), channel_id=1, source_target_pairs={{0,2},{1,3},{2,0},{3,1},{4,6},{5,7},{6,4},{7,5},{8,10},{9,11},{10,... | collective-permute-start | bytes 49160 | tf_op jit(solution)/shard_map/ppermute | solution.py:20
  75.2 5.0 %collective-permute-start.12 = (bf16[64,128]{1,0:T(8,128)(2,1)S(1)}, bf16[64,128]{1,0:T(8,128)(2,1)S(1)}, u32[]{:S(2)}, u32[]{:S(2)}) collective-permute-start(bf16[64,128]{1,0:T(8,128)(2,1)S(1)} %get-tuple-element.37), channel_id=1, source_target_pairs={{0,3},{1,0},{2,1},{3,2},{4,7},{5,4},{6,5},{7,6},{8,11},{9,8},{10,9... | collective-permute-start | bytes 49160 | tf_op jit(solution)/shard_map/ppermute | solution.py:20
  80.2 3.2 %collective-permute-start.13 = (bf16[4,64,128]{2,1,0:T(8,128)(2,1)S(1)}, bf16[4,64,128]{2,1,0:T(8,128)(2,1)S(1)}, u32[]{:S(2)}, u32[]{:S(2)}) collective-permute-start(bf16[4,64,128]{2,1,0:T(8,128)(2,1)S(1)} %get-tuple-element.32), channel_id=1, source_target_pairs={{0,16},{16,0},{1,17},{17,1},{2,18},{18,2},{3,19},{19,3},{4,20},{20... | collective-permute-start | bytes 196616 | tf_op jit(solution)/shard_map/ppermute | solution.py:20
  83.8 3.7 %collective-permute-start.14 = (f32[64,128]{1,0:T(8,128)S(1)}, f32[64,128]{1,0:T(8,128)S(1)}, u32[]{:S(2)}, u32[]{:S(2)}) collective-permute-start(f32[64,128]{1,0:T(8,128)S(1)} %fusion.15), channel_id=1, source_target_pairs={{0,4},{4,8},{8,12},{12,0},{1,5},{5,9},{9,13},{13,1},{2,6},{6,10},{... | collective-permute-start | bytes 98312 | tf_op jit(solution)/shard_map/ppermute | solution.py:20
  86.4 3.1 %collective-permute-start.15 = (f32[64,128]{1,0:T(8,128)S(1)}, f32[64,128]{1,0:T(8,128)S(1)}, u32[]{:S(2)}, u32[]{:S(2)}) collective-permute-start(f32[64,128]{1,0:T(8,128)S(1)} %fusion.15), channel_id=1, source_target_pairs={{0,8},{4,12},{8,0},{12,4},{1,9},{5,13},{9,1},{13,5},{2,10},{6,14},... | collective-permute-start | bytes 98312 | tf_op jit(solution)/shard_map/ppermute | solution.py:20
  87.1 3.3 %collective-permute-start.16 = (f32[64,128]{1,0:T(8,128)S(1)}, f32[64,128]{1,0:T(8,128)S(1)}, u32[]{:S(2)}, u32[]{:S(2)}) collective-permute-start(f32[64,128]{1,0:T(8,128)S(1)} %fusion.15), channel_id=1, source_target_pairs={{0,12},{4,0},{8,4},{12,8},{1,13},{5,1},{9,5},{13,9},{2,14},{6,2},{... | collective-permute-start | bytes 98312 | tf_op jit(solution)/shard_map/ppermute | solution.py:20
  90.7 4.8 %collective-permute-start.17 = (bf16[64,128]{1,0:T(8,128)(2,1)S(1)}, bf16[64,128]{1,0:T(8,128)(2,1)S(1)}, u32[]{:S(2)}, u32[]{:S(2)}) collective-permute-start(bf16[64,128]{1,0:T(8,128)(2,1)S(1)} %get-tuple-element.39), channel_id=1, source_target_pairs={{0,1},{1,2},{2,3},{3,0},{4,5},{5,6},{6,7},{7,4},{8,9},{9,10},{10,1... | collective-permute-start | bytes 49160 | tf_op jit(solution)/shard_map/ppermute | solution.py:20
  92.5 3.6 %collective-permute-start.18 = (bf16[64,128]{1,0:T(8,128)(2,1)S(1)}, bf16[64,128]{1,0:T(8,128)(2,1)S(1)}, u32[]{:S(2)}, u32[]{:S(2)}) collective-permute-start(bf16[64,128]{1,0:T(8,128)(2,1)S(1)} %get-tuple-element.39), channel_id=1, source_target_pairs={{0,2},{1,3},{2,0},{3,1},{4,6},{5,7},{6,4},{7,5},{8,10},{9,11},{10,... | collective-permute-start | bytes 49160 | tf_op jit(solution)/shard_map/ppermute | solution.py:20
  94.0 2.6 %collective-permute-start.19 = (bf16[64,128]{1,0:T(8,128)(2,1)S(1)}, bf16[64,128]{1,0:T(8,128)(2,1)S(1)}, u32[]{:S(2)}, u32[]{:S(2)}) collective-permute-start(bf16[64,128]{1,0:T(8,128)(2,1)S(1)} %get-tuple-element.39), channel_id=1, source_target_pairs={{0,3},{1,0},{2,1},{3,2},{4,7},{5,4},{6,5},{7,6},{8,11},{9,8},{10,9... | collective-permute-start | bytes 49160 | tf_op jit(solution)/shard_map/ppermute | solution.py:20
  96.6 3.2 %collective-permute-start.20 = (bf16[4,64,128]{2,1,0:T(8,128)(2,1)S(1)}, bf16[4,64,128]{2,1,0:T(8,128)(2,1)S(1)}, u32[]{:S(2)}, u32[]{:S(2)}) collective-permute-start(bf16[4,64,128]{2,1,0:T(8,128)(2,1)S(1)} %get-tuple-element.30), channel_id=1, source_target_pairs={{0,16},{16,0},{1,17},{17,1},{2,18},{18,2},{3,19},{19,3},{4,20},{20... | collective-permute-start | bytes 196616 | tf_op jit(solution)/shard_map/ppermute | solution.py:20
  100.1 4.2 %collective-permute-start.21 = (f32[64,128]{1,0:T(8,128)S(1)}, f32[64,128]{1,0:T(8,128)S(1)}, u32[]{:S(2)}, u32[]{:S(2)}) collective-permute-start(f32[64,128]{1,0:T(8,128)S(1)} %fusion.12), channel_id=1, source_target_pairs={{0,4},{4,8},{8,12},{12,0},{1,5},{5,9},{9,13},{13,1},{2,6},{6,10},{... | collective-permute-start | bytes 98312 | tf_op jit(solution)/shard_map/ppermute | solution.py:20
  103.3 3.0 %collective-permute-start.22 = (f32[64,128]{1,0:T(8,128)S(1)}, f32[64,128]{1,0:T(8,128)S(1)}, u32[]{:S(2)}, u32[]{:S(2)}) collective-permute-start(f32[64,128]{1,0:T(8,128)S(1)} %fusion.12), channel_id=1, source_target_pairs={{0,8},{4,12},{8,0},{12,4},{1,9},{5,13},{9,1},{13,5},{2,10},{6,14},... | collective-permute-start | bytes 98312 | tf_op jit(solution)/shard_map/ppermute | solution.py:20
  103.9 3.3 %collective-permute-start.23 = (f32[64,128]{1,0:T(8,128)S(1)}, f32[64,128]{1,0:T(8,128)S(1)}, u32[]{:S(2)}, u32[]{:S(2)}) collective-permute-start(f32[64,128]{1,0:T(8,128)S(1)} %fusion.12), channel_id=1, source_target_pairs={{0,12},{4,0},{8,4},{12,8},{1,13},{5,1},{9,5},{13,9},{2,14},{6,2},{... | collective-permute-start | bytes 98312 | tf_op jit(solution)/shard_map/ppermute | solution.py:20
  107.5 4.9 %collective-permute-start.24 = (bf16[64,128]{1,0:T(8,128)(2,1)S(1)}, bf16[64,128]{1,0:T(8,128)(2,1)S(1)}, u32[]{:S(2)}, u32[]{:S(2)}) collective-permute-start(bf16[64,128]{1,0:T(8,128)(2,1)S(1)} %get-tuple-element.41), channel_id=1, source_target_pairs={{0,1},{1,2},{2,3},{3,0},{4,5},{5,6},{6,7},{7,4},{8,9},{9,10},{10,1... | collective-permute-start | bytes 49160 | tf_op jit(solution)/shard_map/ppermute | solution.py:20
  107.8 4.6 %collective-permute-start.25 = (bf16[64,128]{1,0:T(8,128)(2,1)S(1)}, bf16[64,128]{1,0:T(8,128)(2,1)S(1)}, u32[]{:S(2)}, u32[]{:S(2)}) collective-permute-start(bf16[64,128]{1,0:T(8,128)(2,1)S(1)} %get-tuple-element.41), channel_id=1, source_target_pairs={{0,2},{1,3},{2,0},{3,1},{4,6},{5,7},{6,4},{7,5},{8,10},{9,11},{10,... | collective-permute-start | bytes 49160 | tf_op jit(solution)/shard_map/ppermute | solution.py:20
  110.1 2.6 %collective-permute-start.26 = (bf16[64,128]{1,0:T(8,128)(2,1)S(1)}, bf16[64,128]{1,0:T(8,128)(2,1)S(1)}, u32[]{:S(2)}, u32[]{:S(2)}) collective-permute-start(bf16[64,128]{1,0:T(8,128)(2,1)S(1)} %get-tuple-element.41), channel_id=1, source_target_pairs={{0,3},{1,0},{2,1},{3,2},{4,7},{5,4},{6,5},{7,6},{8,11},{9,8},{10,9... | collective-permute-start | bytes 49160 | tf_op jit(solution)/shard_map/ppermute | solution.py:20
  112.7 3.2 %collective-permute-start.27 = (bf16[4,64,128]{2,1,0:T(8,128)(2,1)S(1)}, bf16[4,64,128]{2,1,0:T(8,128)(2,1)S(1)}, u32[]{:S(2)}, u32[]{:S(2)}) collective-permute-start(bf16[4,64,128]{2,1,0:T(8,128)(2,1)S(1)} %get-tuple-element.28), channel_id=1, source_target_pairs={{0,16},{16,0},{1,17},{17,1},{2,18},{18,2},{3,19},{19,3},{4,20},{20... | collective-permute-start | bytes 196616 | tf_op jit(solution)/shard_map/ppermute | solution.py:20
  116.2 3.9 %collective-permute-start.28 = (f32[64,128]{1,0:T(8,128)S(1)}, f32[64,128]{1,0:T(8,128)S(1)}, u32[]{:S(2)}, u32[]{:S(2)}) collective-permute-start(f32[64,128]{1,0:T(8,128)S(1)} %fusion.9), channel_id=1, source_target_pairs={{0,4},{4,8},{8,12},{12,0},{1,5},{5,9},{9,13},{13,1},{2,6},{6,10},{... | collective-permute-start | bytes 98312 | tf_op jit(solution)/shard_map/ppermute | solution.py:20
  119.1 3.2 %collective-permute-start.29 = (f32[64,128]{1,0:T(8,128)S(1)}, f32[64,128]{1,0:T(8,128)S(1)}, u32[]{:S(2)}, u32[]{:S(2)}) collective-permute-start(f32[64,128]{1,0:T(8,128)S(1)} %fusion.9), channel_id=1, source_target_pairs={{0,8},{4,12},{8,0},{12,4},{1,9},{5,13},{9,1},{13,5},{2,10},{6,14},... | collective-permute-start | bytes 98312 | tf_op jit(solution)/shard_map/ppermute | solution.py:20
  120.1 3.3 %collective-permute-start.30 = (f32[64,128]{1,0:T(8,128)S(1)}, f32[64,128]{1,0:T(8,128)S(1)}, u32[]{:S(2)}, u32[]{:S(2)}) collective-permute-start(f32[64,128]{1,0:T(8,128)S(1)} %fusion.9), channel_id=1, source_target_pairs={{0,12},{4,0},{8,4},{12,8},{1,13},{5,1},{9,5},{13,9},{2,14},{6,2},{... | collective-permute-start | bytes 98312 | tf_op jit(solution)/shard_map/ppermute | solution.py:20
  (4 other events, 35.5 us)

commit v15 on v14

--- a/solution.py
+++ b/solution.py
@@ -118,8 +118,10 @@
     first_rounded, weights_mine, weights_above, known, spread = lax.optimization_barrier(
         (first_rounded, weights_mine, weights_above, known, spread)
     )
-    rows = jnp.sum(lax.all_to_all(spread, OWNERS, 0, 0, tiled=True), axis=0)
-    rows_hi, rows_lo = split_bf16(jnp.dot(precond_mine, rows, precision=lax.Precision.HIGHEST))
+    received = lax.all_to_all(spread, OWNERS, 0, 0, tiled=True).reshape(nodes, nodes)
+    precond_tiled = jnp.tile(precond_mine, (1, owners))
+    rows = jnp.dot(precond_tiled, received, precision=lax.Precision.HIGHEST)
+    rows_hi, rows_lo = split_bf16(rows)
     node = jnp.arange(nodes, dtype=jnp.int32)
     source = jnp.repeat(ring_owner_order(), block_nodes) * block_nodes + node % block_nodes
     order = (node[:, None] == source[None, :]).astype(jnp.bfloat16)

time: 125 us -> 125 us (level)
  matrix products: 26.3 us -> 28.1 us
  other arithmetic: 5.71 us -> 4.4 us
    dot_general x1, matrix products: 0.21 us -> 2.01 us  [body(): rows = jnp.dot(precond_tiled, received, precision=lax.Precision.HIGHEST)]
    reduce_sum x1 -> x0, other arithmetic: 1.31 us -> none  [body(): rows = jnp.sum(lax.all_to_all(spread, OWNERS, 0, 0, tiled=True), axis=0)]
where the time goes in v15:
time: 125 us
  waiting for transfers between devices  50.3 us (40%)
  starting transfers between devices  41.2 us (33%)
  matrix products  28.1 us (22%)
  other arithmetic  4.4 us (4%)
    ppermute x31, starting transfers between devices, ring_parts(): parts.append(lax.ppermute(block, axis, route))  37 us
    ppermute x31, waiting for transfers between devices, ring_parts(): parts.append(lax.ppermute(block, axis, route))  26.1 us
    all_to_all x1, waiting for transfers between devices, body(): lax.all_to_all(spread, OWNERS, 0, 0, tiled=True).reshape(nodes, nodes)  24.2 us
    dot_general x1, matrix products, schur_rows(): solved = jnp.dot(inverse, coupled, preferred_element_type=jnp.float32)  10.1 us
    all_to_all x1, starting transfers between devices, body(): lax.all_to_all(spread, OWNERS, 0, 0, tiled=True).reshape(nodes, nodes)  4.25 us
    dot_general x1, matrix products, moved(): jnp.dot(rows.astype(jnp.bfloat16), place, preferred_element_type=jnp.floa...  3.36 us
    dot_general x1, matrix products, schur_rows(): lax.dot_general(coupled, solved_hi, contract, preferred_element_type=jnp....  2.53 us
  transfers between devices with their start and end apart: 32, of which 23 were waited for; matrix products, arithmetic and copies ran while one was open for 21% of the time, Pallas kernels for 0%

profile of v15, /device:TPU:1, one launch (start us, length us, event | category | flops | bytes accessed | tf_op | source)
XLA Modules:
  0.0 124.8 jit_solution(6901807124661575356)
XLA Ops:
  1.8 2.6 %collective-permute-start.4 = (f32[64,256]{1,0:T(8,128)S(1)}, f32[64,256]{1,0:T(8,128)S(1)}, u32[]{:S(2)}, u32[]{:S(2)}) collective-permute-start(f32[64,256]{1,0:T(8,128)S(1)} %pad_maximum_fusion.15), channel_id=1, source_target_pairs={{0,4},{4,8},{8,12},{12,0},{1,5},{5,9},{9,13},{13,1},{2,6},{6,10},{... | collective-permute-start | bytes 196616 | tf_op jit(solution)/shard_map/ppermute | solution.py:20
  5.3 1.3 %collective-permute-start = (bf16[64,128]{1,0:T(8,128)(2,1)S(1)}, bf16[64,128]{1,0:T(8,128)(2,1)S(1)}, u32[]{:S(2)}, u32[]{:S(2)}) collective-permute-start(bf16[64,128]{1,0:T(8,128)(2,1)S(1)} %get-tuple-element.36), channel_id=1, source_target_pairs={{0,1},{1,2},{2,3},{3,0},{4,5},{5,6},{6,7},{7,4},{8,9},{9,10},{10,1... | collective-permute-start | bytes 49160 | tf_op jit(solution)/shard_map/ppermute | solution.py:20
  6.6 2.3 %collective-permute-start.1 = (bf16[64,128]{1,0:T(8,128)(2,1)S(1)}, bf16[64,128]{1,0:T(8,128)(2,1)S(1)}, u32[]{:S(2)}, u32[]{:S(2)}) collective-permute-start(bf16[64,128]{1,0:T(8,128)(2,1)S(1)} %get-tuple-element.36), channel_id=1, source_target_pairs={{0,2},{1,3},{2,0},{3,1},{4,6},{5,7},{6,4},{7,5},{8,10},{9,11},{10,... | collective-permute-start | bytes 49160 | tf_op jit(solution)/shard_map/ppermute | solution.py:20
  8.9 1.1 collective-permute-start.2
  11.6 1.7 %convolution_convert_fusion = bf16[512,2560]{1,0:T(8,128)(2,1)S(1)} fusion(bf16[1,1,2560,512]{3,2,1,0:T(8,128)(2,1)S(1)} %copy-done, s32[512]{0:T(512)S(1)} %fusion.53), kind=kOutput, calls=%fused_computation.5 | convolution fusion | flops 1344012288 | bytes 5244928 | tf_op jit(solution)/shard_map/dot_general | solution.py:52
  13.3 10.1 %fusion = f32[512,2560]{1,0:T(8,128)S(1)} fusion(bf16[512,2560]{1,0:T(8,128)(2,1)S(1)} %convolution_convert_fusion, bf16[1,1,2560,2560]{3,2,1,0:T(8,128)(2,1)} %param.17), kind=kOutput, calls=%fused_computation | convolution fusion | flops 6710886400 | bytes 20971520 | tf_op jit(solution)/shard_map/dot_general | solution.py:54
  23.4 1.6 %fusion.3 = f32[512,512]{1,0:T(8,128)S(1)} fusion(bf16[512,2560]{1,0:T(8,128)(2,1)S(1)} %convolution_convert_fusion, f32[512,2560]{1,0:T(8,128)S(1)} %fusion), kind=kOutput, calls=%fused_computation.6 | convolution fusion | flops 1346109440 | bytes 8912896 | tf_op jit(solution)/shard_map/dot_general | solution.py:57
  25.0 2.5 %fusion.7 = f32[512,512]{1,0:T(8,128)} fusion(f32[512,512]{1,0:T(8,128)S(1)} %fusion.3, bf16[512,2560]{1,0:T(8,128)(2,1)S(1)} %convolution_convert_fusion, f32[512,2560]{1,0:T(8,128)S(1)} %fusion), kind=kOutput, calls=%fused_computation.10 | convolution fusion | flops 1345060864 | bytes 9961472 | tf_op jit(solution)/shard_map/dot_general | solution.py:56
  27.5 3.4 %convolution_subtract_fusion = f32[512,512]{1,0:T(8,128)} fusion(f32[512,512]{1,0:T(8,128)} %fusion.7, bf16[1,1,512,512]{3,2,1,0:T(8,128)(2,1)} %param.15, s32[512]{0:T(512)S(1)} %fusion.53), kind=kOutput, calls=%fused_computation.9 | convolution fusion | flops 537919488 | bytes 2623488 | tf_op jit(solution)/shard_map/dot_general | solution.py:49
  30.9 1.2 collective-permute-start.5
  32.1 1.3 %collective-permute-start.3 = (bf16[4,64,128]{2,1,0:T(8,128)(2,1)S(1)}, bf16[4,64,128]{2,1,0:T(8,128)(2,1)S(1)}, u32[]{:S(2)}, u32[]{:S(2)}) collective-permute-start(bf16[4,64,128]{2,1,0:T(8,128)(2,1)S(1)} %get-tuple-element.34), channel_id=1, source_target_pairs={{0,16},{16,0},{1,17},{17,1},{2,18},{18,2},{3,19},{19,3},{4,20},{20... | collective-permute-start | bytes 196616 | tf_op jit(solution)/shard_map/ppermute | solution.py:20
  35.8 4.2 %all-to-all-start = ((f32[8,64,512]{2,1,0:T(8,128)}), f32[8,64,512]{2,1,0:T(8,128)}, u32[]{:S(2)}, u32[]{:S(2)}) async-start(f32[8,64,512]{2,1,0:T(8,128)} %bitcast.202), calls=%async_computation | async-start | bytes 2097152 | tf_op jit(solution)/shard_map/all_to_all | solution.py:121
  40.4 24.2 %all-to-all-done = f32[8,64,512]{2,1,0:T(8,128)} async-done(((f32[8,64,512]{2,1,0:T(8,128)}), f32[8,64,512]{2,1,0:T(8,128)}, u32[]{:S(2)}, u32[]{:S(2)}) %all-to-all-start) | async-done | bytes 1048608 | tf_op jit(solution)/shard_map/all_to_all | solution.py:121
  64.7 2.0 %convolution_bitcast_fusion = f32[64,512]{1,0:T(8,128)S(1)} fusion(f32[8,64,512]{2,1,0:T(8,128)} %all-to-all-done, f32[64,64]{1,0:T(8,128)S(1)} %get-tuple-element.44), kind=kOutput, calls=%fused_computation.12 | convolution fusion | flops 201326592 | bytes 1196032 | tf_op jit(solution)/shard_map/dot_general | solution.py:123
  67.6 4.1 %collective-permute-start.7 = (f32[64,128]{1,0:T(8,128)S(1)}, f32[64,128]{1,0:T(8,128)S(1)}, u32[]{:S(2)}, u32[]{:S(2)}) collective-permute-start(f32[64,128]{1,0:T(8,128)S(1)} %fusion.18), channel_id=1, source_target_pairs={{0,4},{4,8},{8,12},{12,0},{1,5},{5,9},{9,13},{13,1},{2,6},{6,10},{... | collective-permute-start | bytes 98312 | tf_op jit(solution)/shard_map/ppermute | solution.py:20
  72.7 1.7 %collective-permute-done.8 = f32[64,128]{1,0:T(8,128)S(1)} collective-permute-done((f32[64,128]{1,0:T(8,128)S(1)}, f32[64,128]{1,0:T(8,128)S(1)}, u32[]{:S(2)}, u32[]{:S(2)}) %collective-permute-start.8) | collective-permute-done | bytes 32800 | tf_op jit(solution)/shard_map/ppermute | solution.py:20
  75.7 3.2 %collective-permute-start.12 = (bf16[64,128]{1,0:T(8,128)(2,1)S(1)}, bf16[64,128]{1,0:T(8,128)(2,1)S(1)}, u32[]{:S(2)}, u32[]{:S(2)}) collective-permute-start(bf16[64,128]{1,0:T(8,128)(2,1)S(1)} %get-tuple-element.37), channel_id=1, source_target_pairs={{0,3},{1,0},{2,1},{3,2},{4,7},{5,4},{6,5},{7,6},{8,11},{9,8},{10,9... | collective-permute-start | bytes 49160 | tf_op jit(solution)/shard_map/ppermute | solution.py:20
  81.2 2.7 %collective-permute-done.13 = bf16[4,64,128]{2,1,0:T(8,128)(2,1)S(1)} collective-permute-done((bf16[4,64,128]{2,1,0:T(8,128)(2,1)S(1)}, bf16[4,64,128]{2,1,0:T(8,128)(2,1)S(1)}, u32[]{:S(2)}, u32[]{:S(2)}) %collective-permute-start.13) | collective-permute-done | bytes 65568 | tf_op jit(solution)/shard_map/ppermute | solution.py:20
  84.3 2.7 %collective-permute-start.14 = (f32[64,128]{1,0:T(8,128)S(1)}, f32[64,128]{1,0:T(8,128)S(1)}, u32[]{:S(2)}, u32[]{:S(2)}) collective-permute-start(f32[64,128]{1,0:T(8,128)S(1)} %fusion.15), channel_id=1, source_target_pairs={{0,4},{4,8},{8,12},{12,0},{1,5},{5,9},{9,13},{13,1},{2,6},{6,10},{... | collective-permute-start | bytes 98312 | tf_op jit(solution)/shard_map/ppermute | solution.py:20
  88.0 2.1 %collective-permute-done.15 = f32[64,128]{1,0:T(8,128)S(1)} collective-permute-done((f32[64,128]{1,0:T(8,128)S(1)}, f32[64,128]{1,0:T(8,128)S(1)}, u32[]{:S(2)}, u32[]{:S(2)}) %collective-permute-start.15) | collective-permute-done | bytes 32800 | tf_op jit(solution)/shard_map/ppermute | solution.py:20
  91.2 1.8 %collective-permute-start.17 = (bf16[64,128]{1,0:T(8,128)(2,1)S(1)}, bf16[64,128]{1,0:T(8,128)(2,1)S(1)}, u32[]{:S(2)}, u32[]{:S(2)}) collective-permute-start(bf16[64,128]{1,0:T(8,128)(2,1)S(1)} %get-tuple-element.39), channel_id=1, source_target_pairs={{0,1},{1,2},{2,3},{3,0},{4,5},{5,6},{6,7},{7,4},{8,9},{9,10},{10,1... | collective-permute-start | bytes 49160 | tf_op jit(solution)/shard_map/ppermute | solution.py:20
  93.0 1.5 %collective-permute-start.18 = (bf16[64,128]{1,0:T(8,128)(2,1)S(1)}, bf16[64,128]{1,0:T(8,128)(2,1)S(1)}, u32[]{:S(2)}, u32[]{:S(2)}) collective-permute-start(bf16[64,128]{1,0:T(8,128)(2,1)S(1)} %get-tuple-element.39), channel_id=1, source_target_pairs={{0,2},{1,3},{2,0},{3,1},{4,6},{5,7},{6,4},{7,5},{8,10},{9,11},{10,... | collective-permute-start | bytes 49160 | tf_op jit(solution)/shard_map/ppermute | solution.py:20
  97.6 2.7 %collective-permute-done.20 = bf16[4,64,128]{2,1,0:T(8,128)(2,1)S(1)} collective-permute-done((bf16[4,64,128]{2,1,0:T(8,128)(2,1)S(1)}, bf16[4,64,128]{2,1,0:T(8,128)(2,1)S(1)}, u32[]{:S(2)}, u32[]{:S(2)}) %collective-permute-start.20) | collective-permute-done | bytes 65568 | tf_op jit(solution)/shard_map/ppermute | solution.py:20
  100.6 3.2 %collective-permute-start.21 = (f32[64,128]{1,0:T(8,128)S(1)}, f32[64,128]{1,0:T(8,128)S(1)}, u32[]{:S(2)}, u32[]{:S(2)}) collective-permute-start(f32[64,128]{1,0:T(8,128)S(1)} %fusion.12), channel_id=1, source_target_pairs={{0,4},{4,8},{8,12},{12,0},{1,5},{5,9},{9,13},{13,1},{2,6},{6,10},{... | collective-permute-start | bytes 98312 | tf_op jit(solution)/shard_map/ppermute | solution.py:20
  104.8 1.9 %collective-permute-done.22 = f32[64,128]{1,0:T(8,128)S(1)} collective-permute-done((f32[64,128]{1,0:T(8,128)S(1)}, f32[64,128]{1,0:T(8,128)S(1)}, u32[]{:S(2)}, u32[]{:S(2)}) %collective-permute-start.22) | collective-permute-done | bytes 32800 | tf_op jit(solution)/shard_map/ppermute | solution.py:20
  108.3 2.3 %collective-permute-start.25 = (bf16[64,128]{1,0:T(8,128)(2,1)S(1)}, bf16[64,128]{1,0:T(8,128)(2,1)S(1)}, u32[]{:S(2)}, u32[]{:S(2)}) collective-permute-start(bf16[64,128]{1,0:T(8,128)(2,1)S(1)} %get-tuple-element.41), channel_id=1, source_target_pairs={{0,2},{1,3},{2,0},{3,1},{4,6},{5,7},{6,4},{7,5},{8,10},{9,11},{10,... | collective-permute-start | bytes 49160 | tf_op jit(solution)/shard_map/ppermute | solution.py:20
  111.9 1.0 collective-permute-done.24
  113.6 2.7 %collective-permute-done.27 = bf16[4,64,128]{2,1,0:T(8,128)(2,1)S(1)} collective-permute-done((bf16[4,64,128]{2,1,0:T(8,128)(2,1)S(1)}, bf16[4,64,128]{2,1,0:T(8,128)(2,1)S(1)}, u32[]{:S(2)}, u32[]{:S(2)}) %collective-permute-start.27) | collective-permute-done | bytes 65568 | tf_op jit(solution)/shard_map/ppermute | solution.py:20
  116.7 2.9 %collective-permute-start.28 = (f32[64,128]{1,0:T(8,128)S(1)}, f32[64,128]{1,0:T(8,128)S(1)}, u32[]{:S(2)}, u32[]{:S(2)}) collective-permute-start(f32[64,128]{1,0:T(8,128)S(1)} %fusion.9), channel_id=1, source_target_pairs={{0,4},{4,8},{8,12},{12,0},{1,5},{5,9},{9,13},{13,1},{2,6},{6,10},{... | collective-permute-start | bytes 98312 | tf_op jit(solution)/shard_map/ppermute | solution.py:20
  119.6 1.0 collective-permute-start.29
  120.6 2.2 %collective-permute-done.29 = f32[64,128]{1,0:T(8,128)S(1)} collective-permute-done((f32[64,128]{1,0:T(8,128)S(1)}, f32[64,128]{1,0:T(8,128)S(1)}, u32[]{:S(2)}, u32[]{:S(2)}) %collective-permute-start.29) | collective-permute-done | bytes 32800 | tf_op jit(solution)/shard_map/ppermute | solution.py:20
  122.9 1.1 collective-permute-done.30
  (104 shorter events, 24.1 us)
Async XLA Ops:
  1.7 31.7 %collective-permute-start.6 = (f32[64,256]{1,0:T(8,128)S(1)}, f32[64,256]{1,0:T(8,128)S(1)}, u32[]{:S(2)}, u32[]{:S(2)}) collective-permute-start(f32[64,256]{1,0:T(8,128)S(1)} %pad_maximum_fusion.15), channel_id=1, source_target_pairs={{0,12},{4,0},{8,4},{12,8},{1,13},{5,1},{9,5},{13,9},{2,14},{6,2},{... | collective-permute-start | bytes 196616 | tf_op jit(solution)/shard_map/ppermute | solution.py:20
  1.8 31.6 %collective-permute-start.4 = (f32[64,256]{1,0:T(8,128)S(1)}, f32[64,256]{1,0:T(8,128)S(1)}, u32[]{:S(2)}, u32[]{:S(2)}) collective-permute-start(f32[64,256]{1,0:T(8,128)S(1)} %pad_maximum_fusion.15), channel_id=1, source_target_pairs={{0,4},{4,8},{8,12},{12,0},{1,5},{5,9},{9,13},{13,1},{2,6},{6,10},{... | collective-permute-start | bytes 196616 | tf_op jit(solution)/shard_map/ppermute | solution.py:20
  5.3 25.6 %collective-permute-start = (bf16[64,128]{1,0:T(8,128)(2,1)S(1)}, bf16[64,128]{1,0:T(8,128)(2,1)S(1)}, u32[]{:S(2)}, u32[]{:S(2)}) collective-permute-start(bf16[64,128]{1,0:T(8,128)(2,1)S(1)} %get-tuple-element.36), channel_id=1, source_target_pairs={{0,1},{1,2},{2,3},{3,0},{4,5},{5,6},{6,7},{7,4},{8,9},{9,10},{10,1... | collective-permute-start | bytes 49160 | tf_op jit(solution)/shard_map/ppermute | solution.py:20
  6.6 25.5 %collective-permute-start.1 = (bf16[64,128]{1,0:T(8,128)(2,1)S(1)}, bf16[64,128]{1,0:T(8,128)(2,1)S(1)}, u32[]{:S(2)}, u32[]{:S(2)}) collective-permute-start(bf16[64,128]{1,0:T(8,128)(2,1)S(1)} %get-tuple-element.36), channel_id=1, source_target_pairs={{0,2},{1,3},{2,0},{3,1},{4,6},{5,7},{6,4},{7,5},{8,10},{9,11},{10,... | collective-permute-start | bytes 49160 | tf_op jit(solution)/shard_map/ppermute | solution.py:20
  8.9 23.2 %collective-permute-start.2 = (bf16[64,128]{1,0:T(8,128)(2,1)S(1)}, bf16[64,128]{1,0:T(8,128)(2,1)S(1)}, u32[]{:S(2)}, u32[]{:S(2)}) collective-permute-start(bf16[64,128]{1,0:T(8,128)(2,1)S(1)} %get-tuple-element.36), channel_id=1, source_target_pairs={{0,3},{1,0},{2,1},{3,2},{4,7},{5,4},{6,5},{7,6},{8,11},{9,8},{10,9... | collective-permute-start | bytes 49160 | tf_op jit(solution)/shard_map/ppermute | solution.py:20
  30.9 3.2 %collective-permute-start.5 = (f32[64,256]{1,0:T(8,128)S(1)}, f32[64,256]{1,0:T(8,128)S(1)}, u32[]{:S(2)}, u32[]{:S(2)}) collective-permute-start(f32[64,256]{1,0:T(8,128)S(1)} %pad_maximum_fusion.15), channel_id=1, source_target_pairs={{0,8},{4,12},{8,0},{12,4},{1,9},{5,13},{9,1},{13,5},{2,10},{6,14},... | collective-permute-start | bytes 196616 | tf_op jit(solution)/shard_map/ppermute | solution.py:20
  32.1 3.7 %collective-permute-start.3 = (bf16[4,64,128]{2,1,0:T(8,128)(2,1)S(1)}, bf16[4,64,128]{2,1,0:T(8,128)(2,1)S(1)}, u32[]{:S(2)}, u32[]{:S(2)}) collective-permute-start(bf16[4,64,128]{2,1,0:T(8,128)(2,1)S(1)} %get-tuple-element.34), channel_id=1, source_target_pairs={{0,16},{16,0},{1,17},{17,1},{2,18},{18,2},{3,19},{19,3},{4,20},{20... | collective-permute-start | bytes 196616 | tf_op jit(solution)/shard_map/ppermute | solution.py:20
  35.8 28.8 %all-to-all-start = ((f32[8,64,512]{2,1,0:T(8,128)}), f32[8,64,512]{2,1,0:T(8,128)}, u32[]{:S(2)}, u32[]{:S(2)}) async-start(f32[8,64,512]{2,1,0:T(8,128)} %bitcast.202), calls=%async_computation | async-start | bytes 2097152 | tf_op jit(solution)/shard_map/all_to_all | solution.py:121
  67.6 5.1 %collective-permute-start.7 = (f32[64,128]{1,0:T(8,128)S(1)}, f32[64,128]{1,0:T(8,128)S(1)}, u32[]{:S(2)}, u32[]{:S(2)}) collective-permute-start(f32[64,128]{1,0:T(8,128)S(1)} %fusion.18), channel_id=1, source_target_pairs={{0,4},{4,8},{8,12},{12,0},{1,5},{5,9},{9,13},{13,1},{2,6},{6,10},{... | collective-permute-start | bytes 98312 | tf_op jit(solution)/shard_map/ppermute | solution.py:20
  71.7 2.8 %collective-permute-start.8 = (f32[64,128]{1,0:T(8,128)S(1)}, f32[64,128]{1,0:T(8,128)S(1)}, u32[]{:S(2)}, u32[]{:S(2)}) collective-permute-start(f32[64,128]{1,0:T(8,128)S(1)} %fusion.18), channel_id=1, source_target_pairs={{0,8},{4,12},{8,0},{12,4},{1,9},{5,13},{9,1},{13,5},{2,10},{6,14},... | collective-permute-start | bytes 98312 | tf_op jit(solution)/shard_map/ppermute | solution.py:20
  72.0 3.3 %collective-permute-start.9 = (f32[64,128]{1,0:T(8,128)S(1)}, f32[64,128]{1,0:T(8,128)S(1)}, u32[]{:S(2)}, u32[]{:S(2)}) collective-permute-start(f32[64,128]{1,0:T(8,128)S(1)} %fusion.18), channel_id=1, source_target_pairs={{0,12},{4,0},{8,4},{12,8},{1,13},{5,1},{9,5},{13,9},{2,14},{6,2},{... | collective-permute-start | bytes 98312 | tf_op jit(solution)/shard_map/ppermute | solution.py:20
  75.6 4.4 %collective-permute-start.10 = (bf16[64,128]{1,0:T(8,128)(2,1)S(1)}, bf16[64,128]{1,0:T(8,128)(2,1)S(1)}, u32[]{:S(2)}, u32[]{:S(2)}) collective-permute-start(bf16[64,128]{1,0:T(8,128)(2,1)S(1)} %get-tuple-element.37), channel_id=1, source_target_pairs={{0,1},{1,2},{2,3},{3,0},{4,5},{5,6},{6,7},{7,4},{8,9},{9,10},{10,1... | collective-permute-start | bytes 49160 | tf_op jit(solution)/shard_map/ppermute | solution.py:20
  75.7 4.4 %collective-permute-start.11 = (bf16[64,128]{1,0:T(8,128)(2,1)S(1)}, bf16[64,128]{1,0:T(8,128)(2,1)S(1)}, u32[]{:S(2)}, u32[]{:S(2)}) collective-permute-start(bf16[64,128]{1,0:T(8,128)(2,1)S(1)} %get-tuple-element.37), channel_id=1, source_target_pairs={{0,2},{1,3},{2,0},{3,1},{4,6},{5,7},{6,4},{7,5},{8,10},{9,11},{10,... | collective-permute-start | bytes 49160 | tf_op jit(solution)/shard_map/ppermute | solution.py:20
  75.7 5.0 %collective-permute-start.12 = (bf16[64,128]{1,0:T(8,128)(2,1)S(1)}, bf16[64,128]{1,0:T(8,128)(2,1)S(1)}, u32[]{:S(2)}, u32[]{:S(2)}) collective-permute-start(bf16[64,128]{1,0:T(8,128)(2,1)S(1)} %get-tuple-element.37), channel_id=1, source_target_pairs={{0,3},{1,0},{2,1},{3,2},{4,7},{5,4},{6,5},{7,6},{8,11},{9,8},{10,9... | collective-permute-start | bytes 49160 | tf_op jit(solution)/shard_map/ppermute | solution.py:20
  80.7 3.2 %collective-permute-start.13 = (bf16[4,64,128]{2,1,0:T(8,128)(2,1)S(1)}, bf16[4,64,128]{2,1,0:T(8,128)(2,1)S(1)}, u32[]{:S(2)}, u32[]{:S(2)}) collective-permute-start(bf16[4,64,128]{2,1,0:T(8,128)(2,1)S(1)} %get-tuple-element.32), channel_id=1, source_target_pairs={{0,16},{16,0},{1,17},{17,1},{2,18},{18,2},{3,19},{19,3},{4,20},{20... | collective-permute-start | bytes 196616 | tf_op jit(solution)/shard_map/ppermute | solution.py:20
  84.3 3.7 %collective-permute-start.14 = (f32[64,128]{1,0:T(8,128)S(1)}, f32[64,128]{1,0:T(8,128)S(1)}, u32[]{:S(2)}, u32[]{:S(2)}) collective-permute-start(f32[64,128]{1,0:T(8,128)S(1)} %fusion.15), channel_id=1, source_target_pairs={{0,4},{4,8},{8,12},{12,0},{1,5},{5,9},{9,13},{13,1},{2,6},{6,10},{... | collective-permute-start | bytes 98312 | tf_op jit(solution)/shard_map/ppermute | solution.py:20
  87.0 3.1 %collective-permute-start.15 = (f32[64,128]{1,0:T(8,128)S(1)}, f32[64,128]{1,0:T(8,128)S(1)}, u32[]{:S(2)}, u32[]{:S(2)}) collective-permute-start(f32[64,128]{1,0:T(8,128)S(1)} %fusion.15), channel_id=1, source_target_pairs={{0,8},{4,12},{8,0},{12,4},{1,9},{5,13},{9,1},{13,5},{2,10},{6,14},... | collective-permute-start | bytes 98312 | tf_op jit(solution)/shard_map/ppermute | solution.py:20
  87.6 3.3 %collective-permute-start.16 = (f32[64,128]{1,0:T(8,128)S(1)}, f32[64,128]{1,0:T(8,128)S(1)}, u32[]{:S(2)}, u32[]{:S(2)}) collective-permute-start(f32[64,128]{1,0:T(8,128)S(1)} %fusion.15), channel_id=1, source_target_pairs={{0,12},{4,0},{8,4},{12,8},{1,13},{5,1},{9,5},{13,9},{2,14},{6,2},{... | collective-permute-start | bytes 98312 | tf_op jit(solution)/shard_map/ppermute | solution.py:20
  91.2 4.8 %collective-permute-start.17 = (bf16[64,128]{1,0:T(8,128)(2,1)S(1)}, bf16[64,128]{1,0:T(8,128)(2,1)S(1)}, u32[]{:S(2)}, u32[]{:S(2)}) collective-permute-start(bf16[64,128]{1,0:T(8,128)(2,1)S(1)} %get-tuple-element.39), channel_id=1, source_target_pairs={{0,1},{1,2},{2,3},{3,0},{4,5},{5,6},{6,7},{7,4},{8,9},{9,10},{10,1... | collective-permute-start | bytes 49160 | tf_op jit(solution)/shard_map/ppermute | solution.py:20
  93.0 3.6 %collective-permute-start.18 = (bf16[64,128]{1,0:T(8,128)(2,1)S(1)}, bf16[64,128]{1,0:T(8,128)(2,1)S(1)}, u32[]{:S(2)}, u32[]{:S(2)}) collective-permute-start(bf16[64,128]{1,0:T(8,128)(2,1)S(1)} %get-tuple-element.39), channel_id=1, source_target_pairs={{0,2},{1,3},{2,0},{3,1},{4,6},{5,7},{6,4},{7,5},{8,10},{9,11},{10,... | collective-permute-start | bytes 49160 | tf_op jit(solution)/shard_map/ppermute | solution.py:20
  94.5 2.6 %collective-permute-start.19 = (bf16[64,128]{1,0:T(8,128)(2,1)S(1)}, bf16[64,128]{1,0:T(8,128)(2,1)S(1)}, u32[]{:S(2)}, u32[]{:S(2)}) collective-permute-start(bf16[64,128]{1,0:T(8,128)(2,1)S(1)} %get-tuple-element.39), channel_id=1, source_target_pairs={{0,3},{1,0},{2,1},{3,2},{4,7},{5,4},{6,5},{7,6},{8,11},{9,8},{10,9... | collective-permute-start | bytes 49160 | tf_op jit(solution)/shard_map/ppermute | solution.py:20
  97.1 3.2 %collective-permute-start.20 = (bf16[4,64,128]{2,1,0:T(8,128)(2,1)S(1)}, bf16[4,64,128]{2,1,0:T(8,128)(2,1)S(1)}, u32[]{:S(2)}, u32[]{:S(2)}) collective-permute-start(bf16[4,64,128]{2,1,0:T(8,128)(2,1)S(1)} %get-tuple-element.30), channel_id=1, source_target_pairs={{0,16},{16,0},{1,17},{17,1},{2,18},{18,2},{3,19},{19,3},{4,20},{20... | collective-permute-start | bytes 196616 | tf_op jit(solution)/shard_map/ppermute | solution.py:20
  100.6 4.2 %collective-permute-start.21 = (f32[64,128]{1,0:T(8,128)S(1)}, f32[64,128]{1,0:T(8,128)S(1)}, u32[]{:S(2)}, u32[]{:S(2)}) collective-permute-start(f32[64,128]{1,0:T(8,128)S(1)} %fusion.12), channel_id=1, source_target_pairs={{0,4},{4,8},{8,12},{12,0},{1,5},{5,9},{9,13},{13,1},{2,6},{6,10},{... | collective-permute-start | bytes 98312 | tf_op jit(solution)/shard_map/ppermute | solution.py:20
  103.8 3.0 %collective-permute-start.22 = (f32[64,128]{1,0:T(8,128)S(1)}, f32[64,128]{1,0:T(8,128)S(1)}, u32[]{:S(2)}, u32[]{:S(2)}) collective-permute-start(f32[64,128]{1,0:T(8,128)S(1)} %fusion.12), channel_id=1, source_target_pairs={{0,8},{4,12},{8,0},{12,4},{1,9},{5,13},{9,1},{13,5},{2,10},{6,14},... | collective-permute-start | bytes 98312 | tf_op jit(solution)/shard_map/ppermute | solution.py:20
  104.4 3.3 %collective-permute-start.23 = (f32[64,128]{1,0:T(8,128)S(1)}, f32[64,128]{1,0:T(8,128)S(1)}, u32[]{:S(2)}, u32[]{:S(2)}) collective-permute-start(f32[64,128]{1,0:T(8,128)S(1)} %fusion.12), channel_id=1, source_target_pairs={{0,12},{4,0},{8,4},{12,8},{1,13},{5,1},{9,5},{13,9},{2,14},{6,2},{... | collective-permute-start | bytes 98312 | tf_op jit(solution)/shard_map/ppermute | solution.py:20
  108.0 4.9 %collective-permute-start.24 = (bf16[64,128]{1,0:T(8,128)(2,1)S(1)}, bf16[64,128]{1,0:T(8,128)(2,1)S(1)}, u32[]{:S(2)}, u32[]{:S(2)}) collective-permute-start(bf16[64,128]{1,0:T(8,128)(2,1)S(1)} %get-tuple-element.41), channel_id=1, source_target_pairs={{0,1},{1,2},{2,3},{3,0},{4,5},{5,6},{6,7},{7,4},{8,9},{9,10},{10,1... | collective-permute-start | bytes 49160 | tf_op jit(solution)/shard_map/ppermute | solution.py:20
  108.3 4.6 %collective-permute-start.25 = (bf16[64,128]{1,0:T(8,128)(2,1)S(1)}, bf16[64,128]{1,0:T(8,128)(2,1)S(1)}, u32[]{:S(2)}, u32[]{:S(2)}) collective-permute-start(bf16[64,128]{1,0:T(8,128)(2,1)S(1)} %get-tuple-element.41), channel_id=1, source_target_pairs={{0,2},{1,3},{2,0},{3,1},{4,6},{5,7},{6,4},{7,5},{8,10},{9,11},{10,... | collective-permute-start | bytes 49160 | tf_op jit(solution)/shard_map/ppermute | solution.py:20
  110.6 2.6 %collective-permute-start.26 = (bf16[64,128]{1,0:T(8,128)(2,1)S(1)}, bf16[64,128]{1,0:T(8,128)(2,1)S(1)}, u32[]{:S(2)}, u32[]{:S(2)}) collective-permute-start(bf16[64,128]{1,0:T(8,128)(2,1)S(1)} %get-tuple-element.41), channel_id=1, source_target_pairs={{0,3},{1,0},{2,1},{3,2},{4,7},{5,4},{6,5},{7,6},{8,11},{9,8},{10,9... | collective-permute-start | bytes 49160 | tf_op jit(solution)/shard_map/ppermute | solution.py:20
  113.2 3.2 %collective-permute-start.27 = (bf16[4,64,128]{2,1,0:T(8,128)(2,1)S(1)}, bf16[4,64,128]{2,1,0:T(8,128)(2,1)S(1)}, u32[]{:S(2)}, u32[]{:S(2)}) collective-permute-start(bf16[4,64,128]{2,1,0:T(8,128)(2,1)S(1)} %get-tuple-element.28), channel_id=1, source_target_pairs={{0,16},{16,0},{1,17},{17,1},{2,18},{18,2},{3,19},{19,3},{4,20},{20... | collective-permute-start | bytes 196616 | tf_op jit(solution)/shard_map/ppermute | solution.py:20
  116.7 4.0 %collective-permute-start.28 = (f32[64,128]{1,0:T(8,128)S(1)}, f32[64,128]{1,0:T(8,128)S(1)}, u32[]{:S(2)}, u32[]{:S(2)}) collective-permute-start(f32[64,128]{1,0:T(8,128)S(1)} %fusion.9), channel_id=1, source_target_pairs={{0,4},{4,8},{8,12},{12,0},{1,5},{5,9},{9,13},{13,1},{2,6},{6,10},{... | collective-permute-start | bytes 98312 | tf_op jit(solution)/shard_map/ppermute | solution.py:20
  119.6 3.2 %collective-permute-start.29 = (f32[64,128]{1,0:T(8,128)S(1)}, f32[64,128]{1,0:T(8,128)S(1)}, u32[]{:S(2)}, u32[]{:S(2)}) collective-permute-start(f32[64,128]{1,0:T(8,128)S(1)} %fusion.9), channel_id=1, source_target_pairs={{0,8},{4,12},{8,0},{12,4},{1,9},{5,13},{9,1},{13,5},{2,10},{6,14},... | collective-permute-start | bytes 98312 | tf_op jit(solution)/shard_map/ppermute | solution.py:20
  120.6 3.3 %collective-permute-start.30 = (f32[64,128]{1,0:T(8,128)S(1)}, f32[64,128]{1,0:T(8,128)S(1)}, u32[]{:S(2)}, u32[]{:S(2)}) collective-permute-start(f32[64,128]{1,0:T(8,128)S(1)} %fusion.9), channel_id=1, source_target_pairs={{0,12},{4,0},{8,4},{12,8},{1,13},{5,1},{9,5},{13,9},{2,14},{6,2},{... | collective-permute-start | bytes 98312 | tf_op jit(solution)/shard_map/ppermute | solution.py:20
  (4 other events, 35.6 us)

commit v16 on v14

--- a/solution.py
+++ b/solution.py
@@ -22,15 +22,15 @@
 
 
 def gather_owners(block):
-    inner = ring_parts(block, "iface")
-    outer = ring_parts(inner, "sub")
+    inner = ring_parts(block, "sub")
+    outer = ring_parts(inner, "iface")
     return outer.reshape((-1,) + block.shape)
 
 
 def ring_owner_order():
     subs, ifaces = lax.axis_size("sub"), lax.axis_size("iface")
-    sub_back = (lax.axis_index("sub") - jnp.arange(subs)[:, None]) % subs
-    iface_back = (lax.axis_index("iface") - jnp.arange(ifaces)[None, :]) % ifaces
+    iface_back = (lax.axis_index("iface") - jnp.arange(ifaces)[:, None]) % ifaces
+    sub_back = (lax.axis_index("sub") - jnp.arange(subs)[None, :]) % subs
     return (sub_back * ifaces + iface_back).reshape(-1)
 
 

time: 125 us -> 126 us (level)
    ppermute x31, waiting for transfers between devices: 26.1 us -> 27.4 us  [ring_parts(): parts.append(lax.ppermute(block, axis, route))]
  transfers between devices with their start and end apart: 32 -> 32, of which waited for: 23 -> 24; matrix products, arithmetic and copies ran while one was open for 21% -> 19% of each run, Pallas kernels for 0% -> 0%
where the time goes in v16:
time: 126 us; the launch traced here: 125 us
  waiting for transfers between devices  51.2 us (41%)
  starting transfers between devices  41.3 us (33%)
  matrix products  26.3 us (21%)
  other arithmetic  5.7 us (5%)
    ppermute x31, starting transfers between devices, ring_parts(): parts.append(lax.ppermute(block, axis, route))  37.1 us
    ppermute x31, waiting for transfers between devices, ring_parts(): parts.append(lax.ppermute(block, axis, route))  27.4 us
    all_to_all x1, waiting for transfers between devices, body(): rows = jnp.sum(lax.all_to_all(spread, OWNERS, 0, 0, tiled=True), axis=0)  23.8 us
    dot_general x1, matrix products, schur_rows(): solved = jnp.dot(inverse, coupled, preferred_element_type=jnp.float32)  10.1 us
    all_to_all x1, starting transfers between devices, body(): rows = jnp.sum(lax.all_to_all(spread, OWNERS, 0, 0, tiled=True), axis=0)  4.25 us
    dot_general x1, matrix products, moved(): jnp.dot(rows.astype(jnp.bfloat16), place, preferred_element_type=jnp.floa...  3.36 us
    dot_general x1, matrix products, schur_rows(): lax.dot_general(coupled, solved_hi, contract, preferred_element_type=jnp....  2.53 us
  transfers between devices with their start and end apart: 32, of which 24 were waited for; matrix products, arithmetic and copies ran while one was open for 19% of the time, Pallas kernels for 0%

profile of v16, /device:TPU:1, one launch (start us, length us, event | category | flops | bytes accessed | tf_op | source)
XLA Modules:
  0.0 125.4 jit_solution(6747306512855804915)
XLA Ops:
  1.8 2.6 %collective-permute-start.4 = (f32[64,256]{1,0:T(8,128)S(1)}, f32[64,256]{1,0:T(8,128)S(1)}, u32[]{:S(2)}, u32[]{:S(2)}) collective-permute-start(f32[64,256]{1,0:T(8,128)S(1)} %pad_maximum_fusion.14), channel_id=1, source_target_pairs={{0,4},{4,8},{8,12},{12,0},{1,5},{5,9},{9,13},{13,1},{2,6},{6,10},{... | collective-permute-start | bytes 196616 | tf_op jit(solution)/shard_map/ppermute | solution.py:20
  5.3 1.2 collective-permute-start
  8.1 1.7 %convolution_convert_fusion = bf16[512,2560]{1,0:T(8,128)(2,1)S(1)} fusion(bf16[1,1,2560,512]{3,2,1,0:T(8,128)(2,1)S(1)} %copy-done, s32[512]{0:T(512)S(1)} %fusion.53), kind=kOutput, calls=%fused_computation.5 | convolution fusion | flops 1344012288 | bytes 5244928 | tf_op jit(solution)/shard_map/dot_general | solution.py:52
  9.9 10.1 %fusion = f32[512,2560]{1,0:T(8,128)S(1)} fusion(bf16[512,2560]{1,0:T(8,128)(2,1)S(1)} %convolution_convert_fusion, bf16[1,1,2560,2560]{3,2,1,0:T(8,128)(2,1)} %param.17), kind=kOutput, calls=%fused_computation | convolution fusion | flops 6710886400 | bytes 20971520 | tf_op jit(solution)/shard_map/dot_general | solution.py:54
  20.0 1.6 %fusion.3 = f32[512,512]{1,0:T(8,128)S(1)} fusion(bf16[512,2560]{1,0:T(8,128)(2,1)S(1)} %convolution_convert_fusion, f32[512,2560]{1,0:T(8,128)S(1)} %fusion), kind=kOutput, calls=%fused_computation.6 | convolution fusion | flops 1346109440 | bytes 8912896 | tf_op jit(solution)/shard_map/dot_general | solution.py:57
  21.5 2.5 %fusion.7 = f32[512,512]{1,0:T(8,128)} fusion(f32[512,512]{1,0:T(8,128)S(1)} %fusion.3, bf16[512,2560]{1,0:T(8,128)(2,1)S(1)} %convolution_convert_fusion, f32[512,2560]{1,0:T(8,128)S(1)} %fusion), kind=kOutput, calls=%fused_computation.10 | convolution fusion | flops 1345060864 | bytes 9961472 | tf_op jit(solution)/shard_map/dot_general | solution.py:56
  24.1 3.4 %convolution_subtract_fusion = f32[512,512]{1,0:T(8,128)} fusion(f32[512,512]{1,0:T(8,128)} %fusion.7, bf16[1,1,512,512]{3,2,1,0:T(8,128)(2,1)} %param.15, s32[512]{0:T(512)S(1)} %fusion.53), kind=kOutput, calls=%fused_computation.9 | convolution fusion | flops 537919488 | bytes 2623488 | tf_op jit(solution)/shard_map/dot_general | solution.py:49
  27.4 1.4 %collective-permute-start.1 = (bf16[2,64,128]{2,1,0:T(8,128)(2,1)S(1)}, bf16[2,64,128]{2,1,0:T(8,128)(2,1)S(1)}, u32[]{:S(2)}, u32[]{:S(2)}) collective-permute-start(bf16[2,64,128]{2,1,0:T(8,128)(2,1)S(1)} %get-tuple-element.34), channel_id=1, source_target_pairs={{0,1},{1,2},{2,3},{3,0},{4,5},{5,6},{6,7},{7,4},{8,9},{9,10},{10,1... | collective-permute-start | bytes 98312 | tf_op jit(solution)/shard_map/ppermute | solution.py:20
  28.8 2.3 %collective-permute-start.2 = (bf16[2,64,128]{2,1,0:T(8,128)(2,1)S(1)}, bf16[2,64,128]{2,1,0:T(8,128)(2,1)S(1)}, u32[]{:S(2)}, u32[]{:S(2)}) collective-permute-start(bf16[2,64,128]{2,1,0:T(8,128)(2,1)S(1)} %get-tuple-element.34), channel_id=1, source_target_pairs={{0,2},{1,3},{2,0},{3,1},{4,6},{5,7},{6,4},{7,5},{8,10},{9,11},{10,... | collective-permute-start | bytes 98312 | tf_op jit(solution)/shard_map/ppermute | solution.py:20
  32.2 1.6 %collective-permute-start.5 = (f32[64,256]{1,0:T(8,128)S(1)}, f32[64,256]{1,0:T(8,128)S(1)}, u32[]{:S(2)}, u32[]{:S(2)}) collective-permute-start(f32[64,256]{1,0:T(8,128)S(1)} %pad_maximum_fusion.14), channel_id=1, source_target_pairs={{0,8},{4,12},{8,0},{12,4},{1,9},{5,13},{9,1},{13,5},{2,10},{6,14},... | collective-permute-start | bytes 196616 | tf_op jit(solution)/shard_map/ppermute | solution.py:20
  34.0 1.4 %collective-permute-done.5 = f32[64,256]{1,0:T(8,128)S(1)} collective-permute-done((f32[64,256]{1,0:T(8,128)S(1)}, f32[64,256]{1,0:T(8,128)S(1)}, u32[]{:S(2)}, u32[]{:S(2)}) %collective-permute-start.5) | collective-permute-done | bytes 65568 | tf_op jit(solution)/shard_map/ppermute | solution.py:20
  37.1 4.2 %all-to-all-start = ((f32[8,64,512]{2,1,0:T(8,128)}), f32[8,64,512]{2,1,0:T(8,128)}, u32[]{:S(2)}, u32[]{:S(2)}) async-start(f32[8,64,512]{2,1,0:T(8,128)} %bitcast.202), calls=%async_computation | async-start | bytes 2097152 | tf_op jit(solution)/shard_map/all_to_all | solution.py:121
  41.7 23.8 %all-to-all-done = f32[8,64,512]{2,1,0:T(8,128)} async-done(((f32[8,64,512]{2,1,0:T(8,128)}), f32[8,64,512]{2,1,0:T(8,128)}, u32[]{:S(2)}, u32[]{:S(2)}) %all-to-all-start) | async-done | bytes 1048608 | tf_op jit(solution)/shard_map/all_to_all | solution.py:121
  65.5 1.3 %reduce_sum.9 = f32[64,512]{1,0:T(8,128)S(1)} reduce(f32[8,64,512]{2,1,0:T(8,128)} %all-to-all-done, f32[]{:T(128)} %constant.85.clone.1), dimensions={0}, to_apply=%region_0.1 | reduce | flops 229376 | bytes 1179652 | tf_op jit(solution)/shard_map/reduce_sum | solution.py:121
  68.0 4.8 %collective-permute-start.7 = (f32[64,128]{1,0:T(8,128)S(1)}, f32[64,128]{1,0:T(8,128)S(1)}, u32[]{:S(2)}, u32[]{:S(2)}) collective-permute-start(f32[64,128]{1,0:T(8,128)S(1)} %fusion.18), channel_id=1, source_target_pairs={{0,4},{4,8},{8,12},{12,0},{1,5},{5,9},{9,13},{13,1},{2,6},{6,10},{... | collective-permute-start | bytes 98312 | tf_op jit(solution)/shard_map/ppermute | solution.py:20
  73.8 1.7 %collective-permute-done.8 = f32[64,128]{1,0:T(8,128)S(1)} collective-permute-done((f32[64,128]{1,0:T(8,128)S(1)}, f32[64,128]{1,0:T(8,128)S(1)}, u32[]{:S(2)}, u32[]{:S(2)}) %collective-permute-start.8) | collective-permute-done | bytes 32800 | tf_op jit(solution)/shard_map/ppermute | solution.py:20
  77.3 1.8 %collective-permute-done.10 = bf16[64,128]{1,0:T(8,128)(2,1)S(1)} collective-permute-done((bf16[64,128]{1,0:T(8,128)(2,1)S(1)}, bf16[64,128]{1,0:T(8,128)(2,1)S(1)}, u32[]{:S(2)}, u32[]{:S(2)}) %collective-permute-start.10) | collective-permute-done | bytes 16416 | tf_op jit(solution)/shard_map/ppermute | solution.py:20
  79.2 3.2 %collective-permute-start.13 = (bf16[2,64,128]{2,1,0:T(8,128)(2,1)S(1)}, bf16[2,64,128]{2,1,0:T(8,128)(2,1)S(1)}, u32[]{:S(2)}, u32[]{:S(2)}) collective-permute-start(bf16[2,64,128]{2,1,0:T(8,128)(2,1)S(1)} %get-tuple-element.32), channel_id=1, source_target_pairs={{0,3},{1,0},{2,1},{3,2},{4,7},{5,4},{6,5},{7,6},{8,11},{9,8},{10,9... | collective-permute-start | bytes 98312 | tf_op jit(solution)/shard_map/ppermute | solution.py:20
  82.5 1.2 collective-permute-done.11
  84.3 3.2 %collective-permute-start.14 = (f32[64,128]{1,0:T(8,128)S(1)}, f32[64,128]{1,0:T(8,128)S(1)}, u32[]{:S(2)}, u32[]{:S(2)}) collective-permute-start(f32[64,128]{1,0:T(8,128)S(1)} %fusion.15), channel_id=1, source_target_pairs={{0,4},{4,8},{8,12},{12,0},{1,5},{5,9},{9,13},{13,1},{2,6},{6,10},{... | collective-permute-start | bytes 98312 | tf_op jit(solution)/shard_map/ppermute | solution.py:20
  88.6 2.3 %collective-permute-done.15 = f32[64,128]{1,0:T(8,128)S(1)} collective-permute-done((f32[64,128]{1,0:T(8,128)S(1)}, f32[64,128]{1,0:T(8,128)S(1)}, u32[]{:S(2)}, u32[]{:S(2)}) %collective-permute-start.15) | collective-permute-done | bytes 32800 | tf_op jit(solution)/shard_map/ppermute | solution.py:20
  92.8 2.4 %collective-permute-done.17 = bf16[64,128]{1,0:T(8,128)(2,1)S(1)} collective-permute-done((bf16[64,128]{1,0:T(8,128)(2,1)S(1)}, bf16[64,128]{1,0:T(8,128)(2,1)S(1)}, u32[]{:S(2)}, u32[]{:S(2)}) %collective-permute-start.17) | collective-permute-done | bytes 16416 | tf_op jit(solution)/shard_map/ppermute | solution.py:20
  95.2 1.7 %collective-permute-start.18 = (bf16[2,64,128]{2,1,0:T(8,128)(2,1)S(1)}, bf16[2,64,128]{2,1,0:T(8,128)(2,1)S(1)}, u32[]{:S(2)}, u32[]{:S(2)}) collective-permute-start(bf16[2,64,128]{2,1,0:T(8,128)(2,1)S(1)} %get-tuple-element.30), channel_id=1, source_target_pairs={{0,1},{1,2},{2,3},{3,0},{4,5},{5,6},{6,7},{7,4},{8,9},{9,10},{10,1... | collective-permute-start | bytes 98312 | tf_op jit(solution)/shard_map/ppermute | solution.py:20
  97.0 1.5 %collective-permute-start.19 = (bf16[2,64,128]{2,1,0:T(8,128)(2,1)S(1)}, bf16[2,64,128]{2,1,0:T(8,128)(2,1)S(1)}, u32[]{:S(2)}, u32[]{:S(2)}) collective-permute-start(bf16[2,64,128]{2,1,0:T(8,128)(2,1)S(1)} %get-tuple-element.30), channel_id=1, source_target_pairs={{0,2},{1,3},{2,0},{3,1},{4,6},{5,7},{6,4},{7,5},{8,10},{9,11},{10,... | collective-permute-start | bytes 98312 | tf_op jit(solution)/shard_map/ppermute | solution.py:20
  99.8 1.7 %collective-permute-done.19 = bf16[2,64,128]{2,1,0:T(8,128)(2,1)S(1)} collective-permute-done((bf16[2,64,128]{2,1,0:T(8,128)(2,1)S(1)}, bf16[2,64,128]{2,1,0:T(8,128)(2,1)S(1)}, u32[]{:S(2)}, u32[]{:S(2)}) %collective-permute-start.19) | collective-permute-done | bytes 32800 | tf_op jit(solution)/shard_map/ppermute | solution.py:20
  101.8 2.6 %collective-permute-start.21 = (f32[64,128]{1,0:T(8,128)S(1)}, f32[64,128]{1,0:T(8,128)S(1)}, u32[]{:S(2)}, u32[]{:S(2)}) collective-permute-start(f32[64,128]{1,0:T(8,128)S(1)} %fusion.12), channel_id=1, source_target_pairs={{0,4},{4,8},{8,12},{12,0},{1,5},{5,9},{9,13},{13,1},{2,6},{6,10},{... | collective-permute-start | bytes 98312 | tf_op jit(solution)/shard_map/ppermute | solution.py:20
  105.4 2.3 %collective-permute-done.22 = f32[64,128]{1,0:T(8,128)S(1)} collective-permute-done((f32[64,128]{1,0:T(8,128)S(1)}, f32[64,128]{1,0:T(8,128)S(1)}, u32[]{:S(2)}, u32[]{:S(2)}) %collective-permute-start.22) | collective-permute-done | bytes 32800 | tf_op jit(solution)/shard_map/ppermute | solution.py:20
  109.6 2.4 %collective-permute-done.24 = bf16[64,128]{1,0:T(8,128)(2,1)S(1)} collective-permute-done((bf16[64,128]{1,0:T(8,128)(2,1)S(1)}, bf16[64,128]{1,0:T(8,128)(2,1)S(1)}, u32[]{:S(2)}, u32[]{:S(2)}) %collective-permute-start.24) | collective-permute-done | bytes 16416 | tf_op jit(solution)/shard_map/ppermute | solution.py:20
  112.3 2.2 %collective-permute-start.26 = (bf16[2,64,128]{2,1,0:T(8,128)(2,1)S(1)}, bf16[2,64,128]{2,1,0:T(8,128)(2,1)S(1)}, u32[]{:S(2)}, u32[]{:S(2)}) collective-permute-start(bf16[2,64,128]{2,1,0:T(8,128)(2,1)S(1)} %get-tuple-element.28), channel_id=1, source_target_pairs={{0,2},{1,3},{2,0},{3,1},{4,6},{5,7},{6,4},{7,5},{8,10},{9,11},{10,... | collective-permute-start | bytes 98312 | tf_op jit(solution)/shard_map/ppermute | solution.py:20
  116.6 1.3 %collective-permute-done.27 = bf16[2,64,128]{2,1,0:T(8,128)(2,1)S(1)} collective-permute-done((bf16[2,64,128]{2,1,0:T(8,128)(2,1)S(1)}, bf16[2,64,128]{2,1,0:T(8,128)(2,1)S(1)}, u32[]{:S(2)}, u32[]{:S(2)}) %collective-permute-start.27) | collective-permute-done | bytes 32800 | tf_op jit(solution)/shard_map/ppermute | solution.py:20
  118.3 2.1 %collective-permute-start.28 = (f32[64,128]{1,0:T(8,128)S(1)}, f32[64,128]{1,0:T(8,128)S(1)}, u32[]{:S(2)}, u32[]{:S(2)}) collective-permute-start(f32[64,128]{1,0:T(8,128)S(1)} %fusion.9), channel_id=1, source_target_pairs={{0,4},{4,8},{8,12},{12,0},{1,5},{5,9},{9,13},{13,1},{2,6},{6,10},{... | collective-permute-start | bytes 98312 | tf_op jit(solution)/shard_map/ppermute | solution.py:20
  121.4 2.3 %collective-permute-done.29 = f32[64,128]{1,0:T(8,128)S(1)} collective-permute-done((f32[64,128]{1,0:T(8,128)S(1)}, f32[64,128]{1,0:T(8,128)S(1)}, u32[]{:S(2)}, u32[]{:S(2)}) %collective-permute-start.29) | collective-permute-done | bytes 32800 | tf_op jit(solution)/shard_map/ppermute | solution.py:20
  (105 shorter events, 25.1 us)
Async XLA Ops:
  1.7 32.2 %collective-permute-start.6 = (f32[64,256]{1,0:T(8,128)S(1)}, f32[64,256]{1,0:T(8,128)S(1)}, u32[]{:S(2)}, u32[]{:S(2)}) collective-permute-start(f32[64,256]{1,0:T(8,128)S(1)} %pad_maximum_fusion.14), channel_id=1, source_target_pairs={{0,12},{4,0},{8,4},{12,8},{1,13},{5,1},{9,5},{13,9},{2,14},{6,2},{... | collective-permute-start | bytes 196616 | tf_op jit(solution)/shard_map/ppermute | solution.py:20
  1.8 32.2 %collective-permute-start.4 = (f32[64,256]{1,0:T(8,128)S(1)}, f32[64,256]{1,0:T(8,128)S(1)}, u32[]{:S(2)}, u32[]{:S(2)}) collective-permute-start(f32[64,256]{1,0:T(8,128)S(1)} %pad_maximum_fusion.14), channel_id=1, source_target_pairs={{0,4},{4,8},{8,12},{12,0},{1,5},{5,9},{9,13},{13,1},{2,6},{6,10},{... | collective-permute-start | bytes 196616 | tf_op jit(solution)/shard_map/ppermute | solution.py:20
  5.3 22.2 %collective-permute-start = (bf16[64,128]{1,0:T(8,128)(2,1)S(1)}, bf16[64,128]{1,0:T(8,128)(2,1)S(1)}, u32[]{:S(2)}, u32[]{:S(2)}) collective-permute-start(bf16[64,128]{1,0:T(8,128)(2,1)S(1)} %get-tuple-element.36), channel_id=1, source_target_pairs={{0,16},{16,0},{1,17},{17,1},{2,18},{18,2},{3,19},{19,3},{4,20},{20... | collective-permute-start | bytes 49160 | tf_op jit(solution)/shard_map/ppermute | solution.py:20
  27.4 4.7 %collective-permute-start.1 = (bf16[2,64,128]{2,1,0:T(8,128)(2,1)S(1)}, bf16[2,64,128]{2,1,0:T(8,128)(2,1)S(1)}, u32[]{:S(2)}, u32[]{:S(2)}) collective-permute-start(bf16[2,64,128]{2,1,0:T(8,128)(2,1)S(1)} %get-tuple-element.34), channel_id=1, source_target_pairs={{0,1},{1,2},{2,3},{3,0},{4,5},{5,6},{6,7},{7,4},{8,9},{9,10},{10,1... | collective-permute-start | bytes 98312 | tf_op jit(solution)/shard_map/ppermute | solution.py:20
  28.8 5.0 %collective-permute-start.2 = (bf16[2,64,128]{2,1,0:T(8,128)(2,1)S(1)}, bf16[2,64,128]{2,1,0:T(8,128)(2,1)S(1)}, u32[]{:S(2)}, u32[]{:S(2)}) collective-permute-start(bf16[2,64,128]{2,1,0:T(8,128)(2,1)S(1)} %get-tuple-element.34), channel_id=1, source_target_pairs={{0,2},{1,3},{2,0},{3,1},{4,6},{5,7},{6,4},{7,5},{8,10},{9,11},{10,... | collective-permute-start | bytes 98312 | tf_op jit(solution)/shard_map/ppermute | solution.py:20
  31.1 2.9 %collective-permute-start.3 = (bf16[2,64,128]{2,1,0:T(8,128)(2,1)S(1)}, bf16[2,64,128]{2,1,0:T(8,128)(2,1)S(1)}, u32[]{:S(2)}, u32[]{:S(2)}) collective-permute-start(bf16[2,64,128]{2,1,0:T(8,128)(2,1)S(1)} %get-tuple-element.34), channel_id=1, source_target_pairs={{0,3},{1,0},{2,1},{3,2},{4,7},{5,4},{6,5},{7,6},{8,11},{9,8},{10,9... | collective-permute-start | bytes 98312 | tf_op jit(solution)/shard_map/ppermute | solution.py:20
  32.2 3.2 %collective-permute-start.5 = (f32[64,256]{1,0:T(8,128)S(1)}, f32[64,256]{1,0:T(8,128)S(1)}, u32[]{:S(2)}, u32[]{:S(2)}) collective-permute-start(f32[64,256]{1,0:T(8,128)S(1)} %pad_maximum_fusion.14), channel_id=1, source_target_pairs={{0,8},{4,12},{8,0},{12,4},{1,9},{5,13},{9,1},{13,5},{2,10},{6,14},... | collective-permute-start | bytes 196616 | tf_op jit(solution)/shard_map/ppermute | solution.py:20
  37.1 28.4 %all-to-all-start = ((f32[8,64,512]{2,1,0:T(8,128)}), f32[8,64,512]{2,1,0:T(8,128)}, u32[]{:S(2)}, u32[]{:S(2)}) async-start(f32[8,64,512]{2,1,0:T(8,128)} %bitcast.202), calls=%async_computation | async-start | bytes 2097152 | tf_op jit(solution)/shard_map/all_to_all | solution.py:121
  68.0 5.8 %collective-permute-start.7 = (f32[64,128]{1,0:T(8,128)S(1)}, f32[64,128]{1,0:T(8,128)S(1)}, u32[]{:S(2)}, u32[]{:S(2)}) collective-permute-start(f32[64,128]{1,0:T(8,128)S(1)} %fusion.18), channel_id=1, source_target_pairs={{0,4},{4,8},{8,12},{12,0},{1,5},{5,9},{9,13},{13,1},{2,6},{6,10},{... | collective-permute-start | bytes 98312 | tf_op jit(solution)/shard_map/ppermute | solution.py:20
  72.8 2.8 %collective-permute-start.8 = (f32[64,128]{1,0:T(8,128)S(1)}, f32[64,128]{1,0:T(8,128)S(1)}, u32[]{:S(2)}, u32[]{:S(2)}) collective-permute-start(f32[64,128]{1,0:T(8,128)S(1)} %fusion.18), channel_id=1, source_target_pairs={{0,8},{4,12},{8,0},{12,4},{1,9},{5,13},{9,1},{13,5},{2,10},{6,14},... | collective-permute-start | bytes 98312 | tf_op jit(solution)/shard_map/ppermute | solution.py:20
  72.8 3.4 %collective-permute-start.9 = (f32[64,128]{1,0:T(8,128)S(1)}, f32[64,128]{1,0:T(8,128)S(1)}, u32[]{:S(2)}, u32[]{:S(2)}) collective-permute-start(f32[64,128]{1,0:T(8,128)S(1)} %fusion.18), channel_id=1, source_target_pairs={{0,12},{4,0},{8,4},{12,8},{1,13},{5,1},{9,5},{13,9},{2,14},{6,2},{... | collective-permute-start | bytes 98312 | tf_op jit(solution)/shard_map/ppermute | solution.py:20
  76.4 2.7 %collective-permute-start.10 = (bf16[64,128]{1,0:T(8,128)(2,1)S(1)}, bf16[64,128]{1,0:T(8,128)(2,1)S(1)}, u32[]{:S(2)}, u32[]{:S(2)}) collective-permute-start(bf16[64,128]{1,0:T(8,128)(2,1)S(1)} %get-tuple-element.37), channel_id=1, source_target_pairs={{0,16},{16,0},{1,17},{17,1},{2,18},{18,2},{3,19},{19,3},{4,20},{20... | collective-permute-start | bytes 49160 | tf_op jit(solution)/shard_map/ppermute | solution.py:20
  79.1 4.6 %collective-permute-start.11 = (bf16[2,64,128]{2,1,0:T(8,128)(2,1)S(1)}, bf16[2,64,128]{2,1,0:T(8,128)(2,1)S(1)}, u32[]{:S(2)}, u32[]{:S(2)}) collective-permute-start(bf16[2,64,128]{2,1,0:T(8,128)(2,1)S(1)} %get-tuple-element.32), channel_id=1, source_target_pairs={{0,1},{1,2},{2,3},{3,0},{4,5},{5,6},{6,7},{7,4},{8,9},{9,10},{10,1... | collective-permute-start | bytes 98312 | tf_op jit(solution)/shard_map/ppermute | solution.py:20
  79.1 4.6 %collective-permute-start.12 = (bf16[2,64,128]{2,1,0:T(8,128)(2,1)S(1)}, bf16[2,64,128]{2,1,0:T(8,128)(2,1)S(1)}, u32[]{:S(2)}, u32[]{:S(2)}) collective-permute-start(bf16[2,64,128]{2,1,0:T(8,128)(2,1)S(1)} %get-tuple-element.32), channel_id=1, source_target_pairs={{0,2},{1,3},{2,0},{3,1},{4,6},{5,7},{6,4},{7,5},{8,10},{9,11},{10,... | collective-permute-start | bytes 98312 | tf_op jit(solution)/shard_map/ppermute | solution.py:20
  79.2 4.8 %collective-permute-start.13 = (bf16[2,64,128]{2,1,0:T(8,128)(2,1)S(1)}, bf16[2,64,128]{2,1,0:T(8,128)(2,1)S(1)}, u32[]{:S(2)}, u32[]{:S(2)}) collective-permute-start(bf16[2,64,128]{2,1,0:T(8,128)(2,1)S(1)} %get-tuple-element.32), channel_id=1, source_target_pairs={{0,3},{1,0},{2,1},{3,2},{4,7},{5,4},{6,5},{7,6},{8,11},{9,8},{10,9... | collective-permute-start | bytes 98312 | tf_op jit(solution)/shard_map/ppermute | solution.py:20
  84.3 4.2 %collective-permute-start.14 = (f32[64,128]{1,0:T(8,128)S(1)}, f32[64,128]{1,0:T(8,128)S(1)}, u32[]{:S(2)}, u32[]{:S(2)}) collective-permute-start(f32[64,128]{1,0:T(8,128)S(1)} %fusion.15), channel_id=1, source_target_pairs={{0,4},{4,8},{8,12},{12,0},{1,5},{5,9},{9,13},{13,1},{2,6},{6,10},{... | collective-permute-start | bytes 98312 | tf_op jit(solution)/shard_map/ppermute | solution.py:20
  87.6 3.3 %collective-permute-start.15 = (f32[64,128]{1,0:T(8,128)S(1)}, f32[64,128]{1,0:T(8,128)S(1)}, u32[]{:S(2)}, u32[]{:S(2)}) collective-permute-start(f32[64,128]{1,0:T(8,128)S(1)} %fusion.15), channel_id=1, source_target_pairs={{0,8},{4,12},{8,0},{12,4},{1,9},{5,13},{9,1},{13,5},{2,10},{6,14},... | collective-permute-start | bytes 98312 | tf_op jit(solution)/shard_map/ppermute | solution.py:20
  88.3 3.3 %collective-permute-start.16 = (f32[64,128]{1,0:T(8,128)S(1)}, f32[64,128]{1,0:T(8,128)S(1)}, u32[]{:S(2)}, u32[]{:S(2)}) collective-permute-start(f32[64,128]{1,0:T(8,128)S(1)} %fusion.15), channel_id=1, source_target_pairs={{0,12},{4,0},{8,4},{12,8},{1,13},{5,1},{9,5},{13,9},{2,14},{6,2},{... | collective-permute-start | bytes 98312 | tf_op jit(solution)/shard_map/ppermute | solution.py:20
  92.2 3.1 %collective-permute-start.17 = (bf16[64,128]{1,0:T(8,128)(2,1)S(1)}, bf16[64,128]{1,0:T(8,128)(2,1)S(1)}, u32[]{:S(2)}, u32[]{:S(2)}) collective-permute-start(bf16[64,128]{1,0:T(8,128)(2,1)S(1)} %get-tuple-element.39), channel_id=1, source_target_pairs={{0,16},{16,0},{1,17},{17,1},{2,18},{18,2},{3,19},{19,3},{4,20},{20... | collective-permute-start | bytes 49160 | tf_op jit(solution)/shard_map/ppermute | solution.py:20
  95.2 4.6 %collective-permute-start.18 = (bf16[2,64,128]{2,1,0:T(8,128)(2,1)S(1)}, bf16[2,64,128]{2,1,0:T(8,128)(2,1)S(1)}, u32[]{:S(2)}, u32[]{:S(2)}) collective-permute-start(bf16[2,64,128]{2,1,0:T(8,128)(2,1)S(1)} %get-tuple-element.30), channel_id=1, source_target_pairs={{0,1},{1,2},{2,3},{3,0},{4,5},{5,6},{6,7},{7,4},{8,9},{9,10},{10,1... | collective-permute-start | bytes 98312 | tf_op jit(solution)/shard_map/ppermute | solution.py:20
  97.0 4.5 %collective-permute-start.19 = (bf16[2,64,128]{2,1,0:T(8,128)(2,1)S(1)}, bf16[2,64,128]{2,1,0:T(8,128)(2,1)S(1)}, u32[]{:S(2)}, u32[]{:S(2)}) collective-permute-start(bf16[2,64,128]{2,1,0:T(8,128)(2,1)S(1)} %get-tuple-element.30), channel_id=1, source_target_pairs={{0,2},{1,3},{2,0},{3,1},{4,6},{5,7},{6,4},{7,5},{8,10},{9,11},{10,... | collective-permute-start | bytes 98312 | tf_op jit(solution)/shard_map/ppermute | solution.py:20
  98.5 3.0 %collective-permute-start.20 = (bf16[2,64,128]{2,1,0:T(8,128)(2,1)S(1)}, bf16[2,64,128]{2,1,0:T(8,128)(2,1)S(1)}, u32[]{:S(2)}, u32[]{:S(2)}) collective-permute-start(bf16[2,64,128]{2,1,0:T(8,128)(2,1)S(1)} %get-tuple-element.30), channel_id=1, source_target_pairs={{0,3},{1,0},{2,1},{3,2},{4,7},{5,4},{6,5},{7,6},{8,11},{9,8},{10,9... | collective-permute-start | bytes 98312 | tf_op jit(solution)/shard_map/ppermute | solution.py:20
  101.8 3.6 %collective-permute-start.21 = (f32[64,128]{1,0:T(8,128)S(1)}, f32[64,128]{1,0:T(8,128)S(1)}, u32[]{:S(2)}, u32[]{:S(2)}) collective-permute-start(f32[64,128]{1,0:T(8,128)S(1)} %fusion.12), channel_id=1, source_target_pairs={{0,4},{4,8},{8,12},{12,0},{1,5},{5,9},{9,13},{13,1},{2,6},{6,10},{... | collective-permute-start | bytes 98312 | tf_op jit(solution)/shard_map/ppermute | solution.py:20
  104.4 3.3 %collective-permute-start.22 = (f32[64,128]{1,0:T(8,128)S(1)}, f32[64,128]{1,0:T(8,128)S(1)}, u32[]{:S(2)}, u32[]{:S(2)}) collective-permute-start(f32[64,128]{1,0:T(8,128)S(1)} %fusion.12), channel_id=1, source_target_pairs={{0,8},{4,12},{8,0},{12,4},{1,9},{5,13},{9,1},{13,5},{2,10},{6,14},... | collective-permute-start | bytes 98312 | tf_op jit(solution)/shard_map/ppermute | solution.py:20
  105.2 3.3 %collective-permute-start.23 = (f32[64,128]{1,0:T(8,128)S(1)}, f32[64,128]{1,0:T(8,128)S(1)}, u32[]{:S(2)}, u32[]{:S(2)}) collective-permute-start(f32[64,128]{1,0:T(8,128)S(1)} %fusion.12), channel_id=1, source_target_pairs={{0,12},{4,0},{8,4},{12,8},{1,13},{5,1},{9,5},{13,9},{2,14},{6,2},{... | collective-permute-start | bytes 98312 | tf_op jit(solution)/shard_map/ppermute | solution.py:20
  109.0 3.1 %collective-permute-start.24 = (bf16[64,128]{1,0:T(8,128)(2,1)S(1)}, bf16[64,128]{1,0:T(8,128)(2,1)S(1)}, u32[]{:S(2)}, u32[]{:S(2)}) collective-permute-start(bf16[64,128]{1,0:T(8,128)(2,1)S(1)} %get-tuple-element.41), channel_id=1, source_target_pairs={{0,16},{16,0},{1,17},{17,1},{2,18},{18,2},{3,19},{19,3},{4,20},{20... | collective-permute-start | bytes 49160 | tf_op jit(solution)/shard_map/ppermute | solution.py:20
  112.1 4.6 %collective-permute-start.25 = (bf16[2,64,128]{2,1,0:T(8,128)(2,1)S(1)}, bf16[2,64,128]{2,1,0:T(8,128)(2,1)S(1)}, u32[]{:S(2)}, u32[]{:S(2)}) collective-permute-start(bf16[2,64,128]{2,1,0:T(8,128)(2,1)S(1)} %get-tuple-element.28), channel_id=1, source_target_pairs={{0,1},{1,2},{2,3},{3,0},{4,5},{5,6},{6,7},{7,4},{8,9},{9,10},{10,1... | collective-permute-start | bytes 98312 | tf_op jit(solution)/shard_map/ppermute | solution.py:20
  112.3 4.3 %collective-permute-start.26 = (bf16[2,64,128]{2,1,0:T(8,128)(2,1)S(1)}, bf16[2,64,128]{2,1,0:T(8,128)(2,1)S(1)}, u32[]{:S(2)}, u32[]{:S(2)}) collective-permute-start(bf16[2,64,128]{2,1,0:T(8,128)(2,1)S(1)} %get-tuple-element.28), channel_id=1, source_target_pairs={{0,2},{1,3},{2,0},{3,1},{4,6},{5,7},{6,4},{7,5},{8,10},{9,11},{10,... | collective-permute-start | bytes 98312 | tf_op jit(solution)/shard_map/ppermute | solution.py:20
  114.5 3.5 %collective-permute-start.27 = (bf16[2,64,128]{2,1,0:T(8,128)(2,1)S(1)}, bf16[2,64,128]{2,1,0:T(8,128)(2,1)S(1)}, u32[]{:S(2)}, u32[]{:S(2)}) collective-permute-start(bf16[2,64,128]{2,1,0:T(8,128)(2,1)S(1)} %get-tuple-element.28), channel_id=1, source_target_pairs={{0,3},{1,0},{2,1},{3,2},{4,7},{5,4},{6,5},{7,6},{8,11},{9,8},{10,9... | collective-permute-start | bytes 98312 | tf_op jit(solution)/shard_map/ppermute | solution.py:20
  118.3 3.1 %collective-permute-start.28 = (f32[64,128]{1,0:T(8,128)S(1)}, f32[64,128]{1,0:T(8,128)S(1)}, u32[]{:S(2)}, u32[]{:S(2)}) collective-permute-start(f32[64,128]{1,0:T(8,128)S(1)} %fusion.9), channel_id=1, source_target_pairs={{0,4},{4,8},{8,12},{12,0},{1,5},{5,9},{9,13},{13,1},{2,6},{6,10},{... | collective-permute-start | bytes 98312 | tf_op jit(solution)/shard_map/ppermute | solution.py:20
  120.4 3.3 %collective-permute-start.29 = (f32[64,128]{1,0:T(8,128)S(1)}, f32[64,128]{1,0:T(8,128)S(1)}, u32[]{:S(2)}, u32[]{:S(2)}) collective-permute-start(f32[64,128]{1,0:T(8,128)S(1)} %fusion.9), channel_id=1, source_target_pairs={{0,8},{4,12},{8,0},{12,4},{1,9},{5,13},{9,1},{13,5},{2,10},{6,14},... | collective-permute-start | bytes 98312 | tf_op jit(solution)/shard_map/ppermute | solution.py:20
  121.2 3.3 %collective-permute-start.30 = (f32[64,128]{1,0:T(8,128)S(1)}, f32[64,128]{1,0:T(8,128)S(1)}, u32[]{:S(2)}, u32[]{:S(2)}) collective-permute-start(f32[64,128]{1,0:T(8,128)S(1)} %fusion.9), channel_id=1, source_target_pairs={{0,12},{4,0},{8,4},{12,8},{1,13},{5,1},{9,5},{13,9},{2,14},{6,2},{... | collective-permute-start | bytes 98312 | tf_op jit(solution)/shard_map/ppermute | solution.py:20
  (4 other events, 46.5 us)

commit v17 on v14

--- a/solution.py
+++ b/solution.py
@@ -115,28 +115,33 @@
         return temps_mine + jnp.dot(precond_mine, rhs - from_above, precision=high)
 
     known = known_part(temps_mine, temps_above)
-    first_rounded, weights_mine, weights_above, known, spread = lax.optimization_barrier(
-        (first_rounded, weights_mine, weights_above, known, spread)
-    )
-    rows = jnp.sum(lax.all_to_all(spread, OWNERS, 0, 0, tiled=True), axis=0)
-    rows_hi, rows_lo = split_bf16(jnp.dot(precond_mine, rows, precision=lax.Precision.HIGHEST))
     node = jnp.arange(nodes, dtype=jnp.int32)
     source = jnp.repeat(ring_owner_order(), block_nodes) * block_nodes + node % block_nodes
     order = (node[:, None] == source[None, :]).astype(jnp.bfloat16)
-    rows_hi = jnp.dot(rows_hi, order, preferred_element_type=jnp.float32).astype(jnp.bfloat16)
-    rows_lo = jnp.dot(rows_lo, order, preferred_element_type=jnp.float32).astype(jnp.bfloat16)
+    first_nodes = jnp.dot(order, first_rounded.reshape(nodes, load_count), preferred_element_type=jnp.float32)
+    first_nodes = first_nodes.astype(jnp.bfloat16)
+    first_nodes, weights_mine, weights_above, known, spread = lax.optimization_barrier(
+        (first_nodes, weights_mine, weights_above, known, spread)
+    )
+    rows = jnp.sum(lax.all_to_all(spread, OWNERS, 0, 0, tiled=True), axis=0)
+    node_hi, node_lo = split_bf16(jnp.dot(precond_mine, rows, precision=lax.Precision.HIGHEST))
+    rows_hi = jnp.dot(node_hi, order, preferred_element_type=jnp.float32).astype(jnp.bfloat16)
+    rows_lo = jnp.dot(node_lo, order, preferred_element_type=jnp.float32).astype(jnp.bfloat16)
 
     for sweep_index in range(SWEEPS):
         if sweep_index == 0:
-            rounded = first_rounded
+            update = known - (
+                jnp.dot(node_hi, first_nodes, preferred_element_type=jnp.float32)
+                + jnp.dot(node_lo, first_nodes, preferred_element_type=jnp.float32)
+            )
         else:
             rounded = gather_owners(temps_mine.astype(jnp.bfloat16))
             known = known_part(temps_mine, temps_above)
-        rounded = rounded.reshape(nodes, load_count)
-        update = known - (
-            jnp.dot(rows_hi, rounded, preferred_element_type=jnp.float32)
-            + jnp.dot(rows_lo, rounded, preferred_element_type=jnp.float32)
-        )
+            rounded = rounded.reshape(nodes, load_count)
+            update = known - (
+                jnp.dot(rows_hi, rounded, preferred_element_type=jnp.float32)
+                + jnp.dot(rows_lo, rounded, preferred_element_type=jnp.float32)
+            )
         updates = ring_parts(update, "section")
         temps_mine = jnp.einsum("kij,kjl->il", weights_mine, updates, precision=high)
         temps_above = jnp.einsum("kij,kjl->il", weights_above, updates, precision=high)

time: 125 us -> 128 us (1.024); the launches traced: 124 us -> 126 us
  blocking collectives: 0 us -> 30.3 us
  waiting for transfers between devices: 50.3 us -> 23.5 us
  starting transfers between devices: 41.2 us -> 38.9 us
    all_to_all x0 -> x1, blocking collectives: none -> 30.3 us  [body(): rows = jnp.sum(lax.all_to_all(spread, OWNERS, 0, 0, tiled=True), axis=0)]
    all_to_all x1 -> x0, waiting for transfers between devices: 24.2 us -> none  [body(): rows = jnp.sum(lax.all_to_all(spread, OWNERS, 0, 0, tiled=True), axis=0)]
    all_to_all x1 -> x0, starting transfers between devices: 4.25 us -> none  [body(): rows = jnp.sum(lax.all_to_all(spread, OWNERS, 0, 0, tiled=True), axis=0)]
    ppermute x31, waiting for transfers between devices: 26.1 us -> 23.5 us  [ring_parts(): parts.append(lax.ppermute(block, axis, route))]
    ppermute x31, starting transfers between devices: 36.9 us -> 38.9 us  [ring_parts(): parts.append(lax.ppermute(block, axis, route))]
  transfers between devices with their start and end apart: 32 -> 31, of which waited for: 23 -> 19; matrix products, arithmetic and copies ran while one was open for 21% -> 21% of each run, Pallas kernels for 0% -> 0%
where the time goes in v17:
time: 128 us; the launch traced here: 126 us
  starting transfers between devices  38.9 us (30%)
  blocking collectives  30.3 us (24%)
  matrix products  26.7 us (21%)
  waiting for transfers between devices  23.5 us (18%)
  other arithmetic  5.66 us (4%)
    ppermute x31, starting transfers between devices, ring_parts(): parts.append(lax.ppermute(block, axis, route))  38.9 us
    all_to_all x1, blocking collectives, body(): rows = jnp.sum(lax.all_to_all(spread, OWNERS, 0, 0, tiled=True), axis=0)  30.3 us
    ppermute x31, waiting for transfers between devices, ring_parts(): parts.append(lax.ppermute(block, axis, route))  23.5 us
    dot_general x1, matrix products, schur_rows(): solved = jnp.dot(inverse, coupled, preferred_element_type=jnp.float32)  10.1 us
    dot_general x1, matrix products, moved(): jnp.dot(rows.astype(jnp.bfloat16), place, preferred_element_type=jnp.floa...  3.37 us
  transfers between devices with their start and end apart: 31, of which 19 were waited for; matrix products, arithmetic and copies ran while one was open for 21% of the time, Pallas kernels for 0%

profile of v17, /device:TPU:1, one launch (start us, length us, event | category | flops | bytes accessed | tf_op | source)
XLA Modules:
  0.0 125.8 jit_solution(13033134153981411147)
XLA Ops:
  0.0 0.9 fusion.72
  0.9 4.2 %collective-permute-start.2 = (bf16[64,128]{1,0:T(8,128)(2,1)S(1)}, bf16[64,128]{1,0:T(8,128)(2,1)S(1)}, u32[]{:S(2)}, u32[]{:S(2)}) collective-permute-start(bf16[64,128]{1,0:T(8,128)(2,1)S(1)} %get-tuple-element.36), channel_id=1, source_target_pairs={{0,3},{1,0},{2,1},{3,2},{4,7},{5,4},{6,5},{7,6},{8,11},{9,8},{10,9... | collective-permute-start | bytes 49160 | tf_op jit(solution)/shard_map/ppermute | solution.py:20
  7.1 1.2 collective-permute-start.5
  8.4 1.9 %collective-permute-start.4 = (f32[64,256]{1,0:T(8,128)S(1)}, f32[64,256]{1,0:T(8,128)S(1)}, u32[]{:S(2)}, u32[]{:S(2)}) collective-permute-start(f32[64,256]{1,0:T(8,128)S(1)} %pad_maximum_fusion.15), channel_id=1, source_target_pairs={{0,4},{4,8},{8,12},{12,0},{1,5},{5,9},{9,13},{13,1},{2,6},{6,10},{... | collective-permute-start | bytes 196616 | tf_op jit(solution)/shard_map/ppermute | solution.py:20
  12.3 1.7 %convolution_convert_fusion = bf16[512,2560]{1,0:T(8,128)(2,1)S(1)} fusion(bf16[1,1,2560,512]{3,2,1,0:T(8,128)(2,1)S(1)} %copy-done, s32[512]{0:T(512)S(1)} %fusion.55), kind=kOutput, calls=%fused_computation.5 | convolution fusion | flops 1344012288 | bytes 5244928 | tf_op jit(solution)/shard_map/dot_general | solution.py:52
  14.0 10.1 %fusion = f32[512,2560]{1,0:T(8,128)S(1)} fusion(bf16[512,2560]{1,0:T(8,128)(2,1)S(1)} %convolution_convert_fusion, bf16[1,1,2560,2560]{3,2,1,0:T(8,128)(2,1)} %param.17), kind=kOutput, calls=%fused_computation | convolution fusion | flops 6710886400 | bytes 20971520 | tf_op jit(solution)/shard_map/dot_general | solution.py:54
  24.1 1.6 %fusion.3 = f32[512,512]{1,0:T(8,128)S(1)} fusion(bf16[512,2560]{1,0:T(8,128)(2,1)S(1)} %convolution_convert_fusion, f32[512,2560]{1,0:T(8,128)S(1)} %fusion), kind=kOutput, calls=%fused_computation.6 | convolution fusion | flops 1346109440 | bytes 8912896 | tf_op jit(solution)/shard_map/dot_general | solution.py:57
  25.7 2.5 %fusion.7 = f32[512,512]{1,0:T(8,128)} fusion(f32[512,512]{1,0:T(8,128)S(1)} %fusion.3, bf16[512,2560]{1,0:T(8,128)(2,1)S(1)} %convolution_convert_fusion, f32[512,2560]{1,0:T(8,128)S(1)} %fusion), kind=kOutput, calls=%fused_computation.10 | convolution fusion | flops 1345060864 | bytes 9961472 | tf_op jit(solution)/shard_map/dot_general | solution.py:56
  28.2 3.4 %convolution_subtract_fusion = f32[512,512]{1,0:T(8,128)} fusion(f32[512,512]{1,0:T(8,128)} %fusion.7, bf16[1,1,512,512]{3,2,1,0:T(8,128)(2,1)} %param.15, s32[512]{0:T(512)S(1)} %fusion.55), kind=kOutput, calls=%fused_computation.9 | convolution fusion | flops 537919488 | bytes 2623488 | tf_op jit(solution)/shard_map/dot_general | solution.py:49
  31.7 1.2 collective-permute-start.3
  33.0 2.4 %collective-permute-done.6 = f32[64,256]{1,0:T(8,128)S(1)} collective-permute-done((f32[64,256]{1,0:T(8,128)S(1)}, f32[64,256]{1,0:T(8,128)S(1)}, u32[]{:S(2)}, u32[]{:S(2)}) %collective-permute-start.6) | collective-permute-done | bytes 65568 | tf_op jit(solution)/shard_map/ppermute | solution.py:20
  37.4 30.3 %all_to_all.5 = f32[8,64,512]{2,1,0:T(8,128)} all-to-all(f32[8,64,512]{2,1,0:T(8,128)S(1)} %bitcast.198), channel_id=1, replica_groups=mesh['sub'=2,'section'=4,'iface'=4] {'sub','iface'}, dimensions={0} | all-to-all | bytes 2097152 | tf_op jit(solution)/shard_map/all_to_all | solution.py:126
  67.8 1.3 %reduce_sum.9 = f32[64,512]{1,0:T(8,128)S(1)} reduce(f32[8,64,512]{2,1,0:T(8,128)} %all_to_all.5, f32[]{:T(128)} %constant.94.clone.1), dimensions={0}, to_apply=%region_0.1 | reduce | flops 229376 | bytes 1179652 | tf_op jit(solution)/shard_map/reduce_sum | solution.py:126
  69.6 1.9 %collective-permute-start.9 = (f32[64,128]{1,0:T(8,128)S(1)}, f32[64,128]{1,0:T(8,128)S(1)}, u32[]{:S(2)}, u32[]{:S(2)}) collective-permute-start(f32[64,128]{1,0:T(8,128)S(1)} %fusion.18), channel_id=1, source_target_pairs={{0,12},{4,0},{8,4},{12,8},{1,13},{5,1},{9,5},{13,9},{2,14},{6,2},{... | collective-permute-start | bytes 98312 | tf_op jit(solution)/shard_map/ppermute | solution.py:20
  71.5 1.6 %collective-permute-start.8 = (f32[64,128]{1,0:T(8,128)S(1)}, f32[64,128]{1,0:T(8,128)S(1)}, u32[]{:S(2)}, u32[]{:S(2)}) collective-permute-start(f32[64,128]{1,0:T(8,128)S(1)} %fusion.18), channel_id=1, source_target_pairs={{0,8},{4,12},{8,0},{12,4},{1,9},{5,13},{9,1},{13,5},{2,10},{6,14},... | collective-permute-start | bytes 98312 | tf_op jit(solution)/shard_map/ppermute | solution.py:20
  73.1 1.6 %collective-permute-start.7 = (f32[64,128]{1,0:T(8,128)S(1)}, f32[64,128]{1,0:T(8,128)S(1)}, u32[]{:S(2)}, u32[]{:S(2)}) collective-permute-start(f32[64,128]{1,0:T(8,128)S(1)} %fusion.18), channel_id=1, source_target_pairs={{0,4},{4,8},{8,12},{12,0},{1,5},{5,9},{9,13},{13,1},{2,6},{6,10},{... | collective-permute-start | bytes 98312 | tf_op jit(solution)/shard_map/ppermute | solution.py:20
  76.1 1.4 %collective-permute-start.10 = (bf16[64,128]{1,0:T(8,128)(2,1)S(1)}, bf16[64,128]{1,0:T(8,128)(2,1)S(1)}, u32[]{:S(2)}, u32[]{:S(2)}) collective-permute-start(bf16[64,128]{1,0:T(8,128)(2,1)S(1)} %get-tuple-element.37), channel_id=1, source_target_pairs={{0,1},{1,2},{2,3},{3,0},{4,5},{5,6},{6,7},{7,4},{8,9},{9,10},{10,1... | collective-permute-start | bytes 49160 | tf_op jit(solution)/shard_map/ppermute | solution.py:20
  78.6 1.0 collective-permute-done.11
  79.6 1.3 %collective-permute-done.10 = bf16[64,128]{1,0:T(8,128)(2,1)S(1)} collective-permute-done((bf16[64,128]{1,0:T(8,128)(2,1)S(1)}, bf16[64,128]{1,0:T(8,128)(2,1)S(1)}, u32[]{:S(2)}, u32[]{:S(2)}) %collective-permute-start.10) | collective-permute-done | bytes 16416 | tf_op jit(solution)/shard_map/ppermute | solution.py:20
  81.4 2.7 %collective-permute-done.13 = bf16[4,64,128]{2,1,0:T(8,128)(2,1)S(1)} collective-permute-done((bf16[4,64,128]{2,1,0:T(8,128)(2,1)S(1)}, bf16[4,64,128]{2,1,0:T(8,128)(2,1)S(1)}, u32[]{:S(2)}, u32[]{:S(2)}) %collective-permute-start.13) | collective-permute-done | bytes 65568 | tf_op jit(solution)/shard_map/ppermute | solution.py:20
  84.4 4.0 %collective-permute-start.16 = (f32[64,128]{1,0:T(8,128)S(1)}, f32[64,128]{1,0:T(8,128)S(1)}, u32[]{:S(2)}, u32[]{:S(2)}) collective-permute-start(f32[64,128]{1,0:T(8,128)S(1)} %fusion.15), channel_id=1, source_target_pairs={{0,12},{4,0},{8,4},{12,8},{1,13},{5,1},{9,5},{13,9},{2,14},{6,2},{... | collective-permute-start | bytes 98312 | tf_op jit(solution)/shard_map/ppermute | solution.py:20
  88.4 1.0 collective-permute-start.15
  91.8 1.6 %collective-permute-start.19 = (bf16[64,128]{1,0:T(8,128)(2,1)S(1)}, bf16[64,128]{1,0:T(8,128)(2,1)S(1)}, u32[]{:S(2)}, u32[]{:S(2)}) collective-permute-start(bf16[64,128]{1,0:T(8,128)(2,1)S(1)} %get-tuple-element.39), channel_id=1, source_target_pairs={{0,3},{1,0},{2,1},{3,2},{4,7},{5,4},{6,5},{7,6},{8,11},{9,8},{10,9... | collective-permute-start | bytes 49160 | tf_op jit(solution)/shard_map/ppermute | solution.py:20
  94.4 2.5 %collective-permute-done.18 = bf16[64,128]{1,0:T(8,128)(2,1)S(1)} collective-permute-done((bf16[64,128]{1,0:T(8,128)(2,1)S(1)}, bf16[64,128]{1,0:T(8,128)(2,1)S(1)}, u32[]{:S(2)}, u32[]{:S(2)}) %collective-permute-start.18) | collective-permute-done | bytes 16416 | tf_op jit(solution)/shard_map/ppermute | solution.py:20
  98.3 2.7 %collective-permute-done.20 = bf16[4,64,128]{2,1,0:T(8,128)(2,1)S(1)} collective-permute-done((bf16[4,64,128]{2,1,0:T(8,128)(2,1)S(1)}, bf16[4,64,128]{2,1,0:T(8,128)(2,1)S(1)}, u32[]{:S(2)}, u32[]{:S(2)}) %collective-permute-start.20) | collective-permute-done | bytes 65568 | tf_op jit(solution)/shard_map/ppermute | solution.py:20
  101.3 4.5 %collective-permute-start.23 = (f32[64,128]{1,0:T(8,128)S(1)}, f32[64,128]{1,0:T(8,128)S(1)}, u32[]{:S(2)}, u32[]{:S(2)}) collective-permute-start(f32[64,128]{1,0:T(8,128)S(1)} %fusion.12), channel_id=1, source_target_pairs={{0,12},{4,0},{8,4},{12,8},{1,13},{5,1},{9,5},{13,9},{2,14},{6,2},{... | collective-permute-start | bytes 98312 | tf_op jit(solution)/shard_map/ppermute | solution.py:20
  106.5 1.1 collective-permute-start.21
  110.1 1.4 %collective-permute-start.24 = (bf16[64,128]{1,0:T(8,128)(2,1)S(1)}, bf16[64,128]{1,0:T(8,128)(2,1)S(1)}, u32[]{:S(2)}, u32[]{:S(2)}) collective-permute-start(bf16[64,128]{1,0:T(8,128)(2,1)S(1)} %get-tuple-element.41), channel_id=1, source_target_pairs={{0,1},{1,2},{2,3},{3,0},{4,5},{5,6},{6,7},{7,4},{8,9},{9,10},{10,1... | collective-permute-start | bytes 49160 | tf_op jit(solution)/shard_map/ppermute | solution.py:20
  111.7 1.3 %collective-permute-done.25 = bf16[64,128]{1,0:T(8,128)(2,1)S(1)} collective-permute-done((bf16[64,128]{1,0:T(8,128)(2,1)S(1)}, bf16[64,128]{1,0:T(8,128)(2,1)S(1)}, u32[]{:S(2)}, u32[]{:S(2)}) %collective-permute-start.25) | collective-permute-done | bytes 16416 | tf_op jit(solution)/shard_map/ppermute | solution.py:20
  113.1 1.4 %collective-permute-done.24 = bf16[64,128]{1,0:T(8,128)(2,1)S(1)} collective-permute-done((bf16[64,128]{1,0:T(8,128)(2,1)S(1)}, bf16[64,128]{1,0:T(8,128)(2,1)S(1)}, u32[]{:S(2)}, u32[]{:S(2)}) %collective-permute-start.24) | collective-permute-done | bytes 16416 | tf_op jit(solution)/shard_map/ppermute | solution.py:20
  115.0 2.7 %collective-permute-done.27 = bf16[4,64,128]{2,1,0:T(8,128)(2,1)S(1)} collective-permute-done((bf16[4,64,128]{2,1,0:T(8,128)(2,1)S(1)}, bf16[4,64,128]{2,1,0:T(8,128)(2,1)S(1)}, u32[]{:S(2)}, u32[]{:S(2)}) %collective-permute-start.27) | collective-permute-done | bytes 65568 | tf_op jit(solution)/shard_map/ppermute | solution.py:20
  118.0 4.2 %collective-permute-start.30 = (f32[64,128]{1,0:T(8,128)S(1)}, f32[64,128]{1,0:T(8,128)S(1)}, u32[]{:S(2)}, u32[]{:S(2)}) collective-permute-start(f32[64,128]{1,0:T(8,128)S(1)} %fusion.9), channel_id=1, source_target_pairs={{0,12},{4,0},{8,4},{12,8},{1,13},{5,1},{9,5},{13,9},{2,14},{6,2},{... | collective-permute-start | bytes 98312 | tf_op jit(solution)/shard_map/ppermute | solution.py:20
  (107 shorter events, 22.8 us)
Async XLA Ops:
  0.0 12.3 %copy-start = (bf16[1,1,2560,512]{3,2,1,0:T(8,128)(2,1)S(1)}, bf16[1,1,2560,512]{3,2,1,0:T(8,128)(2,1)}, u32[]{:S(2)}) copy-start(bf16[1,1,2560,512]{3,2,1,0:T(8,128)(2,1)} %param.16) | copy-start | bytes 7864324
  0.9 30.7 %collective-permute-start.2 = (bf16[64,128]{1,0:T(8,128)(2,1)S(1)}, bf16[64,128]{1,0:T(8,128)(2,1)S(1)}, u32[]{:S(2)}, u32[]{:S(2)}) collective-permute-start(bf16[64,128]{1,0:T(8,128)(2,1)S(1)} %get-tuple-element.36), channel_id=1, source_target_pairs={{0,3},{1,0},{2,1},{3,2},{4,7},{5,4},{6,5},{7,6},{8,11},{9,8},{10,9... | collective-permute-start | bytes 49160 | tf_op jit(solution)/shard_map/ppermute | solution.py:20
  5.1 26.6 %collective-permute-start.1 = (bf16[64,128]{1,0:T(8,128)(2,1)S(1)}, bf16[64,128]{1,0:T(8,128)(2,1)S(1)}, u32[]{:S(2)}, u32[]{:S(2)}) collective-permute-start(bf16[64,128]{1,0:T(8,128)(2,1)S(1)} %get-tuple-element.36), channel_id=1, source_target_pairs={{0,2},{1,3},{2,0},{3,1},{4,6},{5,7},{6,4},{7,5},{8,10},{9,11},{10,... | collective-permute-start | bytes 49160 | tf_op jit(solution)/shard_map/ppermute | solution.py:20
  5.1 26.6 %collective-permute-start = (bf16[64,128]{1,0:T(8,128)(2,1)S(1)}, bf16[64,128]{1,0:T(8,128)(2,1)S(1)}, u32[]{:S(2)}, u32[]{:S(2)}) collective-permute-start(bf16[64,128]{1,0:T(8,128)(2,1)S(1)} %get-tuple-element.36), channel_id=1, source_target_pairs={{0,1},{1,2},{2,3},{3,0},{4,5},{5,6},{6,7},{7,4},{8,9},{9,10},{10,1... | collective-permute-start | bytes 49160 | tf_op jit(solution)/shard_map/ppermute | solution.py:20
  7.1 28.7 %collective-permute-start.5 = (f32[64,256]{1,0:T(8,128)S(1)}, f32[64,256]{1,0:T(8,128)S(1)}, u32[]{:S(2)}, u32[]{:S(2)}) collective-permute-start(f32[64,256]{1,0:T(8,128)S(1)} %pad_maximum_fusion.15), channel_id=1, source_target_pairs={{0,8},{4,12},{8,0},{12,4},{1,9},{5,13},{9,1},{13,5},{2,10},{6,14},... | collective-permute-start | bytes 196616 | tf_op jit(solution)/shard_map/ppermute | solution.py:20
  8.4 27.5 %collective-permute-start.4 = (f32[64,256]{1,0:T(8,128)S(1)}, f32[64,256]{1,0:T(8,128)S(1)}, u32[]{:S(2)}, u32[]{:S(2)}) collective-permute-start(f32[64,256]{1,0:T(8,128)S(1)} %pad_maximum_fusion.15), channel_id=1, source_target_pairs={{0,4},{4,8},{8,12},{12,0},{1,5},{5,9},{9,13},{13,1},{2,6},{6,10},{... | collective-permute-start | bytes 196616 | tf_op jit(solution)/shard_map/ppermute | solution.py:20
  31.6 3.7 %collective-permute-start.6 = (f32[64,256]{1,0:T(8,128)S(1)}, f32[64,256]{1,0:T(8,128)S(1)}, u32[]{:S(2)}, u32[]{:S(2)}) collective-permute-start(f32[64,256]{1,0:T(8,128)S(1)} %pad_maximum_fusion.15), channel_id=1, source_target_pairs={{0,12},{4,0},{8,4},{12,8},{1,13},{5,1},{9,5},{13,9},{2,14},{6,2},{... | collective-permute-start | bytes 196616 | tf_op jit(solution)/shard_map/ppermute | solution.py:20
  31.7 5.4 %collective-permute-start.3 = (bf16[4,64,128]{2,1,0:T(8,128)(2,1)S(1)}, bf16[4,64,128]{2,1,0:T(8,128)(2,1)S(1)}, u32[]{:S(2)}, u32[]{:S(2)}) collective-permute-start(bf16[4,64,128]{2,1,0:T(8,128)(2,1)S(1)} %get-tuple-element.34), channel_id=1, source_target_pairs={{0,16},{16,0},{1,17},{17,1},{2,18},{18,2},{3,19},{19,3},{4,20},{20... | collective-permute-start | bytes 196616 | tf_op jit(solution)/shard_map/ppermute | solution.py:20
  69.6 5.7 %collective-permute-start.9 = (f32[64,128]{1,0:T(8,128)S(1)}, f32[64,128]{1,0:T(8,128)S(1)}, u32[]{:S(2)}, u32[]{:S(2)}) collective-permute-start(f32[64,128]{1,0:T(8,128)S(1)} %fusion.18), channel_id=1, source_target_pairs={{0,12},{4,0},{8,4},{12,8},{1,13},{5,1},{9,5},{13,9},{2,14},{6,2},{... | collective-permute-start | bytes 98312 | tf_op jit(solution)/shard_map/ppermute | solution.py:20
  71.5 3.8 %collective-permute-start.8 = (f32[64,128]{1,0:T(8,128)S(1)}, f32[64,128]{1,0:T(8,128)S(1)}, u32[]{:S(2)}, u32[]{:S(2)}) collective-permute-start(f32[64,128]{1,0:T(8,128)S(1)} %fusion.18), channel_id=1, source_target_pairs={{0,8},{4,12},{8,0},{12,4},{1,9},{5,13},{9,1},{13,5},{2,10},{6,14},... | collective-permute-start | bytes 98312 | tf_op jit(solution)/shard_map/ppermute | solution.py:20
  73.1 2.6 %collective-permute-start.7 = (f32[64,128]{1,0:T(8,128)S(1)}, f32[64,128]{1,0:T(8,128)S(1)}, u32[]{:S(2)}, u32[]{:S(2)}) collective-permute-start(f32[64,128]{1,0:T(8,128)S(1)} %fusion.18), channel_id=1, source_target_pairs={{0,4},{4,8},{8,12},{12,0},{1,5},{5,9},{9,13},{13,1},{2,6},{6,10},{... | collective-permute-start | bytes 98312 | tf_op jit(solution)/shard_map/ppermute | solution.py:20
  76.0 2.6 %collective-permute-start.12 = (bf16[64,128]{1,0:T(8,128)(2,1)S(1)}, bf16[64,128]{1,0:T(8,128)(2,1)S(1)}, u32[]{:S(2)}, u32[]{:S(2)}) collective-permute-start(bf16[64,128]{1,0:T(8,128)(2,1)S(1)} %get-tuple-element.37), channel_id=1, source_target_pairs={{0,3},{1,0},{2,1},{3,2},{4,7},{5,4},{6,5},{7,6},{8,11},{9,8},{10,9... | collective-permute-start | bytes 49160 | tf_op jit(solution)/shard_map/ppermute | solution.py:20
  76.0 3.6 %collective-permute-start.11 = (bf16[64,128]{1,0:T(8,128)(2,1)S(1)}, bf16[64,128]{1,0:T(8,128)(2,1)S(1)}, u32[]{:S(2)}, u32[]{:S(2)}) collective-permute-start(bf16[64,128]{1,0:T(8,128)(2,1)S(1)} %get-tuple-element.37), channel_id=1, source_target_pairs={{0,2},{1,3},{2,0},{3,1},{4,6},{5,7},{6,4},{7,5},{8,10},{9,11},{10,... | collective-permute-start | bytes 49160 | tf_op jit(solution)/shard_map/ppermute | solution.py:20
  76.1 4.8 %collective-permute-start.10 = (bf16[64,128]{1,0:T(8,128)(2,1)S(1)}, bf16[64,128]{1,0:T(8,128)(2,1)S(1)}, u32[]{:S(2)}, u32[]{:S(2)}) collective-permute-start(bf16[64,128]{1,0:T(8,128)(2,1)S(1)} %get-tuple-element.37), channel_id=1, source_target_pairs={{0,1},{1,2},{2,3},{3,0},{4,5},{5,6},{6,7},{7,4},{8,9},{9,10},{10,1... | collective-permute-start | bytes 49160 | tf_op jit(solution)/shard_map/ppermute | solution.py:20
  80.9 3.2 %collective-permute-start.13 = (bf16[4,64,128]{2,1,0:T(8,128)(2,1)S(1)}, bf16[4,64,128]{2,1,0:T(8,128)(2,1)S(1)}, u32[]{:S(2)}, u32[]{:S(2)}) collective-permute-start(bf16[4,64,128]{2,1,0:T(8,128)(2,1)S(1)} %get-tuple-element.32), channel_id=1, source_target_pairs={{0,16},{16,0},{1,17},{17,1},{2,18},{18,2},{3,19},{19,3},{4,20},{20... | collective-permute-start | bytes 196616 | tf_op jit(solution)/shard_map/ppermute | solution.py:20
  84.4 6.6 %collective-permute-start.16 = (f32[64,128]{1,0:T(8,128)S(1)}, f32[64,128]{1,0:T(8,128)S(1)}, u32[]{:S(2)}, u32[]{:S(2)}) collective-permute-start(f32[64,128]{1,0:T(8,128)S(1)} %fusion.15), channel_id=1, source_target_pairs={{0,12},{4,0},{8,4},{12,8},{1,13},{5,1},{9,5},{13,9},{2,14},{6,2},{... | collective-permute-start | bytes 98312 | tf_op jit(solution)/shard_map/ppermute | solution.py:20
  88.4 2.9 %collective-permute-start.15 = (f32[64,128]{1,0:T(8,128)S(1)}, f32[64,128]{1,0:T(8,128)S(1)}, u32[]{:S(2)}, u32[]{:S(2)}) collective-permute-start(f32[64,128]{1,0:T(8,128)S(1)} %fusion.15), channel_id=1, source_target_pairs={{0,8},{4,12},{8,0},{12,4},{1,9},{5,13},{9,1},{13,5},{2,10},{6,14},... | collective-permute-start | bytes 98312 | tf_op jit(solution)/shard_map/ppermute | solution.py:20
  89.5 1.8 %collective-permute-start.14 = (f32[64,128]{1,0:T(8,128)S(1)}, f32[64,128]{1,0:T(8,128)S(1)}, u32[]{:S(2)}, u32[]{:S(2)}) collective-permute-start(f32[64,128]{1,0:T(8,128)S(1)} %fusion.15), channel_id=1, source_target_pairs={{0,4},{4,8},{8,12},{12,0},{1,5},{5,9},{9,13},{13,1},{2,6},{6,10},{... | collective-permute-start | bytes 98312 | tf_op jit(solution)/shard_map/ppermute | solution.py:20
  91.8 2.6 %collective-permute-start.19 = (bf16[64,128]{1,0:T(8,128)(2,1)S(1)}, bf16[64,128]{1,0:T(8,128)(2,1)S(1)}, u32[]{:S(2)}, u32[]{:S(2)}) collective-permute-start(bf16[64,128]{1,0:T(8,128)(2,1)S(1)} %get-tuple-element.39), channel_id=1, source_target_pairs={{0,3},{1,0},{2,1},{3,2},{4,7},{5,4},{6,5},{7,6},{8,11},{9,8},{10,9... | collective-permute-start | bytes 49160 | tf_op jit(solution)/shard_map/ppermute | solution.py:20
  93.4 3.5 %collective-permute-start.18 = (bf16[64,128]{1,0:T(8,128)(2,1)S(1)}, bf16[64,128]{1,0:T(8,128)(2,1)S(1)}, u32[]{:S(2)}, u32[]{:S(2)}) collective-permute-start(bf16[64,128]{1,0:T(8,128)(2,1)S(1)} %get-tuple-element.39), channel_id=1, source_target_pairs={{0,2},{1,3},{2,0},{3,1},{4,6},{5,7},{6,4},{7,5},{8,10},{9,11},{10,... | collective-permute-start | bytes 49160 | tf_op jit(solution)/shard_map/ppermute | solution.py:20
  93.4 4.4 %collective-permute-start.17 = (bf16[64,128]{1,0:T(8,128)(2,1)S(1)}, bf16[64,128]{1,0:T(8,128)(2,1)S(1)}, u32[]{:S(2)}, u32[]{:S(2)}) collective-permute-start(bf16[64,128]{1,0:T(8,128)(2,1)S(1)} %get-tuple-element.39), channel_id=1, source_target_pairs={{0,1},{1,2},{2,3},{3,0},{4,5},{5,6},{6,7},{7,4},{8,9},{9,10},{10,1... | collective-permute-start | bytes 49160 | tf_op jit(solution)/shard_map/ppermute | solution.py:20
  97.8 3.2 %collective-permute-start.20 = (bf16[4,64,128]{2,1,0:T(8,128)(2,1)S(1)}, bf16[4,64,128]{2,1,0:T(8,128)(2,1)S(1)}, u32[]{:S(2)}, u32[]{:S(2)}) collective-permute-start(bf16[4,64,128]{2,1,0:T(8,128)(2,1)S(1)} %get-tuple-element.30), channel_id=1, source_target_pairs={{0,16},{16,0},{1,17},{17,1},{2,18},{18,2},{3,19},{19,3},{4,20},{20... | collective-permute-start | bytes 196616 | tf_op jit(solution)/shard_map/ppermute | solution.py:20
  101.3 6.6 %collective-permute-start.23 = (f32[64,128]{1,0:T(8,128)S(1)}, f32[64,128]{1,0:T(8,128)S(1)}, u32[]{:S(2)}, u32[]{:S(2)}) collective-permute-start(f32[64,128]{1,0:T(8,128)S(1)} %fusion.12), channel_id=1, source_target_pairs={{0,12},{4,0},{8,4},{12,8},{1,13},{5,1},{9,5},{13,9},{2,14},{6,2},{... | collective-permute-start | bytes 98312 | tf_op jit(solution)/shard_map/ppermute | solution.py:20
  105.8 2.8 %collective-permute-start.22 = (f32[64,128]{1,0:T(8,128)S(1)}, f32[64,128]{1,0:T(8,128)S(1)}, u32[]{:S(2)}, u32[]{:S(2)}) collective-permute-start(f32[64,128]{1,0:T(8,128)S(1)} %fusion.12), channel_id=1, source_target_pairs={{0,8},{4,12},{8,0},{12,4},{1,9},{5,13},{9,1},{13,5},{2,10},{6,14},... | collective-permute-start | bytes 98312 | tf_op jit(solution)/shard_map/ppermute | solution.py:20
  106.5 2.1 %collective-permute-start.21 = (f32[64,128]{1,0:T(8,128)S(1)}, f32[64,128]{1,0:T(8,128)S(1)}, u32[]{:S(2)}, u32[]{:S(2)}) collective-permute-start(f32[64,128]{1,0:T(8,128)S(1)} %fusion.12), channel_id=1, source_target_pairs={{0,4},{4,8},{8,12},{12,0},{1,5},{5,9},{9,13},{13,1},{2,6},{6,10},{... | collective-permute-start | bytes 98312 | tf_op jit(solution)/shard_map/ppermute | solution.py:20
  109.1 2.7 %collective-permute-start.26 = (bf16[64,128]{1,0:T(8,128)(2,1)S(1)}, bf16[64,128]{1,0:T(8,128)(2,1)S(1)}, u32[]{:S(2)}, u32[]{:S(2)}) collective-permute-start(bf16[64,128]{1,0:T(8,128)(2,1)S(1)} %get-tuple-element.41), channel_id=1, source_target_pairs={{0,3},{1,0},{2,1},{3,2},{4,7},{5,4},{6,5},{7,6},{8,11},{9,8},{10,9... | collective-permute-start | bytes 49160 | tf_op jit(solution)/shard_map/ppermute | solution.py:20
  109.6 3.5 %collective-permute-start.25 = (bf16[64,128]{1,0:T(8,128)(2,1)S(1)}, bf16[64,128]{1,0:T(8,128)(2,1)S(1)}, u32[]{:S(2)}, u32[]{:S(2)}) collective-permute-start(bf16[64,128]{1,0:T(8,128)(2,1)S(1)} %get-tuple-element.41), channel_id=1, source_target_pairs={{0,2},{1,3},{2,0},{3,1},{4,6},{5,7},{6,4},{7,5},{8,10},{9,11},{10,... | collective-permute-start | bytes 49160 | tf_op jit(solution)/shard_map/ppermute | solution.py:20
  110.1 4.4 %collective-permute-start.24 = (bf16[64,128]{1,0:T(8,128)(2,1)S(1)}, bf16[64,128]{1,0:T(8,128)(2,1)S(1)}, u32[]{:S(2)}, u32[]{:S(2)}) collective-permute-start(bf16[64,128]{1,0:T(8,128)(2,1)S(1)} %get-tuple-element.41), channel_id=1, source_target_pairs={{0,1},{1,2},{2,3},{3,0},{4,5},{5,6},{6,7},{7,4},{8,9},{9,10},{10,1... | collective-permute-start | bytes 49160 | tf_op jit(solution)/shard_map/ppermute | solution.py:20
  114.5 3.2 %collective-permute-start.27 = (bf16[4,64,128]{2,1,0:T(8,128)(2,1)S(1)}, bf16[4,64,128]{2,1,0:T(8,128)(2,1)S(1)}, u32[]{:S(2)}, u32[]{:S(2)}) collective-permute-start(bf16[4,64,128]{2,1,0:T(8,128)(2,1)S(1)} %get-tuple-element.28), channel_id=1, source_target_pairs={{0,16},{16,0},{1,17},{17,1},{2,18},{18,2},{3,19},{19,3},{4,20},{20... | collective-permute-start | bytes 196616 | tf_op jit(solution)/shard_map/ppermute | solution.py:20
  118.0 6.5 %collective-permute-start.30 = (f32[64,128]{1,0:T(8,128)S(1)}, f32[64,128]{1,0:T(8,128)S(1)}, u32[]{:S(2)}, u32[]{:S(2)}) collective-permute-start(f32[64,128]{1,0:T(8,128)S(1)} %fusion.9), channel_id=1, source_target_pairs={{0,12},{4,0},{8,4},{12,8},{1,13},{5,1},{9,5},{13,9},{2,14},{6,2},{... | collective-permute-start | bytes 98312 | tf_op jit(solution)/shard_map/ppermute | solution.py:20
  122.2 2.8 %collective-permute-start.29 = (f32[64,128]{1,0:T(8,128)S(1)}, f32[64,128]{1,0:T(8,128)S(1)}, u32[]{:S(2)}, u32[]{:S(2)}) collective-permute-start(f32[64,128]{1,0:T(8,128)S(1)} %fusion.9), channel_id=1, source_target_pairs={{0,8},{4,12},{8,0},{12,4},{1,9},{5,13},{9,1},{13,5},{2,10},{6,14},... | collective-permute-start | bytes 98312 | tf_op jit(solution)/shard_map/ppermute | solution.py:20
  123.0 2.0 %collective-permute-start.28 = (f32[64,128]{1,0:T(8,128)S(1)}, f32[64,128]{1,0:T(8,128)S(1)}, u32[]{:S(2)}, u32[]{:S(2)}) collective-permute-start(f32[64,128]{1,0:T(8,128)S(1)} %fusion.9), channel_id=1, source_target_pairs={{0,4},{4,8},{8,12},{12,0},{1,5},{5,9},{9,13},{13,1},{2,6},{6,10},{... | collective-permute-start | bytes 98312 | tf_op jit(solution)/shard_map/ppermute | solution.py:20
  (4 other events, 27.8 us)

commit v18 on v14

--- a/solution.py
+++ b/solution.py
@@ -126,6 +126,7 @@
     rows_hi = jnp.dot(rows_hi, order, preferred_element_type=jnp.float32).astype(jnp.bfloat16)
     rows_lo = jnp.dot(rows_lo, order, preferred_element_type=jnp.float32).astype(jnp.bfloat16)
 
+    weights_both = jnp.stack([weights_mine, weights_above])
     for sweep_index in range(SWEEPS):
         if sweep_index == 0:
             rounded = first_rounded
@@ -138,8 +139,8 @@
             + jnp.dot(rows_lo, rounded, preferred_element_type=jnp.float32)
         )
         updates = ring_parts(update, "section")
-        temps_mine = jnp.einsum("kij,kjl->il", weights_mine, updates, precision=high)
-        temps_above = jnp.einsum("kij,kjl->il", weights_above, updates, precision=high)
+        swept = jnp.einsum("skij,kjl->sil", weights_both, updates, precision=high)
+        temps_mine, temps_above = swept[0], swept[1]
     return temps_mine[None]
 
 

time: 125 us -> 125 us (level)
  transfers between devices with their start and end apart: 32 -> 32, of which waited for: 23 -> 23; matrix products, arithmetic and copies ran while one was open for 21% -> 20% of each run, Pallas kernels for 0% -> 0%
where the time goes in v18:
time: 125 us
  waiting for transfers between devices  51 us (41%)
  starting transfers between devices  41.2 us (33%)
  matrix products  25.2 us (20%)
  other arithmetic  5.71 us (5%)
    ppermute x31, starting transfers between devices, ring_parts(): parts.append(lax.ppermute(block, axis, route))  36.9 us
    ppermute x31, waiting for transfers between devices, ring_parts(): parts.append(lax.ppermute(block, axis, route))  26.8 us
    all_to_all x1, waiting for transfers between devices, body(): rows = jnp.sum(lax.all_to_all(spread, OWNERS, 0, 0, tiled=True), axis=0)  24.2 us
    dot_general x1, matrix products, schur_rows(): solved = jnp.dot(inverse, coupled, preferred_element_type=jnp.float32)  10.1 us
    all_to_all x1, starting transfers between devices, body(): rows = jnp.sum(lax.all_to_all(spread, OWNERS, 0, 0, tiled=True), axis=0)  4.25 us
    dot_general x1, matrix products, moved(): jnp.dot(rows.astype(jnp.bfloat16), place, preferred_element_type=jnp.floa...  3.36 us
    dot_general x1, matrix products, schur_rows(): lax.dot_general(coupled, solved_hi, contract, preferred_element_type=jnp....  2.52 us
  transfers between devices with their start and end apart: 32, of which 23 were waited for; matrix products, arithmetic and copies ran while one was open for 20% of the time, Pallas kernels for 0%

profile of v18, /device:TPU:1, one launch (start us, length us, event | category | flops | bytes accessed | tf_op | source)
XLA Modules:
  0.0 124.5 jit_solution(7252000532243154517)
XLA Ops:
  1.8 2.6 %collective-permute-start.4 = (f32[64,256]{1,0:T(8,128)S(1)}, f32[64,256]{1,0:T(8,128)S(1)}, u32[]{:S(2)}, u32[]{:S(2)}) collective-permute-start(f32[64,256]{1,0:T(8,128)S(1)} %pad_maximum_fusion.11), channel_id=1, source_target_pairs={{0,4},{4,8},{8,12},{12,0},{1,5},{5,9},{9,13},{13,1},{2,6},{6,10},{... | collective-permute-start | bytes 196616 | tf_op jit(solution)/shard_map/ppermute | solution.py:20
  5.3 1.3 %collective-permute-start = (bf16[64,128]{1,0:T(8,128)(2,1)S(1)}, bf16[64,128]{1,0:T(8,128)(2,1)S(1)}, u32[]{:S(2)}, u32[]{:S(2)}) collective-permute-start(bf16[64,128]{1,0:T(8,128)(2,1)S(1)} %get-tuple-element.42), channel_id=1, source_target_pairs={{0,1},{1,2},{2,3},{3,0},{4,5},{5,6},{6,7},{7,4},{8,9},{9,10},{10,1... | collective-permute-start | bytes 49160 | tf_op jit(solution)/shard_map/ppermute | solution.py:20
  6.6 2.3 %collective-permute-start.1 = (bf16[64,128]{1,0:T(8,128)(2,1)S(1)}, bf16[64,128]{1,0:T(8,128)(2,1)S(1)}, u32[]{:S(2)}, u32[]{:S(2)}) collective-permute-start(bf16[64,128]{1,0:T(8,128)(2,1)S(1)} %get-tuple-element.42), channel_id=1, source_target_pairs={{0,2},{1,3},{2,0},{3,1},{4,6},{5,7},{6,4},{7,5},{8,10},{9,11},{10,... | collective-permute-start | bytes 49160 | tf_op jit(solution)/shard_map/ppermute | solution.py:20
  8.9 1.1 collective-permute-start.2
  11.6 1.7 %convolution_convert_fusion = bf16[512,2560]{1,0:T(8,128)(2,1)S(1)} fusion(bf16[1,1,2560,512]{3,2,1,0:T(8,128)(2,1)S(1)} %copy-done, s32[512]{0:T(512)S(1)} %fusion.70), kind=kOutput, calls=%fused_computation.5 | convolution fusion | flops 1344012288 | bytes 5244928 | tf_op jit(solution)/shard_map/dot_general | solution.py:52
  13.3 10.1 %fusion = f32[512,2560]{1,0:T(8,128)S(1)} fusion(bf16[512,2560]{1,0:T(8,128)(2,1)S(1)} %convolution_convert_fusion, bf16[1,1,2560,2560]{3,2,1,0:T(8,128)(2,1)} %param.17), kind=kOutput, calls=%fused_computation | convolution fusion | flops 6710886400 | bytes 20971520 | tf_op jit(solution)/shard_map/dot_general | solution.py:54
  23.4 1.6 %fusion.3 = f32[512,512]{1,0:T(8,128)S(1)} fusion(bf16[512,2560]{1,0:T(8,128)(2,1)S(1)} %convolution_convert_fusion, f32[512,2560]{1,0:T(8,128)S(1)} %fusion), kind=kOutput, calls=%fused_computation.6 | convolution fusion | flops 1346109440 | bytes 8912896 | tf_op jit(solution)/shard_map/dot_general | solution.py:57
  25.0 2.5 %fusion.7 = f32[512,512]{1,0:T(8,128)} fusion(f32[512,512]{1,0:T(8,128)S(1)} %fusion.3, bf16[512,2560]{1,0:T(8,128)(2,1)S(1)} %convolution_convert_fusion, f32[512,2560]{1,0:T(8,128)S(1)} %fusion), kind=kOutput, calls=%fused_computation.10 | convolution fusion | flops 1345060864 | bytes 9961472 | tf_op jit(solution)/shard_map/dot_general | solution.py:56
  27.5 3.4 %convolution_subtract_fusion = f32[512,512]{1,0:T(8,128)} fusion(f32[512,512]{1,0:T(8,128)} %fusion.7, bf16[1,1,512,512]{3,2,1,0:T(8,128)(2,1)} %param.15, s32[512]{0:T(512)S(1)} %fusion.70), kind=kOutput, calls=%fused_computation.9 | convolution fusion | flops 537919488 | bytes 2623488 | tf_op jit(solution)/shard_map/dot_general | solution.py:49
  30.9 1.2 collective-permute-start.5
  32.1 1.3 %collective-permute-start.3 = (bf16[4,64,128]{2,1,0:T(8,128)(2,1)S(1)}, bf16[4,64,128]{2,1,0:T(8,128)(2,1)S(1)}, u32[]{:S(2)}, u32[]{:S(2)}) collective-permute-start(bf16[4,64,128]{2,1,0:T(8,128)(2,1)S(1)} %get-tuple-element.40), channel_id=1, source_target_pairs={{0,16},{16,0},{1,17},{17,1},{2,18},{18,2},{3,19},{19,3},{4,20},{20... | collective-permute-start | bytes 196616 | tf_op jit(solution)/shard_map/ppermute | solution.py:20
  35.8 4.2 %all-to-all-start = ((f32[8,64,512]{2,1,0:T(8,128)}), f32[8,64,512]{2,1,0:T(8,128)}, u32[]{:S(2)}, u32[]{:S(2)}) async-start(f32[8,64,512]{2,1,0:T(8,128)} %bitcast.226), calls=%async_computation | async-start | bytes 2097152 | tf_op jit(solution)/shard_map/all_to_all | solution.py:121
  40.4 24.2 %all-to-all-done = f32[8,64,512]{2,1,0:T(8,128)} async-done(((f32[8,64,512]{2,1,0:T(8,128)}), f32[8,64,512]{2,1,0:T(8,128)}, u32[]{:S(2)}, u32[]{:S(2)}) %all-to-all-start) | async-done | bytes 1048608 | tf_op jit(solution)/shard_map/all_to_all | solution.py:121
  64.6 1.3 %reduce_sum.9 = f32[64,512]{1,0:T(8,128)S(1)} reduce(f32[8,64,512]{2,1,0:T(8,128)} %all-to-all-done, f32[]{:T(128)} %constant.85.clone.1), dimensions={0}, to_apply=%region_0.1 | reduce | flops 229376 | bytes 1179652 | tf_op jit(solution)/shard_map/reduce_sum | solution.py:121
  67.1 4.1 %collective-permute-start.7 = (f32[64,128]{1,0:T(8,128)S(1)}, f32[64,128]{1,0:T(8,128)S(1)}, u32[]{:S(2)}, u32[]{:S(2)}) collective-permute-start(f32[64,128]{1,0:T(8,128)S(1)} %fusion.18), channel_id=1, source_target_pairs={{0,4},{4,8},{8,12},{12,0},{1,5},{5,9},{9,13},{13,1},{2,6},{6,10},{... | collective-permute-start | bytes 98312 | tf_op jit(solution)/shard_map/ppermute | solution.py:20
  72.2 1.7 %collective-permute-done.8 = f32[64,128]{1,0:T(8,128)S(1)} collective-permute-done((f32[64,128]{1,0:T(8,128)S(1)}, f32[64,128]{1,0:T(8,128)S(1)}, u32[]{:S(2)}, u32[]{:S(2)}) %collective-permute-start.8) | collective-permute-done | bytes 32800 | tf_op jit(solution)/shard_map/ppermute | solution.py:20
  75.3 3.2 %collective-permute-start.12 = (bf16[64,128]{1,0:T(8,128)(2,1)S(1)}, bf16[64,128]{1,0:T(8,128)(2,1)S(1)}, u32[]{:S(2)}, u32[]{:S(2)}) collective-permute-start(bf16[64,128]{1,0:T(8,128)(2,1)S(1)} %get-tuple-element.38), channel_id=1, source_target_pairs={{0,3},{1,0},{2,1},{3,2},{4,7},{5,4},{6,5},{7,6},{8,11},{9,8},{10,9... | collective-permute-start | bytes 49160 | tf_op jit(solution)/shard_map/ppermute | solution.py:20
  80.8 2.7 %collective-permute-done.13 = bf16[4,64,128]{2,1,0:T(8,128)(2,1)S(1)} collective-permute-done((bf16[4,64,128]{2,1,0:T(8,128)(2,1)S(1)}, bf16[4,64,128]{2,1,0:T(8,128)(2,1)S(1)}, u32[]{:S(2)}, u32[]{:S(2)}) %collective-permute-start.13) | collective-permute-done | bytes 65568 | tf_op jit(solution)/shard_map/ppermute | solution.py:20
  83.8 2.7 %collective-permute-start.14 = (f32[64,128]{1,0:T(8,128)S(1)}, f32[64,128]{1,0:T(8,128)S(1)}, u32[]{:S(2)}, u32[]{:S(2)}) collective-permute-start(f32[64,128]{1,0:T(8,128)S(1)} %fusion.15), channel_id=1, source_target_pairs={{0,4},{4,8},{8,12},{12,0},{1,5},{5,9},{9,13},{13,1},{2,6},{6,10},{... | collective-permute-start | bytes 98312 | tf_op jit(solution)/shard_map/ppermute | solution.py:20
  87.5 2.1 %collective-permute-done.15 = f32[64,128]{1,0:T(8,128)S(1)} collective-permute-done((f32[64,128]{1,0:T(8,128)S(1)}, f32[64,128]{1,0:T(8,128)S(1)}, u32[]{:S(2)}, u32[]{:S(2)}) %collective-permute-start.15) | collective-permute-done | bytes 32800 | tf_op jit(solution)/shard_map/ppermute | solution.py:20
  90.8 1.8 %collective-permute-start.17 = (bf16[64,128]{1,0:T(8,128)(2,1)S(1)}, bf16[64,128]{1,0:T(8,128)(2,1)S(1)}, u32[]{:S(2)}, u32[]{:S(2)}) collective-permute-start(bf16[64,128]{1,0:T(8,128)(2,1)S(1)} %get-tuple-element.34), channel_id=1, source_target_pairs={{0,1},{1,2},{2,3},{3,0},{4,5},{5,6},{6,7},{7,4},{8,9},{9,10},{10,1... | collective-permute-start | bytes 49160 | tf_op jit(solution)/shard_map/ppermute | solution.py:20
  92.6 1.5 %collective-permute-start.18 = (bf16[64,128]{1,0:T(8,128)(2,1)S(1)}, bf16[64,128]{1,0:T(8,128)(2,1)S(1)}, u32[]{:S(2)}, u32[]{:S(2)}) collective-permute-start(bf16[64,128]{1,0:T(8,128)(2,1)S(1)} %get-tuple-element.34), channel_id=1, source_target_pairs={{0,2},{1,3},{2,0},{3,1},{4,6},{5,7},{6,4},{7,5},{8,10},{9,11},{10,... | collective-permute-start | bytes 49160 | tf_op jit(solution)/shard_map/ppermute | solution.py:20
  97.2 2.7 %collective-permute-done.20 = bf16[4,64,128]{2,1,0:T(8,128)(2,1)S(1)} collective-permute-done((bf16[4,64,128]{2,1,0:T(8,128)(2,1)S(1)}, bf16[4,64,128]{2,1,0:T(8,128)(2,1)S(1)}, u32[]{:S(2)}, u32[]{:S(2)}) %collective-permute-start.20) | collective-permute-done | bytes 65568 | tf_op jit(solution)/shard_map/ppermute | solution.py:20
  100.3 3.2 %collective-permute-start.21 = (f32[64,128]{1,0:T(8,128)S(1)}, f32[64,128]{1,0:T(8,128)S(1)}, u32[]{:S(2)}, u32[]{:S(2)}) collective-permute-start(f32[64,128]{1,0:T(8,128)S(1)} %fusion.12), channel_id=1, source_target_pairs={{0,4},{4,8},{8,12},{12,0},{1,5},{5,9},{9,13},{13,1},{2,6},{6,10},{... | collective-permute-start | bytes 98312 | tf_op jit(solution)/shard_map/ppermute | solution.py:20
  104.5 1.9 %collective-permute-done.22 = f32[64,128]{1,0:T(8,128)S(1)} collective-permute-done((f32[64,128]{1,0:T(8,128)S(1)}, f32[64,128]{1,0:T(8,128)S(1)}, u32[]{:S(2)}, u32[]{:S(2)}) %collective-permute-start.22) | collective-permute-done | bytes 32800 | tf_op jit(solution)/shard_map/ppermute | solution.py:20
  108.0 2.3 %collective-permute-start.25 = (bf16[64,128]{1,0:T(8,128)(2,1)S(1)}, bf16[64,128]{1,0:T(8,128)(2,1)S(1)}, u32[]{:S(2)}, u32[]{:S(2)}) collective-permute-start(bf16[64,128]{1,0:T(8,128)(2,1)S(1)} %get-tuple-element.30), channel_id=1, source_target_pairs={{0,2},{1,3},{2,0},{3,1},{4,6},{5,7},{6,4},{7,5},{8,10},{9,11},{10,... | collective-permute-start | bytes 49160 | tf_op jit(solution)/shard_map/ppermute | solution.py:20
  111.3 1.3 %collective-permute-done.24 = bf16[64,128]{1,0:T(8,128)(2,1)S(1)} collective-permute-done((bf16[64,128]{1,0:T(8,128)(2,1)S(1)}, bf16[64,128]{1,0:T(8,128)(2,1)S(1)}, u32[]{:S(2)}, u32[]{:S(2)}) %collective-permute-start.24) | collective-permute-done | bytes 16416 | tf_op jit(solution)/shard_map/ppermute | solution.py:20
  113.3 2.7 %collective-permute-done.27 = bf16[4,64,128]{2,1,0:T(8,128)(2,1)S(1)} collective-permute-done((bf16[4,64,128]{2,1,0:T(8,128)(2,1)S(1)}, bf16[4,64,128]{2,1,0:T(8,128)(2,1)S(1)}, u32[]{:S(2)}, u32[]{:S(2)}) %collective-permute-start.27) | collective-permute-done | bytes 65568 | tf_op jit(solution)/shard_map/ppermute | solution.py:20
  116.4 2.9 %collective-permute-start.28 = (f32[64,128]{1,0:T(8,128)S(1)}, f32[64,128]{1,0:T(8,128)S(1)}, u32[]{:S(2)}, u32[]{:S(2)}) collective-permute-start(f32[64,128]{1,0:T(8,128)S(1)} %fusion.9), channel_id=1, source_target_pairs={{0,4},{4,8},{8,12},{12,0},{1,5},{5,9},{9,13},{13,1},{2,6},{6,10},{... | collective-permute-start | bytes 98312 | tf_op jit(solution)/shard_map/ppermute | solution.py:20
  119.3 1.0 collective-permute-start.29
  120.3 2.2 %collective-permute-done.29 = f32[64,128]{1,0:T(8,128)S(1)} collective-permute-done((f32[64,128]{1,0:T(8,128)S(1)}, f32[64,128]{1,0:T(8,128)S(1)}, u32[]{:S(2)}, u32[]{:S(2)}) %collective-permute-start.29) | collective-permute-done | bytes 32800 | tf_op jit(solution)/shard_map/ppermute | solution.py:20
  122.5 1.1 collective-permute-done.30
  (106 shorter events, 24.3 us)
Async XLA Ops:
  1.7 31.7 %collective-permute-start.6 = (f32[64,256]{1,0:T(8,128)S(1)}, f32[64,256]{1,0:T(8,128)S(1)}, u32[]{:S(2)}, u32[]{:S(2)}) collective-permute-start(f32[64,256]{1,0:T(8,128)S(1)} %pad_maximum_fusion.11), channel_id=1, source_target_pairs={{0,12},{4,0},{8,4},{12,8},{1,13},{5,1},{9,5},{13,9},{2,14},{6,2},{... | collective-permute-start | bytes 196616 | tf_op jit(solution)/shard_map/ppermute | solution.py:20
  1.8 31.6 %collective-permute-start.4 = (f32[64,256]{1,0:T(8,128)S(1)}, f32[64,256]{1,0:T(8,128)S(1)}, u32[]{:S(2)}, u32[]{:S(2)}) collective-permute-start(f32[64,256]{1,0:T(8,128)S(1)} %pad_maximum_fusion.11), channel_id=1, source_target_pairs={{0,4},{4,8},{8,12},{12,0},{1,5},{5,9},{9,13},{13,1},{2,6},{6,10},{... | collective-permute-start | bytes 196616 | tf_op jit(solution)/shard_map/ppermute | solution.py:20
  5.3 25.6 %collective-permute-start = (bf16[64,128]{1,0:T(8,128)(2,1)S(1)}, bf16[64,128]{1,0:T(8,128)(2,1)S(1)}, u32[]{:S(2)}, u32[]{:S(2)}) collective-permute-start(bf16[64,128]{1,0:T(8,128)(2,1)S(1)} %get-tuple-element.42), channel_id=1, source_target_pairs={{0,1},{1,2},{2,3},{3,0},{4,5},{5,6},{6,7},{7,4},{8,9},{9,10},{10,1... | collective-permute-start | bytes 49160 | tf_op jit(solution)/shard_map/ppermute | solution.py:20
  6.6 25.5 %collective-permute-start.1 = (bf16[64,128]{1,0:T(8,128)(2,1)S(1)}, bf16[64,128]{1,0:T(8,128)(2,1)S(1)}, u32[]{:S(2)}, u32[]{:S(2)}) collective-permute-start(bf16[64,128]{1,0:T(8,128)(2,1)S(1)} %get-tuple-element.42), channel_id=1, source_target_pairs={{0,2},{1,3},{2,0},{3,1},{4,6},{5,7},{6,4},{7,5},{8,10},{9,11},{10,... | collective-permute-start | bytes 49160 | tf_op jit(solution)/shard_map/ppermute | solution.py:20
  8.9 23.2 %collective-permute-start.2 = (bf16[64,128]{1,0:T(8,128)(2,1)S(1)}, bf16[64,128]{1,0:T(8,128)(2,1)S(1)}, u32[]{:S(2)}, u32[]{:S(2)}) collective-permute-start(bf16[64,128]{1,0:T(8,128)(2,1)S(1)} %get-tuple-element.42), channel_id=1, source_target_pairs={{0,3},{1,0},{2,1},{3,2},{4,7},{5,4},{6,5},{7,6},{8,11},{9,8},{10,9... | collective-permute-start | bytes 49160 | tf_op jit(solution)/shard_map/ppermute | solution.py:20
  30.9 3.2 %collective-permute-start.5 = (f32[64,256]{1,0:T(8,128)S(1)}, f32[64,256]{1,0:T(8,128)S(1)}, u32[]{:S(2)}, u32[]{:S(2)}) collective-permute-start(f32[64,256]{1,0:T(8,128)S(1)} %pad_maximum_fusion.11), channel_id=1, source_target_pairs={{0,8},{4,12},{8,0},{12,4},{1,9},{5,13},{9,1},{13,5},{2,10},{6,14},... | collective-permute-start | bytes 196616 | tf_op jit(solution)/shard_map/ppermute | solution.py:20
  32.1 3.7 %collective-permute-start.3 = (bf16[4,64,128]{2,1,0:T(8,128)(2,1)S(1)}, bf16[4,64,128]{2,1,0:T(8,128)(2,1)S(1)}, u32[]{:S(2)}, u32[]{:S(2)}) collective-permute-start(bf16[4,64,128]{2,1,0:T(8,128)(2,1)S(1)} %get-tuple-element.40), channel_id=1, source_target_pairs={{0,16},{16,0},{1,17},{17,1},{2,18},{18,2},{3,19},{19,3},{4,20},{20... | collective-permute-start | bytes 196616 | tf_op jit(solution)/shard_map/ppermute | solution.py:20
  35.8 28.8 %all-to-all-start = ((f32[8,64,512]{2,1,0:T(8,128)}), f32[8,64,512]{2,1,0:T(8,128)}, u32[]{:S(2)}, u32[]{:S(2)}) async-start(f32[8,64,512]{2,1,0:T(8,128)} %bitcast.226), calls=%async_computation | async-start | bytes 2097152 | tf_op jit(solution)/shard_map/all_to_all | solution.py:121
  67.1 5.1 %collective-permute-start.7 = (f32[64,128]{1,0:T(8,128)S(1)}, f32[64,128]{1,0:T(8,128)S(1)}, u32[]{:S(2)}, u32[]{:S(2)}) collective-permute-start(f32[64,128]{1,0:T(8,128)S(1)} %fusion.18), channel_id=1, source_target_pairs={{0,4},{4,8},{8,12},{12,0},{1,5},{5,9},{9,13},{13,1},{2,6},{6,10},{... | collective-permute-start | bytes 98312 | tf_op jit(solution)/shard_map/ppermute | solution.py:20
  71.2 2.8 %collective-permute-start.8 = (f32[64,128]{1,0:T(8,128)S(1)}, f32[64,128]{1,0:T(8,128)S(1)}, u32[]{:S(2)}, u32[]{:S(2)}) collective-permute-start(f32[64,128]{1,0:T(8,128)S(1)} %fusion.18), channel_id=1, source_target_pairs={{0,8},{4,12},{8,0},{12,4},{1,9},{5,13},{9,1},{13,5},{2,10},{6,14},... | collective-permute-start | bytes 98312 | tf_op jit(solution)/shard_map/ppermute | solution.py:20
  71.5 3.3 %collective-permute-start.9 = (f32[64,128]{1,0:T(8,128)S(1)}, f32[64,128]{1,0:T(8,128)S(1)}, u32[]{:S(2)}, u32[]{:S(2)}) collective-permute-start(f32[64,128]{1,0:T(8,128)S(1)} %fusion.18), channel_id=1, source_target_pairs={{0,12},{4,0},{8,4},{12,8},{1,13},{5,1},{9,5},{13,9},{2,14},{6,2},{... | collective-permute-start | bytes 98312 | tf_op jit(solution)/shard_map/ppermute | solution.py:20
  75.2 4.4 %collective-permute-start.10 = (bf16[64,128]{1,0:T(8,128)(2,1)S(1)}, bf16[64,128]{1,0:T(8,128)(2,1)S(1)}, u32[]{:S(2)}, u32[]{:S(2)}) collective-permute-start(bf16[64,128]{1,0:T(8,128)(2,1)S(1)} %get-tuple-element.38), channel_id=1, source_target_pairs={{0,1},{1,2},{2,3},{3,0},{4,5},{5,6},{6,7},{7,4},{8,9},{9,10},{10,1... | collective-permute-start | bytes 49160 | tf_op jit(solution)/shard_map/ppermute | solution.py:20
  75.2 4.4 %collective-permute-start.11 = (bf16[64,128]{1,0:T(8,128)(2,1)S(1)}, bf16[64,128]{1,0:T(8,128)(2,1)S(1)}, u32[]{:S(2)}, u32[]{:S(2)}) collective-permute-start(bf16[64,128]{1,0:T(8,128)(2,1)S(1)} %get-tuple-element.38), channel_id=1, source_target_pairs={{0,2},{1,3},{2,0},{3,1},{4,6},{5,7},{6,4},{7,5},{8,10},{9,11},{10,... | collective-permute-start | bytes 49160 | tf_op jit(solution)/shard_map/ppermute | solution.py:20
  75.3 5.0 %collective-permute-start.12 = (bf16[64,128]{1,0:T(8,128)(2,1)S(1)}, bf16[64,128]{1,0:T(8,128)(2,1)S(1)}, u32[]{:S(2)}, u32[]{:S(2)}) collective-permute-start(bf16[64,128]{1,0:T(8,128)(2,1)S(1)} %get-tuple-element.38), channel_id=1, source_target_pairs={{0,3},{1,0},{2,1},{3,2},{4,7},{5,4},{6,5},{7,6},{8,11},{9,8},{10,9... | collective-permute-start | bytes 49160 | tf_op jit(solution)/shard_map/ppermute | solution.py:20
  80.3 3.2 %collective-permute-start.13 = (bf16[4,64,128]{2,1,0:T(8,128)(2,1)S(1)}, bf16[4,64,128]{2,1,0:T(8,128)(2,1)S(1)}, u32[]{:S(2)}, u32[]{:S(2)}) collective-permute-start(bf16[4,64,128]{2,1,0:T(8,128)(2,1)S(1)} %get-tuple-element.36), channel_id=1, source_target_pairs={{0,16},{16,0},{1,17},{17,1},{2,18},{18,2},{3,19},{19,3},{4,20},{20... | collective-permute-start | bytes 196616 | tf_op jit(solution)/shard_map/ppermute | solution.py:20
  83.8 3.7 %collective-permute-start.14 = (f32[64,128]{1,0:T(8,128)S(1)}, f32[64,128]{1,0:T(8,128)S(1)}, u32[]{:S(2)}, u32[]{:S(2)}) collective-permute-start(f32[64,128]{1,0:T(8,128)S(1)} %fusion.15), channel_id=1, source_target_pairs={{0,4},{4,8},{8,12},{12,0},{1,5},{5,9},{9,13},{13,1},{2,6},{6,10},{... | collective-permute-start | bytes 98312 | tf_op jit(solution)/shard_map/ppermute | solution.py:20
  86.5 3.1 %collective-permute-start.15 = (f32[64,128]{1,0:T(8,128)S(1)}, f32[64,128]{1,0:T(8,128)S(1)}, u32[]{:S(2)}, u32[]{:S(2)}) collective-permute-start(f32[64,128]{1,0:T(8,128)S(1)} %fusion.15), channel_id=1, source_target_pairs={{0,8},{4,12},{8,0},{12,4},{1,9},{5,13},{9,1},{13,5},{2,10},{6,14},... | collective-permute-start | bytes 98312 | tf_op jit(solution)/shard_map/ppermute | solution.py:20
  87.2 3.3 %collective-permute-start.16 = (f32[64,128]{1,0:T(8,128)S(1)}, f32[64,128]{1,0:T(8,128)S(1)}, u32[]{:S(2)}, u32[]{:S(2)}) collective-permute-start(f32[64,128]{1,0:T(8,128)S(1)} %fusion.15), channel_id=1, source_target_pairs={{0,12},{4,0},{8,4},{12,8},{1,13},{5,1},{9,5},{13,9},{2,14},{6,2},{... | collective-permute-start | bytes 98312 | tf_op jit(solution)/shard_map/ppermute | solution.py:20
  90.8 4.8 %collective-permute-start.17 = (bf16[64,128]{1,0:T(8,128)(2,1)S(1)}, bf16[64,128]{1,0:T(8,128)(2,1)S(1)}, u32[]{:S(2)}, u32[]{:S(2)}) collective-permute-start(bf16[64,128]{1,0:T(8,128)(2,1)S(1)} %get-tuple-element.34), channel_id=1, source_target_pairs={{0,1},{1,2},{2,3},{3,0},{4,5},{5,6},{6,7},{7,4},{8,9},{9,10},{10,1... | collective-permute-start | bytes 49160 | tf_op jit(solution)/shard_map/ppermute | solution.py:20
  92.6 3.6 %collective-permute-start.18 = (bf16[64,128]{1,0:T(8,128)(2,1)S(1)}, bf16[64,128]{1,0:T(8,128)(2,1)S(1)}, u32[]{:S(2)}, u32[]{:S(2)}) collective-permute-start(bf16[64,128]{1,0:T(8,128)(2,1)S(1)} %get-tuple-element.34), channel_id=1, source_target_pairs={{0,2},{1,3},{2,0},{3,1},{4,6},{5,7},{6,4},{7,5},{8,10},{9,11},{10,... | collective-permute-start | bytes 49160 | tf_op jit(solution)/shard_map/ppermute | solution.py:20
  94.1 2.6 %collective-permute-start.19 = (bf16[64,128]{1,0:T(8,128)(2,1)S(1)}, bf16[64,128]{1,0:T(8,128)(2,1)S(1)}, u32[]{:S(2)}, u32[]{:S(2)}) collective-permute-start(bf16[64,128]{1,0:T(8,128)(2,1)S(1)} %get-tuple-element.34), channel_id=1, source_target_pairs={{0,3},{1,0},{2,1},{3,2},{4,7},{5,4},{6,5},{7,6},{8,11},{9,8},{10,9... | collective-permute-start | bytes 49160 | tf_op jit(solution)/shard_map/ppermute | solution.py:20
  96.8 3.2 %collective-permute-start.20 = (bf16[4,64,128]{2,1,0:T(8,128)(2,1)S(1)}, bf16[4,64,128]{2,1,0:T(8,128)(2,1)S(1)}, u32[]{:S(2)}, u32[]{:S(2)}) collective-permute-start(bf16[4,64,128]{2,1,0:T(8,128)(2,1)S(1)} %get-tuple-element.32), channel_id=1, source_target_pairs={{0,16},{16,0},{1,17},{17,1},{2,18},{18,2},{3,19},{19,3},{4,20},{20... | collective-permute-start | bytes 196616 | tf_op jit(solution)/shard_map/ppermute | solution.py:20
  100.3 4.2 %collective-permute-start.21 = (f32[64,128]{1,0:T(8,128)S(1)}, f32[64,128]{1,0:T(8,128)S(1)}, u32[]{:S(2)}, u32[]{:S(2)}) collective-permute-start(f32[64,128]{1,0:T(8,128)S(1)} %fusion.12), channel_id=1, source_target_pairs={{0,4},{4,8},{8,12},{12,0},{1,5},{5,9},{9,13},{13,1},{2,6},{6,10},{... | collective-permute-start | bytes 98312 | tf_op jit(solution)/shard_map/ppermute | solution.py:20
  103.5 3.0 %collective-permute-start.22 = (f32[64,128]{1,0:T(8,128)S(1)}, f32[64,128]{1,0:T(8,128)S(1)}, u32[]{:S(2)}, u32[]{:S(2)}) collective-permute-start(f32[64,128]{1,0:T(8,128)S(1)} %fusion.12), channel_id=1, source_target_pairs={{0,8},{4,12},{8,0},{12,4},{1,9},{5,13},{9,1},{13,5},{2,10},{6,14},... | collective-permute-start | bytes 98312 | tf_op jit(solution)/shard_map/ppermute | solution.py:20
  104.0 3.3 %collective-permute-start.23 = (f32[64,128]{1,0:T(8,128)S(1)}, f32[64,128]{1,0:T(8,128)S(1)}, u32[]{:S(2)}, u32[]{:S(2)}) collective-permute-start(f32[64,128]{1,0:T(8,128)S(1)} %fusion.12), channel_id=1, source_target_pairs={{0,12},{4,0},{8,4},{12,8},{1,13},{5,1},{9,5},{13,9},{2,14},{6,2},{... | collective-permute-start | bytes 98312 | tf_op jit(solution)/shard_map/ppermute | solution.py:20
  107.7 4.9 %collective-permute-start.24 = (bf16[64,128]{1,0:T(8,128)(2,1)S(1)}, bf16[64,128]{1,0:T(8,128)(2,1)S(1)}, u32[]{:S(2)}, u32[]{:S(2)}) collective-permute-start(bf16[64,128]{1,0:T(8,128)(2,1)S(1)} %get-tuple-element.30), channel_id=1, source_target_pairs={{0,1},{1,2},{2,3},{3,0},{4,5},{5,6},{6,7},{7,4},{8,9},{9,10},{10,1... | collective-permute-start | bytes 49160 | tf_op jit(solution)/shard_map/ppermute | solution.py:20
  108.0 4.6 %collective-permute-start.25 = (bf16[64,128]{1,0:T(8,128)(2,1)S(1)}, bf16[64,128]{1,0:T(8,128)(2,1)S(1)}, u32[]{:S(2)}, u32[]{:S(2)}) collective-permute-start(bf16[64,128]{1,0:T(8,128)(2,1)S(1)} %get-tuple-element.30), channel_id=1, source_target_pairs={{0,2},{1,3},{2,0},{3,1},{4,6},{5,7},{6,4},{7,5},{8,10},{9,11},{10,... | collective-permute-start | bytes 49160 | tf_op jit(solution)/shard_map/ppermute | solution.py:20
  110.3 2.6 %collective-permute-start.26 = (bf16[64,128]{1,0:T(8,128)(2,1)S(1)}, bf16[64,128]{1,0:T(8,128)(2,1)S(1)}, u32[]{:S(2)}, u32[]{:S(2)}) collective-permute-start(bf16[64,128]{1,0:T(8,128)(2,1)S(1)} %get-tuple-element.30), channel_id=1, source_target_pairs={{0,3},{1,0},{2,1},{3,2},{4,7},{5,4},{6,5},{7,6},{8,11},{9,8},{10,9... | collective-permute-start | bytes 49160 | tf_op jit(solution)/shard_map/ppermute | solution.py:20
  112.9 3.2 %collective-permute-start.27 = (bf16[4,64,128]{2,1,0:T(8,128)(2,1)S(1)}, bf16[4,64,128]{2,1,0:T(8,128)(2,1)S(1)}, u32[]{:S(2)}, u32[]{:S(2)}) collective-permute-start(bf16[4,64,128]{2,1,0:T(8,128)(2,1)S(1)} %get-tuple-element.28), channel_id=1, source_target_pairs={{0,16},{16,0},{1,17},{17,1},{2,18},{18,2},{3,19},{19,3},{4,20},{20... | collective-permute-start | bytes 196616 | tf_op jit(solution)/shard_map/ppermute | solution.py:20
  116.4 3.9 %collective-permute-start.28 = (f32[64,128]{1,0:T(8,128)S(1)}, f32[64,128]{1,0:T(8,128)S(1)}, u32[]{:S(2)}, u32[]{:S(2)}) collective-permute-start(f32[64,128]{1,0:T(8,128)S(1)} %fusion.9), channel_id=1, source_target_pairs={{0,4},{4,8},{8,12},{12,0},{1,5},{5,9},{9,13},{13,1},{2,6},{6,10},{... | collective-permute-start | bytes 98312 | tf_op jit(solution)/shard_map/ppermute | solution.py:20
  119.3 3.2 %collective-permute-start.29 = (f32[64,128]{1,0:T(8,128)S(1)}, f32[64,128]{1,0:T(8,128)S(1)}, u32[]{:S(2)}, u32[]{:S(2)}) collective-permute-start(f32[64,128]{1,0:T(8,128)S(1)} %fusion.9), channel_id=1, source_target_pairs={{0,8},{4,12},{8,0},{12,4},{1,9},{5,13},{9,1},{13,5},{2,10},{6,14},... | collective-permute-start | bytes 98312 | tf_op jit(solution)/shard_map/ppermute | solution.py:20
  120.3 3.3 %collective-permute-start.30 = (f32[64,128]{1,0:T(8,128)S(1)}, f32[64,128]{1,0:T(8,128)S(1)}, u32[]{:S(2)}, u32[]{:S(2)}) collective-permute-start(f32[64,128]{1,0:T(8,128)S(1)} %fusion.9), channel_id=1, source_target_pairs={{0,12},{4,0},{8,4},{12,8},{1,13},{5,1},{9,5},{13,9},{2,14},{6,2},{... | collective-permute-start | bytes 98312 | tf_op jit(solution)/shard_map/ppermute | solution.py:20
  (4 other events, 35.5 us)

commit v19 on v14

--- a/solution.py
+++ b/solution.py
@@ -53,8 +53,9 @@
         boundary = moved(boundary)
     solved = jnp.dot(inverse, coupled, preferred_element_type=jnp.float32)
     solved_hi, solved_lo = split_bf16(solved)
-    pulled = lax.dot_general(coupled, solved_hi, contract, preferred_element_type=jnp.float32)
-    pulled = pulled + lax.dot_general(coupled, solved_lo, contract, preferred_element_type=jnp.float32)
+    both = jnp.concatenate([solved_hi, solved_lo], axis=1)
+    pulled = lax.dot_general(coupled, both, contract, preferred_element_type=jnp.float32)
+    pulled = pulled[:, : solved.shape[1]] + pulled[:, solved.shape[1] :]
     schur = boundary.astype(jnp.float32) - pulled
     if picks != owners:
         schur_hi, schur_lo = split_bf16(schur)

time: 125 us -> 129 us (1.032)
  matrix products: 26.3 us -> 30.8 us
    dot_general x2 -> x1, matrix products: 4.08 us -> 6.75 us  [schur_rows(): lax.dot_general(coupled, both, contract, preferred_element_type=jnp.float32)]
    dot_general x1, matrix products: 10.1 us -> 11.6 us  [schur_rows(): solved = jnp.dot(inverse, coupled, preferred_element_type=jnp.float32)]
  transfers between devices with their start and end apart: 32 -> 32, of which waited for: 23 -> 23; matrix products, arithmetic and copies ran while one was open for 21% -> 23% of each run, Pallas kernels for 0% -> 0%
where the time goes in v19:
time: 129 us
  waiting for transfers between devices  50.3 us (39%)
  starting transfers between devices  41.2 us (32%)
  matrix products  30.8 us (24%)
  other arithmetic  5.71 us (4%)
    ppermute x31, starting transfers between devices, ring_parts(): parts.append(lax.ppermute(block, axis, route))  36.9 us
    ppermute x31, waiting for transfers between devices, ring_parts(): parts.append(lax.ppermute(block, axis, route))  26.1 us
    all_to_all x1, waiting for transfers between devices, body(): rows = jnp.sum(lax.all_to_all(spread, OWNERS, 0, 0, tiled=True), axis=0)  24.2 us
    dot_general x1, matrix products, schur_rows(): solved = jnp.dot(inverse, coupled, preferred_element_type=jnp.float32)  11.6 us
    dot_general x1, matrix products, schur_rows(): lax.dot_general(coupled, both, contract, preferred_element_type=jnp.float32)  6.75 us
    all_to_all x1, starting transfers between devices, body(): rows = jnp.sum(lax.all_to_all(spread, OWNERS, 0, 0, tiled=True), axis=0)  4.25 us
    dot_general x1, matrix products, moved(): jnp.dot(rows.astype(jnp.bfloat16), place, preferred_element_type=jnp.floa...  3.68 us
  transfers between devices with their start and end apart: 32, of which 23 were waited for; matrix products, arithmetic and copies ran while one was open for 23% of the time, Pallas kernels for 0%

profile of v19, /device:TPU:1, one launch (start us, length us, event | category | flops | bytes accessed | tf_op | source)
XLA Modules:
  0.0 128.8 jit_solution(9176774871369344104)
XLA Ops:
  1.8 2.6 %collective-permute-start.4 = (f32[64,256]{1,0:T(8,128)S(1)}, f32[64,256]{1,0:T(8,128)S(1)}, u32[]{:S(2)}, u32[]{:S(2)}) collective-permute-start(f32[64,256]{1,0:T(8,128)S(1)} %pad_maximum_fusion.15), channel_id=1, source_target_pairs={{0,4},{4,8},{8,12},{12,0},{1,5},{5,9},{9,13},{13,1},{2,6},{6,10},{... | collective-permute-start | bytes 196616 | tf_op jit(solution)/shard_map/ppermute | solution.py:20
  5.3 1.3 %collective-permute-start = (bf16[64,128]{1,0:T(8,128)(2,1)S(1)}, bf16[64,128]{1,0:T(8,128)(2,1)S(1)}, u32[]{:S(2)}, u32[]{:S(2)}) collective-permute-start(bf16[64,128]{1,0:T(8,128)(2,1)S(1)} %get-tuple-element.38), channel_id=1, source_target_pairs={{0,1},{1,2},{2,3},{3,0},{4,5},{5,6},{6,7},{7,4},{8,9},{9,10},{10,1... | collective-permute-start | bytes 49160 | tf_op jit(solution)/shard_map/ppermute | solution.py:20
  6.6 2.3 %collective-permute-start.1 = (bf16[64,128]{1,0:T(8,128)(2,1)S(1)}, bf16[64,128]{1,0:T(8,128)(2,1)S(1)}, u32[]{:S(2)}, u32[]{:S(2)}) collective-permute-start(bf16[64,128]{1,0:T(8,128)(2,1)S(1)} %get-tuple-element.38), channel_id=1, source_target_pairs={{0,2},{1,3},{2,0},{3,1},{4,6},{5,7},{6,4},{7,5},{8,10},{9,11},{10,... | collective-permute-start | bytes 49160 | tf_op jit(solution)/shard_map/ppermute | solution.py:20
  8.9 1.1 collective-permute-start.2
  11.6 1.7 %convolution_convert_fusion = bf16[512,2560]{1,0:T(8,128)(2,1)S(1)} fusion(bf16[1,1,2560,512]{3,2,1,0:T(8,128)(2,1)S(1)} %copy-done, s32[512]{0:T(512)S(1)} %fusion.53), kind=kOutput, calls=%fused_computation.9 | convolution fusion | flops 1344012288 | bytes 5244928 | tf_op jit(solution)/shard_map/dot_general | solution.py:52
  13.3 11.6 %reduce-precision_convert_fusion = (bf16[2560,512]{0,1:T(8,128)(2,1)}, bf16[2560,512]{0,1:T(8,128)(2,1)}) fusion(bf16[512,2560]{1,0:T(8,128)(2,1)S(1)} %convolution_convert_fusion, bf16[1,1,2560,2560]{3,2,1,0:T(8,128)(2,1)} %param.17), kind=kOutput, calls=%fused_computation.3 | convolution fusion | flops 6716129280 | bytes 20971520 | tf_op jit(solution)/shard_map/dot_general | solution.py:54
  24.9 6.8 %fusion.3 = f32[512,1024]{1,0:T(8,128)} fusion(bf16[512,2560]{1,0:T(8,128)(2,1)S(1)} %convolution_convert_fusion, bf16[2560,512]{0,1:T(8,128)(2,1)} %get-tuple-element.28, bf16[2560,512]{0,1:T(8,128)(2,1)} %get-tuple-element.27), kind=kOutput, calls=%fused_computation.5 | convolution fusion | flops 2694840320 | bytes 9961472 | tf_op jit(solution)/shard_map/dot_general | solution.py:57
  31.7 3.7 %convolution_subtract_fusion = f32[512,512]{1,0:T(8,128)} fusion(f32[512,1024]{1,0:T(8,128)} %fusion.3, bf16[1,1,512,512]{3,2,1,0:T(8,128)(2,1)} %param.15, s32[512]{0:T(512)S(1)} %fusion.53), kind=kOutput, calls=%fused_computation.11 | convolution fusion | flops 538181632 | bytes 3674112 | tf_op jit(solution)/shard_map/dot_general | solution.py:49
  35.4 1.2 collective-permute-start.5
  36.6 1.3 collective-permute-start.3
  40.3 4.3 %all-to-all-start = ((f32[8,64,512]{2,1,0:T(8,128)}), f32[8,64,512]{2,1,0:T(8,128)}, u32[]{:S(2)}, u32[]{:S(2)}) async-start(f32[8,64,512]{2,1,0:T(8,128)} %bitcast.199), calls=%async_computation | async-start | bytes 2097152 | tf_op jit(solution)/shard_map/all_to_all | solution.py:122
  44.9 24.2 %all-to-all-done = f32[8,64,512]{2,1,0:T(8,128)} async-done(((f32[8,64,512]{2,1,0:T(8,128)}), f32[8,64,512]{2,1,0:T(8,128)}, u32[]{:S(2)}, u32[]{:S(2)}) %all-to-all-start) | async-done | bytes 1048608 | tf_op jit(solution)/shard_map/all_to_all | solution.py:122
  69.2 1.3 %reduce_sum.9 = f32[64,512]{1,0:T(8,128)S(1)} reduce(f32[8,64,512]{2,1,0:T(8,128)} %all-to-all-done, f32[]{:T(128)} %constant.85.clone.1), dimensions={0}, to_apply=%region_0.1 | reduce | flops 229376 | bytes 1179652 | tf_op jit(solution)/shard_map/reduce_sum | solution.py:122
  71.6 4.1 %collective-permute-start.7 = (f32[64,128]{1,0:T(8,128)S(1)}, f32[64,128]{1,0:T(8,128)S(1)}, u32[]{:S(2)}, u32[]{:S(2)}) collective-permute-start(f32[64,128]{1,0:T(8,128)S(1)} %fusion.18), channel_id=1, source_target_pairs={{0,4},{4,8},{8,12},{12,0},{1,5},{5,9},{9,13},{13,1},{2,6},{6,10},{... | collective-permute-start | bytes 98312 | tf_op jit(solution)/shard_map/ppermute | solution.py:20
  76.7 1.7 %collective-permute-done.8 = f32[64,128]{1,0:T(8,128)S(1)} collective-permute-done((f32[64,128]{1,0:T(8,128)S(1)}, f32[64,128]{1,0:T(8,128)S(1)}, u32[]{:S(2)}, u32[]{:S(2)}) %collective-permute-start.8) | collective-permute-done | bytes 32800 | tf_op jit(solution)/shard_map/ppermute | solution.py:20
  79.7 3.2 %collective-permute-start.12 = (bf16[64,128]{1,0:T(8,128)(2,1)S(1)}, bf16[64,128]{1,0:T(8,128)(2,1)S(1)}, u32[]{:S(2)}, u32[]{:S(2)}) collective-permute-start(bf16[64,128]{1,0:T(8,128)(2,1)S(1)} %get-tuple-element.39), channel_id=1, source_target_pairs={{0,3},{1,0},{2,1},{3,2},{4,7},{5,4},{6,5},{7,6},{8,11},{9,8},{10,9... | collective-permute-start | bytes 49160 | tf_op jit(solution)/shard_map/ppermute | solution.py:20
  85.2 2.7 %collective-permute-done.13 = bf16[4,64,128]{2,1,0:T(8,128)(2,1)S(1)} collective-permute-done((bf16[4,64,128]{2,1,0:T(8,128)(2,1)S(1)}, bf16[4,64,128]{2,1,0:T(8,128)(2,1)S(1)}, u32[]{:S(2)}, u32[]{:S(2)}) %collective-permute-start.13) | collective-permute-done | bytes 65568 | tf_op jit(solution)/shard_map/ppermute | solution.py:20
  88.3 2.7 %collective-permute-start.14 = (f32[64,128]{1,0:T(8,128)S(1)}, f32[64,128]{1,0:T(8,128)S(1)}, u32[]{:S(2)}, u32[]{:S(2)}) collective-permute-start(f32[64,128]{1,0:T(8,128)S(1)} %fusion.15), channel_id=1, source_target_pairs={{0,4},{4,8},{8,12},{12,0},{1,5},{5,9},{9,13},{13,1},{2,6},{6,10},{... | collective-permute-start | bytes 98312 | tf_op jit(solution)/shard_map/ppermute | solution.py:20
  92.0 2.1 %collective-permute-done.15 = f32[64,128]{1,0:T(8,128)S(1)} collective-permute-done((f32[64,128]{1,0:T(8,128)S(1)}, f32[64,128]{1,0:T(8,128)S(1)}, u32[]{:S(2)}, u32[]{:S(2)}) %collective-permute-start.15) | collective-permute-done | bytes 32800 | tf_op jit(solution)/shard_map/ppermute | solution.py:20
  95.2 1.8 %collective-permute-start.17 = (bf16[64,128]{1,0:T(8,128)(2,1)S(1)}, bf16[64,128]{1,0:T(8,128)(2,1)S(1)}, u32[]{:S(2)}, u32[]{:S(2)}) collective-permute-start(bf16[64,128]{1,0:T(8,128)(2,1)S(1)} %get-tuple-element.41), channel_id=1, source_target_pairs={{0,1},{1,2},{2,3},{3,0},{4,5},{5,6},{6,7},{7,4},{8,9},{9,10},{10,1... | collective-permute-start | bytes 49160 | tf_op jit(solution)/shard_map/ppermute | solution.py:20
  97.0 1.5 %collective-permute-start.18 = (bf16[64,128]{1,0:T(8,128)(2,1)S(1)}, bf16[64,128]{1,0:T(8,128)(2,1)S(1)}, u32[]{:S(2)}, u32[]{:S(2)}) collective-permute-start(bf16[64,128]{1,0:T(8,128)(2,1)S(1)} %get-tuple-element.41), channel_id=1, source_target_pairs={{0,2},{1,3},{2,0},{3,1},{4,6},{5,7},{6,4},{7,5},{8,10},{9,11},{10,... | collective-permute-start | bytes 49160 | tf_op jit(solution)/shard_map/ppermute | solution.py:20
  101.6 2.7 %collective-permute-done.20 = bf16[4,64,128]{2,1,0:T(8,128)(2,1)S(1)} collective-permute-done((bf16[4,64,128]{2,1,0:T(8,128)(2,1)S(1)}, bf16[4,64,128]{2,1,0:T(8,128)(2,1)S(1)}, u32[]{:S(2)}, u32[]{:S(2)}) %collective-permute-start.20) | collective-permute-done | bytes 65568 | tf_op jit(solution)/shard_map/ppermute | solution.py:20
  104.7 3.2 %collective-permute-start.21 = (f32[64,128]{1,0:T(8,128)S(1)}, f32[64,128]{1,0:T(8,128)S(1)}, u32[]{:S(2)}, u32[]{:S(2)}) collective-permute-start(f32[64,128]{1,0:T(8,128)S(1)} %fusion.12), channel_id=1, source_target_pairs={{0,4},{4,8},{8,12},{12,0},{1,5},{5,9},{9,13},{13,1},{2,6},{6,10},{... | collective-permute-start | bytes 98312 | tf_op jit(solution)/shard_map/ppermute | solution.py:20
  108.9 1.9 %collective-permute-done.22 = f32[64,128]{1,0:T(8,128)S(1)} collective-permute-done((f32[64,128]{1,0:T(8,128)S(1)}, f32[64,128]{1,0:T(8,128)S(1)}, u32[]{:S(2)}, u32[]{:S(2)}) %collective-permute-start.22) | collective-permute-done | bytes 32800 | tf_op jit(solution)/shard_map/ppermute | solution.py:20
  110.8 1.0 collective-permute-done.23
  112.3 2.3 %collective-permute-start.25 = (bf16[64,128]{1,0:T(8,128)(2,1)S(1)}, bf16[64,128]{1,0:T(8,128)(2,1)S(1)}, u32[]{:S(2)}, u32[]{:S(2)}) collective-permute-start(bf16[64,128]{1,0:T(8,128)(2,1)S(1)} %get-tuple-element.43), channel_id=1, source_target_pairs={{0,2},{1,3},{2,0},{3,1},{4,6},{5,7},{6,4},{7,5},{8,10},{9,11},{10,... | collective-permute-start | bytes 49160 | tf_op jit(solution)/shard_map/ppermute | solution.py:20
  115.9 1.0 collective-permute-done.24
  117.7 2.7 %collective-permute-done.27 = bf16[4,64,128]{2,1,0:T(8,128)(2,1)S(1)} collective-permute-done((bf16[4,64,128]{2,1,0:T(8,128)(2,1)S(1)}, bf16[4,64,128]{2,1,0:T(8,128)(2,1)S(1)}, u32[]{:S(2)}, u32[]{:S(2)}) %collective-permute-start.27) | collective-permute-done | bytes 65568 | tf_op jit(solution)/shard_map/ppermute | solution.py:20
  120.7 2.9 %collective-permute-start.28 = (f32[64,128]{1,0:T(8,128)S(1)}, f32[64,128]{1,0:T(8,128)S(1)}, u32[]{:S(2)}, u32[]{:S(2)}) collective-permute-start(f32[64,128]{1,0:T(8,128)S(1)} %fusion.9), channel_id=1, source_target_pairs={{0,4},{4,8},{8,12},{12,0},{1,5},{5,9},{9,13},{13,1},{2,6},{6,10},{... | collective-permute-start | bytes 98312 | tf_op jit(solution)/shard_map/ppermute | solution.py:20
  123.6 1.0 collective-permute-start.29
  124.6 2.2 %collective-permute-done.29 = f32[64,128]{1,0:T(8,128)S(1)} collective-permute-done((f32[64,128]{1,0:T(8,128)S(1)}, f32[64,128]{1,0:T(8,128)S(1)}, u32[]{:S(2)}, u32[]{:S(2)}) %collective-permute-start.29) | collective-permute-done | bytes 32800 | tf_op jit(solution)/shard_map/ppermute | solution.py:20
  126.9 1.1 collective-permute-done.30
  (104 shorter events, 23.4 us)
Async XLA Ops:
  1.7 36.2 %collective-permute-start.6 = (f32[64,256]{1,0:T(8,128)S(1)}, f32[64,256]{1,0:T(8,128)S(1)}, u32[]{:S(2)}, u32[]{:S(2)}) collective-permute-start(f32[64,256]{1,0:T(8,128)S(1)} %pad_maximum_fusion.15), channel_id=1, source_target_pairs={{0,12},{4,0},{8,4},{12,8},{1,13},{5,1},{9,5},{13,9},{2,14},{6,2},{... | collective-permute-start | bytes 196616 | tf_op jit(solution)/shard_map/ppermute | solution.py:20
  1.8 36.1 %collective-permute-start.4 = (f32[64,256]{1,0:T(8,128)S(1)}, f32[64,256]{1,0:T(8,128)S(1)}, u32[]{:S(2)}, u32[]{:S(2)}) collective-permute-start(f32[64,256]{1,0:T(8,128)S(1)} %pad_maximum_fusion.15), channel_id=1, source_target_pairs={{0,4},{4,8},{8,12},{12,0},{1,5},{5,9},{9,13},{13,1},{2,6},{6,10},{... | collective-permute-start | bytes 196616 | tf_op jit(solution)/shard_map/ppermute | solution.py:20
  5.3 30.1 %collective-permute-start = (bf16[64,128]{1,0:T(8,128)(2,1)S(1)}, bf16[64,128]{1,0:T(8,128)(2,1)S(1)}, u32[]{:S(2)}, u32[]{:S(2)}) collective-permute-start(bf16[64,128]{1,0:T(8,128)(2,1)S(1)} %get-tuple-element.38), channel_id=1, source_target_pairs={{0,1},{1,2},{2,3},{3,0},{4,5},{5,6},{6,7},{7,4},{8,9},{9,10},{10,1... | collective-permute-start | bytes 49160 | tf_op jit(solution)/shard_map/ppermute | solution.py:20
  6.6 30.0 %collective-permute-start.1 = (bf16[64,128]{1,0:T(8,128)(2,1)S(1)}, bf16[64,128]{1,0:T(8,128)(2,1)S(1)}, u32[]{:S(2)}, u32[]{:S(2)}) collective-permute-start(bf16[64,128]{1,0:T(8,128)(2,1)S(1)} %get-tuple-element.38), channel_id=1, source_target_pairs={{0,2},{1,3},{2,0},{3,1},{4,6},{5,7},{6,4},{7,5},{8,10},{9,11},{10,... | collective-permute-start | bytes 49160 | tf_op jit(solution)/shard_map/ppermute | solution.py:20
  8.9 27.7 %collective-permute-start.2 = (bf16[64,128]{1,0:T(8,128)(2,1)S(1)}, bf16[64,128]{1,0:T(8,128)(2,1)S(1)}, u32[]{:S(2)}, u32[]{:S(2)}) collective-permute-start(bf16[64,128]{1,0:T(8,128)(2,1)S(1)} %get-tuple-element.38), channel_id=1, source_target_pairs={{0,3},{1,0},{2,1},{3,2},{4,7},{5,4},{6,5},{7,6},{8,11},{9,8},{10,9... | collective-permute-start | bytes 49160 | tf_op jit(solution)/shard_map/ppermute | solution.py:20
  35.4 3.2 %collective-permute-start.5 = (f32[64,256]{1,0:T(8,128)S(1)}, f32[64,256]{1,0:T(8,128)S(1)}, u32[]{:S(2)}, u32[]{:S(2)}) collective-permute-start(f32[64,256]{1,0:T(8,128)S(1)} %pad_maximum_fusion.15), channel_id=1, source_target_pairs={{0,8},{4,12},{8,0},{12,4},{1,9},{5,13},{9,1},{13,5},{2,10},{6,14},... | collective-permute-start | bytes 196616 | tf_op jit(solution)/shard_map/ppermute | solution.py:20
  36.6 3.7 %collective-permute-start.3 = (bf16[4,64,128]{2,1,0:T(8,128)(2,1)S(1)}, bf16[4,64,128]{2,1,0:T(8,128)(2,1)S(1)}, u32[]{:S(2)}, u32[]{:S(2)}) collective-permute-start(bf16[4,64,128]{2,1,0:T(8,128)(2,1)S(1)} %get-tuple-element.36), channel_id=1, source_target_pairs={{0,16},{16,0},{1,17},{17,1},{2,18},{18,2},{3,19},{19,3},{4,20},{20... | collective-permute-start | bytes 196616 | tf_op jit(solution)/shard_map/ppermute | solution.py:20
  40.3 28.8 %all-to-all-start = ((f32[8,64,512]{2,1,0:T(8,128)}), f32[8,64,512]{2,1,0:T(8,128)}, u32[]{:S(2)}, u32[]{:S(2)}) async-start(f32[8,64,512]{2,1,0:T(8,128)} %bitcast.199), calls=%async_computation | async-start | bytes 2097152 | tf_op jit(solution)/shard_map/all_to_all | solution.py:122
  71.6 5.1 %collective-permute-start.7 = (f32[64,128]{1,0:T(8,128)S(1)}, f32[64,128]{1,0:T(8,128)S(1)}, u32[]{:S(2)}, u32[]{:S(2)}) collective-permute-start(f32[64,128]{1,0:T(8,128)S(1)} %fusion.18), channel_id=1, source_target_pairs={{0,4},{4,8},{8,12},{12,0},{1,5},{5,9},{9,13},{13,1},{2,6},{6,10},{... | collective-permute-start | bytes 98312 | tf_op jit(solution)/shard_map/ppermute | solution.py:20
  75.7 2.8 %collective-permute-start.8 = (f32[64,128]{1,0:T(8,128)S(1)}, f32[64,128]{1,0:T(8,128)S(1)}, u32[]{:S(2)}, u32[]{:S(2)}) collective-permute-start(f32[64,128]{1,0:T(8,128)S(1)} %fusion.18), channel_id=1, source_target_pairs={{0,8},{4,12},{8,0},{12,4},{1,9},{5,13},{9,1},{13,5},{2,10},{6,14},... | collective-permute-start | bytes 98312 | tf_op jit(solution)/shard_map/ppermute | solution.py:20
  76.0 3.3 %collective-permute-start.9 = (f32[64,128]{1,0:T(8,128)S(1)}, f32[64,128]{1,0:T(8,128)S(1)}, u32[]{:S(2)}, u32[]{:S(2)}) collective-permute-start(f32[64,128]{1,0:T(8,128)S(1)} %fusion.18), channel_id=1, source_target_pairs={{0,12},{4,0},{8,4},{12,8},{1,13},{5,1},{9,5},{13,9},{2,14},{6,2},{... | collective-permute-start | bytes 98312 | tf_op jit(solution)/shard_map/ppermute | solution.py:20
  79.6 4.4 %collective-permute-start.10 = (bf16[64,128]{1,0:T(8,128)(2,1)S(1)}, bf16[64,128]{1,0:T(8,128)(2,1)S(1)}, u32[]{:S(2)}, u32[]{:S(2)}) collective-permute-start(bf16[64,128]{1,0:T(8,128)(2,1)S(1)} %get-tuple-element.39), channel_id=1, source_target_pairs={{0,1},{1,2},{2,3},{3,0},{4,5},{5,6},{6,7},{7,4},{8,9},{9,10},{10,1... | collective-permute-start | bytes 49160 | tf_op jit(solution)/shard_map/ppermute | solution.py:20
  79.7 4.4 %collective-permute-start.11 = (bf16[64,128]{1,0:T(8,128)(2,1)S(1)}, bf16[64,128]{1,0:T(8,128)(2,1)S(1)}, u32[]{:S(2)}, u32[]{:S(2)}) collective-permute-start(bf16[64,128]{1,0:T(8,128)(2,1)S(1)} %get-tuple-element.39), channel_id=1, source_target_pairs={{0,2},{1,3},{2,0},{3,1},{4,6},{5,7},{6,4},{7,5},{8,10},{9,11},{10,... | collective-permute-start | bytes 49160 | tf_op jit(solution)/shard_map/ppermute | solution.py:20
  79.7 5.0 %collective-permute-start.12 = (bf16[64,128]{1,0:T(8,128)(2,1)S(1)}, bf16[64,128]{1,0:T(8,128)(2,1)S(1)}, u32[]{:S(2)}, u32[]{:S(2)}) collective-permute-start(bf16[64,128]{1,0:T(8,128)(2,1)S(1)} %get-tuple-element.39), channel_id=1, source_target_pairs={{0,3},{1,0},{2,1},{3,2},{4,7},{5,4},{6,5},{7,6},{8,11},{9,8},{10,9... | collective-permute-start | bytes 49160 | tf_op jit(solution)/shard_map/ppermute | solution.py:20
  84.8 3.2 %collective-permute-start.13 = (bf16[4,64,128]{2,1,0:T(8,128)(2,1)S(1)}, bf16[4,64,128]{2,1,0:T(8,128)(2,1)S(1)}, u32[]{:S(2)}, u32[]{:S(2)}) collective-permute-start(bf16[4,64,128]{2,1,0:T(8,128)(2,1)S(1)} %get-tuple-element.34), channel_id=1, source_target_pairs={{0,16},{16,0},{1,17},{17,1},{2,18},{18,2},{3,19},{19,3},{4,20},{20... | collective-permute-start | bytes 196616 | tf_op jit(solution)/shard_map/ppermute | solution.py:20
  88.3 3.7 %collective-permute-start.14 = (f32[64,128]{1,0:T(8,128)S(1)}, f32[64,128]{1,0:T(8,128)S(1)}, u32[]{:S(2)}, u32[]{:S(2)}) collective-permute-start(f32[64,128]{1,0:T(8,128)S(1)} %fusion.15), channel_id=1, source_target_pairs={{0,4},{4,8},{8,12},{12,0},{1,5},{5,9},{9,13},{13,1},{2,6},{6,10},{... | collective-permute-start | bytes 98312 | tf_op jit(solution)/shard_map/ppermute | solution.py:20
  91.0 3.1 %collective-permute-start.15 = (f32[64,128]{1,0:T(8,128)S(1)}, f32[64,128]{1,0:T(8,128)S(1)}, u32[]{:S(2)}, u32[]{:S(2)}) collective-permute-start(f32[64,128]{1,0:T(8,128)S(1)} %fusion.15), channel_id=1, source_target_pairs={{0,8},{4,12},{8,0},{12,4},{1,9},{5,13},{9,1},{13,5},{2,10},{6,14},... | collective-permute-start | bytes 98312 | tf_op jit(solution)/shard_map/ppermute | solution.py:20
  91.6 3.3 %collective-permute-start.16 = (f32[64,128]{1,0:T(8,128)S(1)}, f32[64,128]{1,0:T(8,128)S(1)}, u32[]{:S(2)}, u32[]{:S(2)}) collective-permute-start(f32[64,128]{1,0:T(8,128)S(1)} %fusion.15), channel_id=1, source_target_pairs={{0,12},{4,0},{8,4},{12,8},{1,13},{5,1},{9,5},{13,9},{2,14},{6,2},{... | collective-permute-start | bytes 98312 | tf_op jit(solution)/shard_map/ppermute | solution.py:20
  95.2 4.8 %collective-permute-start.17 = (bf16[64,128]{1,0:T(8,128)(2,1)S(1)}, bf16[64,128]{1,0:T(8,128)(2,1)S(1)}, u32[]{:S(2)}, u32[]{:S(2)}) collective-permute-start(bf16[64,128]{1,0:T(8,128)(2,1)S(1)} %get-tuple-element.41), channel_id=1, source_target_pairs={{0,1},{1,2},{2,3},{3,0},{4,5},{5,6},{6,7},{7,4},{8,9},{9,10},{10,1... | collective-permute-start | bytes 49160 | tf_op jit(solution)/shard_map/ppermute | solution.py:20
  97.0 3.6 %collective-permute-start.18 = (bf16[64,128]{1,0:T(8,128)(2,1)S(1)}, bf16[64,128]{1,0:T(8,128)(2,1)S(1)}, u32[]{:S(2)}, u32[]{:S(2)}) collective-permute-start(bf16[64,128]{1,0:T(8,128)(2,1)S(1)} %get-tuple-element.41), channel_id=1, source_target_pairs={{0,2},{1,3},{2,0},{3,1},{4,6},{5,7},{6,4},{7,5},{8,10},{9,11},{10,... | collective-permute-start | bytes 49160 | tf_op jit(solution)/shard_map/ppermute | solution.py:20
  98.5 2.6 %collective-permute-start.19 = (bf16[64,128]{1,0:T(8,128)(2,1)S(1)}, bf16[64,128]{1,0:T(8,128)(2,1)S(1)}, u32[]{:S(2)}, u32[]{:S(2)}) collective-permute-start(bf16[64,128]{1,0:T(8,128)(2,1)S(1)} %get-tuple-element.41), channel_id=1, source_target_pairs={{0,3},{1,0},{2,1},{3,2},{4,7},{5,4},{6,5},{7,6},{8,11},{9,8},{10,9... | collective-permute-start | bytes 49160 | tf_op jit(solution)/shard_map/ppermute | solution.py:20
  101.1 3.2 %collective-permute-start.20 = (bf16[4,64,128]{2,1,0:T(8,128)(2,1)S(1)}, bf16[4,64,128]{2,1,0:T(8,128)(2,1)S(1)}, u32[]{:S(2)}, u32[]{:S(2)}) collective-permute-start(bf16[4,64,128]{2,1,0:T(8,128)(2,1)S(1)} %get-tuple-element.32), channel_id=1, source_target_pairs={{0,16},{16,0},{1,17},{17,1},{2,18},{18,2},{3,19},{19,3},{4,20},{20... | collective-permute-start | bytes 196616 | tf_op jit(solution)/shard_map/ppermute | solution.py:20
  104.7 4.2 %collective-permute-start.21 = (f32[64,128]{1,0:T(8,128)S(1)}, f32[64,128]{1,0:T(8,128)S(1)}, u32[]{:S(2)}, u32[]{:S(2)}) collective-permute-start(f32[64,128]{1,0:T(8,128)S(1)} %fusion.12), channel_id=1, source_target_pairs={{0,4},{4,8},{8,12},{12,0},{1,5},{5,9},{9,13},{13,1},{2,6},{6,10},{... | collective-permute-start | bytes 98312 | tf_op jit(solution)/shard_map/ppermute | solution.py:20
  107.8 3.0 %collective-permute-start.22 = (f32[64,128]{1,0:T(8,128)S(1)}, f32[64,128]{1,0:T(8,128)S(1)}, u32[]{:S(2)}, u32[]{:S(2)}) collective-permute-start(f32[64,128]{1,0:T(8,128)S(1)} %fusion.12), channel_id=1, source_target_pairs={{0,8},{4,12},{8,0},{12,4},{1,9},{5,13},{9,1},{13,5},{2,10},{6,14},... | collective-permute-start | bytes 98312 | tf_op jit(solution)/shard_map/ppermute | solution.py:20
  108.4 3.3 %collective-permute-start.23 = (f32[64,128]{1,0:T(8,128)S(1)}, f32[64,128]{1,0:T(8,128)S(1)}, u32[]{:S(2)}, u32[]{:S(2)}) collective-permute-start(f32[64,128]{1,0:T(8,128)S(1)} %fusion.12), channel_id=1, source_target_pairs={{0,12},{4,0},{8,4},{12,8},{1,13},{5,1},{9,5},{13,9},{2,14},{6,2},{... | collective-permute-start | bytes 98312 | tf_op jit(solution)/shard_map/ppermute | solution.py:20
  112.0 4.9 %collective-permute-start.24 = (bf16[64,128]{1,0:T(8,128)(2,1)S(1)}, bf16[64,128]{1,0:T(8,128)(2,1)S(1)}, u32[]{:S(2)}, u32[]{:S(2)}) collective-permute-start(bf16[64,128]{1,0:T(8,128)(2,1)S(1)} %get-tuple-element.43), channel_id=1, source_target_pairs={{0,1},{1,2},{2,3},{3,0},{4,5},{5,6},{6,7},{7,4},{8,9},{9,10},{10,1... | collective-permute-start | bytes 49160 | tf_op jit(solution)/shard_map/ppermute | solution.py:20
  112.3 4.6 %collective-permute-start.25 = (bf16[64,128]{1,0:T(8,128)(2,1)S(1)}, bf16[64,128]{1,0:T(8,128)(2,1)S(1)}, u32[]{:S(2)}, u32[]{:S(2)}) collective-permute-start(bf16[64,128]{1,0:T(8,128)(2,1)S(1)} %get-tuple-element.43), channel_id=1, source_target_pairs={{0,2},{1,3},{2,0},{3,1},{4,6},{5,7},{6,4},{7,5},{8,10},{9,11},{10,... | collective-permute-start | bytes 49160 | tf_op jit(solution)/shard_map/ppermute | solution.py:20
  114.6 2.6 %collective-permute-start.26 = (bf16[64,128]{1,0:T(8,128)(2,1)S(1)}, bf16[64,128]{1,0:T(8,128)(2,1)S(1)}, u32[]{:S(2)}, u32[]{:S(2)}) collective-permute-start(bf16[64,128]{1,0:T(8,128)(2,1)S(1)} %get-tuple-element.43), channel_id=1, source_target_pairs={{0,3},{1,0},{2,1},{3,2},{4,7},{5,4},{6,5},{7,6},{8,11},{9,8},{10,9... | collective-permute-start | bytes 49160 | tf_op jit(solution)/shard_map/ppermute | solution.py:20
  117.2 3.2 %collective-permute-start.27 = (bf16[4,64,128]{2,1,0:T(8,128)(2,1)S(1)}, bf16[4,64,128]{2,1,0:T(8,128)(2,1)S(1)}, u32[]{:S(2)}, u32[]{:S(2)}) collective-permute-start(bf16[4,64,128]{2,1,0:T(8,128)(2,1)S(1)} %get-tuple-element.30), channel_id=1, source_target_pairs={{0,16},{16,0},{1,17},{17,1},{2,18},{18,2},{3,19},{19,3},{4,20},{20... | collective-permute-start | bytes 196616 | tf_op jit(solution)/shard_map/ppermute | solution.py:20
  120.7 3.9 %collective-permute-start.28 = (f32[64,128]{1,0:T(8,128)S(1)}, f32[64,128]{1,0:T(8,128)S(1)}, u32[]{:S(2)}, u32[]{:S(2)}) collective-permute-start(f32[64,128]{1,0:T(8,128)S(1)} %fusion.9), channel_id=1, source_target_pairs={{0,4},{4,8},{8,12},{12,0},{1,5},{5,9},{9,13},{13,1},{2,6},{6,10},{... | collective-permute-start | bytes 98312 | tf_op jit(solution)/shard_map/ppermute | solution.py:20
  123.6 3.2 %collective-permute-start.29 = (f32[64,128]{1,0:T(8,128)S(1)}, f32[64,128]{1,0:T(8,128)S(1)}, u32[]{:S(2)}, u32[]{:S(2)}) collective-permute-start(f32[64,128]{1,0:T(8,128)S(1)} %fusion.9), channel_id=1, source_target_pairs={{0,8},{4,12},{8,0},{12,4},{1,9},{5,13},{9,1},{13,5},{2,10},{6,14},... | collective-permute-start | bytes 98312 | tf_op jit(solution)/shard_map/ppermute | solution.py:20
  124.6 3.3 %collective-permute-start.30 = (f32[64,128]{1,0:T(8,128)S(1)}, f32[64,128]{1,0:T(8,128)S(1)}, u32[]{:S(2)}, u32[]{:S(2)}) collective-permute-start(f32[64,128]{1,0:T(8,128)S(1)} %fusion.9), channel_id=1, source_target_pairs={{0,12},{4,0},{8,4},{12,8},{1,13},{5,1},{9,5},{13,9},{2,14},{6,2},{... | collective-permute-start | bytes 98312 | tf_op jit(solution)/shard_map/ppermute | solution.py:20
  (4 other events, 36.5 us)
